TPU v7x, 512 devices: a whole 4x4x16 slice. The times are simulated.
512 devices in a mesh: gx: 32 (over z_hi, x, core), gy: 4 (over y), gz: 4 (over z_lo).
Axes of the slice: x: 4, y: 4, z: 16 (z_hi: 4, z_lo: 4; z = z_hi * 4 + z_lo), core: 2. Of those that a mesh axis runs over, the one named last changes fastest.
Arguments:
- level_set: float32 [1024, 128, 512], P('gx', 'gy', 'gz'), may hold values from -6 to 6
- velocity: bfloat16 [3, 1024, 128, 512], P(None, 'gx', 'gy', 'gz'), may hold values from -1 to 1
- active_brick: int32 [32, 4, 4], P('gx', 'gy', 'gz'), may hold values 0 or 1
- depth_order: int32 [4], replicated, may hold values from 0 to 3, as said below
Outputs:
- level_out: float32 [1024, 128, 512], P('gx', 'gy', 'gz')
- image: float32 [4, 2048, 256], P(None, ('gx', 'gz'), 'gy')
Inputs may be any that keep to these rules, and one draw needn't show every extreme that they name: `depth_order`: either 0, 1, .. in slab order or the reverse.
All inputs are finite; a program needn't handle non-finite values. No bound on the sum of `active_brick` on one device may be relied on, other than what follows from the above.
Results may differ from a plain program's by a relative error of at most 0.0003.
Values may be sent and summed in bfloat16 or wider, within the bound.
No kernel may reach another device: no remote copies, remote signals or barrier semaphores. Data moves between devices by JAX's collectives and lax.ppermute only.
A program may use at most 64 MiB of HBM per device.

v0:
```python
import jax
import jax.numpy as jnp
from jax import lax
from jax.sharding import PartitionSpec as P

CZ = 128


time_step = 0.4
weno_floor = 1e-06


def extended(x, sides, width):
    for axis, dim in sides:
        size, length = (lax.axis_size(axis), x.shape[dim])
        up = [(i, (i + 1) % size) for i in range(size)]
        down = [(j, i) for i, j in up]
        last = lax.slice_in_dim(x, length - width, length, axis=dim)
        initial = lax.slice_in_dim(x, 0, width, axis=dim)
        before = lax.ppermute(last, axis, up)
        after = lax.ppermute(initial, axis, down)
        x = jnp.concatenate([before, x, after], axis=dim)
    return x


def square(operand):
    return operand * operand


def weno_value(diff_one, diff_two, diff_three, diff_four, diff_five):
    candidate_one = diff_one / 3.0 - 7.0 * diff_two / 6.0 + 11.0 * diff_three / 6.0
    candidate_two = -diff_two / 6.0 + 5.0 * diff_three / 6.0 + diff_four / 3.0
    candidate_three = diff_three / 3.0 + 5.0 * diff_four / 6.0 - diff_five / 6.0
    smooth_one = 13.0 / 12.0 * square(diff_one - 2.0 * diff_two + diff_three) + 0.25 * square(
        diff_one - 4.0 * diff_two + 3.0 * diff_three
    )
    smooth_two = 13.0 / 12.0 * square(diff_two - 2.0 * diff_three + diff_four) + 0.25 * square(
        diff_two - diff_four
    )
    smooth_three = 13.0 / 12.0 * square(diff_three - 2.0 * diff_four + diff_five) + 0.25 * square(
        3.0 * diff_three - 4.0 * diff_four + diff_five
    )
    weight_one = 0.1 / square(weno_floor + smooth_one)
    weight_two = 0.6 / square(weno_floor + smooth_two)
    weight_three = 0.3 / square(weno_floor + smooth_three)
    return (
        weight_one * candidate_one + weight_two * candidate_two + weight_three * candidate_three
    ) / (weight_one + weight_two + weight_three)


def window(padded, axis_dim, offset):
    slicing = [slice(3, extent - 3) for extent in padded.shape]
    length = padded.shape[axis_dim] - 6
    slicing[axis_dim] = slice(3 + offset, 3 + offset + length)
    return padded[tuple(slicing)]


def local_rate(padded, velocity_window):
    summed = jnp.zeros(velocity_window.shape[1:], jnp.float32)
    for axis_dim in range(3):
        jump_list = [
            window(padded, axis_dim, offset) - window(padded, axis_dim, offset - 1)
            for offset in range(-2, 4)
        ]
        from_left = weno_value(jump_list[0], jump_list[1], jump_list[2], jump_list[3], jump_list[4])
        from_right = weno_value(
            jump_list[5], jump_list[4], jump_list[3], jump_list[2], jump_list[1]
        )
        speed_axis = velocity_window[axis_dim].astype(jnp.float32)
        summed = (
            summed
            + jnp.maximum(speed_axis, 0.0) * from_left
            + jnp.minimum(speed_axis, 0.0) * from_right
        )
    return -summed


def shade(samples, alive, ascending):
    opacity = alive * (2.0 / CZ) / (1.0 + 4.0 * samples * samples)
    log_clear = jnp.log1p(-opacity)
    depth = jnp.arange(CZ)
    ahead = jnp.where(
        ascending, depth[:, None] < depth[None, :], depth[:, None] > depth[None, :]
    ).astype(jnp.float32)
    flat_logs = log_clear.reshape(-1, CZ)
    before = jnp.dot(flat_logs, ahead, precision=lax.Precision.HIGHEST).reshape(log_clear.shape)
    weight = jnp.exp(before) * opacity
    bright = jnp.tanh(samples)
    red = jnp.sum(weight * (0.5 + 0.5 * bright), -1)
    green = jnp.sum(weight * (0.5 - 0.5 * bright), -1)
    blue = jnp.sum(weight / (1.0 + samples * samples), -1)
    clear = jnp.exp(jnp.sum(log_clear, -1))
    return jnp.stack([red, green, blue, clear])


def alternate(grid_pairs):
    row_list = [jnp.stack(pixel_pair, -1) for pixel_pair in grid_pairs]
    joined = jnp.stack(row_list, -3)
    joined_shape = joined.shape
    return joined.reshape(joined_shape[:-4] + (joined_shape[-4] * 2, joined_shape[-2] * 2))


def over(front_part, back_part):
    colour = front_part[:3] + front_part[3:] * back_part[:3]
    clear = front_part[3:] * back_part[3:]
    return jnp.concatenate([colour, clear], 0)


def shards(level_set, velocity, active_brick, depth_order):

    def section_rate(level_field):
        padded = extended(level_field, (("gx", 0), ("gy", 1), ("gz", 2)), 3)
        return local_rate(padded, velocity)

    section_one = level_set + time_step * section_rate(level_set)
    section_two = 0.75 * level_set + 0.25 * (section_one + time_step * section_rate(section_one))
    advanced = level_set / 3.0 + 2.0 / 3.0 * (section_two + time_step * section_rate(section_two))
    alive = active_brick[0, 0, 0] > 0
    level_out = jnp.where(alive, advanced, level_set)
    alive_float = alive.astype(jnp.float32)
    group = lax.axis_size("gz")
    ascending = depth_order[0] < depth_order[group - 1]
    rim = extended(level_out.astype(jnp.bfloat16), (("gx", 0), ("gy", 1)), 1).astype(
        level_out.dtype
    )
    left_x = 0.75 * rim[1:-1] + 0.25 * rim[:-2]
    right_x = 0.75 * rim[1:-1] + 0.25 * rim[2:]
    grid_pairs = []
    for along_x in (left_x, right_x):
        pair_list = []
        for neighbour in (along_x[:, :-2], along_x[:, 2:]):
            samples = 0.75 * along_x[:, 1:-1] + 0.25 * neighbour
            pair_list.append(shade(samples, alive_float, ascending))
        grid_pairs.append(pair_list)
    slab_image = alternate(grid_pairs)
    rows_each = slab_image.shape[1] // group
    columns = slab_image.shape[2]
    pieces = slab_image.reshape(4, group, rows_each, columns)
    received = lax.all_to_all(pieces, "gz", split_axis=1, concat_axis=1, tiled=True)
    blended = jnp.concatenate(
        [
            jnp.zeros((3, rows_each, columns), jnp.float32),
            jnp.ones((1, rows_each, columns), jnp.float32),
        ],
        0,
    )
    for rank_value in range(group):
        chooser = (depth_order == rank_value).astype(jnp.float32)
        piece_now = jnp.einsum("s,csij->cij", chooser, received, precision=lax.Precision.HIGHEST)
        blended = over(blended, piece_now)
    image = jnp.concatenate([blended[:3], 1.0 - blended[3:]], 0)
    return (level_out, image)


def solution(mesh):
    placed = (P("gx", "gy", "gz"), P(None, "gx", "gy", "gz"), P("gx", "gy", "gz"), P())
    return jax.shard_map(
        shards,
        mesh=mesh,
        in_specs=placed,
        out_specs=(P("gx", "gy", "gz"), P(None, ("gx", "gz"), "gy")),
        check_vma=False,
    )
```

profile of v0, /device:TPU:8, one launch (start us, length us, event | category | flops | bytes accessed | tf_op | source)
XLA Modules:
  0.0 195.8 jit_solution(901559053685275974)
XLA Ops:
  1.5 1.9 collective-permute-start
  3.4 14.4 %collective-permute-start.1 = (f32[3,32,128]{2,1,0:T(8,128)S(1)}, f32[3,32,128]{2,1,0:T(8,128)S(1)}, u32[]{:S(2)}, u32[]{:S(2)}) collective-permute-start(f32[3,32,128]{2,1,0:T(8,128)S(1)} %get-tuple-element.55), channel_id=1, source_target_pairs={{16,0},{32,16},{48,32},{64,48},{80,64},{96,80},{112,96},{128,112},... | collective-permute-start | bytes 147464 | tf_op jit(solution)/shard_map/ppermute | solution.py:21
  17.8 1.2 constant_dynamic-update-slice_fusion
  19.5 4.3 %collective-permute-start.3 = (f32[38,3,128]{2,1,0:T(4,128)S(1)}, f32[38,3,128]{2,1,0:T(4,128)S(1)}, u32[]{:S(2)}, u32[]{:S(2)}) collective-permute-start(f32[38,3,128]{2,1,0:T(4,128)S(1)} %get-tuple-element.47), channel_id=1, source_target_pairs={{4,0},{8,4},{12,8},{0,12},{5,1},{9,5},{13,9},{1,13},{6,2},{10,6},{... | collective-permute-start | bytes 175112 | tf_op jit(solution)/shard_map/ppermute | solution.py:21
  23.8 1.9 collective-permute-start.2
  25.8 4.3 %collective-permute-done.2 = f32[38,3,128]{2,1,0:T(4,128)S(1)} collective-permute-done((f32[38,3,128]{2,1,0:T(4,128)S(1)}, f32[38,3,128]{2,1,0:T(4,128)S(1)}, u32[]{:S(2)}, u32[]{:S(2)}) %collective-permute-start.2) | collective-permute-done | bytes 58400 | tf_op jit(solution)/shard_map/ppermute | solution.py:20
  31.5 2.0 %collective-permute-start.4 = (f32[38,38,3]{1,0,2:T(8,128)}, f32[38,38,3]{1,0,2:T(8,128)S(1)}, u32[]{:S(2)}, u32[]{:S(2)}) collective-permute-start(f32[38,38,3]{1,0,2:T(8,128)} %copy.7), channel_id=1, source_target_pairs={{0,1},{1,2},{2,3},{3,0},{4,5},{5,6},{6,7},{7,4},{8,9},{9,10},{10,1... | collective-permute-start | bytes 51992 | tf_op jit(solution)/shard_map/ppermute | solution.py:20
  33.8 5.6 %collective-permute-start.5 = (f32[38,38,3]{1,0,2:T(8,128)S(1)}, f32[38,38,3]{1,0,2:T(8,128)S(1)}, u32[]{:S(2)}, u32[]{:S(2)}) collective-permute-start(f32[38,38,3]{1,0,2:T(8,128)S(1)} %copy.9), channel_id=1, source_target_pairs={{1,0},{2,1},{3,2},{0,3},{5,4},{6,5},{7,6},{4,7},{9,8},{10,9},{11,1... | collective-permute-start | bytes 51992 | tf_op jit(solution)/shard_map/ppermute | solution.py:21
  40.0 1.3 collective-permute-done.5
  41.3 1.3 copy.10
  42.6 2.0 %maximum_maximum_fusion = (f32[38,38,131]{2,1,0:T(8,128)S(1)}, f32[38,38,131]{2,1,0:T(8,128)S(1)}) fusion(f32[38,3,128]{2,1,0:T(4,128)S(1)} %collective-permute-done.3, f32[38,32,128]{2,1,0:T(8,128)S(1)} %get-tuple-element.67, f32[38,3,128]{2,1,0:T(4,128)S(1)} %collective-permute-done.2, f32[38,38,3]{2,1,0:T(8,128)S(1)} %copy.8, f32[38,38,3]{2,1,0:T(8,128)} %copy.10), kind=kLoop, calls=%fused_computation | loop fusion | flops 1134984 | bytes 2287296 | tf_op jit(solution)/shard_map/concatenate | solution.py:22
  44.6 8.4 %fusion.27 = f32[32,32,128]{2,1,0:T(8,128)S(1)} fusion(f32[32,32,128]{2,1,0:T(8,128)S(1)} %copy-done, f32[38,38,131]{2,1,0:T(8,128)S(1)} %get-tuple-element.29, f32[38,38,131]{2,1,0:T(8,128)S(1)} %get-tuple-element.28, f32[38,3,128]{2,1,0:T(4,128)S(1)} %collective-permute-done.3, f32[38,32,128]{2,1,0:T(8,128)S(1)} %get-tuple-element.67, ...), kind=kLoop, calls=%fused_computation.81 | loop fusion | flops 54919168 | bytes 8865792 | tf_op jit(solution)/shard_map/add | solution.py:115
  53.0 7.5 %collective-permute-start.7 = (f32[3,32,128]{2,1,0:T(8,128)S(1)}, f32[3,32,128]{2,1,0:T(8,128)S(1)}, u32[]{:S(2)}, u32[]{:S(2)}) collective-permute-start(f32[3,32,128]{2,1,0:T(8,128)S(1)} %get-tuple-element.51), channel_id=1, source_target_pairs={{16,0},{32,16},{48,32},{64,48},{80,64},{96,80},{112,96},{128,112},... | collective-permute-start | bytes 147464 | tf_op jit(solution)/shard_map/ppermute | solution.py:21
  60.5 1.9 collective-permute-start.6
  62.5 9.5 %collective-permute-done.6 = f32[3,32,128]{2,1,0:T(8,128)S(1)} collective-permute-done((f32[3,32,128]{2,1,0:T(8,128)S(1)}, f32[3,32,128]{2,1,0:T(8,128)S(1)}, u32[]{:S(2)}, u32[]{:S(2)}) %collective-permute-start.6) | collective-permute-done | bytes 49184 | tf_op jit(solution)/shard_map/ppermute | solution.py:20
  72.0 3.8 %collective-permute-start.9 = (f32[38,3,128]{2,1,0:T(4,128)S(1)}, f32[38,3,128]{2,1,0:T(4,128)S(1)}, u32[]{:S(2)}, u32[]{:S(2)}) collective-permute-start(f32[38,3,128]{2,1,0:T(4,128)S(1)} %get-tuple-element.45), channel_id=1, source_target_pairs={{4,0},{8,4},{12,8},{0,12},{5,1},{9,5},{13,9},{1,13},{6,2},{10,6},{... | collective-permute-start | bytes 175112 | tf_op jit(solution)/shard_map/ppermute | solution.py:21
  75.8 2.0 %collective-permute-start.8 = (f32[38,3,128]{2,1,0:T(4,128)S(1)}, f32[38,3,128]{2,1,0:T(4,128)S(1)}, u32[]{:S(2)}, u32[]{:S(2)}) collective-permute-start(f32[38,3,128]{2,1,0:T(4,128)S(1)} %get-tuple-element.44), channel_id=1, source_target_pairs={{0,4},{4,8},{8,12},{12,0},{1,5},{5,9},{9,13},{13,1},{2,6},{6,10},{... | collective-permute-start | bytes 175112 | tf_op jit(solution)/shard_map/ppermute | solution.py:20
  78.3 3.8 %collective-permute-done.8 = f32[38,3,128]{2,1,0:T(4,128)S(1)} collective-permute-done((f32[38,3,128]{2,1,0:T(4,128)S(1)}, f32[38,3,128]{2,1,0:T(4,128)S(1)}, u32[]{:S(2)}, u32[]{:S(2)}) %collective-permute-start.8) | collective-permute-done | bytes 58400 | tf_op jit(solution)/shard_map/ppermute | solution.py:20
  82.9 2.5 %collective-permute-start.10 = (f32[38,38,3]{1,0,2:T(8,128)S(1)}, f32[38,38,3]{1,0,2:T(8,128)S(1)}, u32[]{:S(2)}, u32[]{:S(2)}) collective-permute-start(f32[38,38,3]{1,0,2:T(8,128)S(1)} %copy.11), channel_id=1, source_target_pairs={{0,1},{1,2},{2,3},{3,0},{4,5},{5,6},{6,7},{7,4},{8,9},{9,10},{10,1... | collective-permute-start | bytes 51992 | tf_op jit(solution)/shard_map/ppermute | solution.py:20
  85.8 5.2 %collective-permute-start.11 = (f32[38,38,3]{1,0,2:T(8,128)S(1)}, f32[38,38,3]{1,0,2:T(8,128)S(1)}, u32[]{:S(2)}, u32[]{:S(2)}) collective-permute-start(f32[38,38,3]{1,0,2:T(8,128)S(1)} %copy.13), channel_id=1, source_target_pairs={{1,0},{2,1},{3,2},{0,3},{5,4},{6,5},{7,6},{4,7},{9,8},{10,9},{11,1... | collective-permute-start | bytes 51992 | tf_op jit(solution)/shard_map/ppermute | solution.py:21
  91.1 1.3 copy.12
  92.8 1.3 copy.14
  94.1 2.2 %maximum_maximum_fusion.1 = (f32[38,38,131]{2,1,0:T(8,128)S(1)}, f32[38,38,131]{2,1,0:T(8,128)S(1)}) fusion(f32[38,3,128]{2,1,0:T(4,128)S(1)} %collective-permute-done.9, f32[3,32,128]{2,1,0:T(8,128)S(1)} %collective-permute-done.7, f32[32,32,128]{2,1,0:T(8,128)S(1)} %fusion.27, f32[3,32,128]{2,1,0:T(8,128)S(1)} %collective-permute-done.6, ...), kind=kLoop, calls=%fused_computation.2 | loop fusion | flops 1891640 | bytes 2287296 | tf_op jit(solution)/shard_map/concatenate | solution.py:22
  96.2 8.6 %fusion.37 = f32[32,32,128]{2,1,0:T(8,128)S(1)} fusion(f32[32,32,128]{2,1,0:T(8,128)S(1)} %fusion.27, f32[38,38,131]{2,1,0:T(8,128)S(1)} %get-tuple-element.25, f32[38,38,131]{2,1,0:T(8,128)S(1)} %get-tuple-element.24, f32[38,35,128]{2,1,0:T(8,128)S(1)} %get-tuple-element.43, f32[38,35,128]{2,1,0:T(8,128)S(1)} %get-tuple-element.42, ...), kind=kLoop, calls=%fused_computation.91 | loop fusion | flops 55312384 | bytes 8749056 | tf_op jit(solution)/shard_map/add | solution.py:116
  104.9 1.9 collective-permute-start.13
  106.8 2.4 %collective-permute-start.12 = (f32[3,32,128]{2,1,0:T(8,128)S(1)}, f32[3,32,128]{2,1,0:T(8,128)S(1)}, u32[]{:S(2)}, u32[]{:S(2)}) collective-permute-start(f32[3,32,128]{2,1,0:T(8,128)S(1)} %get-tuple-element.48), channel_id=1, source_target_pairs={{0,16},{16,32},{32,48},{48,64},{64,80},{80,96},{96,112},{112,128},... | collective-permute-start | bytes 147464 | tf_op jit(solution)/shard_map/ppermute | solution.py:20
  109.2 9.1 %collective-permute-done.12 = f32[3,32,128]{2,1,0:T(8,128)S(1)} collective-permute-done((f32[3,32,128]{2,1,0:T(8,128)S(1)}, f32[3,32,128]{2,1,0:T(8,128)S(1)}, u32[]{:S(2)}, u32[]{:S(2)}) %collective-permute-start.12) | collective-permute-done | bytes 49184 | tf_op jit(solution)/shard_map/ppermute | solution.py:20
  118.3 3.1 %collective-permute-start.15 = (f32[38,3,128]{2,1,0:T(4,128)S(1)}, f32[38,3,128]{2,1,0:T(4,128)S(1)}, u32[]{:S(2)}, u32[]{:S(2)}) collective-permute-start(f32[38,3,128]{2,1,0:T(4,128)S(1)} %get-tuple-element.41), channel_id=1, source_target_pairs={{4,0},{8,4},{12,8},{0,12},{5,1},{9,5},{13,9},{1,13},{6,2},{10,6},{... | collective-permute-start | bytes 175112 | tf_op jit(solution)/shard_map/ppermute | solution.py:21
  121.5 2.7 %collective-permute-start.14 = (f32[38,3,128]{2,1,0:T(4,128)S(1)}, f32[38,3,128]{2,1,0:T(4,128)S(1)}, u32[]{:S(2)}, u32[]{:S(2)}) collective-permute-start(f32[38,3,128]{2,1,0:T(4,128)S(1)} %get-tuple-element.40), channel_id=1, source_target_pairs={{0,4},{4,8},{8,12},{12,0},{1,5},{5,9},{9,13},{13,1},{2,6},{6,10},{... | collective-permute-start | bytes 175112 | tf_op jit(solution)/shard_map/ppermute | solution.py:20
  124.9 2.9 %collective-permute-done.14 = f32[38,3,128]{2,1,0:T(4,128)S(1)} collective-permute-done((f32[38,3,128]{2,1,0:T(4,128)S(1)}, f32[38,3,128]{2,1,0:T(4,128)S(1)}, u32[]{:S(2)}, u32[]{:S(2)}) %collective-permute-start.14) | collective-permute-done | bytes 58400 | tf_op jit(solution)/shard_map/ppermute | solution.py:20
  128.5 3.8 %collective-permute-start.16 = (f32[38,38,3]{1,0,2:T(8,128)S(1)}, f32[38,38,3]{1,0,2:T(8,128)S(1)}, u32[]{:S(2)}, u32[]{:S(2)}) collective-permute-start(f32[38,38,3]{1,0,2:T(8,128)S(1)} %copy.15), channel_id=1, source_target_pairs={{0,1},{1,2},{2,3},{3,0},{4,5},{5,6},{6,7},{7,4},{8,9},{9,10},{10,1... | collective-permute-start | bytes 51992 | tf_op jit(solution)/shard_map/ppermute | solution.py:20
  132.8 4.9 %collective-permute-start.17 = (f32[38,38,3]{1,0,2:T(8,128)S(1)}, f32[38,38,3]{1,0,2:T(8,128)S(1)}, u32[]{:S(2)}, u32[]{:S(2)}) collective-permute-start(f32[38,38,3]{1,0,2:T(8,128)S(1)} %copy.17), channel_id=1, source_target_pairs={{1,0},{2,1},{3,2},{0,3},{5,4},{6,5},{7,6},{4,7},{9,8},{10,9},{11,1... | collective-permute-start | bytes 51992 | tf_op jit(solution)/shard_map/ppermute | solution.py:21
  137.8 1.3 copy.16
  139.3 1.3 copy.18
  140.6 2.2 %maximum_maximum_fusion.2 = (f32[38,38,131]{2,1,0:T(8,128)S(1)}, f32[38,38,131]{2,1,0:T(8,128)S(1)}) fusion(f32[38,3,128]{2,1,0:T(4,128)S(1)} %collective-permute-done.15, f32[3,32,128]{2,1,0:T(8,128)S(1)} %collective-permute-done.13, f32[32,32,128]{2,1,0:T(8,128)S(1)} %fusion.37, f32[3,32,128]{2,1,0:T(8,128)S(1)} %collective-permute-done.12, ...), kind=kLoop, calls=%fused_computation.4 | loop fusion | flops 1891640 | bytes 2287296 | tf_op jit(solution)/shard_map/concatenate | solution.py:22
  142.8 9.4 %fusion.219 = (bf16[32,32,128]{2,1,0:T(8,128)(2,1)S(1)}, f32[32,32,128]{2,1,0:T(8,128)}) fusion(f32[32,32,128]{2,1,0:T(8,128)S(1)} %copy-done, f32[32,32,128]{2,1,0:T(8,128)S(1)} %fusion.37, f32[38,38,131]{2,1,0:T(8,128)S(1)} %get-tuple-element.21, f32[38,38,131]{2,1,0:T(8,128)S(1)} %get-tuple-element.20, bf16[3,32,32,128]{3,2,1,0:T(8,128)(2,1)S(1)} %copy-done.3, ...), kind=kLoop, calls=%fused_computation.358 | loop fusion | flops 55574528 | bytes 9011201 | tf_op jit(solution)/shard_map/convert_element_type | solution.py:123
  152.1 1.9 collective-permute-start.19
  154.0 2.4 %collective-permute-start.18 = (bf16[1,32,128]{2,1,0:T(8,128)(2,1)S(1)}, bf16[1,32,128]{2,1,0:T(8,128)(2,1)S(1)}, u32[]{:S(2)}, u32[]{:S(2)}) collective-permute-start(bf16[1,32,128]{2,1,0:T(8,128)(2,1)S(1)} %get-tuple-element.59), channel_id=1, source_target_pairs={{0,16},{16,32},{32,48},{48,64},{64,80},{80,96},{96,112},{112,128},... | collective-permute-start | bytes 24584 | tf_op jit(solution)/shard_map/ppermute | solution.py:20
  156.5 8.6 %collective-permute-done.18 = bf16[1,32,128]{2,1,0:T(8,128)(2,1)S(1)} collective-permute-done((bf16[1,32,128]{2,1,0:T(8,128)(2,1)S(1)}, bf16[1,32,128]{2,1,0:T(8,128)(2,1)S(1)}, u32[]{:S(2)}, u32[]{:S(2)}) %collective-permute-start.18) | collective-permute-done | bytes 8224 | tf_op jit(solution)/shard_map/ppermute | solution.py:20
  165.1 3.1 %collective-permute-start.21 = (bf16[34,1,128]{2,1,0:T(2,128)(2,1)S(1)}, bf16[34,1,128]{2,1,0:T(2,128)(2,1)S(1)}, u32[]{:S(2)}, u32[]{:S(2)}) collective-permute-start(bf16[34,1,128]{2,1,0:T(2,128)(2,1)S(1)} %get-tuple-element.58), channel_id=1, source_target_pairs={{4,0},{8,4},{12,8},{0,12},{5,1},{9,5},{13,9},{1,13},{6,2},{10,6},{... | collective-permute-start | bytes 26120 | tf_op jit(solution)/shard_map/ppermute | solution.py:21
  168.2 2.7 %collective-permute-start.20 = (bf16[34,1,128]{2,1,0:T(2,128)(2,1)S(1)}, bf16[34,1,128]{2,1,0:T(2,128)(2,1)S(1)}, u32[]{:S(2)}, u32[]{:S(2)}) collective-permute-start(bf16[34,1,128]{2,1,0:T(2,128)(2,1)S(1)} %get-tuple-element.57), channel_id=1, source_target_pairs={{0,4},{4,8},{8,12},{12,0},{1,5},{5,9},{9,13},{13,1},{2,6},{6,10},{... | collective-permute-start | bytes 26120 | tf_op jit(solution)/shard_map/ppermute | solution.py:20
  172.7 1.1 collective-permute-done.20
  174.5 1.2 multiply_reduce_fusion.1
  175.6 1.2 multiply_reduce_fusion.3
  176.8 1.2 multiply_reduce_fusion.5
  178.0 1.2 multiply_reduce_fusion.7
  179.3 1.3 copy.19
  181.4 11.0 %all_to_all.5 = f32[4,1,4096]{2,1,0:T(1,128)S(1)} all-to-all(f32[4,1,4096]{2,1,0:T(1,128)S(1)} %reshape.79), channel_id=1, replica_groups=mesh['gx'=32,'gy'=4,'gz'=4] {'gz'}, dimensions={0} | all-to-all | bytes 131072 | tf_op jit(solution)/shard_map/all_to_all | solution.py:139
  (76 shorter events, 12.9 us)
Async XLA Ops:
  1.5 16.4 %collective-permute-start = (f32[3,32,128]{2,1,0:T(8,128)S(1)}, f32[3,32,128]{2,1,0:T(8,128)S(1)}, u32[]{:S(2)}, u32[]{:S(2)}) collective-permute-start(f32[3,32,128]{2,1,0:T(8,128)S(1)} %get-tuple-element.56), channel_id=1, source_target_pairs={{0,16},{16,32},{32,48},{48,64},{64,80},{80,96},{96,112},{112,128},... | collective-permute-start | bytes 147464 | tf_op jit(solution)/shard_map/ppermute | solution.py:20
  3.4 16.1 %collective-permute-start.1 = (f32[3,32,128]{2,1,0:T(8,128)S(1)}, f32[3,32,128]{2,1,0:T(8,128)S(1)}, u32[]{:S(2)}, u32[]{:S(2)}) collective-permute-start(f32[3,32,128]{2,1,0:T(8,128)S(1)} %get-tuple-element.55), channel_id=1, source_target_pairs={{16,0},{32,16},{48,32},{64,48},{80,64},{96,80},{112,96},{128,112},... | collective-permute-start | bytes 147464 | tf_op jit(solution)/shard_map/ppermute | solution.py:21
  19.5 6.3 %collective-permute-start.3 = (f32[38,3,128]{2,1,0:T(4,128)S(1)}, f32[38,3,128]{2,1,0:T(4,128)S(1)}, u32[]{:S(2)}, u32[]{:S(2)}) collective-permute-start(f32[38,3,128]{2,1,0:T(4,128)S(1)} %get-tuple-element.47), channel_id=1, source_target_pairs={{4,0},{8,4},{12,8},{0,12},{5,1},{9,5},{13,9},{1,13},{6,2},{10,6},{... | collective-permute-start | bytes 175112 | tf_op jit(solution)/shard_map/ppermute | solution.py:21
  23.8 6.3 %collective-permute-start.2 = (f32[38,3,128]{2,1,0:T(4,128)S(1)}, f32[38,3,128]{2,1,0:T(4,128)S(1)}, u32[]{:S(2)}, u32[]{:S(2)}) collective-permute-start(f32[38,3,128]{2,1,0:T(4,128)S(1)} %get-tuple-element.46), channel_id=1, source_target_pairs={{0,4},{4,8},{8,12},{12,0},{1,5},{5,9},{9,13},{13,1},{2,6},{6,10},{... | collective-permute-start | bytes 175112 | tf_op jit(solution)/shard_map/ppermute | solution.py:20
  31.5 8.1 %collective-permute-start.4 = (f32[38,38,3]{1,0,2:T(8,128)}, f32[38,38,3]{1,0,2:T(8,128)S(1)}, u32[]{:S(2)}, u32[]{:S(2)}) collective-permute-start(f32[38,38,3]{1,0,2:T(8,128)} %copy.7), channel_id=1, source_target_pairs={{0,1},{1,2},{2,3},{3,0},{4,5},{5,6},{6,7},{7,4},{8,9},{9,10},{10,1... | collective-permute-start | bytes 51992 | tf_op jit(solution)/shard_map/ppermute | solution.py:20
  33.8 7.5 %collective-permute-start.5 = (f32[38,38,3]{1,0,2:T(8,128)S(1)}, f32[38,38,3]{1,0,2:T(8,128)S(1)}, u32[]{:S(2)}, u32[]{:S(2)}) collective-permute-start(f32[38,38,3]{1,0,2:T(8,128)S(1)} %copy.9), channel_id=1, source_target_pairs={{1,0},{2,1},{3,2},{0,3},{5,4},{6,5},{7,6},{4,7},{9,8},{10,9},{11,1... | collective-permute-start | bytes 51992 | tf_op jit(solution)/shard_map/ppermute | solution.py:21
  42.6 2.0 %copy-start = (f32[32,32,128]{2,1,0:T(8,128)S(1)}, f32[32,32,128]{2,1,0:T(8,128)}, u32[]{:S(2)}) copy-start(f32[32,32,128]{2,1,0:T(8,128)} %param.4) | copy-start | bytes 1572868
  42.6 2.0 %copy-start.1 = (bf16[3,32,32,128]{3,2,1,0:T(8,128)(2,1)S(1)}, bf16[3,32,32,128]{3,2,1,0:T(8,128)(2,1)}, u32[]{:S(2)}) copy-start(bf16[3,32,32,128]{3,2,1,0:T(8,128)(2,1)} %param.5) | copy-start | bytes 2359300
  53.0 9.5 %collective-permute-start.7 = (f32[3,32,128]{2,1,0:T(8,128)S(1)}, f32[3,32,128]{2,1,0:T(8,128)S(1)}, u32[]{:S(2)}, u32[]{:S(2)}) collective-permute-start(f32[3,32,128]{2,1,0:T(8,128)S(1)} %get-tuple-element.51), channel_id=1, source_target_pairs={{16,0},{32,16},{48,32},{64,48},{80,64},{96,80},{112,96},{128,112},... | collective-permute-start | bytes 147464 | tf_op jit(solution)/shard_map/ppermute | solution.py:21
  60.5 11.4 %collective-permute-start.6 = (f32[3,32,128]{2,1,0:T(8,128)S(1)}, f32[3,32,128]{2,1,0:T(8,128)S(1)}, u32[]{:S(2)}, u32[]{:S(2)}) collective-permute-start(f32[3,32,128]{2,1,0:T(8,128)S(1)} %get-tuple-element.50), channel_id=1, source_target_pairs={{0,16},{16,32},{32,48},{48,64},{64,80},{80,96},{96,112},{112,128},... | collective-permute-start | bytes 147464 | tf_op jit(solution)/shard_map/ppermute | solution.py:20
  72.0 6.3 %collective-permute-start.9 = (f32[38,3,128]{2,1,0:T(4,128)S(1)}, f32[38,3,128]{2,1,0:T(4,128)S(1)}, u32[]{:S(2)}, u32[]{:S(2)}) collective-permute-start(f32[38,3,128]{2,1,0:T(4,128)S(1)} %get-tuple-element.45), channel_id=1, source_target_pairs={{4,0},{8,4},{12,8},{0,12},{5,1},{9,5},{13,9},{1,13},{6,2},{10,6},{... | collective-permute-start | bytes 175112 | tf_op jit(solution)/shard_map/ppermute | solution.py:21
  75.8 6.3 %collective-permute-start.8 = (f32[38,3,128]{2,1,0:T(4,128)S(1)}, f32[38,3,128]{2,1,0:T(4,128)S(1)}, u32[]{:S(2)}, u32[]{:S(2)}) collective-permute-start(f32[38,3,128]{2,1,0:T(4,128)S(1)} %get-tuple-element.44), channel_id=1, source_target_pairs={{0,4},{4,8},{8,12},{12,0},{1,5},{5,9},{9,13},{13,1},{2,6},{6,10},{... | collective-permute-start | bytes 175112 | tf_op jit(solution)/shard_map/ppermute | solution.py:20
  82.9 8.2 %collective-permute-start.10 = (f32[38,38,3]{1,0,2:T(8,128)S(1)}, f32[38,38,3]{1,0,2:T(8,128)S(1)}, u32[]{:S(2)}, u32[]{:S(2)}) collective-permute-start(f32[38,38,3]{1,0,2:T(8,128)S(1)} %copy.11), channel_id=1, source_target_pairs={{0,1},{1,2},{2,3},{3,0},{4,5},{5,6},{6,7},{7,4},{8,9},{9,10},{10,1... | collective-permute-start | bytes 51992 | tf_op jit(solution)/shard_map/ppermute | solution.py:20
  85.8 7.0 %collective-permute-start.11 = (f32[38,38,3]{1,0,2:T(8,128)S(1)}, f32[38,38,3]{1,0,2:T(8,128)S(1)}, u32[]{:S(2)}, u32[]{:S(2)}) collective-permute-start(f32[38,38,3]{1,0,2:T(8,128)S(1)} %copy.13), channel_id=1, source_target_pairs={{1,0},{2,1},{3,2},{0,3},{5,4},{6,5},{7,6},{4,7},{9,8},{10,9},{11,1... | collective-permute-start | bytes 51992 | tf_op jit(solution)/shard_map/ppermute | solution.py:21
  94.1 2.2 %copy-start.2 = (bf16[3,32,32,128]{3,2,1,0:T(8,128)(2,1)S(1)}, bf16[3,32,32,128]{3,2,1,0:T(8,128)(2,1)}, u32[]{:S(2)}) copy-start(bf16[3,32,32,128]{3,2,1,0:T(8,128)(2,1)} %param.5) | copy-start | bytes 2359300
  104.9 4.3 %collective-permute-start.13 = (f32[3,32,128]{2,1,0:T(8,128)S(1)}, f32[3,32,128]{2,1,0:T(8,128)S(1)}, u32[]{:S(2)}, u32[]{:S(2)}) collective-permute-start(f32[3,32,128]{2,1,0:T(8,128)S(1)} %get-tuple-element.49), channel_id=1, source_target_pairs={{16,0},{32,16},{48,32},{64,48},{80,64},{96,80},{112,96},{128,112},... | collective-permute-start | bytes 147464 | tf_op jit(solution)/shard_map/ppermute | solution.py:21
  106.8 11.5 %collective-permute-start.12 = (f32[3,32,128]{2,1,0:T(8,128)S(1)}, f32[3,32,128]{2,1,0:T(8,128)S(1)}, u32[]{:S(2)}, u32[]{:S(2)}) collective-permute-start(f32[3,32,128]{2,1,0:T(8,128)S(1)} %get-tuple-element.48), channel_id=1, source_target_pairs={{0,16},{16,32},{32,48},{48,64},{64,80},{80,96},{96,112},{112,128},... | collective-permute-start | bytes 147464 | tf_op jit(solution)/shard_map/ppermute | solution.py:20
  118.3 6.5 %collective-permute-start.15 = (f32[38,3,128]{2,1,0:T(4,128)S(1)}, f32[38,3,128]{2,1,0:T(4,128)S(1)}, u32[]{:S(2)}, u32[]{:S(2)}) collective-permute-start(f32[38,3,128]{2,1,0:T(4,128)S(1)} %get-tuple-element.41), channel_id=1, source_target_pairs={{4,0},{8,4},{12,8},{0,12},{5,1},{9,5},{13,9},{1,13},{6,2},{10,6},{... | collective-permute-start | bytes 175112 | tf_op jit(solution)/shard_map/ppermute | solution.py:21
  121.5 6.3 %collective-permute-start.14 = (f32[38,3,128]{2,1,0:T(4,128)S(1)}, f32[38,3,128]{2,1,0:T(4,128)S(1)}, u32[]{:S(2)}, u32[]{:S(2)}) collective-permute-start(f32[38,3,128]{2,1,0:T(4,128)S(1)} %get-tuple-element.40), channel_id=1, source_target_pairs={{0,4},{4,8},{8,12},{12,0},{1,5},{5,9},{9,13},{13,1},{2,6},{6,10},{... | collective-permute-start | bytes 175112 | tf_op jit(solution)/shard_map/ppermute | solution.py:20
  128.5 9.2 %collective-permute-start.16 = (f32[38,38,3]{1,0,2:T(8,128)S(1)}, f32[38,38,3]{1,0,2:T(8,128)S(1)}, u32[]{:S(2)}, u32[]{:S(2)}) collective-permute-start(f32[38,38,3]{1,0,2:T(8,128)S(1)} %copy.15), channel_id=1, source_target_pairs={{0,1},{1,2},{2,3},{3,0},{4,5},{5,6},{6,7},{7,4},{8,9},{9,10},{10,1... | collective-permute-start | bytes 51992 | tf_op jit(solution)/shard_map/ppermute | solution.py:20
  132.8 6.6 %collective-permute-start.17 = (f32[38,38,3]{1,0,2:T(8,128)S(1)}, f32[38,38,3]{1,0,2:T(8,128)S(1)}, u32[]{:S(2)}, u32[]{:S(2)}) collective-permute-start(f32[38,38,3]{1,0,2:T(8,128)S(1)} %copy.17), channel_id=1, source_target_pairs={{1,0},{2,1},{3,2},{0,3},{5,4},{6,5},{7,6},{4,7},{9,8},{10,9},{11,1... | collective-permute-start | bytes 51992 | tf_op jit(solution)/shard_map/ppermute | solution.py:21
  140.6 2.2 %copy-start.3 = (bf16[3,32,32,128]{3,2,1,0:T(8,128)(2,1)S(1)}, bf16[3,32,32,128]{3,2,1,0:T(8,128)(2,1)}, u32[]{:S(2)}) copy-start(bf16[3,32,32,128]{3,2,1,0:T(8,128)(2,1)} %param.5) | copy-start | bytes 2359300
  142.8 28.2 %copy-start.4 = (s32[4]{0:T(128)S(1)}, s32[4]{0:T(128)}, u32[]{:S(2)}) copy-start(s32[4]{0:T(128)} %param.7) | copy-start | bytes 52
  152.1 4.3 %collective-permute-start.19 = (bf16[1,32,128]{2,1,0:T(8,128)(2,1)S(1)}, bf16[1,32,128]{2,1,0:T(8,128)(2,1)S(1)}, u32[]{:S(2)}, u32[]{:S(2)}) collective-permute-start(bf16[1,32,128]{2,1,0:T(8,128)(2,1)S(1)} %get-tuple-element.60), channel_id=1, source_target_pairs={{16,0},{32,16},{48,32},{64,48},{80,64},{96,80},{112,96},{128,112},... | collective-permute-start | bytes 24584 | tf_op jit(solution)/shard_map/ppermute | solution.py:21
  154.0 11.0 %collective-permute-start.18 = (bf16[1,32,128]{2,1,0:T(8,128)(2,1)S(1)}, bf16[1,32,128]{2,1,0:T(8,128)(2,1)S(1)}, u32[]{:S(2)}, u32[]{:S(2)}) collective-permute-start(bf16[1,32,128]{2,1,0:T(8,128)(2,1)S(1)} %get-tuple-element.59), channel_id=1, source_target_pairs={{0,16},{16,32},{32,48},{48,64},{64,80},{80,96},{96,112},{112,128},... | collective-permute-start | bytes 24584 | tf_op jit(solution)/shard_map/ppermute | solution.py:20
  165.1 7.6 %collective-permute-start.21 = (bf16[34,1,128]{2,1,0:T(2,128)(2,1)S(1)}, bf16[34,1,128]{2,1,0:T(2,128)(2,1)S(1)}, u32[]{:S(2)}, u32[]{:S(2)}) collective-permute-start(bf16[34,1,128]{2,1,0:T(2,128)(2,1)S(1)} %get-tuple-element.58), channel_id=1, source_target_pairs={{4,0},{8,4},{12,8},{0,12},{5,1},{9,5},{13,9},{1,13},{6,2},{10,6},{... | collective-permute-start | bytes 26120 | tf_op jit(solution)/shard_map/ppermute | solution.py:21
  168.2 5.6 %collective-permute-start.20 = (bf16[34,1,128]{2,1,0:T(2,128)(2,1)S(1)}, bf16[34,1,128]{2,1,0:T(2,128)(2,1)S(1)}, u32[]{:S(2)}, u32[]{:S(2)}) collective-permute-start(bf16[34,1,128]{2,1,0:T(2,128)(2,1)S(1)} %get-tuple-element.57), channel_id=1, source_target_pairs={{0,4},{4,8},{8,12},{12,0},{1,5},{5,9},{9,13},{13,1},{2,6},{6,10},{... | collective-permute-start | bytes 26120 | tf_op jit(solution)/shard_map/ppermute | solution.py:20
where the time goes:
time: 197 us; the launch traced here: 196 us
  starting transfers between devices  82.1 us (42%)
  waiting for transfers between devices  42.5 us (22%)
  other arithmetic  35.4 us (18%)
  local copies, waits for them, and re-layouts  15.9 us (8%)
  blocking collectives  11 us (6%)
  matrix products  5.91 us (3%)
  between operations  3.04 us (2%)
    ppermute x11, starting transfers between devices, extended(): after = lax.ppermute(initial, axis, down)  55.8 us
    ppermute x11, waiting for transfers between devices, extended(): before = lax.ppermute(last, axis, up)  39.5 us
    ppermute x11, starting transfers between devices, extended(): before = lax.ppermute(last, axis, up)  26.4 us
    all_to_all x1, blocking collectives, shards(): lax.all_to_all(pieces, 'gz', split_axis=1, concat_axis=1, tiled=True)  11 us
    convert_element_type x1, other arithmetic, shards(): level_out.astype(jnp.bfloat16)  9.35 us
    add x1, other arithmetic, shards(): 0.75 * level_set  8.59 us
    add x1, other arithmetic, shards(): section_one = level_set + time_step * section_rate(level_set)  8.38 us
    concatenate x8, other arithmetic, extended(): x = jnp.concatenate([before, x, after], axis=dim)  6.84 us
  transfers between devices with their start and end apart: 22, of which 15 were waited for; matrix products, arithmetic and copies ran while one was open for 3% of the time, Pallas kernels for 0%

commit v1 on v0

--- a/solution.py
+++ b/solution.py
@@ -21,6 +21,43 @@
         after = lax.ppermute(initial, axis, down)
         x = jnp.concatenate([before, x, after], axis=dim)
     return x
+
+
+def faces(x, sides, width):
+    padded = []
+    for axis, dim in sides:
+        size, length = (lax.axis_size(axis), x.shape[dim])
+        up = [(i, (i + 1) % size) for i in range(size)]
+        down = [(j, i) for i, j in up]
+        last = lax.slice_in_dim(x, length - width, length, axis=dim)
+        initial = lax.slice_in_dim(x, 0, width, axis=dim)
+        before = lax.ppermute(last, axis, up)
+        after = lax.ppermute(initial, axis, down)
+        padded.append(jnp.concatenate([before, x, after], axis=dim))
+    return padded
+
+
+def rim_of(x):
+    nx, ny = lax.axis_size("gx"), lax.axis_size("gy")
+    lx, ly = x.shape[0], x.shape[1]
+    pairs = {}
+    for sx in (-1, 0, 1):
+        for sy in (-1, 0, 1):
+            if sx == 0 and sy == 0:
+                continue
+            pick_x = slice(0, 1) if sx == 1 else (slice(lx - 1, lx) if sx == -1 else slice(0, lx))
+            pick_y = slice(0, 1) if sy == 1 else (slice(ly - 1, ly) if sy == -1 else slice(0, ly))
+            perm = [
+                (i * ny + j, ((i - sx) % nx) * ny + (j - sy) % ny)
+                for i in range(nx)
+                for j in range(ny)
+            ]
+            pairs[(sx, sy)] = lax.ppermute(x[pick_x, pick_y], ("gx", "gy"), perm)
+    rows = []
+    for sx in (-1, 0, 1):
+        row = [pairs[(sx, -1)], x if sx == 0 else pairs[(sx, 0)], pairs[(sx, 1)]]
+        rows.append(jnp.concatenate(row, axis=1))
+    return jnp.concatenate(rows, axis=0)
 
 
 def square(operand):
@@ -49,15 +86,14 @@
 
 
 def window(padded, axis_dim, offset):
-    slicing = [slice(3, extent - 3) for extent in padded.shape]
     length = padded.shape[axis_dim] - 6
-    slicing[axis_dim] = slice(3 + offset, 3 + offset + length)
-    return padded[tuple(slicing)]
+    return lax.slice_in_dim(padded, 3 + offset, 3 + offset + length, axis=axis_dim)
 
 
-def local_rate(padded, velocity_window):
+def local_rate(padded_list, velocity_window):
     summed = jnp.zeros(velocity_window.shape[1:], jnp.float32)
     for axis_dim in range(3):
+        padded = padded_list[axis_dim]
         jump_list = [
             window(padded, axis_dim, offset) - window(padded, axis_dim, offset - 1)
             for offset in range(-2, 4)
@@ -109,7 +145,7 @@
 def shards(level_set, velocity, active_brick, depth_order):
 
     def section_rate(level_field):
-        padded = extended(level_field, (("gx", 0), ("gy", 1), ("gz", 2)), 3)
+        padded = faces(level_field, (("gx", 0), ("gy", 1), ("gz", 2)), 3)
         return local_rate(padded, velocity)
 
     section_one = level_set + time_step * section_rate(level_set)
@@ -120,9 +156,7 @@
     alive_float = alive.astype(jnp.float32)
     group = lax.axis_size("gz")
     ascending = depth_order[0] < depth_order[group - 1]
-    rim = extended(level_out.astype(jnp.bfloat16), (("gx", 0), ("gy", 1)), 1).astype(
-        level_out.dtype
-    )
+    rim = rim_of(level_out.astype(jnp.bfloat16)).astype(level_out.dtype)
     left_x = 0.75 * rim[1:-1] + 0.25 * rim[:-2]
     right_x = 0.75 * rim[1:-1] + 0.25 * rim[2:]
     grid_pairs = []

time: 197 us -> 230 us (1.17)
  the two profiles are of different devices: /device:TPU:8 before, /device:TPU:7 now
where the time goes in v1:
time: 230 us
  starting transfers between devices  113 us (49%)
  waiting for transfers between devices  65.4 us (28%)
  other arithmetic  28.9 us (13%)
  blocking collectives  7.2 us (3%)
  local copies, waits for them, and re-layouts  6.46 us (3%)
  matrix products  5.91 us (3%)
  between operations  3.09 us (1%)
    ppermute x9, starting transfers between devices, faces(): before = lax.ppermute(last, axis, up)  48.3 us
    ppermute x8, starting transfers between devices, rim_of(): pairs[sx, sy] = lax.ppermute(x[pick_x, pick_y], ('gx', 'gy'), perm)  34.4 us
    ppermute x9, starting transfers between devices, faces(): after = lax.ppermute(initial, axis, down)  30 us
    ppermute x9, waiting for transfers between devices, faces(): before = lax.ppermute(last, axis, up)  24.8 us
    ppermute x9, waiting for transfers between devices, faces(): after = lax.ppermute(initial, axis, down)  22.9 us
    ppermute x8, waiting for transfers between devices, rim_of(): pairs[sx, sy] = lax.ppermute(x[pick_x, pick_y], ('gx', 'gy'), perm)  17.7 us
    convert_element_type x2, other arithmetic, shards(): rim = rim_of(level_out.astype(jnp.bfloat16)).astype(level_out.dtype)  9.88 us
    add x1, other arithmetic, shards(): 0.75 * level_set  9.01 us
  transfers between devices with their start and end apart: 26, of which 8 were waited for; matrix products, arithmetic and copies ran while one was open for 1% of the time, Pallas kernels for 0%

profile of v1, /device:TPU:7, one launch (start us, length us, event | category | flops | bytes accessed | tf_op | source)
XLA Modules:
  0.0 229.6 jit_solution(2419294732436916010)
XLA Ops:
  0.6 0.9 fusion.573
  1.5 9.3 %collective-permute-start = (f32[3,32,128]{2,1,0:T(8,128)S(1)}, f32[3,32,128]{2,1,0:T(8,128)S(1)}, u32[]{:S(2)}, u32[]{:S(2)}) collective-permute-start(f32[3,32,128]{2,1,0:T(8,128)S(1)} %get-tuple-element.42), channel_id=1, source_target_pairs={{0,16},{16,32},{32,48},{48,64},{64,80},{80,96},{96,112},{112,128},... | collective-permute-start | bytes 147464 | tf_op jit(solution)/shard_map/ppermute | solution.py:34
  10.8 1.4 fusion.575
  12.2 6.4 %collective-permute-start.5 = (f32[32,32,3]{2,1,0:T(8,128)S(1)}, f32[32,32,3]{2,1,0:T(8,128)S(1)}, u32[]{:S(2)}, u32[]{:S(2)}) collective-permute-start(f32[32,32,3]{2,1,0:T(8,128)S(1)} %get-tuple-element.47), channel_id=1, source_target_pairs={{1,0},{2,1},{3,2},{0,3},{5,4},{6,5},{7,6},{4,7},{9,8},{10,9},{11,1... | collective-permute-start | bytes 36872 | tf_op jit(solution)/shard_map/ppermute | solution.py:35
  18.7 4.6 %collective-permute-start.3 = (f32[32,3,128]{2,1,0:T(4,128)S(1)}, f32[32,3,128]{2,1,0:T(4,128)S(1)}, u32[]{:S(2)}, u32[]{:S(2)}) collective-permute-start(f32[32,3,128]{2,1,0:T(4,128)S(1)} %get-tuple-element.45), channel_id=1, source_target_pairs={{4,0},{8,4},{12,8},{0,12},{5,1},{9,5},{13,9},{1,13},{6,2},{10,6},{... | collective-permute-start | bytes 147464 | tf_op jit(solution)/shard_map/ppermute | solution.py:35
  23.3 1.9 collective-permute-start.1
  25.3 1.9 collective-permute-start.4
  27.2 1.9 collective-permute-start.2
  29.4 5.9 %collective-permute-done.1 = f32[3,32,128]{2,1,0:T(8,128)S(1)} collective-permute-done((f32[3,32,128]{2,1,0:T(8,128)S(1)}, f32[3,32,128]{2,1,0:T(8,128)S(1)}, u32[]{:S(2)}, u32[]{:S(2)}) %collective-permute-start.1) | collective-permute-done | bytes 49184 | tf_op jit(solution)/shard_map/ppermute | solution.py:35
  35.3 2.8 %collective-permute-done.4 = f32[32,32,3]{2,1,0:T(8,128)S(1)} collective-permute-done((f32[32,32,3]{2,1,0:T(8,128)S(1)}, f32[32,32,3]{2,1,0:T(8,128)S(1)}, u32[]{:S(2)}, u32[]{:S(2)}) %collective-permute-start.4) | collective-permute-done | bytes 12320 | tf_op jit(solution)/shard_map/ppermute | solution.py:34
  38.1 8.0 %fusion.27 = f32[32,32,128]{2,1,0:T(8,128)S(1)} fusion(f32[32,32,128]{2,1,0:T(8,128)S(1)} %copy-done, f32[32,32,131]{2,1,0:T(8,128)S(1)} %constant_dynamic-update-slice_fusion.6, f32[32,32,3]{2,1,0:T(8,128)S(1)} %collective-permute-done.4, f32[32,35,128]{2,1,0:T(8,128)S(1)} %constant_dynamic-update-slice_fusion.4, ...), kind=kLoop, calls=%fused_computation.100 | loop fusion | flops 54919168 | bytes 8187904 | tf_op jit(solution)/shard_map/add | solution.py:151
  46.2 2.1 collective-permute-start.8
  48.3 4.4 %collective-permute-start.9 = (f32[32,3,128]{2,1,0:T(4,128)S(1)}, f32[32,3,128]{2,1,0:T(4,128)S(1)}, u32[]{:S(2)}, u32[]{:S(2)}) collective-permute-start(f32[32,3,128]{2,1,0:T(4,128)S(1)} %get-tuple-element.34), channel_id=1, source_target_pairs={{4,0},{8,4},{12,8},{0,12},{5,1},{9,5},{13,9},{1,13},{6,2},{10,6},{... | collective-permute-start | bytes 147464 | tf_op jit(solution)/shard_map/ppermute | solution.py:35
  52.7 11.1 %collective-permute-start.6 = (f32[3,32,128]{2,1,0:T(8,128)S(1)}, f32[3,32,128]{2,1,0:T(8,128)S(1)}, u32[]{:S(2)}, u32[]{:S(2)}) collective-permute-start(f32[3,32,128]{2,1,0:T(8,128)S(1)} %get-tuple-element.33), channel_id=1, source_target_pairs={{0,16},{16,32},{32,48},{48,64},{64,80},{80,96},{96,112},{112,128},... | collective-permute-start | bytes 147464 | tf_op jit(solution)/shard_map/ppermute | solution.py:34
  63.8 1.9 collective-permute-start.7
  65.9 1.9 collective-permute-start.10
  67.8 9.8 %collective-permute-done.10 = f32[32,32,3]{2,1,0:T(8,128)S(1)} collective-permute-done((f32[32,32,3]{2,1,0:T(8,128)S(1)}, f32[32,32,3]{2,1,0:T(8,128)S(1)}, u32[]{:S(2)}, u32[]{:S(2)}) %collective-permute-start.10) | collective-permute-done | bytes 12320 | tf_op jit(solution)/shard_map/ppermute | solution.py:34
  77.6 2.3 %collective-permute-start.11 = (f32[32,32,3]{2,1,0:T(8,128)S(1)}, f32[32,32,3]{2,1,0:T(8,128)S(1)}, u32[]{:S(2)}, u32[]{:S(2)}) collective-permute-start(f32[32,32,3]{2,1,0:T(8,128)S(1)} %get-tuple-element.37), channel_id=1, source_target_pairs={{1,0},{2,1},{3,2},{0,3},{5,4},{6,5},{7,6},{4,7},{9,8},{10,9},{11,1... | collective-permute-start | bytes 36872 | tf_op jit(solution)/shard_map/ppermute | solution.py:35
  80.0 9.7 %collective-permute-done.11 = f32[32,32,3]{2,1,0:T(8,128)S(1)} collective-permute-done((f32[32,32,3]{2,1,0:T(8,128)S(1)}, f32[32,32,3]{2,1,0:T(8,128)S(1)}, u32[]{:S(2)}, u32[]{:S(2)}) %collective-permute-start.11) | collective-permute-done | bytes 12320 | tf_op jit(solution)/shard_map/ppermute | solution.py:35
  89.7 9.0 %fusion.37 = f32[32,32,128]{2,1,0:T(8,128)S(1)} fusion(f32[32,32,128]{2,1,0:T(8,128)S(1)} %fusion.27, f32[32,32,3]{2,1,0:T(8,128)S(1)} %collective-permute-done.11, f32[32,32,3]{2,1,0:T(8,128)S(1)} %collective-permute-done.10, f32[32,3,128]{2,1,0:T(4,128)S(1)} %collective-permute-done.8, f32[32,3,128]{2,1,0:T(4,128)S(1)} %collective-permute-done.9, ...), kind=kLoop, calls=%fused_computation.110 | loop fusion | flops 56885248 | bytes 2580480 | tf_op jit(solution)/shard_map/add | solution.py:152
  98.7 2.0 collective-permute-start.14
  100.7 4.5 %collective-permute-start.15 = (f32[32,3,128]{2,1,0:T(4,128)S(1)}, f32[32,3,128]{2,1,0:T(4,128)S(1)}, u32[]{:S(2)}, u32[]{:S(2)}) collective-permute-start(f32[32,3,128]{2,1,0:T(4,128)S(1)} %get-tuple-element.29), channel_id=1, source_target_pairs={{4,0},{8,4},{12,8},{0,12},{5,1},{9,5},{13,9},{1,13},{6,2},{10,6},{... | collective-permute-start | bytes 147464 | tf_op jit(solution)/shard_map/ppermute | solution.py:35
  105.2 16.2 %collective-permute-start.12 = (f32[3,32,128]{2,1,0:T(8,128)S(1)}, f32[3,32,128]{2,1,0:T(8,128)S(1)}, u32[]{:S(2)}, u32[]{:S(2)}) collective-permute-start(f32[3,32,128]{2,1,0:T(8,128)S(1)} %get-tuple-element.26), channel_id=1, source_target_pairs={{0,16},{16,32},{32,48},{48,64},{64,80},{80,96},{96,112},{112,128},... | collective-permute-start | bytes 147464 | tf_op jit(solution)/shard_map/ppermute | solution.py:34
  121.5 1.9 collective-permute-start.13
  123.6 1.9 collective-permute-start.16
  125.6 12.2 %collective-permute-done.16 = f32[32,32,3]{2,1,0:T(8,128)S(1)} collective-permute-done((f32[32,32,3]{2,1,0:T(8,128)S(1)}, f32[32,32,3]{2,1,0:T(8,128)S(1)}, u32[]{:S(2)}, u32[]{:S(2)}) %collective-permute-start.16) | collective-permute-done | bytes 12320 | tf_op jit(solution)/shard_map/ppermute | solution.py:34
  137.8 1.9 collective-permute-start.17
  140.3 7.3 %collective-permute-done.17 = f32[32,32,3]{2,1,0:T(8,128)S(1)} collective-permute-done((f32[32,32,3]{2,1,0:T(8,128)S(1)}, f32[32,32,3]{2,1,0:T(8,128)S(1)}, u32[]{:S(2)}, u32[]{:S(2)}) %collective-permute-start.17) | collective-permute-done | bytes 12320 | tf_op jit(solution)/shard_map/ppermute | solution.py:35
  147.7 9.7 %fusion.565 = (bf16[32,32,128]{2,1,0:T(8,128)(2,1)S(1)}, f32[32,32,128]{2,1,0:T(8,128)}) fusion(f32[32,32,128]{2,1,0:T(8,128)S(1)} %copy-done, f32[32,32,128]{2,1,0:T(8,128)S(1)} %fusion.37, f32[32,32,3]{2,1,0:T(8,128)S(1)} %collective-permute-done.17, f32[32,32,3]{2,1,0:T(8,128)S(1)} %collective-permute-done.16, bf16[3,32,32,128]{3,2,1,0:T(8,128)(2,1)S(1)} %copy-done.1, ...), kind=kLoop, calls=%fused_computation.752 | loop fusion | flops 57147392 | bytes 2842625 | tf_op jit(solution)/shard_map/convert_element_type | solution.py:159
  157.5 1.9 collective-permute-start.21
  159.4 13.8 %collective-permute-start.18 = (bf16[1,1,128]{2,1,0:T(2,128)(2,1)S(1)}, bf16[1,1,128]{2,1,0:T(2,128)(2,1)S(1)}, u32[]{:S(2)}, u32[]{:S(2)}) collective-permute-start(bf16[1,1,128]{2,1,0:T(2,128)(2,1)S(1)} %get-tuple-element.48), channel_id=1, source_target_pairs={{0,20},{4,24},{8,28},{12,16},{16,36},{20,40},{24,44},{28,32},{32,5... | collective-permute-start | bytes 776 | tf_op jit(solution)/shard_map/ppermute | solution.py:55
  173.2 5.4 %collective-permute-start.22 = (bf16[32,1,128]{2,1,0:T(2,128)(2,1)S(1)}, bf16[32,1,128]{2,1,0:T(2,128)(2,1)S(1)}, u32[]{:S(2)}, u32[]{:S(2)}) collective-permute-start(bf16[32,1,128]{2,1,0:T(2,128)(2,1)S(1)} %get-tuple-element.55), channel_id=1, source_target_pairs={{0,12},{4,0},{8,4},{12,8},{16,28},{20,16},{24,20},{28,24},{32,44},... | collective-permute-start | bytes 24584 | tf_op jit(solution)/shard_map/ppermute | solution.py:55
  178.6 2.2 collective-permute-start.20
  180.8 2.5 %collective-permute-start.19 = (bf16[1,32,128]{2,1,0:T(8,128)(2,1)S(1)}, bf16[1,32,128]{2,1,0:T(8,128)(2,1)S(1)}, u32[]{:S(2)}, u32[]{:S(2)}) collective-permute-start(bf16[1,32,128]{2,1,0:T(8,128)(2,1)S(1)} %get-tuple-element.52), channel_id=1, source_target_pairs={{0,16},{4,20},{8,24},{12,28},{16,32},{20,36},{24,40},{28,44},{32,4... | collective-permute-start | bytes 24584 | tf_op jit(solution)/shard_map/ppermute | solution.py:55
  183.3 3.2 %collective-permute-start.24 = (bf16[1,32,128]{2,1,0:T(8,128)(2,1)S(1)}, bf16[1,32,128]{2,1,0:T(8,128)(2,1)S(1)}, u32[]{:S(2)}, u32[]{:S(2)}) collective-permute-start(bf16[1,32,128]{2,1,0:T(8,128)(2,1)S(1)} %get-tuple-element.53), channel_id=1, source_target_pairs={{0,496},{4,500},{8,504},{12,508},{16,0},{20,4},{24,8},{28,12},{32,... | collective-permute-start | bytes 24584 | tf_op jit(solution)/shard_map/ppermute | solution.py:55
  186.5 3.3 %collective-permute-start.23 = (bf16[1,1,128]{2,1,0:T(2,128)(2,1)S(1)}, bf16[1,1,128]{2,1,0:T(2,128)(2,1)S(1)}, u32[]{:S(2)}, u32[]{:S(2)}) collective-permute-start(bf16[1,1,128]{2,1,0:T(2,128)(2,1)S(1)} %get-tuple-element.50), channel_id=1, source_target_pairs={{0,500},{4,504},{8,508},{12,496},{16,4},{20,8},{24,12},{28,0},{32,... | collective-permute-start | bytes 776 | tf_op jit(solution)/shard_map/ppermute | solution.py:55
  190.4 9.2 %collective-permute-done.23 = bf16[1,1,128]{2,1,0:T(2,128)(2,1)S(1)} collective-permute-done((bf16[1,1,128]{2,1,0:T(2,128)(2,1)S(1)}, bf16[1,1,128]{2,1,0:T(2,128)(2,1)S(1)}, u32[]{:S(2)}, u32[]{:S(2)}) %collective-permute-start.23) | collective-permute-done | bytes 288 | tf_op jit(solution)/shard_map/ppermute | solution.py:55
  199.5 2.1 collective-permute-start.25
  202.8 8.5 %collective-permute-done.25 = bf16[1,1,128]{2,1,0:T(2,128)(2,1)S(1)} collective-permute-done((bf16[1,1,128]{2,1,0:T(2,128)(2,1)S(1)}, bf16[1,1,128]{2,1,0:T(2,128)(2,1)S(1)}, u32[]{:S(2)}, u32[]{:S(2)}) %collective-permute-start.25) | collective-permute-done | bytes 288 | tf_op jit(solution)/shard_map/ppermute | solution.py:55
  212.0 1.2 multiply_reduce_fusion.7
  213.2 1.2 multiply_reduce_fusion.5
  214.3 1.2 multiply_reduce_fusion.3
  215.5 1.2 multiply_reduce_fusion.1
  216.8 1.3 copy.7
  218.1 0.7 copy.8
  218.9 7.2 %all_to_all.5 = f32[4,1,4096]{2,1,0:T(1,128)S(1)} all-to-all(f32[4,1,4096]{2,1,0:T(1,128)S(1)} %reshape.79), channel_id=1, replica_groups=mesh['gx'=32,'gy'=4,'gz'=4] {'gz'}, dimensions={0} | all-to-all | bytes 131072 | tf_op jit(solution)/shard_map/all_to_all | solution.py:173
  226.7 0.8 reduce
  228.9 0.6 pad_maximum_fusion.15
  (63 shorter events, 4.2 us)
Async XLA Ops:
  0.6 18.0 %copy-start = (f32[32,32,128]{2,1,0:T(8,128)S(1)}, f32[32,32,128]{2,1,0:T(8,128)}, u32[]{:S(2)}) copy-start(f32[32,32,128]{2,1,0:T(8,128)} %param.4) | copy-start | bytes 1572868
  1.5 25.7 %collective-permute-start = (f32[3,32,128]{2,1,0:T(8,128)S(1)}, f32[3,32,128]{2,1,0:T(8,128)S(1)}, u32[]{:S(2)}, u32[]{:S(2)}) collective-permute-start(f32[3,32,128]{2,1,0:T(8,128)S(1)} %get-tuple-element.42), channel_id=1, source_target_pairs={{0,16},{16,32},{32,48},{48,64},{64,80},{80,96},{96,112},{112,128},... | collective-permute-start | bytes 147464 | tf_op jit(solution)/shard_map/ppermute | solution.py:34
  12.2 25.9 %copy-start.1 = (bf16[3,32,32,128]{3,2,1,0:T(8,128)(2,1)S(1)}, bf16[3,32,32,128]{3,2,1,0:T(8,128)(2,1)}, u32[]{:S(2)}) copy-start(bf16[3,32,32,128]{3,2,1,0:T(8,128)(2,1)} %param.5) | copy-start | bytes 2359300
  12.2 17.1 %collective-permute-start.5 = (f32[32,32,3]{2,1,0:T(8,128)S(1)}, f32[32,32,3]{2,1,0:T(8,128)S(1)}, u32[]{:S(2)}, u32[]{:S(2)}) collective-permute-start(f32[32,32,3]{2,1,0:T(8,128)S(1)} %get-tuple-element.47), channel_id=1, source_target_pairs={{1,0},{2,1},{3,2},{0,3},{5,4},{6,5},{7,6},{4,7},{9,8},{10,9},{11,1... | collective-permute-start | bytes 36872 | tf_op jit(solution)/shard_map/ppermute | solution.py:35
  18.7 10.7 %collective-permute-start.3 = (f32[32,3,128]{2,1,0:T(4,128)S(1)}, f32[32,3,128]{2,1,0:T(4,128)S(1)}, u32[]{:S(2)}, u32[]{:S(2)}) collective-permute-start(f32[32,3,128]{2,1,0:T(4,128)S(1)} %get-tuple-element.45), channel_id=1, source_target_pairs={{4,0},{8,4},{12,8},{0,12},{5,1},{9,5},{13,9},{1,13},{6,2},{10,6},{... | collective-permute-start | bytes 147464 | tf_op jit(solution)/shard_map/ppermute | solution.py:35
  23.3 12.0 %collective-permute-start.1 = (f32[3,32,128]{2,1,0:T(8,128)S(1)}, f32[3,32,128]{2,1,0:T(8,128)S(1)}, u32[]{:S(2)}, u32[]{:S(2)}) collective-permute-start(f32[3,32,128]{2,1,0:T(8,128)S(1)} %get-tuple-element.43), channel_id=1, source_target_pairs={{16,0},{32,16},{48,32},{64,48},{80,64},{96,80},{112,96},{128,112},... | collective-permute-start | bytes 147464 | tf_op jit(solution)/shard_map/ppermute | solution.py:35
  25.3 12.8 %collective-permute-start.4 = (f32[32,32,3]{2,1,0:T(8,128)S(1)}, f32[32,32,3]{2,1,0:T(8,128)S(1)}, u32[]{:S(2)}, u32[]{:S(2)}) collective-permute-start(f32[32,32,3]{2,1,0:T(8,128)S(1)} %get-tuple-element.46), channel_id=1, source_target_pairs={{0,1},{1,2},{2,3},{3,0},{4,5},{5,6},{6,7},{7,4},{8,9},{9,10},{10,1... | collective-permute-start | bytes 36872 | tf_op jit(solution)/shard_map/ppermute | solution.py:34
  27.2 10.9 %collective-permute-start.2 = (f32[32,3,128]{2,1,0:T(4,128)S(1)}, f32[32,3,128]{2,1,0:T(4,128)S(1)}, u32[]{:S(2)}, u32[]{:S(2)}) collective-permute-start(f32[32,3,128]{2,1,0:T(4,128)S(1)} %get-tuple-element.44), channel_id=1, source_target_pairs={{0,4},{4,8},{8,12},{12,0},{1,5},{5,9},{9,13},{13,1},{2,6},{6,10},{... | collective-permute-start | bytes 147464 | tf_op jit(solution)/shard_map/ppermute | solution.py:34
  46.2 43.4 %collective-permute-start.8 = (f32[32,3,128]{2,1,0:T(4,128)S(1)}, f32[32,3,128]{2,1,0:T(4,128)S(1)}, u32[]{:S(2)}, u32[]{:S(2)}) collective-permute-start(f32[32,3,128]{2,1,0:T(4,128)S(1)} %get-tuple-element.35), channel_id=1, source_target_pairs={{0,4},{4,8},{8,12},{12,0},{1,5},{5,9},{9,13},{13,1},{2,6},{6,10},{... | collective-permute-start | bytes 147464 | tf_op jit(solution)/shard_map/ppermute | solution.py:34
  48.3 41.4 %collective-permute-start.9 = (f32[32,3,128]{2,1,0:T(4,128)S(1)}, f32[32,3,128]{2,1,0:T(4,128)S(1)}, u32[]{:S(2)}, u32[]{:S(2)}) collective-permute-start(f32[32,3,128]{2,1,0:T(4,128)S(1)} %get-tuple-element.34), channel_id=1, source_target_pairs={{4,0},{8,4},{12,8},{0,12},{5,1},{9,5},{13,9},{1,13},{6,2},{10,6},{... | collective-permute-start | bytes 147464 | tf_op jit(solution)/shard_map/ppermute | solution.py:35
  52.7 36.9 %collective-permute-start.6 = (f32[3,32,128]{2,1,0:T(8,128)S(1)}, f32[3,32,128]{2,1,0:T(8,128)S(1)}, u32[]{:S(2)}, u32[]{:S(2)}) collective-permute-start(f32[3,32,128]{2,1,0:T(8,128)S(1)} %get-tuple-element.33), channel_id=1, source_target_pairs={{0,16},{16,32},{32,48},{48,64},{64,80},{80,96},{96,112},{112,128},... | collective-permute-start | bytes 147464 | tf_op jit(solution)/shard_map/ppermute | solution.py:34
  63.8 25.9 %collective-permute-start.7 = (f32[3,32,128]{2,1,0:T(8,128)S(1)}, f32[3,32,128]{2,1,0:T(8,128)S(1)}, u32[]{:S(2)}, u32[]{:S(2)}) collective-permute-start(f32[3,32,128]{2,1,0:T(8,128)S(1)} %get-tuple-element.32), channel_id=1, source_target_pairs={{16,0},{32,16},{48,32},{64,48},{80,64},{96,80},{112,96},{128,112},... | collective-permute-start | bytes 147464 | tf_op jit(solution)/shard_map/ppermute | solution.py:35
  65.9 11.7 %collective-permute-start.10 = (f32[32,32,3]{2,1,0:T(8,128)S(1)}, f32[32,32,3]{2,1,0:T(8,128)S(1)}, u32[]{:S(2)}, u32[]{:S(2)}) collective-permute-start(f32[32,32,3]{2,1,0:T(8,128)S(1)} %get-tuple-element.36), channel_id=1, source_target_pairs={{0,1},{1,2},{2,3},{3,0},{4,5},{5,6},{6,7},{7,4},{8,9},{9,10},{10,1... | collective-permute-start | bytes 36872 | tf_op jit(solution)/shard_map/ppermute | solution.py:34
  77.6 12.0 %collective-permute-start.11 = (f32[32,32,3]{2,1,0:T(8,128)S(1)}, f32[32,32,3]{2,1,0:T(8,128)S(1)}, u32[]{:S(2)}, u32[]{:S(2)}) collective-permute-start(f32[32,32,3]{2,1,0:T(8,128)S(1)} %get-tuple-element.37), channel_id=1, source_target_pairs={{1,0},{2,1},{3,2},{0,3},{5,4},{6,5},{7,6},{4,7},{9,8},{10,9},{11,1... | collective-permute-start | bytes 36872 | tf_op jit(solution)/shard_map/ppermute | solution.py:35
  98.7 48.9 %collective-permute-start.14 = (f32[32,3,128]{2,1,0:T(4,128)S(1)}, f32[32,3,128]{2,1,0:T(4,128)S(1)}, u32[]{:S(2)}, u32[]{:S(2)}) collective-permute-start(f32[32,3,128]{2,1,0:T(4,128)S(1)} %get-tuple-element.28), channel_id=1, source_target_pairs={{0,4},{4,8},{8,12},{12,0},{1,5},{5,9},{9,13},{13,1},{2,6},{6,10},{... | collective-permute-start | bytes 147464 | tf_op jit(solution)/shard_map/ppermute | solution.py:34
  100.7 47.0 %collective-permute-start.15 = (f32[32,3,128]{2,1,0:T(4,128)S(1)}, f32[32,3,128]{2,1,0:T(4,128)S(1)}, u32[]{:S(2)}, u32[]{:S(2)}) collective-permute-start(f32[32,3,128]{2,1,0:T(4,128)S(1)} %get-tuple-element.29), channel_id=1, source_target_pairs={{4,0},{8,4},{12,8},{0,12},{5,1},{9,5},{13,9},{1,13},{6,2},{10,6},{... | collective-permute-start | bytes 147464 | tf_op jit(solution)/shard_map/ppermute | solution.py:35
  105.2 42.4 %collective-permute-start.12 = (f32[3,32,128]{2,1,0:T(8,128)S(1)}, f32[3,32,128]{2,1,0:T(8,128)S(1)}, u32[]{:S(2)}, u32[]{:S(2)}) collective-permute-start(f32[3,32,128]{2,1,0:T(8,128)S(1)} %get-tuple-element.26), channel_id=1, source_target_pairs={{0,16},{16,32},{32,48},{48,64},{64,80},{80,96},{96,112},{112,128},... | collective-permute-start | bytes 147464 | tf_op jit(solution)/shard_map/ppermute | solution.py:34
  121.5 26.2 %collective-permute-start.13 = (f32[3,32,128]{2,1,0:T(8,128)S(1)}, f32[3,32,128]{2,1,0:T(8,128)S(1)}, u32[]{:S(2)}, u32[]{:S(2)}) collective-permute-start(f32[3,32,128]{2,1,0:T(8,128)S(1)} %get-tuple-element.27), channel_id=1, source_target_pairs={{16,0},{32,16},{48,32},{64,48},{80,64},{96,80},{112,96},{128,112},... | collective-permute-start | bytes 147464 | tf_op jit(solution)/shard_map/ppermute | solution.py:35
  123.6 66.2 %copy-start.2 = (s32[4]{0:T(128)S(1)}, s32[4]{0:T(128)}, u32[]{:S(2)}) copy-start(s32[4]{0:T(128)} %param.7) | copy-start | bytes 52
  123.6 14.1 %collective-permute-start.16 = (f32[32,32,3]{2,1,0:T(8,128)S(1)}, f32[32,32,3]{2,1,0:T(8,128)S(1)}, u32[]{:S(2)}, u32[]{:S(2)}) collective-permute-start(f32[32,32,3]{2,1,0:T(8,128)S(1)} %get-tuple-element.30), channel_id=1, source_target_pairs={{0,1},{1,2},{2,3},{3,0},{4,5},{5,6},{6,7},{7,4},{8,9},{9,10},{10,1... | collective-permute-start | bytes 36872 | tf_op jit(solution)/shard_map/ppermute | solution.py:34
  137.8 9.9 %collective-permute-start.17 = (f32[32,32,3]{2,1,0:T(8,128)S(1)}, f32[32,32,3]{2,1,0:T(8,128)S(1)}, u32[]{:S(2)}, u32[]{:S(2)}) collective-permute-start(f32[32,32,3]{2,1,0:T(8,128)S(1)} %get-tuple-element.31), channel_id=1, source_target_pairs={{1,0},{2,1},{3,2},{0,3},{5,4},{6,5},{7,6},{4,7},{9,8},{10,9},{11,1... | collective-permute-start | bytes 36872 | tf_op jit(solution)/shard_map/ppermute | solution.py:35
  157.5 53.9 %collective-permute-start.21 = (bf16[32,1,128]{2,1,0:T(2,128)(2,1)S(1)}, bf16[32,1,128]{2,1,0:T(2,128)(2,1)S(1)}, u32[]{:S(2)}, u32[]{:S(2)}) collective-permute-start(bf16[32,1,128]{2,1,0:T(2,128)(2,1)S(1)} %get-tuple-element.54), channel_id=1, source_target_pairs={{0,4},{4,8},{8,12},{12,0},{16,20},{20,24},{24,28},{28,16},{32,36},... | collective-permute-start | bytes 24584 | tf_op jit(solution)/shard_map/ppermute | solution.py:55
  159.4 23.9 %collective-permute-start.18 = (bf16[1,1,128]{2,1,0:T(2,128)(2,1)S(1)}, bf16[1,1,128]{2,1,0:T(2,128)(2,1)S(1)}, u32[]{:S(2)}, u32[]{:S(2)}) collective-permute-start(bf16[1,1,128]{2,1,0:T(2,128)(2,1)S(1)} %get-tuple-element.48), channel_id=1, source_target_pairs={{0,20},{4,24},{8,28},{12,16},{16,36},{20,40},{24,44},{28,32},{32,5... | collective-permute-start | bytes 776 | tf_op jit(solution)/shard_map/ppermute | solution.py:55
  173.2 38.1 %collective-permute-start.22 = (bf16[32,1,128]{2,1,0:T(2,128)(2,1)S(1)}, bf16[32,1,128]{2,1,0:T(2,128)(2,1)S(1)}, u32[]{:S(2)}, u32[]{:S(2)}) collective-permute-start(bf16[32,1,128]{2,1,0:T(2,128)(2,1)S(1)} %get-tuple-element.55), channel_id=1, source_target_pairs={{0,12},{4,0},{8,4},{12,8},{16,28},{20,16},{24,20},{28,24},{32,44},... | collective-permute-start | bytes 24584 | tf_op jit(solution)/shard_map/ppermute | solution.py:55
  178.6 7.9 %collective-permute-start.20 = (bf16[1,1,128]{2,1,0:T(2,128)(2,1)S(1)}, bf16[1,1,128]{2,1,0:T(2,128)(2,1)S(1)}, u32[]{:S(2)}, u32[]{:S(2)}) collective-permute-start(bf16[1,1,128]{2,1,0:T(2,128)(2,1)S(1)} %get-tuple-element.51), channel_id=1, source_target_pairs={{0,28},{4,16},{8,20},{12,24},{16,44},{20,32},{24,36},{28,40},{32,6... | collective-permute-start | bytes 776 | tf_op jit(solution)/shard_map/ppermute | solution.py:55
  180.8 30.5 %collective-permute-start.19 = (bf16[1,32,128]{2,1,0:T(8,128)(2,1)S(1)}, bf16[1,32,128]{2,1,0:T(8,128)(2,1)S(1)}, u32[]{:S(2)}, u32[]{:S(2)}) collective-permute-start(bf16[1,32,128]{2,1,0:T(8,128)(2,1)S(1)} %get-tuple-element.52), channel_id=1, source_target_pairs={{0,16},{4,20},{8,24},{12,28},{16,32},{20,36},{24,40},{28,44},{32,4... | collective-permute-start | bytes 24584 | tf_op jit(solution)/shard_map/ppermute | solution.py:55
  183.3 28.0 %collective-permute-start.24 = (bf16[1,32,128]{2,1,0:T(8,128)(2,1)S(1)}, bf16[1,32,128]{2,1,0:T(8,128)(2,1)S(1)}, u32[]{:S(2)}, u32[]{:S(2)}) collective-permute-start(bf16[1,32,128]{2,1,0:T(8,128)(2,1)S(1)} %get-tuple-element.53), channel_id=1, source_target_pairs={{0,496},{4,500},{8,504},{12,508},{16,0},{20,4},{24,8},{28,12},{32,... | collective-permute-start | bytes 24584 | tf_op jit(solution)/shard_map/ppermute | solution.py:55
  186.5 13.0 %collective-permute-start.23 = (bf16[1,1,128]{2,1,0:T(2,128)(2,1)S(1)}, bf16[1,1,128]{2,1,0:T(2,128)(2,1)S(1)}, u32[]{:S(2)}, u32[]{:S(2)}) collective-permute-start(bf16[1,1,128]{2,1,0:T(2,128)(2,1)S(1)} %get-tuple-element.50), channel_id=1, source_target_pairs={{0,500},{4,504},{8,508},{12,496},{16,4},{20,8},{24,12},{28,0},{32,... | collective-permute-start | bytes 776 | tf_op jit(solution)/shard_map/ppermute | solution.py:55
  199.5 11.8 %collective-permute-start.25 = (bf16[1,1,128]{2,1,0:T(2,128)(2,1)S(1)}, bf16[1,1,128]{2,1,0:T(2,128)(2,1)S(1)}, u32[]{:S(2)}, u32[]{:S(2)}) collective-permute-start(bf16[1,1,128]{2,1,0:T(2,128)(2,1)S(1)} %get-tuple-element.49), channel_id=1, source_target_pairs={{0,508},{4,496},{8,500},{12,504},{16,12},{20,0},{24,4},{28,8},{32,... | collective-permute-start | bytes 776 | tf_op jit(solution)/shard_map/ppermute | solution.py:55

commit v2 on v0

--- a/solution.py
+++ b/solution.py
@@ -8,19 +8,31 @@
 
 time_step = 0.4
 weno_floor = 1e-06
+SPAN = 3
 
 
-def extended(x, sides, width):
-    for axis, dim in sides:
-        size, length = (lax.axis_size(axis), x.shape[dim])
-        up = [(i, (i + 1) % size) for i in range(size)]
-        down = [(j, i) for i, j in up]
-        last = lax.slice_in_dim(x, length - width, length, axis=dim)
-        initial = lax.slice_in_dim(x, 0, width, axis=dim)
+def exchange(fields, axis, widths, dim):
+    size = lax.axis_size(axis)
+    up = [(i, (i + 1) % size) for i in range(size)]
+    down = [(j, i) for i, j in up]
+    out = []
+    for field, w in zip(fields, widths):
+        d = dim + field.ndim - 3
+        last = lax.slice_in_dim(field, field.shape[d] - w, field.shape[d], axis=d)
+        first = lax.slice_in_dim(field, 0, w, axis=d)
         before = lax.ppermute(last, axis, up)
-        after = lax.ppermute(initial, axis, down)
-        x = jnp.concatenate([before, x, after], axis=dim)
-    return x
+        after = lax.ppermute(first, axis, down)
+        out.append(jnp.concatenate([before, field, after], axis=d))
+    return out
+
+
+def z_faces(x):
+    size, length = (lax.axis_size("gz"), x.shape[2])
+    up = [(i, (i + 1) % size) for i in range(size)]
+    down = [(j, i) for i, j in up]
+    before = lax.ppermute(x[:, :, length - SPAN :], "gz", up)
+    after = lax.ppermute(x[:, :, :SPAN], "gz", down)
+    return jnp.concatenate([before, x, after], axis=2)
 
 
 def square(operand):
@@ -49,15 +61,14 @@
 
 
 def window(padded, axis_dim, offset):
-    slicing = [slice(3, extent - 3) for extent in padded.shape]
-    length = padded.shape[axis_dim] - 6
-    slicing[axis_dim] = slice(3 + offset, 3 + offset + length)
-    return padded[tuple(slicing)]
+    length = padded.shape[axis_dim] - 2 * SPAN
+    return lax.slice_in_dim(padded, SPAN + offset, SPAN + offset + length, axis=axis_dim)
 
 
-def local_rate(padded, velocity_window):
-    summed = jnp.zeros(velocity_window.shape[1:], jnp.float32)
+def local_rate(padded_list, speeds):
+    summed = jnp.zeros(speeds.shape[1:], jnp.float32)
     for axis_dim in range(3):
+        padded = padded_list[axis_dim]
         jump_list = [
             window(padded, axis_dim, offset) - window(padded, axis_dim, offset - 1)
             for offset in range(-2, 4)
@@ -66,7 +77,7 @@
         from_right = weno_value(
             jump_list[5], jump_list[4], jump_list[3], jump_list[2], jump_list[1]
         )
-        speed_axis = velocity_window[axis_dim].astype(jnp.float32)
+        speed_axis = speeds[axis_dim]
         summed = (
             summed
             + jnp.maximum(speed_axis, 0.0) * from_left
@@ -106,23 +117,40 @@
     return jnp.concatenate([colour, clear], 0)
 
 
+def stage_rate(field, speeds):
+    inner = field[SPAN:-SPAN, SPAN:-SPAN]
+    padded = [field[:, SPAN:-SPAN], field[SPAN:-SPAN, :], z_faces(inner)]
+    return inner, local_rate(padded, speeds)
+
+
 def shards(level_set, velocity, active_brick, depth_order):
+    alive = active_brick[0, 0, 0] > 0
+    alive_float = alive.astype(jnp.float32)
+    flags = jnp.broadcast_to(alive_float, level_set.shape)
+    stacked = jnp.stack([level_set] + [velocity[d].astype(jnp.float32) for d in range(3)] + [flags])
+    halo = 3 * SPAN + 1
+    stacked = exchange([stacked], "gx", [halo], 0)[0]
+    stacked = exchange([stacked], "gy", [halo], 1)[0]
+    level_ext = stacked[0]
+    speed_ext = stacked[1:4, SPAN:-SPAN, SPAN:-SPAN]
+    flag_ext = stacked[4, 3 * SPAN : -3 * SPAN, 3 * SPAN : -3 * SPAN]
+    speed_two = speed_ext[:, SPAN:-SPAN, SPAN:-SPAN]
+    speed_three = speed_two[:, SPAN:-SPAN, SPAN:-SPAN]
 
-    def section_rate(level_field):
-        padded = extended(level_field, (("gx", 0), ("gy", 1), ("gz", 2)), 3)
-        return local_rate(padded, velocity)
+    inner, rate = stage_rate(level_ext, speed_ext)
+    section_one = inner + time_step * rate
+    inner, rate = stage_rate(section_one, speed_two)
+    section_two = 0.75 * level_ext[2 * SPAN : -2 * SPAN, 2 * SPAN : -2 * SPAN] + 0.25 * (
+        inner + time_step * rate
+    )
+    inner, rate = stage_rate(section_two, speed_three)
+    level_ring = level_ext[3 * SPAN : -3 * SPAN, 3 * SPAN : -3 * SPAN]
+    advanced = level_ring / 3.0 + 2.0 / 3.0 * (inner + time_step * rate)
+    rim = jnp.where(flag_ext > 0, advanced, level_ring)
+    level_out = rim[1:-1, 1:-1]
 
-    section_one = level_set + time_step * section_rate(level_set)
-    section_two = 0.75 * level_set + 0.25 * (section_one + time_step * section_rate(section_one))
-    advanced = level_set / 3.0 + 2.0 / 3.0 * (section_two + time_step * section_rate(section_two))
-    alive = active_brick[0, 0, 0] > 0
-    level_out = jnp.where(alive, advanced, level_set)
-    alive_float = alive.astype(jnp.float32)
     group = lax.axis_size("gz")
     ascending = depth_order[0] < depth_order[group - 1]
-    rim = extended(level_out.astype(jnp.bfloat16), (("gx", 0), ("gy", 1)), 1).astype(
-        level_out.dtype
-    )
     left_x = 0.75 * rim[1:-1] + 0.25 * rim[:-2]
     right_x = 0.75 * rim[1:-1] + 0.25 * rim[2:]
     grid_pairs = []

time: 197 us -> 211 us (1.071)
  the two profiles are of different devices: /device:TPU:8 before, /device:TPU:32 now
where the time goes in v2:
time: 211 us; the launch traced here: 210 us
  waiting for transfers between devices  59.2 us (28%)
  other arithmetic  58.6 us (28%)
  starting transfers between devices  48.6 us (23%)
  local copies, waits for them, and re-layouts  34.7 us (16%)
  matrix products  5.91 us (3%)
  between operations  3.07 us (1%)
    ppermute x2, waiting for transfers between devices, exchange(): before = lax.ppermute(last, axis, up)  27.9 us
    ppermute x2, waiting for transfers between devices, exchange(): after = lax.ppermute(first, axis, down)  26.2 us
    add x1, other arithmetic, shards(): section_one = inner + time_step * rate  22.6 us
    ppermute x2, starting transfers between devices, exchange(): after = lax.ppermute(first, axis, down)  17 us
    add x1, other arithmetic, shards(): 0.75 * level_ext[2 * SPAN:-2 * SPAN, 2 * SPAN:-2 * SPAN]  16 us
    select_n x1, other arithmetic, shards(): rim = jnp.where(flag_ext > 0, advanced, level_ring)  14.6 us
    ppermute x3, starting transfers between devices, z_faces(): before = lax.ppermute(x[:, :, length - SPAN:], 'gz', up)  13.1 us
    slice x6, local copies, waits for them, and re-layouts, z_faces(): before = lax.ppermute(x[:, :, length - SPAN:], 'gz', up)  8.72 us
  transfers between devices with their start and end apart: 11, of which 7 were waited for; matrix products, arithmetic and copies ran while one was open for 7% of the time, Pallas kernels for 0%

profile of v2, /device:TPU:32, one launch (start us, length us, event | category | flops | bytes accessed | tf_op | source)
XLA Modules:
  0.0 210.0 jit_solution(15218150850532959262)
XLA Ops:
  1.4 1.1 bitcast_dynamic-update-slice_fusion
  2.8 1.9 collective-permute-start
  4.7 13.5 %collective-permute-start.1 = (f32[5,10,32,128]{3,2,1,0:T(8,128)S(1)}, f32[5,10,32,128]{3,2,1,0:T(8,128)S(1)}, u32[]{:S(2)}, u32[]{:S(2)}) collective-permute-start(f32[5,10,32,128]{3,2,1,0:T(8,128)S(1)} %get-tuple-element.21), channel_id=1, source_target_pairs={{16,0},{32,16},{48,32},{64,48},{80,64},{96,80},{112,96},{128,112},... | collective-permute-start | bytes 2457608 | tf_op jit(solution)/shard_map/ppermute | solution.py:24
  18.2 23.1 %collective-permute-done = f32[5,10,32,128]{3,2,1,0:T(8,128)S(1)} collective-permute-done((f32[5,10,32,128]{3,2,1,0:T(8,128)S(1)}, f32[5,10,32,128]{3,2,1,0:T(8,128)S(1)}, u32[]{:S(2)}, u32[]{:S(2)}) %collective-permute-start) | collective-permute-done | bytes 819232 | tf_op jit(solution)/shard_map/ppermute | solution.py:23
  41.3 11.7 %collective-permute-done.1 = f32[5,10,32,128]{3,2,1,0:T(8,128)S(1)} collective-permute-done((f32[5,10,32,128]{3,2,1,0:T(8,128)S(1)}, f32[5,10,32,128]{3,2,1,0:T(8,128)S(1)}, u32[]{:S(2)}, u32[]{:S(2)}) %collective-permute-start.1) | collective-permute-done | bytes 819232 | tf_op jit(solution)/shard_map/ppermute | solution.py:24
  54.2 3.5 %collective-permute-start.3 = (f32[5,52,10,128]{3,1,2,0:T(8,128)S(1)}, f32[5,52,10,128]{3,1,2,0:T(8,128)S(1)}, u32[]{:S(2)}, u32[]{:S(2)}) collective-permute-start(f32[5,52,10,128]{3,1,2,0:T(8,128)S(1)} %copy.8), channel_id=1, source_target_pairs={{4,0},{8,4},{12,8},{0,12},{5,1},{9,5},{13,9},{1,13},{6,2},{10,6},{... | collective-permute-start | bytes 3993608 | tf_op jit(solution)/shard_map/ppermute | solution.py:24
  58.2 2.3 %collective-permute-start.2 = (f32[5,52,10,128]{3,1,2,0:T(8,128)S(1)}, f32[5,52,10,128]{3,1,2,0:T(8,128)S(1)}, u32[]{:S(2)}, u32[]{:S(2)}) collective-permute-start(f32[5,52,10,128]{3,1,2,0:T(8,128)S(1)} %copy.7), channel_id=1, source_target_pairs={{0,4},{4,8},{8,12},{12,0},{1,5},{5,9},{9,13},{13,1},{2,6},{6,10},{... | collective-permute-start | bytes 3993608 | tf_op jit(solution)/shard_map/ppermute | solution.py:23
  60.5 14.5 %collective-permute-done.3 = f32[5,52,10,128]{3,1,2,0:T(8,128)S(1)} collective-permute-done((f32[5,52,10,128]{3,1,2,0:T(8,128)S(1)}, f32[5,52,10,128]{3,1,2,0:T(8,128)S(1)}, u32[]{:S(2)}, u32[]{:S(2)}) %collective-permute-start.3) | collective-permute-done | bytes 1331232 | tf_op jit(solution)/shard_map/ppermute | solution.py:24
  75.4 4.8 %collective-permute-done.2 = f32[5,52,10,128]{3,1,2,0:T(8,128)S(1)} collective-permute-done((f32[5,52,10,128]{3,1,2,0:T(8,128)S(1)}, f32[5,52,10,128]{3,1,2,0:T(8,128)S(1)}, u32[]{:S(2)}, u32[]{:S(2)}) %collective-permute-start.2) | collective-permute-done | bytes 1331232 | tf_op jit(solution)/shard_map/ppermute | solution.py:23
  80.6 2.7 %pad_maximum_fusion = f32[5,52,52,128]{3,2,1,0:T(8,128)S(1)} fusion(f32[5,52,10,128]{3,2,1,0:T(8,128)S(1)} %copy.10, f32[5,10,32,128]{3,2,1,0:T(8,128)S(1)} %collective-permute-done.1, f32[5,32,32,128]{3,2,1,0:T(8,128)S(1)} %broadcast_dynamic-update-slice_fusion, f32[5,10,32,128]{3,2,1,0:T(8,128)S(1)} %collective-permute-done, f32[5,52,10,128]{3,2,1,0:T(8,128)S(1)} %copy.9), kind=kLoop, calls=%fused_computation | loop fusion | flops 6922240 | bytes 13844480 | tf_op jit(solution)/shard_map/concatenate | solution.py:25
  83.4 1.8 fusion.323
  85.2 1.4 copy-done
  86.6 1.7 copy.11
  88.3 6.3 %collective-permute-start.4 = (f32[46,46,3]{1,0,2:T(8,128)S(1)}, f32[46,46,3]{1,0,2:T(8,128)S(1)}, u32[]{:S(2)}, u32[]{:S(2)}) collective-permute-start(f32[46,46,3]{1,0,2:T(8,128)S(1)} %copy.11), channel_id=1, source_target_pairs={{0,1},{1,2},{2,3},{3,0},{4,5},{5,6},{6,7},{7,4},{8,9},{9,10},{10,1... | collective-permute-start | bytes 76184 | tf_op jit(solution)/shard_map/ppermute | solution.py:33
  95.1 1.9 collective-permute-start.5
  97.1 2.5 %slice_bitcast_fusion.1 = f32[46,52,128]{2,1,0:T(8,128)} fusion(f32[5,52,52,128]{3,2,1,0:T(8,128)} %copy-done), kind=kLoop, calls=%fused_computation.27 | loop fusion | bytes 2449408 | tf_op jit(solution)/shard_map/slice | solution.py:122
  99.6 1.2 slice.561
  100.8 1.5 copy.12
  102.3 1.5 copy.14
  103.8 22.6 %fusion.13 = f32[46,46,128]{2,1,0:T(8,128)S(1)} fusion(f32[46,46,128]{2,1,0:T(8,128)} %slice.561, f32[46,46,3]{2,1,0:T(8,128)} %copy.14, f32[46,46,3]{2,1,0:T(8,128)} %copy.12, f32[5,52,52,128]{3,2,1,0:T(8,128)} %copy-done, f32[46,52,128]{2,1,0:T(8,128)} %slice_bitcast_fusion.1, f32[52,52,128]{2,1,0:T(8,128)S(1)} %slice_bitcast_fusion), kind=kLoop, calls=%fused_computation.52 | loop fusion | flops 112672768 | bytes 19551840 | tf_op jit(solution)/shard_map/add | solution.py:141
  126.4 1.2 fusion.324
  127.6 1.5 copy.15
  129.1 3.9 %collective-permute-start.6 = (f32[40,40,3]{1,0,2:T(8,128)S(1)}, f32[40,40,3]{1,0,2:T(8,128)}, u32[]{:S(2)}, u32[]{:S(2)}) collective-permute-start(f32[40,40,3]{1,0,2:T(8,128)S(1)} %copy.15), channel_id=1, source_target_pairs={{0,1},{1,2},{2,3},{3,0},{4,5},{5,6},{6,7},{7,4},{8,9},{9,10},{10,1... | collective-permute-start | bytes 57608 | tf_op jit(solution)/shard_map/ppermute | solution.py:33
  133.0 1.0 copy.17
  134.0 2.1 collective-permute-start.7
  136.1 1.0 slice.589
  137.1 2.1 %copy.16 = f32[40,40,3]{2,1,0:T(8,128)} copy(f32[40,40,3]{1,0,2:T(8,128)} %collective-permute-done.6) | data formatting | bytes 38400 | tf_op jit(solution)/shard_map/ppermute | solution.py:33
  139.2 1.1 collective-permute-done.7
  140.3 1.3 copy.18
  141.6 16.0 %fusion.71 = f32[40,40,128]{2,1,0:T(8,128)S(1)} fusion(f32[52,52,128]{2,1,0:T(8,128)S(1)} %slice_bitcast_fusion, f32[40,40,128]{2,1,0:T(8,128)} %slice.589, f32[40,40,3]{2,1,0:T(8,128)} %copy.18, f32[40,40,3]{2,1,0:T(8,128)} %copy.16, f32[5,52,52,128]{3,2,1,0:T(8,128)} %copy-done, f32[46,46,128]{2,1,0:T(8,128)S(1)} %fusion.13), kind=kLoop, calls=%fused_computation.134 | loop fusion | flops 85811200 | bytes 14784000 | tf_op jit(solution)/shard_map/add | solution.py:143
  157.7 1.1 fusion.325
  158.8 1.5 copy.19
  160.2 2.8 %collective-permute-start.8 = (f32[34,34,3]{1,0,2:T(8,128)S(1)}, f32[34,34,3]{1,0,2:T(8,128)S(1)}, u32[]{:S(2)}, u32[]{:S(2)}) collective-permute-start(f32[34,34,3]{1,0,2:T(8,128)S(1)} %copy.19), channel_id=1, source_target_pairs={{0,1},{1,2},{2,3},{3,0},{4,5},{5,6},{6,7},{7,4},{8,9},{9,10},{10,1... | collective-permute-start | bytes 41624 | tf_op jit(solution)/shard_map/ppermute | solution.py:33
  163.4 3.4 %collective-permute-start.9 = (f32[34,34,3]{1,0,2:T(8,128)S(1)}, f32[34,34,3]{1,0,2:T(8,128)S(1)}, u32[]{:S(2)}, u32[]{:S(2)}) collective-permute-start(f32[34,34,3]{1,0,2:T(8,128)S(1)} %copy.21), channel_id=1, source_target_pairs={{1,0},{2,1},{3,2},{0,3},{5,4},{6,5},{7,6},{4,7},{9,8},{10,9},{11,1... | collective-permute-start | bytes 41624 | tf_op jit(solution)/shard_map/ppermute | solution.py:34
  168.7 0.9 slice.615
  169.6 1.3 copy.20
  171.1 1.3 copy.22
  172.4 14.6 %fusion.167 = f32[34,34,128]{2,1,0:T(8,128)S(1)} fusion(f32[34,34,128]{2,1,0:T(8,128)} %slice.615, f32[34,34,3]{2,1,0:T(8,128)} %copy.22, f32[34,34,3]{2,1,0:T(8,128)} %copy.20, f32[5,52,52,128]{3,2,1,0:T(8,128)} %copy-done, f32[40,40,128]{2,1,0:T(8,128)S(1)} %fusion.71, f32[52,52,128]{2,1,0:T(8,128)S(1)} %slice_bitcast_fusion), kind=kLoop, calls=%fused_computation.268 | loop fusion | flops 62294528 | bytes 11273312 | tf_op jit(solution)/shard_map/jit(_where)/select_n | solution.py:149
  187.4 1.2 multiply_reduce_fusion.7
  188.6 1.2 multiply_reduce_fusion.5
  189.8 1.2 multiply_reduce_fusion.3
  191.0 1.2 multiply_reduce_fusion.1
  192.3 1.3 copy.23
  194.2 0.8 reshape.109
  195.0 6.9 %all-to-all-start = ((f32[4,1,4096]{2,1,0:T(1,128)}), f32[4,1,4096]{2,1,0:T(1,128)S(1)}, u32[]{:S(2)}, u32[]{:S(2)}) async-start(f32[4,1,4096]{2,1,0:T(1,128)} %reshape.109), calls=%async_computation | async-start | bytes 131072 | tf_op jit(solution)/shard_map/all_to_all | solution.py:167
  201.9 0.9 slice.641
  202.8 3.8 %all-to-all-done = f32[4,1,4096]{2,1,0:T(1,128)S(1)} async-done(((f32[4,1,4096]{2,1,0:T(1,128)}), f32[4,1,4096]{2,1,0:T(1,128)S(1)}, u32[]{:S(2)}, u32[]{:S(2)}) %all-to-all-start) | async-done | bytes 65568 | tf_op jit(solution)/shard_map/all_to_all | solution.py:167
  207.1 0.8 reduce
  (48 shorter events, 8.2 us)
Async XLA Ops:
  0.6 1.8 copy-start.1
  2.8 38.5 %collective-permute-start = (f32[5,10,32,128]{3,2,1,0:T(8,128)S(1)}, f32[5,10,32,128]{3,2,1,0:T(8,128)S(1)}, u32[]{:S(2)}, u32[]{:S(2)}) collective-permute-start(f32[5,10,32,128]{3,2,1,0:T(8,128)S(1)} %get-tuple-element.20), channel_id=1, source_target_pairs={{0,16},{16,32},{32,48},{48,64},{64,80},{80,96},{96,112},{112,128},... | collective-permute-start | bytes 2457608 | tf_op jit(solution)/shard_map/ppermute | solution.py:23
  4.7 48.2 %collective-permute-start.1 = (f32[5,10,32,128]{3,2,1,0:T(8,128)S(1)}, f32[5,10,32,128]{3,2,1,0:T(8,128)S(1)}, u32[]{:S(2)}, u32[]{:S(2)}) collective-permute-start(f32[5,10,32,128]{3,2,1,0:T(8,128)S(1)} %get-tuple-element.21), channel_id=1, source_target_pairs={{16,0},{32,16},{48,32},{64,48},{80,64},{96,80},{112,96},{128,112},... | collective-permute-start | bytes 2457608 | tf_op jit(solution)/shard_map/ppermute | solution.py:24
  54.2 20.8 %collective-permute-start.3 = (f32[5,52,10,128]{3,1,2,0:T(8,128)S(1)}, f32[5,52,10,128]{3,1,2,0:T(8,128)S(1)}, u32[]{:S(2)}, u32[]{:S(2)}) collective-permute-start(f32[5,52,10,128]{3,1,2,0:T(8,128)S(1)} %copy.8), channel_id=1, source_target_pairs={{4,0},{8,4},{12,8},{0,12},{5,1},{9,5},{13,9},{1,13},{6,2},{10,6},{... | collective-permute-start | bytes 3993608 | tf_op jit(solution)/shard_map/ppermute | solution.py:24
  58.2 22.0 %collective-permute-start.2 = (f32[5,52,10,128]{3,1,2,0:T(8,128)S(1)}, f32[5,52,10,128]{3,1,2,0:T(8,128)S(1)}, u32[]{:S(2)}, u32[]{:S(2)}) collective-permute-start(f32[5,52,10,128]{3,1,2,0:T(8,128)S(1)} %copy.7), channel_id=1, source_target_pairs={{0,4},{4,8},{8,12},{12,0},{1,5},{5,9},{9,13},{13,1},{2,6},{6,10},{... | collective-permute-start | bytes 3993608 | tf_op jit(solution)/shard_map/ppermute | solution.py:23
  83.3 3.3 %copy-start = (f32[5,52,52,128]{3,2,1,0:T(8,128)}, f32[5,52,52,128]{3,2,1,0:T(8,128)S(1)}, u32[]{:S(2)}) copy-start(f32[5,52,52,128]{3,2,1,0:T(8,128)S(1)} %pad_maximum_fusion) | copy-start | bytes 20766724
  88.3 12.4 %collective-permute-start.4 = (f32[46,46,3]{1,0,2:T(8,128)S(1)}, f32[46,46,3]{1,0,2:T(8,128)S(1)}, u32[]{:S(2)}, u32[]{:S(2)}) collective-permute-start(f32[46,46,3]{1,0,2:T(8,128)S(1)} %copy.11), channel_id=1, source_target_pairs={{0,1},{1,2},{2,3},{3,0},{4,5},{5,6},{6,7},{7,4},{8,9},{9,10},{10,1... | collective-permute-start | bytes 76184 | tf_op jit(solution)/shard_map/ppermute | solution.py:33
  95.1 7.1 %collective-permute-start.5 = (f32[46,46,3]{1,0,2:T(8,128)S(1)}, f32[46,46,3]{1,0,2:T(8,128)S(1)}, u32[]{:S(2)}, u32[]{:S(2)}) collective-permute-start(f32[46,46,3]{1,0,2:T(8,128)S(1)} %copy.13), channel_id=1, source_target_pairs={{1,0},{2,1},{3,2},{0,3},{5,4},{6,5},{7,6},{4,7},{9,8},{10,9},{11,1... | collective-permute-start | bytes 76184 | tf_op jit(solution)/shard_map/ppermute | solution.py:34
  129.1 8.0 %collective-permute-start.6 = (f32[40,40,3]{1,0,2:T(8,128)S(1)}, f32[40,40,3]{1,0,2:T(8,128)}, u32[]{:S(2)}, u32[]{:S(2)}) collective-permute-start(f32[40,40,3]{1,0,2:T(8,128)S(1)} %copy.15), channel_id=1, source_target_pairs={{0,1},{1,2},{2,3},{3,0},{4,5},{5,6},{6,7},{7,4},{8,9},{9,10},{10,1... | collective-permute-start | bytes 57608 | tf_op jit(solution)/shard_map/ppermute | solution.py:33
  134.0 6.3 %collective-permute-start.7 = (f32[40,40,3]{1,0,2:T(8,128)}, f32[40,40,3]{1,0,2:T(8,128)S(1)}, u32[]{:S(2)}, u32[]{:S(2)}) collective-permute-start(f32[40,40,3]{1,0,2:T(8,128)} %copy.17), channel_id=1, source_target_pairs={{1,0},{2,1},{3,2},{0,3},{5,4},{6,5},{7,6},{4,7},{9,8},{10,9},{11,1... | collective-permute-start | bytes 57608 | tf_op jit(solution)/shard_map/ppermute | solution.py:34
  158.8 8.0 %copy-start.2 = (s32[4]{0:T(128)S(1)}, s32[4]{0:T(128)}, u32[]{:S(2)}) copy-start(s32[4]{0:T(128)} %param.7) | copy-start | bytes 52
  160.2 9.4 %collective-permute-start.8 = (f32[34,34,3]{1,0,2:T(8,128)S(1)}, f32[34,34,3]{1,0,2:T(8,128)S(1)}, u32[]{:S(2)}, u32[]{:S(2)}) collective-permute-start(f32[34,34,3]{1,0,2:T(8,128)S(1)} %copy.19), channel_id=1, source_target_pairs={{0,1},{1,2},{2,3},{3,0},{4,5},{5,6},{6,7},{7,4},{8,9},{9,10},{10,1... | collective-permute-start | bytes 41624 | tf_op jit(solution)/shard_map/ppermute | solution.py:33
  163.4 7.6 %collective-permute-start.9 = (f32[34,34,3]{1,0,2:T(8,128)S(1)}, f32[34,34,3]{1,0,2:T(8,128)S(1)}, u32[]{:S(2)}, u32[]{:S(2)}) collective-permute-start(f32[34,34,3]{1,0,2:T(8,128)S(1)} %copy.21), channel_id=1, source_target_pairs={{1,0},{2,1},{3,2},{0,3},{5,4},{6,5},{7,6},{4,7},{9,8},{10,9},{11,1... | collective-permute-start | bytes 41624 | tf_op jit(solution)/shard_map/ppermute | solution.py:34
  195.0 11.5 %all-to-all-start = ((f32[4,1,4096]{2,1,0:T(1,128)}), f32[4,1,4096]{2,1,0:T(1,128)S(1)}, u32[]{:S(2)}, u32[]{:S(2)}) async-start(f32[4,1,4096]{2,1,0:T(1,128)} %reshape.109), calls=%async_computation | async-start | bytes 131072 | tf_op jit(solution)/shard_map/all_to_all | solution.py:167

commit v3 on v2

--- a/solution.py
+++ b/solution.py
@@ -24,6 +24,36 @@
         after = lax.ppermute(first, axis, down)
         out.append(jnp.concatenate([before, field, after], axis=d))
     return out
+
+
+def exchange_packed(fields, axis, widths):
+    size = lax.axis_size(axis)
+    up = [(i, (i + 1) % size) for i in range(size)]
+    down = [(j, i) for i, j in up]
+    dims = [field.ndim - 3 for field in fields]
+    lasts = [
+        lax.slice_in_dim(field, field.shape[d] - w, field.shape[d], axis=d)
+        for field, w, d in zip(fields, widths, dims)
+    ]
+    firsts = [lax.slice_in_dim(field, 0, w, axis=d) for field, w, d in zip(fields, widths, dims)]
+
+    def pack(parts):
+        return jnp.concatenate([part.reshape(-1, part.shape[-1]) for part in parts], 0)
+
+    def unpack(flat, like):
+        out, at = [], 0
+        for part in like:
+            rows = part.size // part.shape[-1]
+            out.append(flat[at : at + rows].reshape(part.shape))
+            at += rows
+        return out
+
+    before = unpack(lax.ppermute(pack(lasts), axis, up), lasts)
+    after = unpack(lax.ppermute(pack(firsts), axis, down), firsts)
+    return [
+        jnp.concatenate([b, field, a], axis=d)
+        for b, field, a, d in zip(before, fields, after, dims)
+    ]
 
 
 def z_faces(x):
@@ -127,9 +157,14 @@
     alive = active_brick[0, 0, 0] > 0
     alive_float = alive.astype(jnp.float32)
     flags = jnp.broadcast_to(alive_float, level_set.shape)
-    stacked = jnp.stack([level_set] + [velocity[d].astype(jnp.float32) for d in range(3)] + [flags])
-    halo = 3 * SPAN + 1
-    stacked = exchange([stacked], "gx", [halo], 0)[0]
+    speeds = velocity.astype(jnp.float32)
+    halo, halo_speed = 3 * SPAN + 1, 2 * SPAN + 1
+    level_x, speed_x, flag_x = exchange_packed(
+        [level_set, speeds, flags], "gx", [halo, halo_speed, 1]
+    )
+    speed_x = jnp.pad(speed_x, ((0, 0), (halo - halo_speed,) * 2, (0, 0), (0, 0)))
+    flag_x = jnp.pad(flag_x, ((halo - 1,) * 2, (0, 0), (0, 0)))
+    stacked = jnp.concatenate([level_x[None], speed_x, flag_x[None]], 0)
     stacked = exchange([stacked], "gy", [halo], 1)[0]
     level_ext = stacked[0]
     speed_ext = stacked[1:4, SPAN:-SPAN, SPAN:-SPAN]

time: 211 us -> 207 us (0.981)
  waiting for transfers between devices: 59.2 us -> 44.5 us
  starting transfers between devices: 48.6 us -> 60 us
    ppermute x2 -> x1, waiting for transfers between devices: 27.9 us -> 5.7 us  [exchange(): before = lax.ppermute(last, axis, up)]
    ppermute x0 -> x2, waiting for transfers between devices: none -> 20.8 us  [the longest x1 20 us: exchange_packed(): after = unpack(lax.ppermute(pack(firsts), axis, down), firsts)]
    ppermute x0 -> x2, starting transfers between devices: none -> 15.4 us  [the longest x1 13.5 us: exchange_packed(): after = unpack(lax.ppermute(pack(firsts), axis, down), firsts)]
    ppermute x2 -> x1, waiting for transfers between devices: 26.2 us -> 14.1 us  [exchange(): after = lax.ppermute(first, axis, down)]
    ppermute x2 -> x1, starting transfers between devices: 17 us -> 4.92 us  [exchange(): after = lax.ppermute(first, axis, down)]
    ppermute x3, starting transfers between devices: 7.36 us -> 17.1 us  [z_faces(): after = lax.ppermute(x[:, :, :SPAN], 'gz', down)]
    ppermute x2 -> x1, starting transfers between devices: 4.23 us -> 1.92 us  [exchange(): before = lax.ppermute(last, axis, up)]
  transfers between devices with their start and end apart: 11 -> 11, of which waited for: 7 -> 6; matrix products, arithmetic and copies ran while one was open for 7% -> 7% of each run, Pallas kernels for 0% -> 0%
where the time goes in v3:
time: 207 us; the launch traced here: 206 us
  starting transfers between devices  60 us (29%)
  other arithmetic  57.7 us (28%)
  waiting for transfers between devices  44.5 us (21%)
  local copies, waits for them, and re-layouts  34.8 us (17%)
  matrix products  5.89 us (3%)
  between operations  3.13 us (2%)
    add x1, other arithmetic, shards(): section_one = inner + time_step * rate  22.6 us
    ppermute x1, waiting for transfers between devices, exchange_packed(): after = unpack(lax.ppermute(pack(firsts), axis, down), firsts)  20 us
    ppermute x3, starting transfers between devices, z_faces(): after = lax.ppermute(x[:, :, :SPAN], 'gz', down)  17.1 us
    add x1, other arithmetic, shards(): 0.75 * level_ext[2 * SPAN:-2 * SPAN, 2 * SPAN:-2 * SPAN]  16 us
    select_n x1, other arithmetic, shards(): rim = jnp.where(flag_ext > 0, advanced, level_ring)  14.6 us
    ppermute x1, waiting for transfers between devices, exchange(): after = lax.ppermute(first, axis, down)  14.1 us
    ppermute x3, starting transfers between devices, z_faces(): before = lax.ppermute(x[:, :, length - SPAN:], 'gz', up)  13.6 us
    ppermute x1, starting transfers between devices, exchange_packed(): after = unpack(lax.ppermute(pack(firsts), axis, down), firsts)  13.5 us
  transfers between devices with their start and end apart: 11, of which 6 were waited for; matrix products, arithmetic and copies ran while one was open for 7% of the time, Pallas kernels for 0%

profile of v3, /device:TPU:32, one launch (start us, length us, event | category | flops | bytes accessed | tf_op | source)
XLA Modules:
  0.0 206.0 jit_solution(12788958935901536493)
XLA Ops:
  1.3 1.1 fusion.326
  2.8 13.5 %collective-permute-start.1 = (f32[1024,128]{1,0:T(8,128)S(1)}, f32[1024,128]{1,0:T(8,128)S(1)}, u32[]{:S(2)}, u32[]{:S(2)}) collective-permute-start(f32[1024,128]{1,0:T(8,128)S(1)} %get-tuple-element.41), channel_id=1, source_target_pairs={{16,0},{32,16},{48,32},{64,48},{80,64},{96,80},{112,96},{128,112},... | collective-permute-start | bytes 1572872 | tf_op jit(solution)/shard_map/ppermute | solution.py:52
  16.3 1.9 collective-permute-start
  18.5 20.0 %collective-permute-done.1 = f32[1024,128]{1,0:T(8,128)S(1)} collective-permute-done((f32[1024,128]{1,0:T(8,128)S(1)}, f32[1024,128]{1,0:T(8,128)S(1)}, u32[]{:S(2)}, u32[]{:S(2)}) %collective-permute-start.1) | collective-permute-done | bytes 524320 | tf_op jit(solution)/shard_map/ppermute | solution.py:52
  38.5 0.8 collective-permute-done
  41.4 4.9 %collective-permute-start.3 = (f32[5,52,10,128]{3,1,2,0:T(8,128)S(1)}, f32[5,52,10,128]{3,1,2,0:T(8,128)S(1)}, u32[]{:S(2)}, u32[]{:S(2)}) collective-permute-start(f32[5,52,10,128]{3,1,2,0:T(8,128)S(1)} %copy.8), channel_id=1, source_target_pairs={{4,0},{8,4},{12,8},{0,12},{5,1},{9,5},{13,9},{1,13},{6,2},{10,6},{... | collective-permute-start | bytes 3993608 | tf_op jit(solution)/shard_map/ppermute | solution.py:24
  46.7 1.9 collective-permute-start.2
  48.6 14.1 %collective-permute-done.3 = f32[5,52,10,128]{3,1,2,0:T(8,128)S(1)} collective-permute-done((f32[5,52,10,128]{3,1,2,0:T(8,128)S(1)}, f32[5,52,10,128]{3,1,2,0:T(8,128)S(1)}, u32[]{:S(2)}, u32[]{:S(2)}) %collective-permute-start.3) | collective-permute-done | bytes 1331232 | tf_op jit(solution)/shard_map/ppermute | solution.py:24
  63.0 5.7 %collective-permute-done.2 = f32[5,52,10,128]{3,1,2,0:T(8,128)S(1)} collective-permute-done((f32[5,52,10,128]{3,1,2,0:T(8,128)S(1)}, f32[5,52,10,128]{3,1,2,0:T(8,128)S(1)}, u32[]{:S(2)}, u32[]{:S(2)}) %collective-permute-start.2) | collective-permute-done | bytes 1331232 | tf_op jit(solution)/shard_map/ppermute | solution.py:23
  69.1 1.1 pad_maximum_fusion
  70.3 1.8 fusion.323
  72.0 1.4 copy-done
  73.5 1.7 copy.11
  75.2 7.8 %collective-permute-start.4 = (f32[46,46,3]{1,0,2:T(8,128)S(1)}, f32[46,46,3]{1,0,2:T(8,128)S(1)}, u32[]{:S(2)}, u32[]{:S(2)}) collective-permute-start(f32[46,46,3]{1,0,2:T(8,128)S(1)} %copy.11), channel_id=1, source_target_pairs={{0,1},{1,2},{2,3},{3,0},{4,5},{5,6},{6,7},{7,4},{8,9},{9,10},{10,1... | collective-permute-start | bytes 76184 | tf_op jit(solution)/shard_map/ppermute | solution.py:63
  83.5 7.5 %collective-permute-start.5 = (f32[46,46,3]{1,0,2:T(8,128)S(1)}, f32[46,46,3]{1,0,2:T(8,128)S(1)}, u32[]{:S(2)}, u32[]{:S(2)}) collective-permute-start(f32[46,46,3]{1,0,2:T(8,128)S(1)} %copy.13), channel_id=1, source_target_pairs={{1,0},{2,1},{3,2},{0,3},{5,4},{6,5},{7,6},{4,7},{9,8},{10,9},{11,1... | collective-permute-start | bytes 76184 | tf_op jit(solution)/shard_map/ppermute | solution.py:64
  91.0 2.5 %slice_bitcast_fusion.1 = f32[46,52,128]{2,1,0:T(8,128)} fusion(f32[5,52,52,128]{3,2,1,0:T(8,128)} %copy-done), kind=kLoop, calls=%fused_computation.32 | loop fusion | bytes 2449408 | tf_op jit(solution)/shard_map/slice | solution.py:152
  93.5 1.2 slice.589
  94.7 1.5 copy.12
  96.2 1.5 copy.14
  97.7 22.6 %fusion.14 = f32[46,46,128]{2,1,0:T(8,128)S(1)} fusion(f32[46,46,128]{2,1,0:T(8,128)} %slice.589, f32[46,46,3]{2,1,0:T(8,128)} %copy.14, f32[46,46,3]{2,1,0:T(8,128)} %copy.12, f32[5,52,52,128]{3,2,1,0:T(8,128)} %copy-done, f32[46,52,128]{2,1,0:T(8,128)} %slice_bitcast_fusion.1, f32[52,52,128]{2,1,0:T(8,128)S(1)} %slice_bitcast_fusion), kind=kLoop, calls=%fused_computation.57 | loop fusion | flops 112672768 | bytes 19551840 | tf_op jit(solution)/shard_map/add | solution.py:176
  120.3 1.2 fusion.324
  121.5 1.5 copy.15
  123.0 1.9 collective-permute-start.6
  125.0 1.0 copy.17
  125.9 5.9 %collective-permute-start.7 = (f32[40,40,3]{1,0,2:T(8,128)}, f32[40,40,3]{1,0,2:T(8,128)S(1)}, u32[]{:S(2)}, u32[]{:S(2)}) collective-permute-start(f32[40,40,3]{1,0,2:T(8,128)} %copy.17), channel_id=1, source_target_pairs={{1,0},{2,1},{3,2},{0,3},{5,4},{6,5},{7,6},{4,7},{9,8},{10,9},{11,1... | collective-permute-start | bytes 57608 | tf_op jit(solution)/shard_map/ppermute | solution.py:64
  131.8 1.0 slice.617
  132.8 2.1 %copy.16 = f32[40,40,3]{2,1,0:T(8,128)} copy(f32[40,40,3]{1,0,2:T(8,128)} %collective-permute-done.6) | data formatting | bytes 38400 | tf_op jit(solution)/shard_map/ppermute | solution.py:63
  134.9 1.3 copy.18
  136.2 16.0 %fusion.72 = f32[40,40,128]{2,1,0:T(8,128)S(1)} fusion(f32[52,52,128]{2,1,0:T(8,128)S(1)} %slice_bitcast_fusion, f32[40,40,128]{2,1,0:T(8,128)} %slice.617, f32[40,40,3]{2,1,0:T(8,128)} %copy.18, f32[40,40,3]{2,1,0:T(8,128)} %copy.16, f32[5,52,52,128]{3,2,1,0:T(8,128)} %copy-done, f32[46,46,128]{2,1,0:T(8,128)S(1)} %fusion.14), kind=kLoop, calls=%fused_computation.141 | loop fusion | flops 85811200 | bytes 14784000 | tf_op jit(solution)/shard_map/add | solution.py:178
  152.3 1.1 fusion.325
  153.4 1.5 copy.19
  154.9 3.9 %collective-permute-start.8 = (f32[34,34,3]{1,0,2:T(8,128)S(1)}, f32[34,34,3]{1,0,2:T(8,128)S(1)}, u32[]{:S(2)}, u32[]{:S(2)}) collective-permute-start(f32[34,34,3]{1,0,2:T(8,128)S(1)} %copy.19), channel_id=1, source_target_pairs={{0,1},{1,2},{2,3},{3,0},{4,5},{5,6},{6,7},{7,4},{8,9},{9,10},{10,1... | collective-permute-start | bytes 41624 | tf_op jit(solution)/shard_map/ppermute | solution.py:63
  159.1 3.7 %collective-permute-start.9 = (f32[34,34,3]{1,0,2:T(8,128)S(1)}, f32[34,34,3]{1,0,2:T(8,128)S(1)}, u32[]{:S(2)}, u32[]{:S(2)}) collective-permute-start(f32[34,34,3]{1,0,2:T(8,128)S(1)} %copy.21), channel_id=1, source_target_pairs={{1,0},{2,1},{3,2},{0,3},{5,4},{6,5},{7,6},{4,7},{9,8},{10,9},{11,1... | collective-permute-start | bytes 41624 | tf_op jit(solution)/shard_map/ppermute | solution.py:64
  164.8 0.9 slice.643
  165.7 1.3 copy.20
  167.1 1.3 copy.22
  168.3 14.6 %fusion.168 = f32[34,34,128]{2,1,0:T(8,128)S(1)} fusion(f32[34,34,128]{2,1,0:T(8,128)} %slice.643, f32[34,34,3]{2,1,0:T(8,128)} %copy.22, f32[34,34,3]{2,1,0:T(8,128)} %copy.20, f32[5,52,52,128]{3,2,1,0:T(8,128)} %copy-done, f32[40,40,128]{2,1,0:T(8,128)S(1)} %fusion.72, f32[52,52,128]{2,1,0:T(8,128)S(1)} %slice_bitcast_fusion), kind=kLoop, calls=%fused_computation.275 | loop fusion | flops 62294528 | bytes 11273312 | tf_op jit(solution)/shard_map/jit(_where)/select_n | solution.py:184
  183.2 1.2 multiply_reduce_fusion.7
  184.4 1.2 multiply_reduce_fusion.5
  185.7 1.2 multiply_reduce_fusion.3
  186.9 1.2 multiply_reduce_fusion.1
  188.2 1.3 copy.23
  189.5 0.7 copy.24
  190.2 0.8 reshape.154
  190.9 7.0 %all-to-all-start = ((f32[4,1,4096]{2,1,0:T(1,128)}), f32[4,1,4096]{2,1,0:T(1,128)S(1)}, u32[]{:S(2)}, u32[]{:S(2)}) async-start(f32[4,1,4096]{2,1,0:T(1,128)} %reshape.154), calls=%async_computation | async-start | bytes 131072 | tf_op jit(solution)/shard_map/all_to_all | solution.py:202
  197.9 0.9 slice.669
  198.8 3.8 %all-to-all-done = f32[4,1,4096]{2,1,0:T(1,128)S(1)} async-done(((f32[4,1,4096]{2,1,0:T(1,128)}), f32[4,1,4096]{2,1,0:T(1,128)S(1)}, u32[]{:S(2)}, u32[]{:S(2)}) %all-to-all-start) | async-done | bytes 65568 | tf_op jit(solution)/shard_map/all_to_all | solution.py:202
  203.1 0.8 reduce
  (61 shorter events, 8.3 us)
Async XLA Ops:
  0.6 1.8 copy-start.2
  2.5 15.8 %copy-start.1 = (bf16[3,32,32,128]{3,2,1,0:T(8,128)(2,1)S(1)}, bf16[3,32,32,128]{3,2,1,0:T(8,128)(2,1)}, u32[]{:S(2)}) copy-start(bf16[3,32,32,128]{3,2,1,0:T(8,128)(2,1)} %param.5) | copy-start | bytes 2359300
  2.8 35.7 %collective-permute-start.1 = (f32[1024,128]{1,0:T(8,128)S(1)}, f32[1024,128]{1,0:T(8,128)S(1)}, u32[]{:S(2)}, u32[]{:S(2)}) collective-permute-start(f32[1024,128]{1,0:T(8,128)S(1)} %get-tuple-element.41), channel_id=1, source_target_pairs={{16,0},{32,16},{48,32},{64,48},{80,64},{96,80},{112,96},{128,112},... | collective-permute-start | bytes 1572872 | tf_op jit(solution)/shard_map/ppermute | solution.py:52
  16.3 23.0 %collective-permute-start = (f32[1024,128]{1,0:T(8,128)S(1)}, f32[1024,128]{1,0:T(8,128)S(1)}, u32[]{:S(2)}, u32[]{:S(2)}) collective-permute-start(f32[1024,128]{1,0:T(8,128)S(1)} %get-tuple-element.40), channel_id=1, source_target_pairs={{0,16},{16,32},{32,48},{48,64},{64,80},{80,96},{96,112},{112,128},... | collective-permute-start | bytes 1572872 | tf_op jit(solution)/shard_map/ppermute | solution.py:51
  41.4 21.4 %collective-permute-start.3 = (f32[5,52,10,128]{3,1,2,0:T(8,128)S(1)}, f32[5,52,10,128]{3,1,2,0:T(8,128)S(1)}, u32[]{:S(2)}, u32[]{:S(2)}) collective-permute-start(f32[5,52,10,128]{3,1,2,0:T(8,128)S(1)} %copy.8), channel_id=1, source_target_pairs={{4,0},{8,4},{12,8},{0,12},{5,1},{9,5},{13,9},{1,13},{6,2},{10,6},{... | collective-permute-start | bytes 3993608 | tf_op jit(solution)/shard_map/ppermute | solution.py:24
  46.7 22.0 %collective-permute-start.2 = (f32[5,52,10,128]{3,1,2,0:T(8,128)S(1)}, f32[5,52,10,128]{3,1,2,0:T(8,128)S(1)}, u32[]{:S(2)}, u32[]{:S(2)}) collective-permute-start(f32[5,52,10,128]{3,1,2,0:T(8,128)S(1)} %copy.7), channel_id=1, source_target_pairs={{0,4},{4,8},{8,12},{12,0},{1,5},{5,9},{9,13},{13,1},{2,6},{6,10},{... | collective-permute-start | bytes 3993608 | tf_op jit(solution)/shard_map/ppermute | solution.py:23
  70.2 3.3 %copy-start = (f32[5,52,52,128]{3,2,1,0:T(8,128)}, f32[5,52,52,128]{3,2,1,0:T(8,128)S(1)}, u32[]{:S(2)}) copy-start(f32[5,52,52,128]{3,2,1,0:T(8,128)S(1)} %pad_maximum_fusion) | copy-start | bytes 20766724
  75.2 19.5 %collective-permute-start.4 = (f32[46,46,3]{1,0,2:T(8,128)S(1)}, f32[46,46,3]{1,0,2:T(8,128)S(1)}, u32[]{:S(2)}, u32[]{:S(2)}) collective-permute-start(f32[46,46,3]{1,0,2:T(8,128)S(1)} %copy.11), channel_id=1, source_target_pairs={{0,1},{1,2},{2,3},{3,0},{4,5},{5,6},{6,7},{7,4},{8,9},{9,10},{10,1... | collective-permute-start | bytes 76184 | tf_op jit(solution)/shard_map/ppermute | solution.py:63
  83.5 12.7 %collective-permute-start.5 = (f32[46,46,3]{1,0,2:T(8,128)S(1)}, f32[46,46,3]{1,0,2:T(8,128)S(1)}, u32[]{:S(2)}, u32[]{:S(2)}) collective-permute-start(f32[46,46,3]{1,0,2:T(8,128)S(1)} %copy.13), channel_id=1, source_target_pairs={{1,0},{2,1},{3,2},{0,3},{5,4},{6,5},{7,6},{4,7},{9,8},{10,9},{11,1... | collective-permute-start | bytes 76184 | tf_op jit(solution)/shard_map/ppermute | solution.py:64
  123.0 9.8 %collective-permute-start.6 = (f32[40,40,3]{1,0,2:T(8,128)S(1)}, f32[40,40,3]{1,0,2:T(8,128)}, u32[]{:S(2)}, u32[]{:S(2)}) collective-permute-start(f32[40,40,3]{1,0,2:T(8,128)S(1)} %copy.15), channel_id=1, source_target_pairs={{0,1},{1,2},{2,3},{3,0},{4,5},{5,6},{6,7},{7,4},{8,9},{9,10},{10,1... | collective-permute-start | bytes 57608 | tf_op jit(solution)/shard_map/ppermute | solution.py:63
  125.9 9.0 %collective-permute-start.7 = (f32[40,40,3]{1,0,2:T(8,128)}, f32[40,40,3]{1,0,2:T(8,128)S(1)}, u32[]{:S(2)}, u32[]{:S(2)}) collective-permute-start(f32[40,40,3]{1,0,2:T(8,128)} %copy.17), channel_id=1, source_target_pairs={{1,0},{2,1},{3,2},{0,3},{5,4},{6,5},{7,6},{4,7},{9,8},{10,9},{11,1... | collective-permute-start | bytes 57608 | tf_op jit(solution)/shard_map/ppermute | solution.py:64
  153.4 9.5 %copy-start.3 = (s32[4]{0:T(128)S(1)}, s32[4]{0:T(128)}, u32[]{:S(2)}) copy-start(s32[4]{0:T(128)} %param.7) | copy-start | bytes 52
  154.9 10.8 %collective-permute-start.8 = (f32[34,34,3]{1,0,2:T(8,128)S(1)}, f32[34,34,3]{1,0,2:T(8,128)S(1)}, u32[]{:S(2)}, u32[]{:S(2)}) collective-permute-start(f32[34,34,3]{1,0,2:T(8,128)S(1)} %copy.19), channel_id=1, source_target_pairs={{0,1},{1,2},{2,3},{3,0},{4,5},{5,6},{6,7},{7,4},{8,9},{9,10},{10,1... | collective-permute-start | bytes 41624 | tf_op jit(solution)/shard_map/ppermute | solution.py:63
  159.1 7.9 %collective-permute-start.9 = (f32[34,34,3]{1,0,2:T(8,128)S(1)}, f32[34,34,3]{1,0,2:T(8,128)S(1)}, u32[]{:S(2)}, u32[]{:S(2)}) collective-permute-start(f32[34,34,3]{1,0,2:T(8,128)S(1)} %copy.21), channel_id=1, source_target_pairs={{1,0},{2,1},{3,2},{0,3},{5,4},{6,5},{7,6},{4,7},{9,8},{10,9},{11,1... | collective-permute-start | bytes 41624 | tf_op jit(solution)/shard_map/ppermute | solution.py:64
  190.9 11.6 %all-to-all-start = ((f32[4,1,4096]{2,1,0:T(1,128)}), f32[4,1,4096]{2,1,0:T(1,128)S(1)}, u32[]{:S(2)}, u32[]{:S(2)}) async-start(f32[4,1,4096]{2,1,0:T(1,128)} %reshape.154), calls=%async_computation | async-start | bytes 131072 | tf_op jit(solution)/shard_map/all_to_all | solution.py:202

commit v4 on v3

--- a/solution.py
+++ b/solution.py
@@ -82,9 +82,12 @@
     smooth_three = 13.0 / 12.0 * square(diff_three - 2.0 * diff_four + diff_five) + 0.25 * square(
         3.0 * diff_three - 4.0 * diff_four + diff_five
     )
-    weight_one = 0.1 / square(weno_floor + smooth_one)
-    weight_two = 0.6 / square(weno_floor + smooth_two)
-    weight_three = 0.3 / square(weno_floor + smooth_three)
+    guard_one = square(weno_floor + smooth_one)
+    guard_two = square(weno_floor + smooth_two)
+    guard_three = square(weno_floor + smooth_three)
+    weight_one = 0.1 * (guard_two * guard_three)
+    weight_two = 0.6 * (guard_one * guard_three)
+    weight_three = 0.3 * (guard_one * guard_two)
     return (
         weight_one * candidate_one + weight_two * candidate_two + weight_three * candidate_three
     ) / (weight_one + weight_two + weight_three)

time: 207 us -> 207 us (level)
  no operation moved by 1% of the time
where the time goes in v4:
time: 207 us; the launch traced here: 206 us
  starting transfers between devices  60 us (29%)
  other arithmetic  57.5 us (28%)
  waiting for transfers between devices  44.5 us (21%)
  local copies, waits for them, and re-layouts  34.8 us (17%)
  matrix products  5.89 us (3%)
  between operations  3.13 us (2%)
    add x1, other arithmetic, shards(): section_one = inner + time_step * rate  22.7 us
    ppermute x1, waiting for transfers between devices, exchange_packed(): after = unpack(lax.ppermute(pack(firsts), axis, down), firsts)  20 us
    ppermute x3, starting transfers between devices, z_faces(): after = lax.ppermute(x[:, :, :SPAN], 'gz', down)  17.1 us
    add x1, other arithmetic, shards(): 0.75 * level_ext[2 * SPAN:-2 * SPAN, 2 * SPAN:-2 * SPAN]  15.9 us
    select_n x1, other arithmetic, shards(): rim = jnp.where(flag_ext > 0, advanced, level_ring)  14.5 us
    ppermute x1, waiting for transfers between devices, exchange(): after = lax.ppermute(first, axis, down)  14.1 us
    ppermute x3, starting transfers between devices, z_faces(): before = lax.ppermute(x[:, :, length - SPAN:], 'gz', up)  13.6 us
    ppermute x1, starting transfers between devices, exchange_packed(): after = unpack(lax.ppermute(pack(firsts), axis, down), firsts)  13.5 us
  transfers between devices with their start and end apart: 11, of which 6 were waited for; matrix products, arithmetic and copies ran while one was open for 7% of the time, Pallas kernels for 0%

profile of v4, /device:TPU:32, one launch (start us, length us, event | category | flops | bytes accessed | tf_op | source)
XLA Modules:
  0.0 205.8 jit_solution(4817798698764909203)
XLA Ops:
  1.3 1.1 fusion.310
  2.8 13.5 %collective-permute-start.1 = (f32[1024,128]{1,0:T(8,128)S(1)}, f32[1024,128]{1,0:T(8,128)S(1)}, u32[]{:S(2)}, u32[]{:S(2)}) collective-permute-start(f32[1024,128]{1,0:T(8,128)S(1)} %get-tuple-element.41), channel_id=1, source_target_pairs={{16,0},{32,16},{48,32},{64,48},{80,64},{96,80},{112,96},{128,112},... | collective-permute-start | bytes 1572872 | tf_op jit(solution)/shard_map/ppermute | solution.py:52
  16.3 1.9 collective-permute-start
  18.5 20.0 %collective-permute-done.1 = f32[1024,128]{1,0:T(8,128)S(1)} collective-permute-done((f32[1024,128]{1,0:T(8,128)S(1)}, f32[1024,128]{1,0:T(8,128)S(1)}, u32[]{:S(2)}, u32[]{:S(2)}) %collective-permute-start.1) | collective-permute-done | bytes 524320 | tf_op jit(solution)/shard_map/ppermute | solution.py:52
  38.5 0.8 collective-permute-done
  41.4 4.9 %collective-permute-start.3 = (f32[5,52,10,128]{3,1,2,0:T(8,128)S(1)}, f32[5,52,10,128]{3,1,2,0:T(8,128)S(1)}, u32[]{:S(2)}, u32[]{:S(2)}) collective-permute-start(f32[5,52,10,128]{3,1,2,0:T(8,128)S(1)} %copy.8), channel_id=1, source_target_pairs={{4,0},{8,4},{12,8},{0,12},{5,1},{9,5},{13,9},{1,13},{6,2},{10,6},{... | collective-permute-start | bytes 3993608 | tf_op jit(solution)/shard_map/ppermute | solution.py:24
  46.7 1.9 collective-permute-start.2
  48.6 14.1 %collective-permute-done.3 = f32[5,52,10,128]{3,1,2,0:T(8,128)S(1)} collective-permute-done((f32[5,52,10,128]{3,1,2,0:T(8,128)S(1)}, f32[5,52,10,128]{3,1,2,0:T(8,128)S(1)}, u32[]{:S(2)}, u32[]{:S(2)}) %collective-permute-start.3) | collective-permute-done | bytes 1331232 | tf_op jit(solution)/shard_map/ppermute | solution.py:24
  63.0 5.7 %collective-permute-done.2 = f32[5,52,10,128]{3,1,2,0:T(8,128)S(1)} collective-permute-done((f32[5,52,10,128]{3,1,2,0:T(8,128)S(1)}, f32[5,52,10,128]{3,1,2,0:T(8,128)S(1)}, u32[]{:S(2)}, u32[]{:S(2)}) %collective-permute-start.2) | collective-permute-done | bytes 1331232 | tf_op jit(solution)/shard_map/ppermute | solution.py:23
  69.1 1.1 pad_maximum_fusion
  70.3 1.8 fusion.307
  72.0 1.4 copy-done
  73.5 1.7 copy.11
  75.2 7.8 %collective-permute-start.4 = (f32[46,46,3]{1,0,2:T(8,128)S(1)}, f32[46,46,3]{1,0,2:T(8,128)S(1)}, u32[]{:S(2)}, u32[]{:S(2)}) collective-permute-start(f32[46,46,3]{1,0,2:T(8,128)S(1)} %copy.11), channel_id=1, source_target_pairs={{0,1},{1,2},{2,3},{3,0},{4,5},{5,6},{6,7},{7,4},{8,9},{9,10},{10,1... | collective-permute-start | bytes 76184 | tf_op jit(solution)/shard_map/ppermute | solution.py:63
  83.5 7.5 %collective-permute-start.5 = (f32[46,46,3]{1,0,2:T(8,128)S(1)}, f32[46,46,3]{1,0,2:T(8,128)S(1)}, u32[]{:S(2)}, u32[]{:S(2)}) collective-permute-start(f32[46,46,3]{1,0,2:T(8,128)S(1)} %copy.13), channel_id=1, source_target_pairs={{1,0},{2,1},{3,2},{0,3},{5,4},{6,5},{7,6},{4,7},{9,8},{10,9},{11,1... | collective-permute-start | bytes 76184 | tf_op jit(solution)/shard_map/ppermute | solution.py:64
  91.0 2.5 %slice_bitcast_fusion.1 = f32[46,52,128]{2,1,0:T(8,128)} fusion(f32[5,52,52,128]{3,2,1,0:T(8,128)} %copy-done), kind=kLoop, calls=%fused_computation.32 | loop fusion | bytes 2449408 | tf_op jit(solution)/shard_map/slice | solution.py:155
  93.5 1.2 slice.589
  94.7 1.5 copy.12
  96.2 1.5 copy.14
  97.7 22.7 %fusion.14 = f32[46,46,128]{2,1,0:T(8,128)S(1)} fusion(f32[46,46,128]{2,1,0:T(8,128)} %slice.589, f32[46,46,3]{2,1,0:T(8,128)} %copy.14, f32[46,46,3]{2,1,0:T(8,128)} %copy.12, f32[5,52,52,128]{3,2,1,0:T(8,128)} %copy-done, f32[46,52,128]{2,1,0:T(8,128)} %slice_bitcast_fusion.1, f32[52,52,128]{2,1,0:T(8,128)S(1)} %slice_bitcast_fusion), kind=kLoop, calls=%fused_computation.57 | loop fusion | flops 117548032 | bytes 19551840 | tf_op jit(solution)/shard_map/add | solution.py:179
  120.4 1.2 fusion.308
  121.6 1.5 copy.15
  123.1 1.9 collective-permute-start.6
  125.0 1.0 copy.17
  126.0 5.9 %collective-permute-start.7 = (f32[40,40,3]{1,0,2:T(8,128)}, f32[40,40,3]{1,0,2:T(8,128)S(1)}, u32[]{:S(2)}, u32[]{:S(2)}) collective-permute-start(f32[40,40,3]{1,0,2:T(8,128)} %copy.17), channel_id=1, source_target_pairs={{1,0},{2,1},{3,2},{0,3},{5,4},{6,5},{7,6},{4,7},{9,8},{10,9},{11,1... | collective-permute-start | bytes 57608 | tf_op jit(solution)/shard_map/ppermute | solution.py:64
  131.9 1.0 slice.617
  132.9 2.1 %copy.16 = f32[40,40,3]{2,1,0:T(8,128)} copy(f32[40,40,3]{1,0,2:T(8,128)} %collective-permute-done.6) | data formatting | bytes 38400 | tf_op jit(solution)/shard_map/ppermute | solution.py:63
  135.0 1.3 copy.18
  136.3 15.9 %fusion.64 = f32[40,40,128]{2,1,0:T(8,128)S(1)} fusion(f32[52,52,128]{2,1,0:T(8,128)S(1)} %slice_bitcast_fusion, f32[40,40,128]{2,1,0:T(8,128)} %slice.617, f32[40,40,3]{2,1,0:T(8,128)} %copy.18, f32[40,40,3]{2,1,0:T(8,128)} %copy.16, f32[5,52,52,128]{3,2,1,0:T(8,128)} %copy-done, f32[46,46,128]{2,1,0:T(8,128)S(1)} %fusion.14), kind=kLoop, calls=%fused_computation.135 | loop fusion | flops 89497600 | bytes 14784000 | tf_op jit(solution)/shard_map/add | solution.py:181
  152.2 1.1 fusion.309
  153.3 1.5 copy.19
  154.8 3.9 %collective-permute-start.8 = (f32[34,34,3]{1,0,2:T(8,128)S(1)}, f32[34,34,3]{1,0,2:T(8,128)S(1)}, u32[]{:S(2)}, u32[]{:S(2)}) collective-permute-start(f32[34,34,3]{1,0,2:T(8,128)S(1)} %copy.19), channel_id=1, source_target_pairs={{0,1},{1,2},{2,3},{3,0},{4,5},{5,6},{6,7},{7,4},{8,9},{9,10},{10,1... | collective-permute-start | bytes 41624 | tf_op jit(solution)/shard_map/ppermute | solution.py:63
  159.1 3.7 %collective-permute-start.9 = (f32[34,34,3]{1,0,2:T(8,128)S(1)}, f32[34,34,3]{1,0,2:T(8,128)S(1)}, u32[]{:S(2)}, u32[]{:S(2)}) collective-permute-start(f32[34,34,3]{1,0,2:T(8,128)S(1)} %copy.21), channel_id=1, source_target_pairs={{1,0},{2,1},{3,2},{0,3},{5,4},{6,5},{7,6},{4,7},{9,8},{10,9},{11,1... | collective-permute-start | bytes 41624 | tf_op jit(solution)/shard_map/ppermute | solution.py:64
  164.7 0.9 slice.643
  165.6 1.3 copy.20
  167.0 1.3 copy.22
  168.2 14.5 %fusion.156 = f32[34,34,128]{2,1,0:T(8,128)S(1)} fusion(f32[34,34,128]{2,1,0:T(8,128)} %slice.643, f32[34,34,3]{2,1,0:T(8,128)} %copy.22, f32[34,34,3]{2,1,0:T(8,128)} %copy.20, f32[5,52,52,128]{3,2,1,0:T(8,128)} %copy-done, f32[40,40,128]{2,1,0:T(8,128)S(1)} %fusion.64, f32[52,52,128]{2,1,0:T(8,128)S(1)} %slice_bitcast_fusion), kind=kLoop, calls=%fused_computation.270 | loop fusion | flops 64957952 | bytes 11273312 | tf_op jit(solution)/shard_map/jit(_where)/select_n | solution.py:187
  183.0 1.2 multiply_reduce_fusion.7
  184.2 1.2 multiply_reduce_fusion.5
  185.5 1.2 multiply_reduce_fusion.3
  186.7 1.2 multiply_reduce_fusion.1
  188.0 1.3 copy.23
  189.3 0.7 copy.24
  190.0 0.8 reshape.154
  190.7 7.0 %all-to-all-start = ((f32[4,1,4096]{2,1,0:T(1,128)}), f32[4,1,4096]{2,1,0:T(1,128)S(1)}, u32[]{:S(2)}, u32[]{:S(2)}) async-start(f32[4,1,4096]{2,1,0:T(1,128)} %reshape.154), calls=%async_computation | async-start | bytes 131072 | tf_op jit(solution)/shard_map/all_to_all | solution.py:205
  197.7 0.9 slice.669
  198.6 3.8 %all-to-all-done = f32[4,1,4096]{2,1,0:T(1,128)S(1)} async-done(((f32[4,1,4096]{2,1,0:T(1,128)}), f32[4,1,4096]{2,1,0:T(1,128)S(1)}, u32[]{:S(2)}, u32[]{:S(2)}) %all-to-all-start) | async-done | bytes 65568 | tf_op jit(solution)/shard_map/all_to_all | solution.py:205
  202.9 0.8 reduce
  (61 shorter events, 8.3 us)
Async XLA Ops:
  0.6 1.8 copy-start.2
  2.5 15.8 %copy-start.1 = (bf16[3,32,32,128]{3,2,1,0:T(8,128)(2,1)S(1)}, bf16[3,32,32,128]{3,2,1,0:T(8,128)(2,1)}, u32[]{:S(2)}) copy-start(bf16[3,32,32,128]{3,2,1,0:T(8,128)(2,1)} %param.5) | copy-start | bytes 2359300
  2.8 35.7 %collective-permute-start.1 = (f32[1024,128]{1,0:T(8,128)S(1)}, f32[1024,128]{1,0:T(8,128)S(1)}, u32[]{:S(2)}, u32[]{:S(2)}) collective-permute-start(f32[1024,128]{1,0:T(8,128)S(1)} %get-tuple-element.41), channel_id=1, source_target_pairs={{16,0},{32,16},{48,32},{64,48},{80,64},{96,80},{112,96},{128,112},... | collective-permute-start | bytes 1572872 | tf_op jit(solution)/shard_map/ppermute | solution.py:52
  16.3 23.0 %collective-permute-start = (f32[1024,128]{1,0:T(8,128)S(1)}, f32[1024,128]{1,0:T(8,128)S(1)}, u32[]{:S(2)}, u32[]{:S(2)}) collective-permute-start(f32[1024,128]{1,0:T(8,128)S(1)} %get-tuple-element.40), channel_id=1, source_target_pairs={{0,16},{16,32},{32,48},{48,64},{64,80},{80,96},{96,112},{112,128},... | collective-permute-start | bytes 1572872 | tf_op jit(solution)/shard_map/ppermute | solution.py:51
  41.4 21.4 %collective-permute-start.3 = (f32[5,52,10,128]{3,1,2,0:T(8,128)S(1)}, f32[5,52,10,128]{3,1,2,0:T(8,128)S(1)}, u32[]{:S(2)}, u32[]{:S(2)}) collective-permute-start(f32[5,52,10,128]{3,1,2,0:T(8,128)S(1)} %copy.8), channel_id=1, source_target_pairs={{4,0},{8,4},{12,8},{0,12},{5,1},{9,5},{13,9},{1,13},{6,2},{10,6},{... | collective-permute-start | bytes 3993608 | tf_op jit(solution)/shard_map/ppermute | solution.py:24
  46.7 22.0 %collective-permute-start.2 = (f32[5,52,10,128]{3,1,2,0:T(8,128)S(1)}, f32[5,52,10,128]{3,1,2,0:T(8,128)S(1)}, u32[]{:S(2)}, u32[]{:S(2)}) collective-permute-start(f32[5,52,10,128]{3,1,2,0:T(8,128)S(1)} %copy.7), channel_id=1, source_target_pairs={{0,4},{4,8},{8,12},{12,0},{1,5},{5,9},{9,13},{13,1},{2,6},{6,10},{... | collective-permute-start | bytes 3993608 | tf_op jit(solution)/shard_map/ppermute | solution.py:23
  70.2 3.3 %copy-start = (f32[5,52,52,128]{3,2,1,0:T(8,128)}, f32[5,52,52,128]{3,2,1,0:T(8,128)S(1)}, u32[]{:S(2)}) copy-start(f32[5,52,52,128]{3,2,1,0:T(8,128)S(1)} %pad_maximum_fusion) | copy-start | bytes 20766724
  75.2 19.5 %collective-permute-start.4 = (f32[46,46,3]{1,0,2:T(8,128)S(1)}, f32[46,46,3]{1,0,2:T(8,128)S(1)}, u32[]{:S(2)}, u32[]{:S(2)}) collective-permute-start(f32[46,46,3]{1,0,2:T(8,128)S(1)} %copy.11), channel_id=1, source_target_pairs={{0,1},{1,2},{2,3},{3,0},{4,5},{5,6},{6,7},{7,4},{8,9},{9,10},{10,1... | collective-permute-start | bytes 76184 | tf_op jit(solution)/shard_map/ppermute | solution.py:63
  83.5 12.7 %collective-permute-start.5 = (f32[46,46,3]{1,0,2:T(8,128)S(1)}, f32[46,46,3]{1,0,2:T(8,128)S(1)}, u32[]{:S(2)}, u32[]{:S(2)}) collective-permute-start(f32[46,46,3]{1,0,2:T(8,128)S(1)} %copy.13), channel_id=1, source_target_pairs={{1,0},{2,1},{3,2},{0,3},{5,4},{6,5},{7,6},{4,7},{9,8},{10,9},{11,1... | collective-permute-start | bytes 76184 | tf_op jit(solution)/shard_map/ppermute | solution.py:64
  123.1 9.8 %collective-permute-start.6 = (f32[40,40,3]{1,0,2:T(8,128)S(1)}, f32[40,40,3]{1,0,2:T(8,128)}, u32[]{:S(2)}, u32[]{:S(2)}) collective-permute-start(f32[40,40,3]{1,0,2:T(8,128)S(1)} %copy.15), channel_id=1, source_target_pairs={{0,1},{1,2},{2,3},{3,0},{4,5},{5,6},{6,7},{7,4},{8,9},{9,10},{10,1... | collective-permute-start | bytes 57608 | tf_op jit(solution)/shard_map/ppermute | solution.py:63
  126.0 9.0 %collective-permute-start.7 = (f32[40,40,3]{1,0,2:T(8,128)}, f32[40,40,3]{1,0,2:T(8,128)S(1)}, u32[]{:S(2)}, u32[]{:S(2)}) collective-permute-start(f32[40,40,3]{1,0,2:T(8,128)} %copy.17), channel_id=1, source_target_pairs={{1,0},{2,1},{3,2},{0,3},{5,4},{6,5},{7,6},{4,7},{9,8},{10,9},{11,1... | collective-permute-start | bytes 57608 | tf_op jit(solution)/shard_map/ppermute | solution.py:64
  153.3 9.5 %copy-start.3 = (s32[4]{0:T(128)S(1)}, s32[4]{0:T(128)}, u32[]{:S(2)}) copy-start(s32[4]{0:T(128)} %param.7) | copy-start | bytes 52
  154.8 10.8 %collective-permute-start.8 = (f32[34,34,3]{1,0,2:T(8,128)S(1)}, f32[34,34,3]{1,0,2:T(8,128)S(1)}, u32[]{:S(2)}, u32[]{:S(2)}) collective-permute-start(f32[34,34,3]{1,0,2:T(8,128)S(1)} %copy.19), channel_id=1, source_target_pairs={{0,1},{1,2},{2,3},{3,0},{4,5},{5,6},{6,7},{7,4},{8,9},{9,10},{10,1... | collective-permute-start | bytes 41624 | tf_op jit(solution)/shard_map/ppermute | solution.py:63
  159.1 7.9 %collective-permute-start.9 = (f32[34,34,3]{1,0,2:T(8,128)S(1)}, f32[34,34,3]{1,0,2:T(8,128)S(1)}, u32[]{:S(2)}, u32[]{:S(2)}) collective-permute-start(f32[34,34,3]{1,0,2:T(8,128)S(1)} %copy.21), channel_id=1, source_target_pairs={{1,0},{2,1},{3,2},{0,3},{5,4},{6,5},{7,6},{4,7},{9,8},{10,9},{11,1... | collective-permute-start | bytes 41624 | tf_op jit(solution)/shard_map/ppermute | solution.py:64
  190.7 11.6 %all-to-all-start = ((f32[4,1,4096]{2,1,0:T(1,128)}), f32[4,1,4096]{2,1,0:T(1,128)S(1)}, u32[]{:S(2)}, u32[]{:S(2)}) async-start(f32[4,1,4096]{2,1,0:T(1,128)} %reshape.154), calls=%async_computation | async-start | bytes 131072 | tf_op jit(solution)/shard_map/all_to_all | solution.py:205

commit v5 on v3

--- a/solution.py
+++ b/solution.py
@@ -147,9 +147,18 @@
     return jnp.concatenate([colour, clear], 0)
 
 
+def x_faces(x, width):
+    size, length = (lax.axis_size("gx"), x.shape[0])
+    up = [(i, (i + 1) % size) for i in range(size)]
+    down = [(j, i) for i, j in up]
+    before = lax.ppermute(x[length - width :], "gx", up)
+    after = lax.ppermute(x[:width], "gx", down)
+    return jnp.concatenate([before, x, after], axis=0)
+
+
 def stage_rate(field, speeds):
-    inner = field[SPAN:-SPAN, SPAN:-SPAN]
-    padded = [field[:, SPAN:-SPAN], field[SPAN:-SPAN, :], z_faces(inner)]
+    inner = field[:, SPAN:-SPAN]
+    padded = [x_faces(inner, SPAN), field, z_faces(inner)]
     return inner, local_rate(padded, speeds)
 
 
@@ -157,32 +166,25 @@
     alive = active_brick[0, 0, 0] > 0
     alive_float = alive.astype(jnp.float32)
     flags = jnp.broadcast_to(alive_float, level_set.shape)
-    speeds = velocity.astype(jnp.float32)
-    halo, halo_speed = 3 * SPAN + 1, 2 * SPAN + 1
-    level_x, speed_x, flag_x = exchange_packed(
-        [level_set, speeds, flags], "gx", [halo, halo_speed, 1]
-    )
-    speed_x = jnp.pad(speed_x, ((0, 0), (halo - halo_speed,) * 2, (0, 0), (0, 0)))
-    flag_x = jnp.pad(flag_x, ((halo - 1,) * 2, (0, 0), (0, 0)))
-    stacked = jnp.concatenate([level_x[None], speed_x, flag_x[None]], 0)
+    stacked = jnp.stack([level_set] + [velocity[d].astype(jnp.float32) for d in range(3)] + [flags])
+    halo = 3 * SPAN + 1
     stacked = exchange([stacked], "gy", [halo], 1)[0]
     level_ext = stacked[0]
-    speed_ext = stacked[1:4, SPAN:-SPAN, SPAN:-SPAN]
-    flag_ext = stacked[4, 3 * SPAN : -3 * SPAN, 3 * SPAN : -3 * SPAN]
-    speed_two = speed_ext[:, SPAN:-SPAN, SPAN:-SPAN]
-    speed_three = speed_two[:, SPAN:-SPAN, SPAN:-SPAN]
-
-    inner, rate = stage_rate(level_ext, speed_ext)
+    speed_one = stacked[1:4, :, SPAN:-SPAN]
+    speed_two = speed_one[:, :, SPAN:-SPAN]
+    speed_three = speed_two[:, :, SPAN:-SPAN]
+    flag_ring = stacked[4, :, 3 * SPAN : -3 * SPAN]
+
+    inner, rate = stage_rate(level_ext, speed_one)
     section_one = inner + time_step * rate
     inner, rate = stage_rate(section_one, speed_two)
-    section_two = 0.75 * level_ext[2 * SPAN : -2 * SPAN, 2 * SPAN : -2 * SPAN] + 0.25 * (
-        inner + time_step * rate
-    )
+    section_two = 0.75 * level_ext[:, 2 * SPAN : -2 * SPAN] + 0.25 * (inner + time_step * rate)
     inner, rate = stage_rate(section_two, speed_three)
-    level_ring = level_ext[3 * SPAN : -3 * SPAN, 3 * SPAN : -3 * SPAN]
+    level_ring = level_ext[:, 3 * SPAN : -3 * SPAN]
     advanced = level_ring / 3.0 + 2.0 / 3.0 * (inner + time_step * rate)
-    rim = jnp.where(flag_ext > 0, advanced, level_ring)
-    level_out = rim[1:-1, 1:-1]
+    ringed = jnp.where(flag_ring > 0, advanced, level_ring)
+    level_out = ringed[:, 1:-1]
+    rim = x_faces(ringed, 1)
 
     group = lax.axis_size("gz")
     ascending = depth_order[0] < depth_order[group - 1]

time: 207 us -> 192 us (0.928)
  the two profiles are of different devices: /device:TPU:32 before, /device:TPU:7 now
where the time goes in v5:
time: 192 us; the launch traced here: 191 us
  starting transfers between devices  84.7 us (44%)
  other arithmetic  46.6 us (24%)
  waiting for transfers between devices  32.1 us (17%)
  local copies, waits for them, and re-layouts  18.3 us (10%)
  matrix products  5.91 us (3%)
  between operations  3.11 us (2%)
    ppermute x4, starting transfers between devices, x_faces(): before = lax.ppermute(x[length - width:], 'gx', up)  42.5 us
    add x1, other arithmetic, shards(): section_one = inner + time_step * rate  14.8 us
    ppermute x1, waiting for transfers between devices, exchange(): after = lax.ppermute(first, axis, down)  14.7 us
    ppermute x3, starting transfers between devices, z_faces(): after = lax.ppermute(x[:, :, :SPAN], 'gz', down)  14 us
    select_n x1, other arithmetic, shards(): ringed = jnp.where(flag_ring > 0, advanced, level_ring)  13.3 us
    add x1, other arithmetic, shards(): 0.75 * level_ext[:, 2 * SPAN:-2 * SPAN] + 0.25 * (inner + time_step * rate)  13 us
    ppermute x3, starting transfers between devices, z_faces(): before = lax.ppermute(x[:, :, length - SPAN:], 'gz', up)  8.84 us
    ppermute x4, waiting for transfers between devices, x_faces(): after = lax.ppermute(x[:width], 'gx', down)  7.88 us
  transfers between devices with their start and end apart: 17, of which 6 were waited for; matrix products, arithmetic and copies ran while one was open for 6% of the time, Pallas kernels for 0%

profile of v5, /device:TPU:7, one launch (start us, length us, event | category | flops | bytes accessed | tf_op | source)
XLA Modules:
  0.0 190.9 jit_solution(5801517981525602925)
XLA Ops:
  1.3 1.1 bitcast_dynamic-update-slice_fusion
  2.4 1.0 convert_dynamic-update-slice_fusion.2
  3.4 1.0 convert_dynamic-update-slice_fusion.1
  4.4 1.0 convert_dynamic-update-slice_fusion
  5.9 4.6 %collective-permute-start.1 = (f32[5,32,10,128]{3,1,2,0:T(8,128)S(1)}, f32[5,32,10,128]{3,1,2,0:T(8,128)S(1)}, u32[]{:S(2)}, u32[]{:S(2)}) collective-permute-start(f32[5,32,10,128]{3,1,2,0:T(8,128)S(1)} %copy.8), channel_id=1, source_target_pairs={{4,0},{8,4},{12,8},{0,12},{5,1},{9,5},{13,9},{1,13},{6,2},{10,6},{... | collective-permute-start | bytes 2457608 | tf_op jit(solution)/shard_map/ppermute | solution.py:24
  10.9 1.9 %collective-permute-start = (f32[5,32,10,128]{3,1,2,0:T(8,128)S(1)}, f32[5,32,10,128]{3,1,2,0:T(8,128)S(1)}, u32[]{:S(2)}, u32[]{:S(2)}) collective-permute-start(f32[5,32,10,128]{3,1,2,0:T(8,128)S(1)} %copy.7), channel_id=1, source_target_pairs={{0,4},{4,8},{8,12},{12,0},{1,5},{5,9},{9,13},{13,1},{2,6},{6,10},{... | collective-permute-start | bytes 2457608 | tf_op jit(solution)/shard_map/ppermute | solution.py:23
  12.8 14.7 %collective-permute-done.1 = f32[5,32,10,128]{3,1,2,0:T(8,128)S(1)} collective-permute-done((f32[5,32,10,128]{3,1,2,0:T(8,128)S(1)}, f32[5,32,10,128]{3,1,2,0:T(8,128)S(1)}, u32[]{:S(2)}, u32[]{:S(2)}) %collective-permute-start.1) | collective-permute-done | bytes 819232 | tf_op jit(solution)/shard_map/ppermute | solution.py:24
  28.0 4.8 %collective-permute-done = f32[5,32,10,128]{3,1,2,0:T(8,128)S(1)} collective-permute-done((f32[5,32,10,128]{3,1,2,0:T(8,128)S(1)}, f32[5,32,10,128]{3,1,2,0:T(8,128)S(1)}, u32[]{:S(2)}, u32[]{:S(2)}) %collective-permute-start) | collective-permute-done | bytes 819232 | tf_op jit(solution)/shard_map/ppermute | solution.py:23
  33.9 0.7 fusion.501
  34.7 10.4 %collective-permute-start.2 = (f32[3,46,128]{2,1,0:T(8,128)}, f32[3,46,128]{2,1,0:T(8,128)S(1)}, u32[]{:S(2)}, u32[]{:S(2)}) collective-permute-start(f32[3,46,128]{2,1,0:T(8,128)} %get-tuple-element.21), channel_id=1, source_target_pairs={{0,16},{16,32},{32,48},{48,64},{64,80},{80,96},{96,112},{112,128},... | collective-permute-start | bytes 211976 | tf_op jit(solution)/shard_map/ppermute | solution.py:154
  45.1 1.9 %collective-permute-start.3 = (f32[3,46,128]{2,1,0:T(8,128)S(1)}, f32[3,46,128]{2,1,0:T(8,128)S(1)}, u32[]{:S(2)}, u32[]{:S(2)}) collective-permute-start(f32[3,46,128]{2,1,0:T(8,128)S(1)} %get-tuple-element.20), channel_id=1, source_target_pairs={{16,0},{32,16},{48,32},{64,48},{80,64},{96,80},{112,96},{128,112},... | collective-permute-start | bytes 211976 | tf_op jit(solution)/shard_map/ppermute | solution.py:155
  47.7 3.5 %collective-permute-start.4 = (f32[32,46,3]{1,0,2:T(8,128)S(1)}, f32[32,46,3]{1,0,2:T(8,128)S(1)}, u32[]{:S(2)}, u32[]{:S(2)}) collective-permute-start(f32[32,46,3]{1,0,2:T(8,128)S(1)} %copy.11), channel_id=1, source_target_pairs={{0,1},{1,2},{2,3},{3,0},{4,5},{5,6},{6,7},{7,4},{8,9},{9,10},{10,1... | collective-permute-start | bytes 53000 | tf_op jit(solution)/shard_map/ppermute | solution.py:63
  51.2 1.0 copy.13
  52.2 4.6 %collective-permute-start.5 = (f32[32,46,3]{1,0,2:T(8,128)}, f32[32,46,3]{1,0,2:T(8,128)S(1)}, u32[]{:S(2)}, u32[]{:S(2)}) collective-permute-start(f32[32,46,3]{1,0,2:T(8,128)} %copy.13), channel_id=1, source_target_pairs={{1,0},{2,1},{3,2},{0,3},{5,4},{6,5},{7,6},{4,7},{9,8},{10,9},{11,1... | collective-permute-start | bytes 53000 | tf_op jit(solution)/shard_map/ppermute | solution.py:64
  57.3 1.0 collective-permute-done.5
  58.3 1.3 copy.14
  59.5 14.8 %fusion.21 = f32[32,46,128]{2,1,0:T(8,128)S(1)} fusion(f32[32,46,128]{2,1,0:T(8,128)S(1)} %slice.546, f32[32,46,3]{2,1,0:T(8,128)} %copy.14, f32[32,46,3]{2,1,0:T(8,128)S(1)} %copy.12, f32[5,32,52,128]{3,2,1,0:T(8,128)} %copy-done, f32[32,52,128]{2,1,0:T(8,128)S(1)} %slice_bitcast_fusion, f32[3,46,128]{2,1,0:T(8,128)S(1)} %collective-permute-done.2, ...), kind=kLoop, calls=%fused_computation.74 | loop fusion | flops 79511552 | bytes 8466944 | tf_op jit(solution)/shard_map/add | solution.py:179
  74.4 10.5 %collective-permute-start.6 = (f32[3,40,128]{2,1,0:T(8,128)S(1)}, f32[3,40,128]{2,1,0:T(8,128)S(1)}, u32[]{:S(2)}, u32[]{:S(2)}) collective-permute-start(f32[3,40,128]{2,1,0:T(8,128)S(1)} %get-tuple-element.25), channel_id=1, source_target_pairs={{0,16},{16,32},{32,48},{48,64},{64,80},{80,96},{96,112},{112,128},... | collective-permute-start | bytes 184328 | tf_op jit(solution)/shard_map/ppermute | solution.py:154
  84.9 1.9 %collective-permute-start.7 = (f32[3,40,128]{2,1,0:T(8,128)S(1)}, f32[3,40,128]{2,1,0:T(8,128)S(1)}, u32[]{:S(2)}, u32[]{:S(2)}) collective-permute-start(f32[3,40,128]{2,1,0:T(8,128)S(1)} %get-tuple-element.24), channel_id=1, source_target_pairs={{16,0},{32,16},{48,32},{64,48},{80,64},{96,80},{112,96},{128,112},... | collective-permute-start | bytes 184328 | tf_op jit(solution)/shard_map/ppermute | solution.py:155
  87.3 3.1 %collective-permute-start.8 = (f32[32,40,3]{1,0,2:T(8,128)S(1)}, f32[32,40,3]{1,0,2:T(8,128)S(1)}, u32[]{:S(2)}, u32[]{:S(2)}) collective-permute-start(f32[32,40,3]{1,0,2:T(8,128)S(1)} %copy.15), channel_id=1, source_target_pairs={{0,1},{1,2},{2,3},{3,0},{4,5},{5,6},{6,7},{7,4},{8,9},{9,10},{10,1... | collective-permute-start | bytes 46088 | tf_op jit(solution)/shard_map/ppermute | solution.py:63
  90.8 4.5 %collective-permute-start.9 = (f32[32,40,3]{1,0,2:T(8,128)S(1)}, f32[32,40,3]{1,0,2:T(8,128)S(1)}, u32[]{:S(2)}, u32[]{:S(2)}) collective-permute-start(f32[32,40,3]{1,0,2:T(8,128)S(1)} %copy.17), channel_id=1, source_target_pairs={{1,0},{2,1},{3,2},{0,3},{5,4},{6,5},{7,6},{4,7},{9,8},{10,9},{11,1... | collective-permute-start | bytes 46088 | tf_op jit(solution)/shard_map/ppermute | solution.py:64
  95.3 1.2 copy.16
  96.5 1.2 copy.18
  97.6 13.0 %fusion.174 = f32[32,40,128]{2,1,0:T(8,128)S(1)} fusion(f32[32,52,128]{2,1,0:T(8,128)S(1)} %slice_bitcast_fusion, f32[32,40,128]{2,1,0:T(8,128)S(1)} %slice.576, f32[32,40,3]{2,1,0:T(8,128)} %copy.18, f32[32,40,3]{2,1,0:T(8,128)} %copy.16, f32[5,32,52,128]{3,2,1,0:T(8,128)} %copy-done, f32[32,46,128]{2,1,0:T(8,128)S(1)} %fusion.21, ...), kind=kLoop, calls=%fused_computation.276 | loop fusion | flops 69632000 | bytes 8017920 | tf_op jit(solution)/shard_map/add | solution.py:181
  110.7 11.5 %collective-permute-start.10 = (f32[3,34,128]{2,1,0:T(8,128)S(1)}, f32[3,34,128]{2,1,0:T(8,128)S(1)}, u32[]{:S(2)}, u32[]{:S(2)}) collective-permute-start(f32[3,34,128]{2,1,0:T(8,128)S(1)} %get-tuple-element.37), channel_id=1, source_target_pairs={{0,16},{16,32},{32,48},{48,64},{64,80},{80,96},{96,112},{112,128},... | collective-permute-start | bytes 156680 | tf_op jit(solution)/shard_map/ppermute | solution.py:154
  122.2 1.9 %collective-permute-start.11 = (f32[3,34,128]{2,1,0:T(8,128)S(1)}, f32[3,34,128]{2,1,0:T(8,128)S(1)}, u32[]{:S(2)}, u32[]{:S(2)}) collective-permute-start(f32[3,34,128]{2,1,0:T(8,128)S(1)} %get-tuple-element.36), channel_id=1, source_target_pairs={{16,0},{32,16},{48,32},{64,48},{80,64},{96,80},{112,96},{128,112},... | collective-permute-start | bytes 156680 | tf_op jit(solution)/shard_map/ppermute | solution.py:155
  124.7 2.2 %collective-permute-start.12 = (f32[32,34,3]{1,0,2:T(8,128)S(1)}, f32[32,34,3]{1,0,2:T(8,128)S(1)}, u32[]{:S(2)}, u32[]{:S(2)}) collective-permute-start(f32[32,34,3]{1,0,2:T(8,128)S(1)} %copy.19), channel_id=1, source_target_pairs={{0,1},{1,2},{2,3},{3,0},{4,5},{5,6},{6,7},{7,4},{8,9},{9,10},{10,1... | collective-permute-start | bytes 39176 | tf_op jit(solution)/shard_map/ppermute | solution.py:63
  127.2 4.9 %collective-permute-start.13 = (f32[32,34,3]{1,0,2:T(8,128)S(1)}, f32[32,34,3]{1,0,2:T(8,128)S(1)}, u32[]{:S(2)}, u32[]{:S(2)}) collective-permute-start(f32[32,34,3]{1,0,2:T(8,128)S(1)} %copy.21), channel_id=1, source_target_pairs={{1,0},{2,1},{3,2},{0,3},{5,4},{6,5},{7,6},{4,7},{9,8},{10,9},{11,1... | collective-permute-start | bytes 39176 | tf_op jit(solution)/shard_map/ppermute | solution.py:64
  132.2 1.2 copy.20
  133.4 1.2 copy.22
  134.6 0.6 collective-permute-done.11
  135.2 13.3 %fusion.181 = f32[32,34,128]{2,1,0:T(8,128)S(1)} fusion(f32[32,34,128]{2,1,0:T(8,128)S(1)} %slice.606, f32[32,34,3]{2,1,0:T(8,128)} %copy.22, f32[32,34,3]{2,1,0:T(8,128)} %copy.20, f32[5,32,52,128]{3,2,1,0:T(8,128)} %copy-done, f32[32,40,128]{2,1,0:T(8,128)S(1)} %fusion.174, f32[3,34,128]{2,1,0:T(8,128)S(1)} %collective-permute-done.10, ...), kind=kLoop, calls=%fused_computation.285 | loop fusion | flops 59465728 | bytes 7372288 | tf_op jit(solution)/shard_map/jit(_where)/select_n | solution.py:185
  148.5 10.1 %collective-permute-start.14 = (f32[1,34,128]{2,1,0:T(8,128)S(1)}, f32[1,34,128]{2,1,0:T(8,128)S(1)}, u32[]{:S(2)}, u32[]{:S(2)}) collective-permute-start(f32[1,34,128]{2,1,0:T(8,128)S(1)} %get-tuple-element.32), channel_id=1, source_target_pairs={{0,16},{16,32},{32,48},{48,64},{64,80},{80,96},{96,112},{112,128},... | collective-permute-start | bytes 52232 | tf_op jit(solution)/shard_map/ppermute | solution.py:154
  158.6 1.9 %collective-permute-start.15 = (f32[1,34,128]{2,1,0:T(8,128)S(1)}, f32[1,34,128]{2,1,0:T(8,128)S(1)}, u32[]{:S(2)}, u32[]{:S(2)}) collective-permute-start(f32[1,34,128]{2,1,0:T(8,128)S(1)} %get-tuple-element.33), channel_id=1, source_target_pairs={{16,0},{32,16},{48,32},{64,48},{80,64},{96,80},{112,96},{128,112},... | collective-permute-start | bytes 52232 | tf_op jit(solution)/shard_map/ppermute | solution.py:155
  160.5 0.6 fusion.508
  162.4 7.3 %collective-permute-done.15 = f32[1,34,128]{2,1,0:T(8,128)S(1)} collective-permute-done((f32[1,34,128]{2,1,0:T(8,128)S(1)}, f32[1,34,128]{2,1,0:T(8,128)S(1)}, u32[]{:S(2)}, u32[]{:S(2)}) %collective-permute-start.15) | collective-permute-done | bytes 17440 | tf_op jit(solution)/shard_map/ppermute | solution.py:155
  170.2 1.2 multiply_reduce_fusion.7
  171.3 1.2 multiply_reduce_fusion.5
  172.5 1.2 multiply_reduce_fusion.3
  173.7 1.2 multiply_reduce_fusion.1
  175.0 1.3 copy.23
  176.3 0.7 copy.24
  177.0 0.8 reshape.108
  177.7 5.1 %all-to-all-start = ((f32[4,1,4096]{2,1,0:T(1,128)}), f32[4,1,4096]{2,1,0:T(1,128)S(1)}, u32[]{:S(2)}, u32[]{:S(2)}) async-start(f32[4,1,4096]{2,1,0:T(1,128)} %reshape.108), calls=%async_computation | async-start | bytes 131072 | tf_op jit(solution)/shard_map/all_to_all | solution.py:204
  182.9 0.9 slice.636
  183.7 3.7 %all-to-all-done = f32[4,1,4096]{2,1,0:T(1,128)S(1)} async-done(((f32[4,1,4096]{2,1,0:T(1,128)}), f32[4,1,4096]{2,1,0:T(1,128)S(1)}, u32[]{:S(2)}, u32[]{:S(2)}) %all-to-all-start) | async-done | bytes 65568 | tf_op jit(solution)/shard_map/all_to_all | solution.py:204
  188.0 0.8 reduce
  190.2 0.6 pad_maximum_fusion.16
  (59 shorter events, 7.8 us)
Async XLA Ops:
  5.9 21.6 %collective-permute-start.1 = (f32[5,32,10,128]{3,1,2,0:T(8,128)S(1)}, f32[5,32,10,128]{3,1,2,0:T(8,128)S(1)}, u32[]{:S(2)}, u32[]{:S(2)}) collective-permute-start(f32[5,32,10,128]{3,1,2,0:T(8,128)S(1)} %copy.8), channel_id=1, source_target_pairs={{4,0},{8,4},{12,8},{0,12},{5,1},{9,5},{13,9},{1,13},{6,2},{10,6},{... | collective-permute-start | bytes 2457608 | tf_op jit(solution)/shard_map/ppermute | solution.py:24
  10.9 22.0 %collective-permute-start = (f32[5,32,10,128]{3,1,2,0:T(8,128)S(1)}, f32[5,32,10,128]{3,1,2,0:T(8,128)S(1)}, u32[]{:S(2)}, u32[]{:S(2)}) collective-permute-start(f32[5,32,10,128]{3,1,2,0:T(8,128)S(1)} %copy.7), channel_id=1, source_target_pairs={{0,4},{4,8},{8,12},{12,0},{1,5},{5,9},{9,13},{13,1},{2,6},{6,10},{... | collective-permute-start | bytes 2457608 | tf_op jit(solution)/shard_map/ppermute | solution.py:23
  33.9 13.5 %copy-start = (f32[5,32,52,128]{3,2,1,0:T(8,128)}, f32[5,32,52,128]{3,2,1,0:T(8,128)S(1)}, u32[]{:S(2)}) copy-start(f32[5,32,52,128]{3,2,1,0:T(8,128)S(1)} %pad_maximum_fusion) | copy-start | bytes 12779524
  34.7 24.9 %collective-permute-start.2 = (f32[3,46,128]{2,1,0:T(8,128)}, f32[3,46,128]{2,1,0:T(8,128)S(1)}, u32[]{:S(2)}, u32[]{:S(2)}) collective-permute-start(f32[3,46,128]{2,1,0:T(8,128)} %get-tuple-element.21), channel_id=1, source_target_pairs={{0,16},{16,32},{32,48},{48,64},{64,80},{80,96},{96,112},{112,128},... | collective-permute-start | bytes 211976 | tf_op jit(solution)/shard_map/ppermute | solution.py:154
  45.1 14.4 %collective-permute-start.3 = (f32[3,46,128]{2,1,0:T(8,128)S(1)}, f32[3,46,128]{2,1,0:T(8,128)S(1)}, u32[]{:S(2)}, u32[]{:S(2)}) collective-permute-start(f32[3,46,128]{2,1,0:T(8,128)S(1)} %get-tuple-element.20), channel_id=1, source_target_pairs={{16,0},{32,16},{48,32},{64,48},{80,64},{96,80},{112,96},{128,112},... | collective-permute-start | bytes 211976 | tf_op jit(solution)/shard_map/ppermute | solution.py:155
  47.7 9.2 %collective-permute-start.4 = (f32[32,46,3]{1,0,2:T(8,128)S(1)}, f32[32,46,3]{1,0,2:T(8,128)S(1)}, u32[]{:S(2)}, u32[]{:S(2)}) collective-permute-start(f32[32,46,3]{1,0,2:T(8,128)S(1)} %copy.11), channel_id=1, source_target_pairs={{0,1},{1,2},{2,3},{3,0},{4,5},{5,6},{6,7},{7,4},{8,9},{9,10},{10,1... | collective-permute-start | bytes 53000 | tf_op jit(solution)/shard_map/ppermute | solution.py:63
  52.2 6.1 %collective-permute-start.5 = (f32[32,46,3]{1,0,2:T(8,128)}, f32[32,46,3]{1,0,2:T(8,128)S(1)}, u32[]{:S(2)}, u32[]{:S(2)}) collective-permute-start(f32[32,46,3]{1,0,2:T(8,128)} %copy.13), channel_id=1, source_target_pairs={{1,0},{2,1},{3,2},{0,3},{5,4},{6,5},{7,6},{4,7},{9,8},{10,9},{11,1... | collective-permute-start | bytes 53000 | tf_op jit(solution)/shard_map/ppermute | solution.py:64
  74.4 23.3 %collective-permute-start.6 = (f32[3,40,128]{2,1,0:T(8,128)S(1)}, f32[3,40,128]{2,1,0:T(8,128)S(1)}, u32[]{:S(2)}, u32[]{:S(2)}) collective-permute-start(f32[3,40,128]{2,1,0:T(8,128)S(1)} %get-tuple-element.25), channel_id=1, source_target_pairs={{0,16},{16,32},{32,48},{48,64},{64,80},{80,96},{96,112},{112,128},... | collective-permute-start | bytes 184328 | tf_op jit(solution)/shard_map/ppermute | solution.py:154
  84.9 12.7 %collective-permute-start.7 = (f32[3,40,128]{2,1,0:T(8,128)S(1)}, f32[3,40,128]{2,1,0:T(8,128)S(1)}, u32[]{:S(2)}, u32[]{:S(2)}) collective-permute-start(f32[3,40,128]{2,1,0:T(8,128)S(1)} %get-tuple-element.24), channel_id=1, source_target_pairs={{16,0},{32,16},{48,32},{64,48},{80,64},{96,80},{112,96},{128,112},... | collective-permute-start | bytes 184328 | tf_op jit(solution)/shard_map/ppermute | solution.py:155
  87.3 7.9 %collective-permute-start.8 = (f32[32,40,3]{1,0,2:T(8,128)S(1)}, f32[32,40,3]{1,0,2:T(8,128)S(1)}, u32[]{:S(2)}, u32[]{:S(2)}) collective-permute-start(f32[32,40,3]{1,0,2:T(8,128)S(1)} %copy.15), channel_id=1, source_target_pairs={{0,1},{1,2},{2,3},{3,0},{4,5},{5,6},{6,7},{7,4},{8,9},{9,10},{10,1... | collective-permute-start | bytes 46088 | tf_op jit(solution)/shard_map/ppermute | solution.py:63
  90.8 5.7 %collective-permute-start.9 = (f32[32,40,3]{1,0,2:T(8,128)S(1)}, f32[32,40,3]{1,0,2:T(8,128)S(1)}, u32[]{:S(2)}, u32[]{:S(2)}) collective-permute-start(f32[32,40,3]{1,0,2:T(8,128)S(1)} %copy.17), channel_id=1, source_target_pairs={{1,0},{2,1},{3,2},{0,3},{5,4},{6,5},{7,6},{4,7},{9,8},{10,9},{11,1... | collective-permute-start | bytes 46088 | tf_op jit(solution)/shard_map/ppermute | solution.py:64
  110.7 23.9 %collective-permute-start.10 = (f32[3,34,128]{2,1,0:T(8,128)S(1)}, f32[3,34,128]{2,1,0:T(8,128)S(1)}, u32[]{:S(2)}, u32[]{:S(2)}) collective-permute-start(f32[3,34,128]{2,1,0:T(8,128)S(1)} %get-tuple-element.37), channel_id=1, source_target_pairs={{0,16},{16,32},{32,48},{48,64},{64,80},{80,96},{96,112},{112,128},... | collective-permute-start | bytes 156680 | tf_op jit(solution)/shard_map/ppermute | solution.py:154
  122.2 13.0 %collective-permute-start.11 = (f32[3,34,128]{2,1,0:T(8,128)S(1)}, f32[3,34,128]{2,1,0:T(8,128)S(1)}, u32[]{:S(2)}, u32[]{:S(2)}) collective-permute-start(f32[3,34,128]{2,1,0:T(8,128)S(1)} %get-tuple-element.36), channel_id=1, source_target_pairs={{16,0},{32,16},{48,32},{64,48},{80,64},{96,80},{112,96},{128,112},... | collective-permute-start | bytes 156680 | tf_op jit(solution)/shard_map/ppermute | solution.py:155
  124.7 7.5 %collective-permute-start.12 = (f32[32,34,3]{1,0,2:T(8,128)S(1)}, f32[32,34,3]{1,0,2:T(8,128)S(1)}, u32[]{:S(2)}, u32[]{:S(2)}) collective-permute-start(f32[32,34,3]{1,0,2:T(8,128)S(1)} %copy.19), channel_id=1, source_target_pairs={{0,1},{1,2},{2,3},{3,0},{4,5},{5,6},{6,7},{7,4},{8,9},{9,10},{10,1... | collective-permute-start | bytes 39176 | tf_op jit(solution)/shard_map/ppermute | solution.py:63
  127.2 6.2 %collective-permute-start.13 = (f32[32,34,3]{1,0,2:T(8,128)S(1)}, f32[32,34,3]{1,0,2:T(8,128)S(1)}, u32[]{:S(2)}, u32[]{:S(2)}) collective-permute-start(f32[32,34,3]{1,0,2:T(8,128)S(1)} %copy.21), channel_id=1, source_target_pairs={{1,0},{2,1},{3,2},{0,3},{5,4},{6,5},{7,6},{4,7},{9,8},{10,9},{11,1... | collective-permute-start | bytes 39176 | tf_op jit(solution)/shard_map/ppermute | solution.py:64
  134.6 25.9 %copy-start.1 = (s32[4]{0:T(128)S(1)}, s32[4]{0:T(128)}, u32[]{:S(2)}) copy-start(s32[4]{0:T(128)} %param.7) | copy-start | bytes 52
  148.5 13.9 %collective-permute-start.14 = (f32[1,34,128]{2,1,0:T(8,128)S(1)}, f32[1,34,128]{2,1,0:T(8,128)S(1)}, u32[]{:S(2)}, u32[]{:S(2)}) collective-permute-start(f32[1,34,128]{2,1,0:T(8,128)S(1)} %get-tuple-element.32), channel_id=1, source_target_pairs={{0,16},{16,32},{32,48},{48,64},{64,80},{80,96},{96,112},{112,128},... | collective-permute-start | bytes 52232 | tf_op jit(solution)/shard_map/ppermute | solution.py:154
  158.6 11.1 %collective-permute-start.15 = (f32[1,34,128]{2,1,0:T(8,128)S(1)}, f32[1,34,128]{2,1,0:T(8,128)S(1)}, u32[]{:S(2)}, u32[]{:S(2)}) collective-permute-start(f32[1,34,128]{2,1,0:T(8,128)S(1)} %get-tuple-element.33), channel_id=1, source_target_pairs={{16,0},{32,16},{48,32},{64,48},{80,64},{96,80},{112,96},{128,112},... | collective-permute-start | bytes 52232 | tf_op jit(solution)/shard_map/ppermute | solution.py:155
  177.7 9.7 %all-to-all-start = ((f32[4,1,4096]{2,1,0:T(1,128)}), f32[4,1,4096]{2,1,0:T(1,128)S(1)}, u32[]{:S(2)}, u32[]{:S(2)}) async-start(f32[4,1,4096]{2,1,0:T(1,128)} %reshape.108), calls=%async_computation | async-start | bytes 131072 | tf_op jit(solution)/shard_map/all_to_all | solution.py:204

commit v6 on v5

--- a/solution.py
+++ b/solution.py
@@ -170,21 +170,45 @@
     halo = 3 * SPAN + 1
     stacked = exchange([stacked], "gy", [halo], 1)[0]
     level_ext = stacked[0]
-    speed_one = stacked[1:4, :, SPAN:-SPAN]
+    carried = stacked[1:5, :, SPAN:-SPAN]
+    speed_one = carried[:3]
     speed_two = speed_one[:, :, SPAN:-SPAN]
-    speed_three = speed_two[:, :, SPAN:-SPAN]
     flag_ring = stacked[4, :, 3 * SPAN : -3 * SPAN]
 
-    inner, rate = stage_rate(level_ext, speed_one)
-    section_one = inner + time_step * rate
+    size = lax.axis_size("gx")
+    up = [(i, (i + 1) % size) for i in range(size)]
+    down = [(j, i) for i, j in up]
+    inner = level_ext[:, SPAN:-SPAN]
+    last = jnp.concatenate([inner[-SPAN:]] + [carried[c, -1:] for c in range(4)], 0)
+    first = jnp.concatenate([inner[:SPAN]] + [carried[c, :1] for c in range(4)], 0)
+    before = lax.ppermute(last, "gx", up)
+    after = lax.ppermute(first, "gx", down)
+    padded = [
+        jnp.concatenate([before[:SPAN], inner, after[:SPAN]], 0),
+        level_ext,
+        z_faces(inner),
+    ]
+    section_one = inner + time_step * local_rate(padded, speed_one)
     inner, rate = stage_rate(section_one, speed_two)
     section_two = 0.75 * level_ext[:, 2 * SPAN : -2 * SPAN] + 0.25 * (inner + time_step * rate)
-    inner, rate = stage_rate(section_two, speed_three)
-    level_ring = level_ext[:, 3 * SPAN : -3 * SPAN]
+
+    ring = slice(2 * SPAN, -2 * SPAN)
+    edge_before = before[SPAN - 1 :, ring]
+    edge_after = jnp.concatenate([after[:1], after[SPAN:]], 0)[:, ring]
+    wide = x_faces(section_two, SPAN + 1)
+    inner = wide[SPAN:-SPAN, SPAN:-SPAN]
+    padded = [wide[:, SPAN:-SPAN], wide[SPAN:-SPAN], z_faces(inner)]
+    speed_three = jnp.concatenate(
+        [edge_before[1:4][:, None], speed_two[:, :, SPAN:-SPAN], edge_after[1:4][:, None]], 1
+    )
+    rate = local_rate(padded, speed_three)
+    level_ring = jnp.concatenate(
+        [edge_before[:1], level_ext[:, 3 * SPAN : -3 * SPAN], edge_after[:1]], 0
+    )
+    flag_three = jnp.concatenate([edge_before[4:5], flag_ring, edge_after[4:5]], 0)
     advanced = level_ring / 3.0 + 2.0 / 3.0 * (inner + time_step * rate)
-    ringed = jnp.where(flag_ring > 0, advanced, level_ring)
-    level_out = ringed[:, 1:-1]
-    rim = x_faces(ringed, 1)
+    rim = jnp.where(flag_three > 0, advanced, level_ring)
+    level_out = rim[1:-1, 1:-1]
 
     group = lax.axis_size("gz")
     ascending = depth_order[0] < depth_order[group - 1]

time: 192 us -> 194 us (1.010)
  the two profiles are of different devices: /device:TPU:7 before, /device:TPU:8 now
where the time goes in v6:
time: 194 us; the launch traced here: 193 us
  starting transfers between devices  74.3 us (38%)
  other arithmetic  53.6 us (28%)
  local copies, waits for them, and re-layouts  35.4 us (18%)
  waiting for transfers between devices  20.3 us (10%)
  matrix products  5.91 us (3%)
  between operations  3.11 us (2%)
    ppermute x2, starting transfers between devices, x_faces(): after = lax.ppermute(x[:width], 'gx', down)  19.3 us
    ppermute x3, starting transfers between devices, z_faces(): after = lax.ppermute(x[:, :, :SPAN], 'gz', down)  16.3 us
    select_n x1, other arithmetic, shards(): rim = jnp.where(flag_three > 0, advanced, level_ring)  15.8 us
    add x1, other arithmetic, shards(): section_one = inner + time_step * local_rate(padded, speed_one)  14.8 us
    ppermute x1, starting transfers between devices, shards(): after = lax.ppermute(first, 'gx', down)  13.2 us
    add x1, other arithmetic, shards(): 0.75 * level_ext[:, 2 * SPAN:-2 * SPAN] + 0.25 * (inner + time_step * rate)  12.6 us
    ppermute x1, waiting for transfers between devices, exchange(): before = lax.ppermute(last, axis, up)  10.1 us
    ppermute x3, starting transfers between devices, z_faces(): before = lax.ppermute(x[:, :, length - SPAN:], 'gz', up)  6.74 us
  transfers between devices with their start and end apart: 15, of which 6 were waited for; matrix products, arithmetic and copies ran while one was open for 13% of the time, Pallas kernels for 0%

profile of v6, /device:TPU:8, one launch (start us, length us, event | category | flops | bytes accessed | tf_op | source)
XLA Modules:
  0.0 192.6 jit_solution(537263086019594385)
XLA Ops:
  1.3 1.1 bitcast_dynamic-update-slice_fusion
  2.4 1.0 convert_dynamic-update-slice_fusion.2
  3.4 1.0 convert_dynamic-update-slice_fusion.1
  4.4 1.0 convert_dynamic-update-slice_fusion
  6.0 3.5 %collective-permute-start = (f32[5,32,10,128]{3,1,2,0:T(8,128)S(1)}, f32[5,32,10,128]{3,1,2,0:T(8,128)S(1)}, u32[]{:S(2)}, u32[]{:S(2)}) collective-permute-start(f32[5,32,10,128]{3,1,2,0:T(8,128)S(1)} %copy.10), channel_id=1, source_target_pairs={{0,4},{4,8},{8,12},{12,0},{1,5},{5,9},{9,13},{13,1},{2,6},{6,10},{... | collective-permute-start | bytes 2457608 | tf_op jit(solution)/shard_map/ppermute | solution.py:23
  9.7 6.1 %collective-permute-start.1 = (f32[5,32,10,128]{3,1,2,0:T(8,128)S(1)}, f32[5,32,10,128]{3,1,2,0:T(8,128)S(1)}, u32[]{:S(2)}, u32[]{:S(2)}) collective-permute-start(f32[5,32,10,128]{3,1,2,0:T(8,128)S(1)} %copy.11), channel_id=1, source_target_pairs={{4,0},{8,4},{12,8},{0,12},{5,1},{9,5},{13,9},{1,13},{6,2},{10,6},{... | collective-permute-start | bytes 2457608 | tf_op jit(solution)/shard_map/ppermute | solution.py:24
  17.8 10.1 %collective-permute-done = f32[5,32,10,128]{3,1,2,0:T(8,128)S(1)} collective-permute-done((f32[5,32,10,128]{3,1,2,0:T(8,128)S(1)}, f32[5,32,10,128]{3,1,2,0:T(8,128)S(1)}, u32[]{:S(2)}, u32[]{:S(2)}) %collective-permute-start) | collective-permute-done | bytes 819232 | tf_op jit(solution)/shard_map/ppermute | solution.py:23
  28.3 3.0 %collective-permute-done.1 = f32[5,32,10,128]{3,1,2,0:T(8,128)S(1)} collective-permute-done((f32[5,32,10,128]{3,1,2,0:T(8,128)S(1)}, f32[5,32,10,128]{3,1,2,0:T(8,128)S(1)}, u32[]{:S(2)}, u32[]{:S(2)}) %collective-permute-start.1) | collective-permute-done | bytes 819232 | tf_op jit(solution)/shard_map/ppermute | solution.py:24
  33.5 1.0 copy-done
  36.9 13.2 %collective-permute-start.3 = (f32[7,46,128]{2,1,0:T(8,128)}, f32[7,46,128]{2,1,0:T(8,128)S(1)}, u32[]{:S(2)}, u32[]{:S(2)}) collective-permute-start(f32[7,46,128]{2,1,0:T(8,128)} %get-tuple-element.18), channel_id=1, source_target_pairs={{16,0},{32,16},{48,32},{64,48},{80,64},{96,80},{112,96},{128,112},... | collective-permute-start | bytes 494600 | tf_op jit(solution)/shard_map/ppermute | solution.py:185
  50.2 1.9 collective-permute-start.2
  52.5 2.9 %collective-permute-start.4 = (f32[32,46,3]{1,0,2:T(8,128)S(1)}, f32[32,46,3]{1,0,2:T(8,128)S(1)}, u32[]{:S(2)}, u32[]{:S(2)}) collective-permute-start(f32[32,46,3]{1,0,2:T(8,128)S(1)} %copy.14), channel_id=1, source_target_pairs={{0,1},{1,2},{2,3},{3,0},{4,5},{5,6},{6,7},{7,4},{8,9},{9,10},{10,1... | collective-permute-start | bytes 53000 | tf_op jit(solution)/shard_map/ppermute | solution.py:63
  55.7 4.7 %collective-permute-start.5 = (f32[32,46,3]{1,0,2:T(8,128)S(1)}, f32[32,46,3]{1,0,2:T(8,128)S(1)}, u32[]{:S(2)}, u32[]{:S(2)}) collective-permute-start(f32[32,46,3]{1,0,2:T(8,128)S(1)} %copy.16), channel_id=1, source_target_pairs={{1,0},{2,1},{3,2},{0,3},{5,4},{6,5},{7,6},{4,7},{9,8},{10,9},{11,1... | collective-permute-start | bytes 53000 | tf_op jit(solution)/shard_map/ppermute | solution.py:64
  60.4 2.1 %slice_bitcast_fusion.1 = f32[32,34,128]{2,1,0:T(8,128)} fusion(f32[5,32,52,128]{3,2,1,0:T(8,128)} %copy-done), kind=kLoop, calls=%fused_computation.392 | loop fusion | bytes 1114112 | tf_op jit(solution)/shard_map/squeeze | solution.py:176
  62.5 3.2 %slice.717 = f32[3,32,34,128]{3,2,1,0:T(8,128)} slice(f32[5,32,52,128]{3,2,1,0:T(8,128)} %copy-done), slice={[1:4], [0:32], [9:43], [0:128]} | slice | bytes 3342336 | tf_op jit(solution)/shard_map/slice | solution.py:202
  67.1 1.3 copy.17
  69.8 14.8 %fusion.21 = f32[32,46,128]{2,1,0:T(8,128)S(1)} fusion(f32[32,46,128]{2,1,0:T(8,128)S(1)} %slice.653, f32[32,46,3]{2,1,0:T(8,128)} %copy.17, f32[32,46,3]{2,1,0:T(8,128)S(1)} %copy.15, f32[5,32,52,128]{3,2,1,0:T(8,128)} %copy-done, f32[32,52,128]{2,1,0:T(8,128)S(1)} %slice_bitcast_fusion, f32[3,46,128]{2,1,0:T(8,128)S(1)} %slice.655, ...), kind=kLoop, calls=%fused_computation.76 | loop fusion | flops 79511552 | bytes 8466944 | tf_op jit(solution)/shard_map/add | solution.py:191
  84.9 0.9 copy.18
  85.8 1.9 collective-permute-start.8
  87.7 0.9 copy.20
  88.6 5.7 %collective-permute-start.9 = (f32[32,40,3]{1,0,2:T(8,128)}, f32[32,40,3]{1,0,2:T(8,128)}, u32[]{:S(2)}, u32[]{:S(2)}) collective-permute-start(f32[32,40,3]{1,0,2:T(8,128)} %copy.20), channel_id=1, source_target_pairs={{1,0},{2,1},{3,2},{0,3},{5,4},{6,5},{7,6},{4,7},{9,8},{10,9},{11,1... | collective-permute-start | bytes 46088 | tf_op jit(solution)/shard_map/ppermute | solution.py:64
  94.4 1.9 collective-permute-start.6
  96.3 9.7 %collective-permute-start.7 = (f32[3,40,128]{2,1,0:T(8,128)S(1)}, f32[3,40,128]{2,1,0:T(8,128)S(1)}, u32[]{:S(2)}, u32[]{:S(2)}) collective-permute-start(f32[3,40,128]{2,1,0:T(8,128)S(1)} %get-tuple-element.34), channel_id=1, source_target_pairs={{16,0},{32,16},{48,32},{64,48},{80,64},{96,80},{112,96},{128,112},... | collective-permute-start | bytes 184328 | tf_op jit(solution)/shard_map/ppermute | solution.py:155
  106.0 1.5 slice_bitcast_fusion.3
  107.5 1.4 fusion.462
  108.9 1.1 copy.19
  110.0 1.9 %copy.21 = f32[32,40,3]{2,1,0:T(8,128)} copy(f32[32,40,3]{1,0,2:T(8,128)} %collective-permute-done.9) | data formatting | bytes 30720 | tf_op jit(solution)/shard_map/ppermute | solution.py:64
  112.0 12.6 %fusion.258 = f32[32,40,128]{2,1,0:T(8,128)S(1)} fusion(f32[32,52,128]{2,1,0:T(8,128)S(1)} %slice_bitcast_fusion, f32[32,40,128]{2,1,0:T(8,128)S(1)} %slice.683, f32[32,40,3]{2,1,0:T(8,128)} %copy.21, f32[32,40,3]{2,1,0:T(8,128)S(1)} %copy.19, f32[5,32,52,128]{3,2,1,0:T(8,128)} %copy-done, f32[32,46,128]{2,1,0:T(8,128)S(1)} %fusion.21, ...), kind=kLoop, calls=%fused_computation.391 | loop fusion | flops 69632000 | bytes 8017920 | tf_op jit(solution)/shard_map/add | solution.py:193
  124.6 1.9 collective-permute-start.10
  126.5 9.7 %collective-permute-start.11 = (f32[4,40,128]{2,1,0:T(8,128)S(1)}, f32[4,40,128]{2,1,0:T(8,128)S(1)}, u32[]{:S(2)}, u32[]{:S(2)}) collective-permute-start(f32[4,40,128]{2,1,0:T(8,128)S(1)} %get-tuple-element.45), channel_id=1, source_target_pairs={{16,0},{32,16},{48,32},{64,48},{80,64},{96,80},{112,96},{128,112},... | collective-permute-start | bytes 245768 | tf_op jit(solution)/shard_map/ppermute | solution.py:155
  136.8 1.5 collective-permute-done.10
  138.7 1.1 fusion.458
  139.8 2.1 %copy.23 = f32[34,34,3]{1,0,2:T(8,128)} copy(f32[34,34,3]{2,1,0:T(8,128)} %get-tuple-element.32) | data formatting | bytes 27744 | tf_op jit(solution)/shard_map/slice | solution.py:63
  141.9 1.9 collective-permute-start.12
  143.8 1.0 copy.25
  144.8 5.9 %collective-permute-start.13 = (f32[34,34,3]{1,0,2:T(8,128)}, f32[34,34,3]{1,0,2:T(8,128)S(1)}, u32[]{:S(2)}, u32[]{:S(2)}) collective-permute-start(f32[34,34,3]{1,0,2:T(8,128)} %copy.25), channel_id=1, source_target_pairs={{1,0},{2,1},{3,2},{0,3},{5,4},{6,5},{7,6},{4,7},{9,8},{10,9},{11,1... | collective-permute-start | bytes 41624 | tf_op jit(solution)/shard_map/ppermute | solution.py:64
  150.7 2.3 %pad_maximum_fusion.1 = f32[3,34,34,128]{3,2,1,0:T(8,128)} fusion(f32[3,1,34,128]{3,2,1,0:T(8,128)S(1)} %slice_bitcast_fusion.2, f32[3,32,34,128]{3,2,1,0:T(8,128)S(1)} %copy-done.1, f32[3,1,34,128]{3,2,1,0:T(8,128)} %slice_bitcast_fusion.3), kind=kLoop, calls=%fused_computation.1 | loop fusion | flops 887808 | bytes 3551232 | tf_op jit(solution)/shard_map/concatenate | solution.py:201
  153.0 0.9 slice.715
  153.9 1.2 copy.24
  155.1 1.2 copy.26
  156.3 15.8 %fusion.160 = f32[34,34,128]{2,1,0:T(8,128)S(1)} fusion(f32[34,34,128]{2,1,0:T(8,128)} %slice.715, f32[34,34,3]{2,1,0:T(8,128)} %copy.26, f32[34,34,3]{2,1,0:T(8,128)S(1)} %copy.24, f32[3,34,34,128]{3,2,1,0:T(8,128)} %pad_maximum_fusion.1, f32[40,40,128]{2,1,0:T(8,128)S(1)} %pad_maximum_fusion.2, f32[4,40,128]{2,1,0:T(8,128)} %copy-done.6, ...), kind=kLoop, calls=%fused_computation.258 | loop fusion | flops 63774208 | bytes 8541280 | tf_op jit(solution)/shard_map/jit(_where)/select_n | solution.py:210
  172.6 1.2 multiply_reduce_fusion.7
  173.7 1.2 multiply_reduce_fusion.5
  174.9 1.2 multiply_reduce_fusion.3
  176.1 1.2 multiply_reduce_fusion.1
  177.4 1.3 copy.27
  180.1 3.3 %all-to-all-start = ((f32[4,1,4096]{2,1,0:T(1,128)}), f32[4,1,4096]{2,1,0:T(1,128)S(1)}, u32[]{:S(2)}, u32[]{:S(2)}) async-start(f32[4,1,4096]{2,1,0:T(1,128)} %reshape.106), calls=%async_computation | async-start | bytes 131072 | tf_op jit(solution)/shard_map/all_to_all | solution.py:228
  184.3 4.8 %all-to-all-done = f32[4,1,4096]{2,1,0:T(1,128)S(1)} async-done(((f32[4,1,4096]{2,1,0:T(1,128)}), f32[4,1,4096]{2,1,0:T(1,128)S(1)}, u32[]{:S(2)}, u32[]{:S(2)}) %all-to-all-start) | async-done | bytes 65568 | tf_op jit(solution)/shard_map/all_to_all | solution.py:228
  (83 shorter events, 17.5 us)
Async XLA Ops:
  5.7 10.2 %copy-start.8 = (s32[4]{0:T(128)S(1)}, s32[4]{0:T(128)}, u32[]{:S(2)}) copy-start(s32[4]{0:T(128)} %param.7) | copy-start | bytes 52
  6.0 21.9 %collective-permute-start = (f32[5,32,10,128]{3,1,2,0:T(8,128)S(1)}, f32[5,32,10,128]{3,1,2,0:T(8,128)S(1)}, u32[]{:S(2)}, u32[]{:S(2)}) collective-permute-start(f32[5,32,10,128]{3,1,2,0:T(8,128)S(1)} %copy.10), channel_id=1, source_target_pairs={{0,4},{4,8},{8,12},{12,0},{1,5},{5,9},{9,13},{13,1},{2,6},{6,10},{... | collective-permute-start | bytes 2457608 | tf_op jit(solution)/shard_map/ppermute | solution.py:23
  9.7 21.6 %collective-permute-start.1 = (f32[5,32,10,128]{3,1,2,0:T(8,128)S(1)}, f32[5,32,10,128]{3,1,2,0:T(8,128)S(1)}, u32[]{:S(2)}, u32[]{:S(2)}) collective-permute-start(f32[5,32,10,128]{3,1,2,0:T(8,128)S(1)} %copy.11), channel_id=1, source_target_pairs={{4,0},{8,4},{12,8},{0,12},{5,1},{9,5},{13,9},{1,13},{6,2},{10,6},{... | collective-permute-start | bytes 2457608 | tf_op jit(solution)/shard_map/ppermute | solution.py:24
  32.4 2.1 %copy-start = (f32[5,32,52,128]{3,2,1,0:T(8,128)}, f32[5,32,52,128]{3,2,1,0:T(8,128)S(1)}, u32[]{:S(2)}) copy-start(f32[5,32,52,128]{3,2,1,0:T(8,128)S(1)} %pad_maximum_fusion) | copy-start | bytes 12779524
  36.9 32.9 %collective-permute-start.3 = (f32[7,46,128]{2,1,0:T(8,128)}, f32[7,46,128]{2,1,0:T(8,128)S(1)}, u32[]{:S(2)}, u32[]{:S(2)}) collective-permute-start(f32[7,46,128]{2,1,0:T(8,128)} %get-tuple-element.18), channel_id=1, source_target_pairs={{16,0},{32,16},{48,32},{64,48},{80,64},{96,80},{112,96},{128,112},... | collective-permute-start | bytes 494600 | tf_op jit(solution)/shard_map/ppermute | solution.py:185
  50.2 18.7 %collective-permute-start.2 = (f32[7,46,128]{2,1,0:T(8,128)}, f32[7,46,128]{2,1,0:T(8,128)}, u32[]{:S(2)}, u32[]{:S(2)}) collective-permute-start(f32[7,46,128]{2,1,0:T(8,128)} %get-tuple-element.19), channel_id=1, source_target_pairs={{0,16},{16,32},{32,48},{48,64},{64,80},{80,96},{96,112},{112,128},... | collective-permute-start | bytes 494600 | tf_op jit(solution)/shard_map/ppermute | solution.py:184
  52.5 14.2 %collective-permute-start.4 = (f32[32,46,3]{1,0,2:T(8,128)S(1)}, f32[32,46,3]{1,0,2:T(8,128)S(1)}, u32[]{:S(2)}, u32[]{:S(2)}) collective-permute-start(f32[32,46,3]{1,0,2:T(8,128)S(1)} %copy.14), channel_id=1, source_target_pairs={{0,1},{1,2},{2,3},{3,0},{4,5},{5,6},{6,7},{7,4},{8,9},{9,10},{10,1... | collective-permute-start | bytes 53000 | tf_op jit(solution)/shard_map/ppermute | solution.py:63
  55.7 11.3 %collective-permute-start.5 = (f32[32,46,3]{1,0,2:T(8,128)S(1)}, f32[32,46,3]{1,0,2:T(8,128)S(1)}, u32[]{:S(2)}, u32[]{:S(2)}) collective-permute-start(f32[32,46,3]{1,0,2:T(8,128)S(1)} %copy.16), channel_id=1, source_target_pairs={{1,0},{2,1},{3,2},{0,3},{5,4},{6,5},{7,6},{4,7},{9,8},{10,9},{11,1... | collective-permute-start | bytes 53000 | tf_op jit(solution)/shard_map/ppermute | solution.py:64
  85.8 23.1 %collective-permute-start.8 = (f32[32,40,3]{1,0,2:T(8,128)}, f32[32,40,3]{1,0,2:T(8,128)}, u32[]{:S(2)}, u32[]{:S(2)}) collective-permute-start(f32[32,40,3]{1,0,2:T(8,128)} %copy.18), channel_id=1, source_target_pairs={{0,1},{1,2},{2,3},{3,0},{4,5},{5,6},{6,7},{7,4},{8,9},{9,10},{10,1... | collective-permute-start | bytes 46088 | tf_op jit(solution)/shard_map/ppermute | solution.py:63
  88.6 21.4 %collective-permute-start.9 = (f32[32,40,3]{1,0,2:T(8,128)}, f32[32,40,3]{1,0,2:T(8,128)}, u32[]{:S(2)}, u32[]{:S(2)}) collective-permute-start(f32[32,40,3]{1,0,2:T(8,128)} %copy.20), channel_id=1, source_target_pairs={{1,0},{2,1},{3,2},{0,3},{5,4},{6,5},{7,6},{4,7},{9,8},{10,9},{11,1... | collective-permute-start | bytes 46088 | tf_op jit(solution)/shard_map/ppermute | solution.py:64
  94.4 17.6 %collective-permute-start.6 = (f32[3,40,128]{2,1,0:T(8,128)S(1)}, f32[3,40,128]{2,1,0:T(8,128)S(1)}, u32[]{:S(2)}, u32[]{:S(2)}) collective-permute-start(f32[3,40,128]{2,1,0:T(8,128)S(1)} %get-tuple-element.35), channel_id=1, source_target_pairs={{0,16},{16,32},{32,48},{48,64},{64,80},{80,96},{96,112},{112,128},... | collective-permute-start | bytes 184328 | tf_op jit(solution)/shard_map/ppermute | solution.py:154
  96.3 15.7 %collective-permute-start.7 = (f32[3,40,128]{2,1,0:T(8,128)S(1)}, f32[3,40,128]{2,1,0:T(8,128)S(1)}, u32[]{:S(2)}, u32[]{:S(2)}) collective-permute-start(f32[3,40,128]{2,1,0:T(8,128)S(1)} %get-tuple-element.34), channel_id=1, source_target_pairs={{16,0},{32,16},{48,32},{64,48},{80,64},{96,80},{112,96},{128,112},... | collective-permute-start | bytes 184328 | tf_op jit(solution)/shard_map/ppermute | solution.py:155
  124.6 15.2 %copy-start.2 = (f32[32,40,128]{2,1,0:T(8,128)}, f32[32,40,128]{2,1,0:T(8,128)S(1)}, u32[]{:S(2)}) copy-start(f32[32,40,128]{2,1,0:T(8,128)S(1)} %fusion.258) | copy-start | bytes 1966084
  124.6 13.8 %collective-permute-start.10 = (f32[4,40,128]{2,1,0:T(8,128)S(1)}, f32[4,40,128]{2,1,0:T(8,128)S(1)}, u32[]{:S(2)}, u32[]{:S(2)}) collective-permute-start(f32[4,40,128]{2,1,0:T(8,128)S(1)} %get-tuple-element.44), channel_id=1, source_target_pairs={{0,16},{16,32},{32,48},{48,64},{64,80},{80,96},{96,112},{112,128},... | collective-permute-start | bytes 245768 | tf_op jit(solution)/shard_map/ppermute | solution.py:154
  126.5 12.1 %collective-permute-start.11 = (f32[4,40,128]{2,1,0:T(8,128)S(1)}, f32[4,40,128]{2,1,0:T(8,128)S(1)}, u32[]{:S(2)}, u32[]{:S(2)}) collective-permute-start(f32[4,40,128]{2,1,0:T(8,128)S(1)} %get-tuple-element.45), channel_id=1, source_target_pairs={{16,0},{32,16},{48,32},{64,48},{80,64},{96,80},{112,96},{128,112},... | collective-permute-start | bytes 245768 | tf_op jit(solution)/shard_map/ppermute | solution.py:155
  138.3 1.4 copy-start.5
  138.6 1.2 copy-start.6
  138.7 12.0 %copy-start.1 = (f32[3,32,34,128]{3,2,1,0:T(8,128)S(1)}, f32[3,32,34,128]{3,2,1,0:T(8,128)}, u32[]{:S(2)}) copy-start(f32[3,32,34,128]{3,2,1,0:T(8,128)} %slice.717) | copy-start | bytes 5013508
  141.9 12.0 %collective-permute-start.12 = (f32[34,34,3]{1,0,2:T(8,128)}, f32[34,34,3]{1,0,2:T(8,128)}, u32[]{:S(2)}, u32[]{:S(2)}) collective-permute-start(f32[34,34,3]{1,0,2:T(8,128)} %copy.23), channel_id=1, source_target_pairs={{0,1},{1,2},{2,3},{3,0},{4,5},{5,6},{6,7},{7,4},{8,9},{9,10},{10,1... | collective-permute-start | bytes 41624 | tf_op jit(solution)/shard_map/ppermute | solution.py:63
  144.8 10.3 %collective-permute-start.13 = (f32[34,34,3]{1,0,2:T(8,128)}, f32[34,34,3]{1,0,2:T(8,128)S(1)}, u32[]{:S(2)}, u32[]{:S(2)}) collective-permute-start(f32[34,34,3]{1,0,2:T(8,128)} %copy.25), channel_id=1, source_target_pairs={{1,0},{2,1},{3,2},{0,3},{5,4},{6,5},{7,6},{4,7},{9,8},{10,9},{11,1... | collective-permute-start | bytes 41624 | tf_op jit(solution)/shard_map/ppermute | solution.py:64
  153.0 3.3 %copy-start.3 = (f32[32,40,128]{2,1,0:T(8,128)S(1)}, f32[32,40,128]{2,1,0:T(8,128)}, u32[]{:S(2)}) copy-start(f32[32,40,128]{2,1,0:T(8,128)} %copy-done.2) | copy-start | bytes 1966084
  153.0 3.3 %copy-start.4 = (f32[32,34,128]{2,1,0:T(8,128)S(1)}, f32[32,34,128]{2,1,0:T(8,128)}, u32[]{:S(2)}) copy-start(f32[32,34,128]{2,1,0:T(8,128)} %slice_bitcast_fusion.1) | copy-start | bytes 1671172
  153.0 3.3 %copy-start.7 = (f32[1,34,128]{2,1,0:T(8,128)S(1)}, f32[1,34,128]{2,1,0:T(8,128)}, u32[]{:S(2)}) copy-start(f32[1,34,128]{2,1,0:T(8,128)} %get-tuple-element.46) | copy-start | bytes 52228
  180.1 9.0 %all-to-all-start = ((f32[4,1,4096]{2,1,0:T(1,128)}), f32[4,1,4096]{2,1,0:T(1,128)S(1)}, u32[]{:S(2)}, u32[]{:S(2)}) async-start(f32[4,1,4096]{2,1,0:T(1,128)} %reshape.106), calls=%async_computation | async-start | bytes 131072 | tf_op jit(solution)/shard_map/all_to_all | solution.py:228

commit v7 on v5

--- a/solution.py
+++ b/solution.py
@@ -166,14 +166,22 @@
     alive = active_brick[0, 0, 0] > 0
     alive_float = alive.astype(jnp.float32)
     flags = jnp.broadcast_to(alive_float, level_set.shape)
-    stacked = jnp.stack([level_set] + [velocity[d].astype(jnp.float32) for d in range(3)] + [flags])
-    halo = 3 * SPAN + 1
-    stacked = exchange([stacked], "gy", [halo], 1)[0]
-    level_ext = stacked[0]
-    speed_one = stacked[1:4, :, SPAN:-SPAN]
+    fields = [level_set] + [velocity[d].astype(jnp.float32) for d in range(3)] + [flags]
+    halo, halo_speed = 3 * SPAN + 1, 2 * SPAN + 1
+    size, length = (lax.axis_size("gy"), level_set.shape[1])
+    up = [(i, (i + 1) % size) for i in range(size)]
+    down = [(j, i) for i, j in up]
+    before = lax.ppermute(jnp.stack([f[:, length - halo :] for f in fields]), "gy", up)
+    after = lax.ppermute(jnp.stack([f[:, :halo] for f in fields]), "gy", down)
+
+    def grown(c, w):
+        return jnp.concatenate([before[c, :, halo - w :], fields[c], after[c, :, :w]], axis=1)
+
+    level_ext = grown(0, halo)
+    speed_one = jnp.stack([grown(c, halo_speed) for c in range(1, 4)])
     speed_two = speed_one[:, :, SPAN:-SPAN]
     speed_three = speed_two[:, :, SPAN:-SPAN]
-    flag_ring = stacked[4, :, 3 * SPAN : -3 * SPAN]
+    flag_ring = grown(4, 1)
 
     inner, rate = stage_rate(level_ext, speed_one)
     section_one = inner + time_step * rate

time: 192 us -> 210 us (1.094)
  the two profiles are of different devices: /device:TPU:7 before, /device:TPU:32 now
where the time goes in v7:
time: 210 us; the launch traced here: 209 us
  starting transfers between devices  80.9 us (39%)
  other arithmetic  54.5 us (26%)
  local copies, waits for them, and re-layouts  35.9 us (17%)
  waiting for transfers between devices  28.6 us (14%)
  matrix products  5.89 us (3%)
  between operations  3.18 us (2%)
    ppermute x4, starting transfers between devices, x_faces(): after = lax.ppermute(x[:width], 'gx', down)  39.7 us
    add x1, other arithmetic, shards(): section_one = inner + time_step * rate  19 us
    ppermute x1, waiting for transfers between devices, shards(): after = lax.ppermute(jnp.stack([f[:, :halo] for f in fields]), 'gy', down)  15.3 us
    select_n x1, other arithmetic, shards(): ringed = jnp.where(flag_ring > 0, advanced, level_ring)  14.9 us
    add x1, other arithmetic, shards(): 0.75 * level_ext[:, 2 * SPAN:-2 * SPAN] + 0.25 * (inner + time_step * rate)  14.8 us
    ppermute x3, starting transfers between devices, z_faces(): after = lax.ppermute(x[:, :, :SPAN], 'gz', down)  12.4 us
    slice x6, local copies, waits for them, and re-layouts, z_faces(): before = lax.ppermute(x[:, :, length - SPAN:], 'gz', up)  8.83 us
    ppermute x4, starting transfers between devices, x_faces(): before = lax.ppermute(x[length - width:], 'gx', up)  7.68 us
  transfers between devices with their start and end apart: 17, of which 4 were waited for; matrix products, arithmetic and copies ran while one was open for 14% of the time, Pallas kernels for 0%

profile of v7, /device:TPU:32, one launch (start us, length us, event | category | flops | bytes accessed | tf_op | source)
XLA Modules:
  0.0 209.0 jit_solution(15223269573327064942)
XLA Ops:
  1.3 1.3 bitcast_convert_fusion
  3.2 4.9 %collective-permute-start.1 = (f32[5,32,10,128]{3,1,2,0:T(8,128)S(1)}, f32[5,32,10,128]{3,1,2,0:T(8,128)S(1)}, u32[]{:S(2)}, u32[]{:S(2)}) collective-permute-start(f32[5,32,10,128]{3,1,2,0:T(8,128)S(1)} %copy.14), channel_id=1, source_target_pairs={{4,0},{8,4},{12,8},{0,12},{5,1},{9,5},{13,9},{1,13},{6,2},{10,6},{... | collective-permute-start | bytes 2457608 | tf_op jit(solution)/shard_map/ppermute | solution.py:175
  8.4 1.9 collective-permute-start
  10.3 15.3 %collective-permute-done.1 = f32[5,32,10,128]{3,1,2,0:T(8,128)S(1)} collective-permute-done((f32[5,32,10,128]{3,1,2,0:T(8,128)S(1)}, f32[5,32,10,128]{3,1,2,0:T(8,128)S(1)}, u32[]{:S(2)}, u32[]{:S(2)}) %collective-permute-start.1) | collective-permute-done | bytes 819232 | tf_op jit(solution)/shard_map/ppermute | solution.py:175
  25.7 5.5 %collective-permute-done = f32[5,32,10,128]{3,1,2,0:T(8,128)S(1)} collective-permute-done((f32[5,32,10,128]{3,1,2,0:T(8,128)S(1)}, f32[5,32,10,128]{3,1,2,0:T(8,128)S(1)}, u32[]{:S(2)}, u32[]{:S(2)}) %collective-permute-start) | collective-permute-done | bytes 819232 | tf_op jit(solution)/shard_map/ppermute | solution.py:174
  32.2 1.2 fusion.502
  36.3 12.3 %collective-permute-start.3 = (f32[3,46,128]{2,1,0:T(8,128)}, f32[3,46,128]{2,1,0:T(8,128)}, u32[]{:S(2)}, u32[]{:S(2)}) collective-permute-start(f32[3,46,128]{2,1,0:T(8,128)} %get-tuple-element.18), channel_id=1, source_target_pairs={{16,0},{32,16},{48,32},{64,48},{80,64},{96,80},{112,96},{128,112},... | collective-permute-start | bytes 211976 | tf_op jit(solution)/shard_map/ppermute | solution.py:155
  48.7 1.9 collective-permute-start.2
  50.6 2.1 copy.23
  52.7 1.0 copy.25
  53.6 2.9 %collective-permute-start.5 = (f32[32,46,3]{1,0,2:T(8,128)}, f32[32,46,3]{1,0,2:T(8,128)S(1)}, u32[]{:S(2)}, u32[]{:S(2)}) collective-permute-start(f32[32,46,3]{1,0,2:T(8,128)} %copy.25), channel_id=1, source_target_pairs={{1,0},{2,1},{3,2},{0,3},{5,4},{6,5},{7,6},{4,7},{9,8},{10,9},{11,1... | collective-permute-start | bytes 53000 | tf_op jit(solution)/shard_map/ppermute | solution.py:64
  56.6 2.9 %collective-permute-start.4 = (f32[32,46,3]{1,0,2:T(8,128)}, f32[32,46,3]{1,0,2:T(8,128)S(1)}, u32[]{:S(2)}, u32[]{:S(2)}) collective-permute-start(f32[32,46,3]{1,0,2:T(8,128)} %copy.23), channel_id=1, source_target_pairs={{0,1},{1,2},{2,3},{3,0},{4,5},{5,6},{6,7},{7,4},{8,9},{9,10},{10,1... | collective-permute-start | bytes 53000 | tf_op jit(solution)/shard_map/ppermute | solution.py:63
  59.5 2.3 %fusion.420 = (f32[1,32,46,128]{3,2,1,0:T(8,128)}, f32[1,32,46,128]{3,2,1,0:T(8,128)}) fusion(f32[32,7,128]{2,1,0:T(8,128)S(1)} %bitcast.250, f32[32,32,128]{2,1,0:T(8,128)S(1)} %get-tuple-element.32, f32[32,7,128]{2,1,0:T(8,128)} %bitcast.256, f32[32,7,128]{2,1,0:T(8,128)S(1)} %bitcast.246, f32[32,32,128]{2,1,0:T(8,128)S(1)} %get-tuple-element.34, ...), kind=kLoop, calls=%fused_computation.566 | loop fusion | flops 753664 | bytes 3014656 | tf_op jit(solution)/shard_map/stack | solution.py:181
  61.9 0.9 slice.599
  63.6 1.3 copy.24
  64.9 1.3 copy.26
  66.2 19.0 %multiply_add_fusion = f32[32,46,128]{2,1,0:T(8,128)S(1)} fusion(f32[32,46,128]{2,1,0:T(8,128)} %slice.599, f32[32,46,3]{2,1,0:T(8,128)} %copy.26, f32[32,46,3]{2,1,0:T(8,128)} %copy.24, f32[32,52,128]{2,1,0:T(8,128)S(1)} %pad_maximum_fusion, f32[3,46,128]{2,1,0:T(8,128)} %collective-permute-done.2, f32[3,46,128]{2,1,0:T(8,128)} %collective-permute-done.3, ...), kind=kLoop, calls=%fused_computation.76 | loop fusion | flops 80642048 | bytes 8466944 | tf_op jit(solution)/shard_map/add | solution.py:187
  85.2 1.1 fusion.506
  86.3 9.2 %collective-permute-start.7 = (f32[3,40,128]{2,1,0:T(8,128)S(1)}, f32[3,40,128]{2,1,0:T(8,128)S(1)}, u32[]{:S(2)}, u32[]{:S(2)}) collective-permute-start(f32[3,40,128]{2,1,0:T(8,128)S(1)} %get-tuple-element.28), channel_id=1, source_target_pairs={{16,0},{32,16},{48,32},{64,48},{80,64},{96,80},{112,96},{128,112},... | collective-permute-start | bytes 184328 | tf_op jit(solution)/shard_map/ppermute | solution.py:155
  95.5 1.9 collective-permute-start.6
  97.5 2.0 copy.27
  99.5 0.9 copy.29
  100.4 3.9 %collective-permute-start.9 = (f32[32,40,3]{1,0,2:T(8,128)}, f32[32,40,3]{1,0,2:T(8,128)}, u32[]{:S(2)}, u32[]{:S(2)}) collective-permute-start(f32[32,40,3]{1,0,2:T(8,128)} %copy.29), channel_id=1, source_target_pairs={{1,0},{2,1},{3,2},{0,3},{5,4},{6,5},{7,6},{4,7},{9,8},{10,9},{11,1... | collective-permute-start | bytes 46088 | tf_op jit(solution)/shard_map/ppermute | solution.py:64
  104.3 2.0 collective-permute-start.8
  106.3 0.9 slice.632
  107.2 4.1 %collective-permute-done.8 = f32[32,40,3]{1,0,2:T(8,128)} collective-permute-done((f32[32,40,3]{1,0,2:T(8,128)}, f32[32,40,3]{1,0,2:T(8,128)}, u32[]{:S(2)}, u32[]{:S(2)}) %collective-permute-start.8) | collective-permute-done | bytes 15392 | tf_op jit(solution)/shard_map/ppermute | solution.py:63
  111.3 1.9 copy.28
  113.2 2.0 copy.30
  115.2 14.8 %fusion.167 = f32[32,40,128]{2,1,0:T(8,128)S(1)} fusion(f32[32,52,128]{2,1,0:T(8,128)S(1)} %pad_maximum_fusion, f32[32,40,128]{2,1,0:T(8,128)} %slice.632, f32[32,40,3]{2,1,0:T(8,128)} %copy.30, f32[32,40,3]{2,1,0:T(8,128)} %copy.28, f32[1,32,46,128]{3,2,1,0:T(8,128)} %get-tuple-element.61, f32[32,46,128]{2,1,0:T(8,128)S(1)} %multiply_add_fusion, ...), kind=kLoop, calls=%fused_computation.266 | loop fusion | flops 69632000 | bytes 8017920 | tf_op jit(solution)/shard_map/add | solution.py:189
  130.0 8.5 %collective-permute-start.11 = (f32[3,34,128]{2,1,0:T(8,128)S(1)}, f32[3,34,128]{2,1,0:T(8,128)S(1)}, u32[]{:S(2)}, u32[]{:S(2)}) collective-permute-start(f32[3,34,128]{2,1,0:T(8,128)S(1)} %get-tuple-element.43), channel_id=1, source_target_pairs={{16,0},{32,16},{48,32},{64,48},{80,64},{96,80},{112,96},{128,112},... | collective-permute-start | bytes 156680 | tf_op jit(solution)/shard_map/ppermute | solution.py:155
  138.6 1.9 collective-permute-start.10
  140.5 1.1 fusion.509
  141.6 1.4 copy.31
  143.0 1.9 collective-permute-start.12
  144.9 0.9 copy.33
  145.8 5.6 %collective-permute-start.13 = (f32[32,34,3]{1,0,2:T(8,128)}, f32[32,34,3]{1,0,2:T(8,128)}, u32[]{:S(2)}, u32[]{:S(2)}) collective-permute-start(f32[32,34,3]{1,0,2:T(8,128)} %copy.33), channel_id=1, source_target_pairs={{1,0},{2,1},{3,2},{0,3},{5,4},{6,5},{7,6},{4,7},{9,8},{10,9},{11,1... | collective-permute-start | bytes 39176 | tf_op jit(solution)/shard_map/ppermute | solution.py:64
  153.9 1.2 copy.32
  155.1 2.0 copy.34
  157.1 14.9 %fusion.174 = f32[32,34,128]{2,1,0:T(8,128)S(1)} fusion(f32[32,34,128]{2,1,0:T(8,128)} %slice.662, f32[32,34,3]{2,1,0:T(8,128)} %copy.34, f32[32,34,3]{2,1,0:T(8,128)} %copy.32, f32[1,32,46,128]{3,2,1,0:T(8,128)S(1)} %copy-done, f32[32,40,128]{2,1,0:T(8,128)S(1)} %fusion.167, f32[1,32,46,128]{3,2,1,0:T(8,128)} %get-tuple-element.62, ...), kind=kLoop, calls=%fused_computation.275 | loop fusion | flops 59744256 | bytes 6848136 | tf_op jit(solution)/shard_map/jit(_where)/select_n | solution.py:193
  172.0 1.9 collective-permute-start.14
  174.0 9.7 %collective-permute-start.15 = (f32[1,34,128]{2,1,0:T(8,128)S(1)}, f32[1,34,128]{2,1,0:T(8,128)S(1)}, u32[]{:S(2)}, u32[]{:S(2)}) collective-permute-start(f32[1,34,128]{2,1,0:T(8,128)S(1)} %get-tuple-element.40), channel_id=1, source_target_pairs={{16,0},{32,16},{48,32},{64,48},{80,64},{96,80},{112,96},{128,112},... | collective-permute-start | bytes 52232 | tf_op jit(solution)/shard_map/ppermute | solution.py:155
  185.7 1.2 multiply_reduce_fusion.7
  186.9 1.2 multiply_reduce_fusion.5
  188.3 1.2 multiply_reduce_fusion.3
  189.4 1.2 multiply_reduce_fusion.1
  190.7 1.3 copy.35
  193.5 7.5 %all-to-all-start = ((f32[4,1,4096]{2,1,0:T(1,128)}), f32[4,1,4096]{2,1,0:T(1,128)S(1)}, u32[]{:S(2)}, u32[]{:S(2)}) async-start(f32[4,1,4096]{2,1,0:T(1,128)} %reshape.103), calls=%async_computation | async-start | bytes 131072 | tf_op jit(solution)/shard_map/all_to_all | solution.py:212
  201.8 3.8 %all-to-all-done = f32[4,1,4096]{2,1,0:T(1,128)S(1)} async-done(((f32[4,1,4096]{2,1,0:T(1,128)}), f32[4,1,4096]{2,1,0:T(1,128)S(1)}, u32[]{:S(2)}, u32[]{:S(2)}) %all-to-all-start) | async-done | bytes 65568 | tf_op jit(solution)/shard_map/all_to_all | solution.py:212
  (94 shorter events, 15.0 us)
Async XLA Ops:
  0.6 2.0 copy-start.3
  3.2 22.4 %collective-permute-start.1 = (f32[5,32,10,128]{3,1,2,0:T(8,128)S(1)}, f32[5,32,10,128]{3,1,2,0:T(8,128)S(1)}, u32[]{:S(2)}, u32[]{:S(2)}) collective-permute-start(f32[5,32,10,128]{3,1,2,0:T(8,128)S(1)} %copy.14), channel_id=1, source_target_pairs={{4,0},{8,4},{12,8},{0,12},{5,1},{9,5},{13,9},{1,13},{6,2},{10,6},{... | collective-permute-start | bytes 2457608 | tf_op jit(solution)/shard_map/ppermute | solution.py:175
  8.4 22.8 %collective-permute-start = (f32[5,32,10,128]{3,1,2,0:T(8,128)S(1)}, f32[5,32,10,128]{3,1,2,0:T(8,128)S(1)}, u32[]{:S(2)}, u32[]{:S(2)}) collective-permute-start(f32[5,32,10,128]{3,1,2,0:T(8,128)S(1)} %copy.13), channel_id=1, source_target_pairs={{0,4},{4,8},{8,12},{12,0},{1,5},{5,9},{9,13},{13,1},{2,6},{6,10},{... | collective-permute-start | bytes 2457608 | tf_op jit(solution)/shard_map/ppermute | solution.py:174
  25.6 7.7 %copy-start.8 = (f32[5,32,10,128]{3,1,2,0:T(8,128)}, f32[5,32,10,128]{3,1,2,0:T(8,128)S(1)}, u32[]{:S(2)}) copy-start(f32[5,32,10,128]{3,1,2,0:T(8,128)S(1)} %collective-permute-done.1) | copy-start | bytes 2457604
  31.2 2.9 %copy-start.9 = (f32[5,32,10,128]{3,1,2,0:T(8,128)}, f32[5,32,10,128]{3,1,2,0:T(8,128)S(1)}, u32[]{:S(2)}) copy-start(f32[5,32,10,128]{3,1,2,0:T(8,128)S(1)} %collective-permute-done) | copy-start | bytes 2457604
  34.2 25.3 %copy-start.4 = (f32[1,32,7,128]{3,2,1,0:T(8,128)}, f32[1,32,7,128]{3,2,1,0:T(8,128)S(1)}, u32[]{:S(2)}) copy-start(f32[1,32,7,128]{3,2,1,0:T(8,128)S(1)} %copy.72) | copy-start | bytes 344068
  36.3 29.8 %collective-permute-start.3 = (f32[3,46,128]{2,1,0:T(8,128)}, f32[3,46,128]{2,1,0:T(8,128)}, u32[]{:S(2)}, u32[]{:S(2)}) collective-permute-start(f32[3,46,128]{2,1,0:T(8,128)} %get-tuple-element.18), channel_id=1, source_target_pairs={{16,0},{32,16},{48,32},{64,48},{80,64},{96,80},{112,96},{128,112},... | collective-permute-start | bytes 211976 | tf_op jit(solution)/shard_map/ppermute | solution.py:155
  48.7 17.5 %collective-permute-start.2 = (f32[3,46,128]{2,1,0:T(8,128)}, f32[3,46,128]{2,1,0:T(8,128)}, u32[]{:S(2)}, u32[]{:S(2)}) collective-permute-start(f32[3,46,128]{2,1,0:T(8,128)} %get-tuple-element.19), channel_id=1, source_target_pairs={{0,16},{16,32},{32,48},{48,64},{64,80},{80,96},{96,112},{112,128},... | collective-permute-start | bytes 211976 | tf_op jit(solution)/shard_map/ppermute | solution.py:154
  53.6 11.2 %collective-permute-start.5 = (f32[32,46,3]{1,0,2:T(8,128)}, f32[32,46,3]{1,0,2:T(8,128)S(1)}, u32[]{:S(2)}, u32[]{:S(2)}) collective-permute-start(f32[32,46,3]{1,0,2:T(8,128)} %copy.25), channel_id=1, source_target_pairs={{1,0},{2,1},{3,2},{0,3},{5,4},{6,5},{7,6},{4,7},{9,8},{10,9},{11,1... | collective-permute-start | bytes 53000 | tf_op jit(solution)/shard_map/ppermute | solution.py:64
  56.6 7.1 %collective-permute-start.4 = (f32[32,46,3]{1,0,2:T(8,128)}, f32[32,46,3]{1,0,2:T(8,128)S(1)}, u32[]{:S(2)}, u32[]{:S(2)}) collective-permute-start(f32[32,46,3]{1,0,2:T(8,128)} %copy.23), channel_id=1, source_target_pairs={{0,1},{1,2},{2,3},{3,0},{4,5},{5,6},{6,7},{7,4},{8,9},{9,10},{10,1... | collective-permute-start | bytes 53000 | tf_op jit(solution)/shard_map/ppermute | solution.py:63
  61.8 0.9 copy-start.6
  61.8 1.0 copy-start.7
  86.3 19.9 %copy-start.5 = (f32[1,32,7,128]{3,2,1,0:T(8,128)S(1)}, f32[1,32,7,128]{3,2,1,0:T(8,128)}, u32[]{:S(2)}) copy-start(f32[1,32,7,128]{3,2,1,0:T(8,128)} %copy.77) | copy-start | bytes 344068
  86.3 28.9 %collective-permute-start.7 = (f32[3,40,128]{2,1,0:T(8,128)S(1)}, f32[3,40,128]{2,1,0:T(8,128)S(1)}, u32[]{:S(2)}, u32[]{:S(2)}) collective-permute-start(f32[3,40,128]{2,1,0:T(8,128)S(1)} %get-tuple-element.28), channel_id=1, source_target_pairs={{16,0},{32,16},{48,32},{64,48},{80,64},{96,80},{112,96},{128,112},... | collective-permute-start | bytes 184328 | tf_op jit(solution)/shard_map/ppermute | solution.py:155
  95.5 19.7 %collective-permute-start.6 = (f32[3,40,128]{2,1,0:T(8,128)S(1)}, f32[3,40,128]{2,1,0:T(8,128)S(1)}, u32[]{:S(2)}, u32[]{:S(2)}) collective-permute-start(f32[3,40,128]{2,1,0:T(8,128)S(1)} %get-tuple-element.29), channel_id=1, source_target_pairs={{0,16},{16,32},{32,48},{48,64},{64,80},{80,96},{96,112},{112,128},... | collective-permute-start | bytes 184328 | tf_op jit(solution)/shard_map/ppermute | solution.py:154
  100.4 12.9 %collective-permute-start.9 = (f32[32,40,3]{1,0,2:T(8,128)}, f32[32,40,3]{1,0,2:T(8,128)}, u32[]{:S(2)}, u32[]{:S(2)}) collective-permute-start(f32[32,40,3]{1,0,2:T(8,128)} %copy.29), channel_id=1, source_target_pairs={{1,0},{2,1},{3,2},{0,3},{5,4},{6,5},{7,6},{4,7},{9,8},{10,9},{11,1... | collective-permute-start | bytes 46088 | tf_op jit(solution)/shard_map/ppermute | solution.py:64
  104.3 7.0 %collective-permute-start.8 = (f32[32,40,3]{1,0,2:T(8,128)}, f32[32,40,3]{1,0,2:T(8,128)}, u32[]{:S(2)}, u32[]{:S(2)}) collective-permute-start(f32[32,40,3]{1,0,2:T(8,128)} %copy.27), channel_id=1, source_target_pairs={{0,1},{1,2},{2,3},{3,0},{4,5},{5,6},{6,7},{7,4},{8,9},{9,10},{10,1... | collective-permute-start | bytes 46088 | tf_op jit(solution)/shard_map/ppermute | solution.py:63
  130.0 27.0 %collective-permute-start.11 = (f32[3,34,128]{2,1,0:T(8,128)S(1)}, f32[3,34,128]{2,1,0:T(8,128)S(1)}, u32[]{:S(2)}, u32[]{:S(2)}) collective-permute-start(f32[3,34,128]{2,1,0:T(8,128)S(1)} %get-tuple-element.43), channel_id=1, source_target_pairs={{16,0},{32,16},{48,32},{64,48},{80,64},{96,80},{112,96},{128,112},... | collective-permute-start | bytes 156680 | tf_op jit(solution)/shard_map/ppermute | solution.py:155
  138.6 18.5 %collective-permute-start.10 = (f32[3,34,128]{2,1,0:T(8,128)S(1)}, f32[3,34,128]{2,1,0:T(8,128)S(1)}, u32[]{:S(2)}, u32[]{:S(2)}) collective-permute-start(f32[3,34,128]{2,1,0:T(8,128)S(1)} %get-tuple-element.44), channel_id=1, source_target_pairs={{0,16},{16,32},{32,48},{48,64},{64,80},{80,96},{96,112},{112,128},... | collective-permute-start | bytes 156680 | tf_op jit(solution)/shard_map/ppermute | solution.py:154
  143.0 10.9 %collective-permute-start.12 = (f32[32,34,3]{1,0,2:T(8,128)S(1)}, f32[32,34,3]{1,0,2:T(8,128)S(1)}, u32[]{:S(2)}, u32[]{:S(2)}) collective-permute-start(f32[32,34,3]{1,0,2:T(8,128)S(1)} %copy.31), channel_id=1, source_target_pairs={{0,1},{1,2},{2,3},{3,0},{4,5},{5,6},{6,7},{7,4},{8,9},{9,10},{10,1... | collective-permute-start | bytes 39176 | tf_op jit(solution)/shard_map/ppermute | solution.py:63
  145.8 9.2 %collective-permute-start.13 = (f32[32,34,3]{1,0,2:T(8,128)}, f32[32,34,3]{1,0,2:T(8,128)}, u32[]{:S(2)}, u32[]{:S(2)}) collective-permute-start(f32[32,34,3]{1,0,2:T(8,128)} %copy.33), channel_id=1, source_target_pairs={{1,0},{2,1},{3,2},{0,3},{5,4},{6,5},{7,6},{4,7},{9,8},{10,9},{11,1... | collective-permute-start | bytes 39176 | tf_op jit(solution)/shard_map/ppermute | solution.py:64
  153.0 4.1 %copy-start = (f32[1,32,46,128]{3,2,1,0:T(8,128)S(1)}, f32[1,32,46,128]{3,2,1,0:T(8,128)}, u32[]{:S(2)}) copy-start(f32[1,32,46,128]{3,2,1,0:T(8,128)} %get-tuple-element.61) | copy-start | bytes 2260996
  157.1 26.6 %copy-start.10 = (s32[4]{0:T(128)S(1)}, s32[4]{0:T(128)}, u32[]{:S(2)}) copy-start(s32[4]{0:T(128)} %param.7) | copy-start | bytes 52
  172.0 13.7 %copy-start.1 = (f32[32,34,128]{2,1,0:T(8,128)}, f32[32,34,128]{2,1,0:T(8,128)S(1)}, u32[]{:S(2)}) copy-start(f32[32,34,128]{2,1,0:T(8,128)S(1)} %fusion.174) | copy-start | bytes 1671172
  172.0 13.4 %collective-permute-start.14 = (f32[1,34,128]{2,1,0:T(8,128)S(1)}, f32[1,34,128]{2,1,0:T(8,128)S(1)}, u32[]{:S(2)}, u32[]{:S(2)}) collective-permute-start(f32[1,34,128]{2,1,0:T(8,128)S(1)} %get-tuple-element.39), channel_id=1, source_target_pairs={{0,16},{16,32},{32,48},{48,64},{64,80},{80,96},{96,112},{112,128},... | collective-permute-start | bytes 52232 | tf_op jit(solution)/shard_map/ppermute | solution.py:154
  174.0 11.5 %collective-permute-start.15 = (f32[1,34,128]{2,1,0:T(8,128)S(1)}, f32[1,34,128]{2,1,0:T(8,128)S(1)}, u32[]{:S(2)}, u32[]{:S(2)}) collective-permute-start(f32[1,34,128]{2,1,0:T(8,128)S(1)} %get-tuple-element.40), channel_id=1, source_target_pairs={{16,0},{32,16},{48,32},{64,48},{80,64},{96,80},{112,96},{128,112},... | collective-permute-start | bytes 52232 | tf_op jit(solution)/shard_map/ppermute | solution.py:155
  192.0 8.9 %copy-start.2 = (f32[32,34,128]{2,1,0:T(8,128)S(1)}, f32[32,34,128]{2,1,0:T(8,128)}, u32[]{:S(2)}) copy-start(f32[32,34,128]{2,1,0:T(8,128)} %copy-done.1) | copy-start | bytes 1671172
  193.5 12.1 %all-to-all-start = ((f32[4,1,4096]{2,1,0:T(1,128)}), f32[4,1,4096]{2,1,0:T(1,128)S(1)}, u32[]{:S(2)}, u32[]{:S(2)}) async-start(f32[4,1,4096]{2,1,0:T(1,128)} %reshape.103), calls=%async_computation | async-start | bytes 131072 | tf_op jit(solution)/shard_map/all_to_all | solution.py:212

commit v8 on v5

--- a/solution.py
+++ b/solution.py
@@ -165,15 +165,29 @@
 def shards(level_set, velocity, active_brick, depth_order):
     alive = active_brick[0, 0, 0] > 0
     alive_float = alive.astype(jnp.float32)
-    flags = jnp.broadcast_to(alive_float, level_set.shape)
-    stacked = jnp.stack([level_set] + [velocity[d].astype(jnp.float32) for d in range(3)] + [flags])
+    stacked = jnp.stack([level_set] + [velocity[d].astype(jnp.float32) for d in range(3)])
     halo = 3 * SPAN + 1
-    stacked = exchange([stacked], "gy", [halo], 1)[0]
+    size, length = (lax.axis_size("gy"), stacked.shape[2])
+    up = [(i, (i + 1) % size) for i in range(size)]
+    down = [(j, i) for i, j in up]
+    last = stacked[:, :, length - halo :]
+    first = stacked[:, :, :halo]
+    last = last.at[1, :, 0].set(alive_float)
+    first = first.at[1, :, halo - 1].set(alive_float)
+    before = lax.ppermute(last, "gy", up)
+    after = lax.ppermute(first, "gy", down)
+    stacked = jnp.concatenate([before, stacked, after], axis=2)
     level_ext = stacked[0]
     speed_one = stacked[1:4, :, SPAN:-SPAN]
     speed_two = speed_one[:, :, SPAN:-SPAN]
     speed_three = speed_two[:, :, SPAN:-SPAN]
-    flag_ring = stacked[4, :, 3 * SPAN : -3 * SPAN]
+    ring_width = length + 2
+    place = lax.broadcasted_iota(jnp.int32, (1, ring_width, 1), 1)
+    flag_ring = jnp.where(
+        place == 0,
+        before[1, 0, 0, 0],
+        jnp.where(place == ring_width - 1, after[1, 0, halo - 1, 0], alive_float),
+    )
 
     inner, rate = stage_rate(level_ext, speed_one)
     section_one = inner + time_step * rate

time: 192 us -> 190 us (0.990)
  the two profiles are of different devices: /device:TPU:7 before, /device:TPU:32 now
where the time goes in v8:
time: 190 us; the launch traced here: 189 us
  starting transfers between devices  80.3 us (42%)
  other arithmetic  50 us (26%)
  local copies, waits for them, and re-layouts  26 us (14%)
  waiting for transfers between devices  23.5 us (12%)
  matrix products  5.91 us (3%)
  between operations  3.19 us (2%)
    ppermute x4, starting transfers between devices, x_faces(): after = lax.ppermute(x[:width], 'gx', down)  39.6 us
    add x1, other arithmetic, shards(): section_one = inner + time_step * rate  19 us
    select_n x1, other arithmetic, shards(): ringed = jnp.where(flag_ring > 0, advanced, level_ring)  13 us
    add x1, other arithmetic, shards(): 0.75 * level_ext[:, 2 * SPAN:-2 * SPAN] + 0.25 * (inner + time_step * rate)  12.8 us
    ppermute x1, waiting for transfers between devices, shards(): after = lax.ppermute(first, 'gy', down)  12.1 us
    ppermute x3, starting transfers between devices, z_faces(): after = lax.ppermute(x[:, :, :SPAN], 'gz', down)  11.9 us
    ppermute x3, starting transfers between devices, z_faces(): before = lax.ppermute(x[:, :, length - SPAN:], 'gz', up)  7.88 us
    ppermute x4, starting transfers between devices, x_faces(): before = lax.ppermute(x[length - width:], 'gx', up)  7.68 us
  transfers between devices with their start and end apart: 17, of which 6 were waited for; matrix products, arithmetic and copies ran while one was open for 9% of the time, Pallas kernels for 0%

profile of v8, /device:TPU:32, one launch (start us, length us, event | category | flops | bytes accessed | tf_op | source)
XLA Modules:
  0.0 188.9 jit_solution(14905239234974205090)
XLA Ops:
  1.3 1.3 slice_convert_fusion.2
  2.9 1.2 fusion.500
  4.0 1.6 scatter.9
  5.7 2.3 %copy.8 = f32[4,32,10,128]{3,1,2,0:T(8,128)} copy(f32[4,32,10,128]{3,2,1,0:T(8,128)} %scatter.9) | data formatting | bytes 1310720 | tf_op jit(solution)/shard_map/scatter | solution.py:176
  7.9 4.9 %collective-permute-start.1 = (f32[4,32,10,128]{3,1,2,0:T(8,128)}, f32[4,32,10,128]{3,1,2,0:T(8,128)}, u32[]{:S(2)}, u32[]{:S(2)}) collective-permute-start(f32[4,32,10,128]{3,1,2,0:T(8,128)} %copy.8), channel_id=1, source_target_pairs={{4,0},{8,4},{12,8},{0,12},{5,1},{9,5},{13,9},{1,13},{6,2},{10,6},{... | collective-permute-start | bytes 1966088 | tf_op jit(solution)/shard_map/ppermute | solution.py:178
  13.2 1.9 %collective-permute-start = (f32[4,32,10,128]{3,1,2,0:T(8,128)S(1)}, f32[4,32,10,128]{3,1,2,0:T(8,128)S(1)}, u32[]{:S(2)}, u32[]{:S(2)}) collective-permute-start(f32[4,32,10,128]{3,1,2,0:T(8,128)S(1)} %copy.7), channel_id=1, source_target_pairs={{0,4},{4,8},{8,12},{12,0},{1,5},{5,9},{9,13},{13,1},{2,6},{6,10},{... | collective-permute-start | bytes 1966088 | tf_op jit(solution)/shard_map/ppermute | solution.py:177
  15.1 12.1 %collective-permute-done.1 = f32[4,32,10,128]{3,1,2,0:T(8,128)} collective-permute-done((f32[4,32,10,128]{3,1,2,0:T(8,128)}, f32[4,32,10,128]{3,1,2,0:T(8,128)}, u32[]{:S(2)}, u32[]{:S(2)}) %collective-permute-start.1) | collective-permute-done | bytes 655392 | tf_op jit(solution)/shard_map/ppermute | solution.py:178
  27.2 1.5 copy.10
  28.6 3.8 %collective-permute-done = f32[4,32,10,128]{3,1,2,0:T(8,128)S(1)} collective-permute-done((f32[4,32,10,128]{3,1,2,0:T(8,128)S(1)}, f32[4,32,10,128]{3,1,2,0:T(8,128)S(1)}, u32[]{:S(2)}, u32[]{:S(2)}) %collective-permute-start) | collective-permute-done | bytes 655392 | tf_op jit(solution)/shard_map/ppermute | solution.py:177
  33.4 12.3 %collective-permute-start.3 = (f32[3,46,128]{2,1,0:T(8,128)S(1)}, f32[3,46,128]{2,1,0:T(8,128)S(1)}, u32[]{:S(2)}, u32[]{:S(2)}) collective-permute-start(f32[3,46,128]{2,1,0:T(8,128)S(1)} %get-tuple-element.44), channel_id=1, source_target_pairs={{16,0},{32,16},{48,32},{64,48},{80,64},{96,80},{112,96},{128,112},... | collective-permute-start | bytes 211976 | tf_op jit(solution)/shard_map/ppermute | solution.py:155
  45.8 1.9 %collective-permute-start.2 = (f32[3,46,128]{2,1,0:T(8,128)S(1)}, f32[3,46,128]{2,1,0:T(8,128)S(1)}, u32[]{:S(2)}, u32[]{:S(2)}) collective-permute-start(f32[3,46,128]{2,1,0:T(8,128)S(1)} %get-tuple-element.45), channel_id=1, source_target_pairs={{0,16},{16,32},{32,48},{48,64},{64,80},{80,96},{96,112},{112,128},... | collective-permute-start | bytes 211976 | tf_op jit(solution)/shard_map/ppermute | solution.py:154
  48.3 2.9 %collective-permute-start.4 = (f32[32,46,3]{1,0,2:T(8,128)S(1)}, f32[32,46,3]{1,0,2:T(8,128)S(1)}, u32[]{:S(2)}, u32[]{:S(2)}) collective-permute-start(f32[32,46,3]{1,0,2:T(8,128)S(1)} %copy.11), channel_id=1, source_target_pairs={{0,1},{1,2},{2,3},{3,0},{4,5},{5,6},{6,7},{7,4},{8,9},{9,10},{10,1... | collective-permute-start | bytes 53000 | tf_op jit(solution)/shard_map/ppermute | solution.py:63
  51.6 2.9 %collective-permute-start.5 = (f32[32,46,3]{1,0,2:T(8,128)S(1)}, f32[32,46,3]{1,0,2:T(8,128)S(1)}, u32[]{:S(2)}, u32[]{:S(2)}) collective-permute-start(f32[32,46,3]{1,0,2:T(8,128)S(1)} %copy.13), channel_id=1, source_target_pairs={{1,0},{2,1},{3,2},{0,3},{5,4},{6,5},{7,6},{4,7},{9,8},{10,9},{11,1... | collective-permute-start | bytes 53000 | tf_op jit(solution)/shard_map/ppermute | solution.py:64
  54.5 0.9 slice.607
  55.5 1.3 copy.12
  56.8 0.8 collective-permute-done.5
  57.6 1.3 copy.14
  58.9 19.0 %fusion.21 = f32[32,46,128]{2,1,0:T(8,128)S(1)} fusion(f32[32,46,128]{2,1,0:T(8,128)} %slice.607, f32[32,46,3]{2,1,0:T(8,128)} %copy.14, f32[32,46,3]{2,1,0:T(8,128)} %copy.12, f32[4,32,52,128]{3,2,1,0:T(8,128)} %copy-done, f32[32,52,128]{2,1,0:T(8,128)S(1)} %slice_bitcast_fusion, f32[3,46,128]{2,1,0:T(8,128)S(1)} %collective-permute-done.2, ...), kind=kLoop, calls=%fused_computation.75 | loop fusion | flops 79511552 | bytes 8466944 | tf_op jit(solution)/shard_map/add | solution.py:193
  77.9 8.3 %collective-permute-start.7 = (f32[3,40,128]{2,1,0:T(8,128)S(1)}, f32[3,40,128]{2,1,0:T(8,128)S(1)}, u32[]{:S(2)}, u32[]{:S(2)}) collective-permute-start(f32[3,40,128]{2,1,0:T(8,128)S(1)} %get-tuple-element.48), channel_id=1, source_target_pairs={{16,0},{32,16},{48,32},{64,48},{80,64},{96,80},{112,96},{128,112},... | collective-permute-start | bytes 184328 | tf_op jit(solution)/shard_map/ppermute | solution.py:155
  86.2 1.9 %collective-permute-start.6 = (f32[3,40,128]{2,1,0:T(8,128)S(1)}, f32[3,40,128]{2,1,0:T(8,128)S(1)}, u32[]{:S(2)}, u32[]{:S(2)}) collective-permute-start(f32[3,40,128]{2,1,0:T(8,128)S(1)} %get-tuple-element.49), channel_id=1, source_target_pairs={{0,16},{16,32},{32,48},{48,64},{64,80},{80,96},{96,112},{112,128},... | collective-permute-start | bytes 184328 | tf_op jit(solution)/shard_map/ppermute | solution.py:154
  88.6 3.0 %collective-permute-start.8 = (f32[32,40,3]{1,0,2:T(8,128)S(1)}, f32[32,40,3]{1,0,2:T(8,128)S(1)}, u32[]{:S(2)}, u32[]{:S(2)}) collective-permute-start(f32[32,40,3]{1,0,2:T(8,128)S(1)} %copy.15), channel_id=1, source_target_pairs={{0,1},{1,2},{2,3},{3,0},{4,5},{5,6},{6,7},{7,4},{8,9},{9,10},{10,1... | collective-permute-start | bytes 46088 | tf_op jit(solution)/shard_map/ppermute | solution.py:63
  92.0 3.6 %collective-permute-start.9 = (f32[32,40,3]{1,0,2:T(8,128)S(1)}, f32[32,40,3]{1,0,2:T(8,128)S(1)}, u32[]{:S(2)}, u32[]{:S(2)}) collective-permute-start(f32[32,40,3]{1,0,2:T(8,128)S(1)} %copy.17), channel_id=1, source_target_pairs={{1,0},{2,1},{3,2},{0,3},{5,4},{6,5},{7,6},{4,7},{9,8},{10,9},{11,1... | collective-permute-start | bytes 46088 | tf_op jit(solution)/shard_map/ppermute | solution.py:64
  95.6 1.2 slice.603
  96.8 1.2 slice.601
  98.1 1.1 copy.16
  99.5 1.1 copy.18
  100.6 12.8 %fusion.174 = f32[32,40,128]{2,1,0:T(8,128)S(1)} fusion(f32[32,52,128]{2,1,0:T(8,128)S(1)} %slice_bitcast_fusion, f32[32,40,128]{2,1,0:T(8,128)S(1)} %slice.637, f32[32,40,3]{2,1,0:T(8,128)} %copy.18, f32[32,40,3]{2,1,0:T(8,128)} %copy.16, f32[4,32,52,128]{3,2,1,0:T(8,128)} %copy-done, f32[32,46,128]{2,1,0:T(8,128)S(1)} %fusion.21, ...), kind=kLoop, calls=%fused_computation.277 | loop fusion | flops 69632000 | bytes 8017920 | tf_op jit(solution)/shard_map/add | solution.py:195
  114.3 9.1 %collective-permute-start.11 = (f32[3,34,128]{2,1,0:T(8,128)}, f32[3,34,128]{2,1,0:T(8,128)}, u32[]{:S(2)}, u32[]{:S(2)}) collective-permute-start(f32[3,34,128]{2,1,0:T(8,128)} %get-tuple-element.63), channel_id=1, source_target_pairs={{16,0},{32,16},{48,32},{64,48},{80,64},{96,80},{112,96},{128,112},... | collective-permute-start | bytes 156680 | tf_op jit(solution)/shard_map/ppermute | solution.py:155
  123.5 1.9 %collective-permute-start.10 = (f32[3,34,128]{2,1,0:T(8,128)}, f32[3,34,128]{2,1,0:T(8,128)}, u32[]{:S(2)}, u32[]{:S(2)}) collective-permute-start(f32[3,34,128]{2,1,0:T(8,128)} %get-tuple-element.64), channel_id=1, source_target_pairs={{0,16},{16,32},{32,48},{48,64},{64,80},{80,96},{96,112},{112,128},... | collective-permute-start | bytes 156680 | tf_op jit(solution)/shard_map/ppermute | solution.py:154
  125.7 0.9 copy.21
  126.7 5.4 %collective-permute-start.13 = (f32[32,34,3]{1,0,2:T(8,128)}, f32[32,34,3]{1,0,2:T(8,128)S(1)}, u32[]{:S(2)}, u32[]{:S(2)}) collective-permute-start(f32[32,34,3]{1,0,2:T(8,128)} %copy.21), channel_id=1, source_target_pairs={{1,0},{2,1},{3,2},{0,3},{5,4},{6,5},{7,6},{4,7},{9,8},{10,9},{11,1... | collective-permute-start | bytes 39176 | tf_op jit(solution)/shard_map/ppermute | solution.py:64
  132.1 1.9 %collective-permute-start.12 = (f32[32,34,3]{1,0,2:T(8,128)S(1)}, f32[32,34,3]{1,0,2:T(8,128)S(1)}, u32[]{:S(2)}, u32[]{:S(2)}) collective-permute-start(f32[32,34,3]{1,0,2:T(8,128)S(1)} %copy.19), channel_id=1, source_target_pairs={{0,1},{1,2},{2,3},{3,0},{4,5},{5,6},{6,7},{7,4},{8,9},{9,10},{10,1... | collective-permute-start | bytes 39176 | tf_op jit(solution)/shard_map/ppermute | solution.py:63
  134.0 1.2 fusion.482
  135.3 2.7 %collective-permute-done.12 = f32[32,34,3]{1,0,2:T(8,128)S(1)} collective-permute-done((f32[32,34,3]{1,0,2:T(8,128)S(1)}, f32[32,34,3]{1,0,2:T(8,128)S(1)}, u32[]{:S(2)}, u32[]{:S(2)}) %collective-permute-start.12) | collective-permute-done | bytes 13088 | tf_op jit(solution)/shard_map/ppermute | solution.py:63
  138.4 1.2 copy.22
  139.6 13.0 %fusion.181 = f32[32,34,128]{2,1,0:T(8,128)S(1)} fusion(f32[32,34,128]{2,1,0:T(8,128)S(1)} %slice.667, f32[32,34,3]{2,1,0:T(8,128)} %copy.22, f32[32,34,3]{2,1,0:T(8,128)S(1)} %copy.20, f32[4,32,52,128]{3,2,1,0:T(8,128)} %copy-done, f32[32,40,128]{2,1,0:T(8,128)S(1)} %fusion.174, f32[3,34,128]{2,1,0:T(8,128)} %collective-permute-done.10, ...), kind=kLoop, calls=%fused_computation.285 | loop fusion | flops 59326464 | bytes 6815266 | tf_op jit(solution)/shard_map/jit(_where)/select_n | solution.py:199
  152.7 1.9 %collective-permute-start.14 = (f32[1,34,128]{2,1,0:T(8,128)S(1)}, f32[1,34,128]{2,1,0:T(8,128)S(1)}, u32[]{:S(2)}, u32[]{:S(2)}) collective-permute-start(f32[1,34,128]{2,1,0:T(8,128)S(1)} %get-tuple-element.59), channel_id=1, source_target_pairs={{0,16},{16,32},{32,48},{48,64},{64,80},{80,96},{96,112},{112,128},... | collective-permute-start | bytes 52232 | tf_op jit(solution)/shard_map/ppermute | solution.py:154
  154.6 9.8 %collective-permute-start.15 = (f32[1,34,128]{2,1,0:T(8,128)S(1)}, f32[1,34,128]{2,1,0:T(8,128)S(1)}, u32[]{:S(2)}, u32[]{:S(2)}) collective-permute-start(f32[1,34,128]{2,1,0:T(8,128)S(1)} %get-tuple-element.60), channel_id=1, source_target_pairs={{16,0},{32,16},{48,32},{64,48},{80,64},{96,80},{112,96},{128,112},... | collective-permute-start | bytes 52232 | tf_op jit(solution)/shard_map/ppermute | solution.py:155
  166.9 1.2 multiply_reduce_fusion.3
  168.1 1.2 multiply_reduce_fusion.1
  169.2 1.2 multiply_reduce_fusion.5
  170.4 1.2 multiply_reduce_fusion.7
  171.7 1.3 copy.23
  173.7 0.8 reshape.192
  174.5 6.4 %all-to-all-start = ((f32[4,1,4096]{2,1,0:T(1,128)}), f32[4,1,4096]{2,1,0:T(1,128)S(1)}, u32[]{:S(2)}, u32[]{:S(2)}) async-start(f32[4,1,4096]{2,1,0:T(1,128)} %reshape.192), calls=%async_computation | async-start | bytes 131072 | tf_op jit(solution)/shard_map/all_to_all | solution.py:218
  180.8 0.9 slice.697
  181.7 3.8 %all-to-all-done = f32[4,1,4096]{2,1,0:T(1,128)S(1)} async-done(((f32[4,1,4096]{2,1,0:T(1,128)}), f32[4,1,4096]{2,1,0:T(1,128)S(1)}, u32[]{:S(2)}, u32[]{:S(2)}) %all-to-all-start) | async-done | bytes 65568 | tf_op jit(solution)/shard_map/all_to_all | solution.py:218
  186.0 0.8 reduce.4
  (66 shorter events, 9.5 us)
Async XLA Ops:
  0.6 2.0 %copy-start.1 = (f32[32,32,128]{2,1,0:T(8,128)S(1)}, f32[32,32,128]{2,1,0:T(8,128)}, u32[]{:S(2)}) copy-start(f32[32,32,128]{2,1,0:T(8,128)} %param.8) | copy-start | bytes 1572868
  7.9 19.2 %collective-permute-start.1 = (f32[4,32,10,128]{3,1,2,0:T(8,128)}, f32[4,32,10,128]{3,1,2,0:T(8,128)}, u32[]{:S(2)}, u32[]{:S(2)}) collective-permute-start(f32[4,32,10,128]{3,1,2,0:T(8,128)} %copy.8), channel_id=1, source_target_pairs={{4,0},{8,4},{12,8},{0,12},{5,1},{9,5},{13,9},{1,13},{6,2},{10,6},{... | collective-permute-start | bytes 1966088 | tf_op jit(solution)/shard_map/ppermute | solution.py:178
  13.2 19.3 %collective-permute-start = (f32[4,32,10,128]{3,1,2,0:T(8,128)S(1)}, f32[4,32,10,128]{3,1,2,0:T(8,128)S(1)}, u32[]{:S(2)}, u32[]{:S(2)}) collective-permute-start(f32[4,32,10,128]{3,1,2,0:T(8,128)S(1)} %copy.7), channel_id=1, source_target_pairs={{0,4},{4,8},{8,12},{12,0},{1,5},{5,9},{9,13},{13,1},{2,6},{6,10},{... | collective-permute-start | bytes 1966088 | tf_op jit(solution)/shard_map/ppermute | solution.py:177
  32.5 0.9 copy-start.2
  33.3 14.7 %copy-start = (f32[4,32,52,128]{3,2,1,0:T(8,128)}, f32[4,32,52,128]{3,2,1,0:T(8,128)S(1)}, u32[]{:S(2)}) copy-start(f32[4,32,52,128]{3,2,1,0:T(8,128)S(1)} %pad_maximum_fusion) | copy-start | bytes 10223620
  33.4 25.4 %collective-permute-start.3 = (f32[3,46,128]{2,1,0:T(8,128)S(1)}, f32[3,46,128]{2,1,0:T(8,128)S(1)}, u32[]{:S(2)}, u32[]{:S(2)}) collective-permute-start(f32[3,46,128]{2,1,0:T(8,128)S(1)} %get-tuple-element.44), channel_id=1, source_target_pairs={{16,0},{32,16},{48,32},{64,48},{80,64},{96,80},{112,96},{128,112},... | collective-permute-start | bytes 211976 | tf_op jit(solution)/shard_map/ppermute | solution.py:155
  45.8 13.1 %collective-permute-start.2 = (f32[3,46,128]{2,1,0:T(8,128)S(1)}, f32[3,46,128]{2,1,0:T(8,128)S(1)}, u32[]{:S(2)}, u32[]{:S(2)}) collective-permute-start(f32[3,46,128]{2,1,0:T(8,128)S(1)} %get-tuple-element.45), channel_id=1, source_target_pairs={{0,16},{16,32},{32,48},{48,64},{64,80},{80,96},{96,112},{112,128},... | collective-permute-start | bytes 211976 | tf_op jit(solution)/shard_map/ppermute | solution.py:154
  48.3 7.1 %collective-permute-start.4 = (f32[32,46,3]{1,0,2:T(8,128)S(1)}, f32[32,46,3]{1,0,2:T(8,128)S(1)}, u32[]{:S(2)}, u32[]{:S(2)}) collective-permute-start(f32[32,46,3]{1,0,2:T(8,128)S(1)} %copy.11), channel_id=1, source_target_pairs={{0,1},{1,2},{2,3},{3,0},{4,5},{5,6},{6,7},{7,4},{8,9},{9,10},{10,1... | collective-permute-start | bytes 53000 | tf_op jit(solution)/shard_map/ppermute | solution.py:63
  51.6 6.0 %collective-permute-start.5 = (f32[32,46,3]{1,0,2:T(8,128)S(1)}, f32[32,46,3]{1,0,2:T(8,128)S(1)}, u32[]{:S(2)}, u32[]{:S(2)}) collective-permute-start(f32[32,46,3]{1,0,2:T(8,128)S(1)} %copy.13), channel_id=1, source_target_pairs={{1,0},{2,1},{3,2},{0,3},{5,4},{6,5},{7,6},{4,7},{9,8},{10,9},{11,1... | collective-permute-start | bytes 53000 | tf_op jit(solution)/shard_map/ppermute | solution.py:64
  77.9 22.7 %collective-permute-start.7 = (f32[3,40,128]{2,1,0:T(8,128)S(1)}, f32[3,40,128]{2,1,0:T(8,128)S(1)}, u32[]{:S(2)}, u32[]{:S(2)}) collective-permute-start(f32[3,40,128]{2,1,0:T(8,128)S(1)} %get-tuple-element.48), channel_id=1, source_target_pairs={{16,0},{32,16},{48,32},{64,48},{80,64},{96,80},{112,96},{128,112},... | collective-permute-start | bytes 184328 | tf_op jit(solution)/shard_map/ppermute | solution.py:155
  86.2 14.4 %collective-permute-start.6 = (f32[3,40,128]{2,1,0:T(8,128)S(1)}, f32[3,40,128]{2,1,0:T(8,128)S(1)}, u32[]{:S(2)}, u32[]{:S(2)}) collective-permute-start(f32[3,40,128]{2,1,0:T(8,128)S(1)} %get-tuple-element.49), channel_id=1, source_target_pairs={{0,16},{16,32},{32,48},{48,64},{64,80},{80,96},{96,112},{112,128},... | collective-permute-start | bytes 184328 | tf_op jit(solution)/shard_map/ppermute | solution.py:154
  88.6 9.4 %collective-permute-start.8 = (f32[32,40,3]{1,0,2:T(8,128)S(1)}, f32[32,40,3]{1,0,2:T(8,128)S(1)}, u32[]{:S(2)}, u32[]{:S(2)}) collective-permute-start(f32[32,40,3]{1,0,2:T(8,128)S(1)} %copy.15), channel_id=1, source_target_pairs={{0,1},{1,2},{2,3},{3,0},{4,5},{5,6},{6,7},{7,4},{8,9},{9,10},{10,1... | collective-permute-start | bytes 46088 | tf_op jit(solution)/shard_map/ppermute | solution.py:63
  92.0 7.5 %collective-permute-start.9 = (f32[32,40,3]{1,0,2:T(8,128)S(1)}, f32[32,40,3]{1,0,2:T(8,128)S(1)}, u32[]{:S(2)}, u32[]{:S(2)}) collective-permute-start(f32[32,40,3]{1,0,2:T(8,128)S(1)} %copy.17), channel_id=1, source_target_pairs={{1,0},{2,1},{3,2},{0,3},{5,4},{6,5},{7,6},{4,7},{9,8},{10,9},{11,1... | collective-permute-start | bytes 46088 | tf_op jit(solution)/shard_map/ppermute | solution.py:64
  114.3 25.3 %collective-permute-start.11 = (f32[3,34,128]{2,1,0:T(8,128)}, f32[3,34,128]{2,1,0:T(8,128)}, u32[]{:S(2)}, u32[]{:S(2)}) collective-permute-start(f32[3,34,128]{2,1,0:T(8,128)} %get-tuple-element.63), channel_id=1, source_target_pairs={{16,0},{32,16},{48,32},{64,48},{80,64},{96,80},{112,96},{128,112},... | collective-permute-start | bytes 156680 | tf_op jit(solution)/shard_map/ppermute | solution.py:155
  123.5 16.2 %collective-permute-start.10 = (f32[3,34,128]{2,1,0:T(8,128)}, f32[3,34,128]{2,1,0:T(8,128)}, u32[]{:S(2)}, u32[]{:S(2)}) collective-permute-start(f32[3,34,128]{2,1,0:T(8,128)} %get-tuple-element.64), channel_id=1, source_target_pairs={{0,16},{16,32},{32,48},{48,64},{64,80},{80,96},{96,112},{112,128},... | collective-permute-start | bytes 156680 | tf_op jit(solution)/shard_map/ppermute | solution.py:154
  126.7 11.8 %collective-permute-start.13 = (f32[32,34,3]{1,0,2:T(8,128)}, f32[32,34,3]{1,0,2:T(8,128)S(1)}, u32[]{:S(2)}, u32[]{:S(2)}) collective-permute-start(f32[32,34,3]{1,0,2:T(8,128)} %copy.21), channel_id=1, source_target_pairs={{1,0},{2,1},{3,2},{0,3},{5,4},{6,5},{7,6},{4,7},{9,8},{10,9},{11,1... | collective-permute-start | bytes 39176 | tf_op jit(solution)/shard_map/ppermute | solution.py:64
  132.1 6.0 %collective-permute-start.12 = (f32[32,34,3]{1,0,2:T(8,128)S(1)}, f32[32,34,3]{1,0,2:T(8,128)S(1)}, u32[]{:S(2)}, u32[]{:S(2)}) collective-permute-start(f32[32,34,3]{1,0,2:T(8,128)S(1)} %copy.19), channel_id=1, source_target_pairs={{0,1},{1,2},{2,3},{3,0},{4,5},{5,6},{6,7},{7,4},{8,9},{9,10},{10,1... | collective-permute-start | bytes 39176 | tf_op jit(solution)/shard_map/ppermute | solution.py:63
  139.6 24.8 %copy-start.3 = (s32[4]{0:T(128)S(1)}, s32[4]{0:T(128)}, u32[]{:S(2)}) copy-start(s32[4]{0:T(128)} %param.11) | copy-start | bytes 52
  152.7 13.7 %collective-permute-start.14 = (f32[1,34,128]{2,1,0:T(8,128)S(1)}, f32[1,34,128]{2,1,0:T(8,128)S(1)}, u32[]{:S(2)}, u32[]{:S(2)}) collective-permute-start(f32[1,34,128]{2,1,0:T(8,128)S(1)} %get-tuple-element.59), channel_id=1, source_target_pairs={{0,16},{16,32},{32,48},{48,64},{64,80},{80,96},{96,112},{112,128},... | collective-permute-start | bytes 52232 | tf_op jit(solution)/shard_map/ppermute | solution.py:154
  154.6 11.8 %collective-permute-start.15 = (f32[1,34,128]{2,1,0:T(8,128)S(1)}, f32[1,34,128]{2,1,0:T(8,128)S(1)}, u32[]{:S(2)}, u32[]{:S(2)}) collective-permute-start(f32[1,34,128]{2,1,0:T(8,128)S(1)} %get-tuple-element.60), channel_id=1, source_target_pairs={{16,0},{32,16},{48,32},{64,48},{80,64},{96,80},{112,96},{128,112},... | collective-permute-start | bytes 52232 | tf_op jit(solution)/shard_map/ppermute | solution.py:155
  174.5 11.0 %all-to-all-start = ((f32[4,1,4096]{2,1,0:T(1,128)}), f32[4,1,4096]{2,1,0:T(1,128)S(1)}, u32[]{:S(2)}, u32[]{:S(2)}) async-start(f32[4,1,4096]{2,1,0:T(1,128)} %reshape.192), calls=%async_computation | async-start | bytes 131072 | tf_op jit(solution)/shard_map/all_to_all | solution.py:218

commit v9 on v8

--- a/solution.py
+++ b/solution.py
@@ -124,7 +124,7 @@
         ascending, depth[:, None] < depth[None, :], depth[:, None] > depth[None, :]
     ).astype(jnp.float32)
     flat_logs = log_clear.reshape(-1, CZ)
-    before = jnp.dot(flat_logs, ahead, precision=lax.Precision.HIGHEST).reshape(log_clear.shape)
+    before = jnp.dot(flat_logs, ahead, precision=lax.Precision.HIGH).reshape(log_clear.shape)
     weight = jnp.exp(before) * opacity
     bright = jnp.tanh(samples)
     red = jnp.sum(weight * (0.5 + 0.5 * bright), -1)

time: 190 us -> 189 us (level)
  no operation moved by 1% of the time
where the time goes in v9:
time: 189 us; the launch traced here: 188 us
  starting transfers between devices  80.3 us (42%)
  other arithmetic  50 us (26%)
  local copies, waits for them, and re-layouts  26 us (14%)
  waiting for transfers between devices  23.5 us (12%)
  matrix products  5.37 us (3%)
  between operations  3.2 us (2%)
    ppermute x4, starting transfers between devices, x_faces(): after = lax.ppermute(x[:width], 'gx', down)  39.6 us
    add x1, other arithmetic, shards(): section_one = inner + time_step * rate  19 us
    select_n x1, other arithmetic, shards(): ringed = jnp.where(flag_ring > 0, advanced, level_ring)  13 us
    add x1, other arithmetic, shards(): 0.75 * level_ext[:, 2 * SPAN:-2 * SPAN] + 0.25 * (inner + time_step * rate)  12.8 us
    ppermute x1, waiting for transfers between devices, shards(): after = lax.ppermute(first, 'gy', down)  12.1 us
    ppermute x3, starting transfers between devices, z_faces(): after = lax.ppermute(x[:, :, :SPAN], 'gz', down)  11.9 us
    ppermute x3, starting transfers between devices, z_faces(): before = lax.ppermute(x[:, :, length - SPAN:], 'gz', up)  7.88 us
    ppermute x4, starting transfers between devices, x_faces(): before = lax.ppermute(x[length - width:], 'gx', up)  7.68 us
  transfers between devices with their start and end apart: 17, of which 6 were waited for; matrix products, arithmetic and copies ran while one was open for 9% of the time, Pallas kernels for 0%

profile of v9, /device:TPU:32, one launch (start us, length us, event | category | flops | bytes accessed | tf_op | source)
XLA Modules:
  0.0 188.4 jit_solution(14519172271682969825)
XLA Ops:
  1.3 1.3 slice_convert_fusion.2
  2.9 1.2 fusion.500
  4.0 1.6 scatter.9
  5.7 2.3 %copy.8 = f32[4,32,10,128]{3,1,2,0:T(8,128)} copy(f32[4,32,10,128]{3,2,1,0:T(8,128)} %scatter.9) | data formatting | bytes 1310720 | tf_op jit(solution)/shard_map/scatter | solution.py:176
  7.9 4.9 %collective-permute-start.1 = (f32[4,32,10,128]{3,1,2,0:T(8,128)}, f32[4,32,10,128]{3,1,2,0:T(8,128)}, u32[]{:S(2)}, u32[]{:S(2)}) collective-permute-start(f32[4,32,10,128]{3,1,2,0:T(8,128)} %copy.8), channel_id=1, source_target_pairs={{4,0},{8,4},{12,8},{0,12},{5,1},{9,5},{13,9},{1,13},{6,2},{10,6},{... | collective-permute-start | bytes 1966088 | tf_op jit(solution)/shard_map/ppermute | solution.py:178
  13.2 1.9 %collective-permute-start = (f32[4,32,10,128]{3,1,2,0:T(8,128)S(1)}, f32[4,32,10,128]{3,1,2,0:T(8,128)S(1)}, u32[]{:S(2)}, u32[]{:S(2)}) collective-permute-start(f32[4,32,10,128]{3,1,2,0:T(8,128)S(1)} %copy.7), channel_id=1, source_target_pairs={{0,4},{4,8},{8,12},{12,0},{1,5},{5,9},{9,13},{13,1},{2,6},{6,10},{... | collective-permute-start | bytes 1966088 | tf_op jit(solution)/shard_map/ppermute | solution.py:177
  15.1 12.1 %collective-permute-done.1 = f32[4,32,10,128]{3,1,2,0:T(8,128)} collective-permute-done((f32[4,32,10,128]{3,1,2,0:T(8,128)}, f32[4,32,10,128]{3,1,2,0:T(8,128)}, u32[]{:S(2)}, u32[]{:S(2)}) %collective-permute-start.1) | collective-permute-done | bytes 655392 | tf_op jit(solution)/shard_map/ppermute | solution.py:178
  27.2 1.5 copy.10
  28.6 3.8 %collective-permute-done = f32[4,32,10,128]{3,1,2,0:T(8,128)S(1)} collective-permute-done((f32[4,32,10,128]{3,1,2,0:T(8,128)S(1)}, f32[4,32,10,128]{3,1,2,0:T(8,128)S(1)}, u32[]{:S(2)}, u32[]{:S(2)}) %collective-permute-start) | collective-permute-done | bytes 655392 | tf_op jit(solution)/shard_map/ppermute | solution.py:177
  33.4 12.3 %collective-permute-start.3 = (f32[3,46,128]{2,1,0:T(8,128)S(1)}, f32[3,46,128]{2,1,0:T(8,128)S(1)}, u32[]{:S(2)}, u32[]{:S(2)}) collective-permute-start(f32[3,46,128]{2,1,0:T(8,128)S(1)} %get-tuple-element.44), channel_id=1, source_target_pairs={{16,0},{32,16},{48,32},{64,48},{80,64},{96,80},{112,96},{128,112},... | collective-permute-start | bytes 211976 | tf_op jit(solution)/shard_map/ppermute | solution.py:155
  45.8 1.9 %collective-permute-start.2 = (f32[3,46,128]{2,1,0:T(8,128)S(1)}, f32[3,46,128]{2,1,0:T(8,128)S(1)}, u32[]{:S(2)}, u32[]{:S(2)}) collective-permute-start(f32[3,46,128]{2,1,0:T(8,128)S(1)} %get-tuple-element.45), channel_id=1, source_target_pairs={{0,16},{16,32},{32,48},{48,64},{64,80},{80,96},{96,112},{112,128},... | collective-permute-start | bytes 211976 | tf_op jit(solution)/shard_map/ppermute | solution.py:154
  48.3 2.9 %collective-permute-start.4 = (f32[32,46,3]{1,0,2:T(8,128)S(1)}, f32[32,46,3]{1,0,2:T(8,128)S(1)}, u32[]{:S(2)}, u32[]{:S(2)}) collective-permute-start(f32[32,46,3]{1,0,2:T(8,128)S(1)} %copy.11), channel_id=1, source_target_pairs={{0,1},{1,2},{2,3},{3,0},{4,5},{5,6},{6,7},{7,4},{8,9},{9,10},{10,1... | collective-permute-start | bytes 53000 | tf_op jit(solution)/shard_map/ppermute | solution.py:63
  51.6 2.9 %collective-permute-start.5 = (f32[32,46,3]{1,0,2:T(8,128)S(1)}, f32[32,46,3]{1,0,2:T(8,128)S(1)}, u32[]{:S(2)}, u32[]{:S(2)}) collective-permute-start(f32[32,46,3]{1,0,2:T(8,128)S(1)} %copy.13), channel_id=1, source_target_pairs={{1,0},{2,1},{3,2},{0,3},{5,4},{6,5},{7,6},{4,7},{9,8},{10,9},{11,1... | collective-permute-start | bytes 53000 | tf_op jit(solution)/shard_map/ppermute | solution.py:64
  54.5 0.9 slice.607
  55.5 1.3 copy.12
  56.8 0.8 collective-permute-done.5
  57.6 1.3 copy.14
  58.9 19.0 %fusion.21 = f32[32,46,128]{2,1,0:T(8,128)S(1)} fusion(f32[32,46,128]{2,1,0:T(8,128)} %slice.607, f32[32,46,3]{2,1,0:T(8,128)} %copy.14, f32[32,46,3]{2,1,0:T(8,128)} %copy.12, f32[4,32,52,128]{3,2,1,0:T(8,128)} %copy-done, f32[32,52,128]{2,1,0:T(8,128)S(1)} %slice_bitcast_fusion, f32[3,46,128]{2,1,0:T(8,128)S(1)} %collective-permute-done.2, ...), kind=kLoop, calls=%fused_computation.75 | loop fusion | flops 79511552 | bytes 8466944 | tf_op jit(solution)/shard_map/add | solution.py:193
  77.9 8.3 %collective-permute-start.7 = (f32[3,40,128]{2,1,0:T(8,128)S(1)}, f32[3,40,128]{2,1,0:T(8,128)S(1)}, u32[]{:S(2)}, u32[]{:S(2)}) collective-permute-start(f32[3,40,128]{2,1,0:T(8,128)S(1)} %get-tuple-element.48), channel_id=1, source_target_pairs={{16,0},{32,16},{48,32},{64,48},{80,64},{96,80},{112,96},{128,112},... | collective-permute-start | bytes 184328 | tf_op jit(solution)/shard_map/ppermute | solution.py:155
  86.2 1.9 %collective-permute-start.6 = (f32[3,40,128]{2,1,0:T(8,128)S(1)}, f32[3,40,128]{2,1,0:T(8,128)S(1)}, u32[]{:S(2)}, u32[]{:S(2)}) collective-permute-start(f32[3,40,128]{2,1,0:T(8,128)S(1)} %get-tuple-element.49), channel_id=1, source_target_pairs={{0,16},{16,32},{32,48},{48,64},{64,80},{80,96},{96,112},{112,128},... | collective-permute-start | bytes 184328 | tf_op jit(solution)/shard_map/ppermute | solution.py:154
  88.6 3.0 %collective-permute-start.8 = (f32[32,40,3]{1,0,2:T(8,128)S(1)}, f32[32,40,3]{1,0,2:T(8,128)S(1)}, u32[]{:S(2)}, u32[]{:S(2)}) collective-permute-start(f32[32,40,3]{1,0,2:T(8,128)S(1)} %copy.15), channel_id=1, source_target_pairs={{0,1},{1,2},{2,3},{3,0},{4,5},{5,6},{6,7},{7,4},{8,9},{9,10},{10,1... | collective-permute-start | bytes 46088 | tf_op jit(solution)/shard_map/ppermute | solution.py:63
  92.0 3.6 %collective-permute-start.9 = (f32[32,40,3]{1,0,2:T(8,128)S(1)}, f32[32,40,3]{1,0,2:T(8,128)S(1)}, u32[]{:S(2)}, u32[]{:S(2)}) collective-permute-start(f32[32,40,3]{1,0,2:T(8,128)S(1)} %copy.17), channel_id=1, source_target_pairs={{1,0},{2,1},{3,2},{0,3},{5,4},{6,5},{7,6},{4,7},{9,8},{10,9},{11,1... | collective-permute-start | bytes 46088 | tf_op jit(solution)/shard_map/ppermute | solution.py:64
  95.6 1.2 slice.603
  96.8 1.2 slice.601
  98.1 1.1 copy.16
  99.5 1.1 copy.18
  100.6 12.8 %fusion.174 = f32[32,40,128]{2,1,0:T(8,128)S(1)} fusion(f32[32,52,128]{2,1,0:T(8,128)S(1)} %slice_bitcast_fusion, f32[32,40,128]{2,1,0:T(8,128)S(1)} %slice.637, f32[32,40,3]{2,1,0:T(8,128)} %copy.18, f32[32,40,3]{2,1,0:T(8,128)} %copy.16, f32[4,32,52,128]{3,2,1,0:T(8,128)} %copy-done, f32[32,46,128]{2,1,0:T(8,128)S(1)} %fusion.21, ...), kind=kLoop, calls=%fused_computation.277 | loop fusion | flops 69632000 | bytes 8017920 | tf_op jit(solution)/shard_map/add | solution.py:195
  114.3 9.1 %collective-permute-start.11 = (f32[3,34,128]{2,1,0:T(8,128)}, f32[3,34,128]{2,1,0:T(8,128)}, u32[]{:S(2)}, u32[]{:S(2)}) collective-permute-start(f32[3,34,128]{2,1,0:T(8,128)} %get-tuple-element.63), channel_id=1, source_target_pairs={{16,0},{32,16},{48,32},{64,48},{80,64},{96,80},{112,96},{128,112},... | collective-permute-start | bytes 156680 | tf_op jit(solution)/shard_map/ppermute | solution.py:155
  123.5 1.9 %collective-permute-start.10 = (f32[3,34,128]{2,1,0:T(8,128)}, f32[3,34,128]{2,1,0:T(8,128)}, u32[]{:S(2)}, u32[]{:S(2)}) collective-permute-start(f32[3,34,128]{2,1,0:T(8,128)} %get-tuple-element.64), channel_id=1, source_target_pairs={{0,16},{16,32},{32,48},{48,64},{64,80},{80,96},{96,112},{112,128},... | collective-permute-start | bytes 156680 | tf_op jit(solution)/shard_map/ppermute | solution.py:154
  125.7 0.9 copy.21
  126.7 5.4 %collective-permute-start.13 = (f32[32,34,3]{1,0,2:T(8,128)}, f32[32,34,3]{1,0,2:T(8,128)S(1)}, u32[]{:S(2)}, u32[]{:S(2)}) collective-permute-start(f32[32,34,3]{1,0,2:T(8,128)} %copy.21), channel_id=1, source_target_pairs={{1,0},{2,1},{3,2},{0,3},{5,4},{6,5},{7,6},{4,7},{9,8},{10,9},{11,1... | collective-permute-start | bytes 39176 | tf_op jit(solution)/shard_map/ppermute | solution.py:64
  132.1 1.9 %collective-permute-start.12 = (f32[32,34,3]{1,0,2:T(8,128)S(1)}, f32[32,34,3]{1,0,2:T(8,128)S(1)}, u32[]{:S(2)}, u32[]{:S(2)}) collective-permute-start(f32[32,34,3]{1,0,2:T(8,128)S(1)} %copy.19), channel_id=1, source_target_pairs={{0,1},{1,2},{2,3},{3,0},{4,5},{5,6},{6,7},{7,4},{8,9},{9,10},{10,1... | collective-permute-start | bytes 39176 | tf_op jit(solution)/shard_map/ppermute | solution.py:63
  134.0 1.2 fusion.482
  135.3 2.7 %collective-permute-done.12 = f32[32,34,3]{1,0,2:T(8,128)S(1)} collective-permute-done((f32[32,34,3]{1,0,2:T(8,128)S(1)}, f32[32,34,3]{1,0,2:T(8,128)S(1)}, u32[]{:S(2)}, u32[]{:S(2)}) %collective-permute-start.12) | collective-permute-done | bytes 13088 | tf_op jit(solution)/shard_map/ppermute | solution.py:63
  138.4 1.2 copy.22
  139.6 13.0 %fusion.181 = f32[32,34,128]{2,1,0:T(8,128)S(1)} fusion(f32[32,34,128]{2,1,0:T(8,128)S(1)} %slice.667, f32[32,34,3]{2,1,0:T(8,128)} %copy.22, f32[32,34,3]{2,1,0:T(8,128)S(1)} %copy.20, f32[4,32,52,128]{3,2,1,0:T(8,128)} %copy-done, f32[32,40,128]{2,1,0:T(8,128)S(1)} %fusion.174, f32[3,34,128]{2,1,0:T(8,128)} %collective-permute-done.10, ...), kind=kLoop, calls=%fused_computation.285 | loop fusion | flops 59326464 | bytes 6815266 | tf_op jit(solution)/shard_map/jit(_where)/select_n | solution.py:199
  152.7 1.9 %collective-permute-start.14 = (f32[1,34,128]{2,1,0:T(8,128)S(1)}, f32[1,34,128]{2,1,0:T(8,128)S(1)}, u32[]{:S(2)}, u32[]{:S(2)}) collective-permute-start(f32[1,34,128]{2,1,0:T(8,128)S(1)} %get-tuple-element.59), channel_id=1, source_target_pairs={{0,16},{16,32},{32,48},{48,64},{64,80},{80,96},{96,112},{112,128},... | collective-permute-start | bytes 52232 | tf_op jit(solution)/shard_map/ppermute | solution.py:154
  154.6 9.8 %collective-permute-start.15 = (f32[1,34,128]{2,1,0:T(8,128)S(1)}, f32[1,34,128]{2,1,0:T(8,128)S(1)}, u32[]{:S(2)}, u32[]{:S(2)}) collective-permute-start(f32[1,34,128]{2,1,0:T(8,128)S(1)} %get-tuple-element.60), channel_id=1, source_target_pairs={{16,0},{32,16},{48,32},{64,48},{80,64},{96,80},{112,96},{128,112},... | collective-permute-start | bytes 52232 | tf_op jit(solution)/shard_map/ppermute | solution.py:155
  166.9 1.0 multiply_reduce_fusion.3
  167.9 1.0 multiply_reduce_fusion.1
  169.0 1.0 multiply_reduce_fusion.5
  170.0 1.0 multiply_reduce_fusion.7
  171.2 1.3 copy.23
  173.2 0.8 reshape.192
  173.9 6.4 %all-to-all-start = ((f32[4,1,4096]{2,1,0:T(1,128)}), f32[4,1,4096]{2,1,0:T(1,128)S(1)}, u32[]{:S(2)}, u32[]{:S(2)}) async-start(f32[4,1,4096]{2,1,0:T(1,128)} %reshape.192), calls=%async_computation | async-start | bytes 131072 | tf_op jit(solution)/shard_map/all_to_all | solution.py:218
  180.3 0.9 slice.697
  181.2 3.8 %all-to-all-done = f32[4,1,4096]{2,1,0:T(1,128)S(1)} async-done(((f32[4,1,4096]{2,1,0:T(1,128)}), f32[4,1,4096]{2,1,0:T(1,128)S(1)}, u32[]{:S(2)}, u32[]{:S(2)}) %all-to-all-start) | async-done | bytes 65568 | tf_op jit(solution)/shard_map/all_to_all | solution.py:218
  185.5 0.8 reduce.4
  (66 shorter events, 9.5 us)
Async XLA Ops:
  0.6 2.0 %copy-start.1 = (f32[32,32,128]{2,1,0:T(8,128)S(1)}, f32[32,32,128]{2,1,0:T(8,128)}, u32[]{:S(2)}) copy-start(f32[32,32,128]{2,1,0:T(8,128)} %param.8) | copy-start | bytes 1572868
  7.9 19.2 %collective-permute-start.1 = (f32[4,32,10,128]{3,1,2,0:T(8,128)}, f32[4,32,10,128]{3,1,2,0:T(8,128)}, u32[]{:S(2)}, u32[]{:S(2)}) collective-permute-start(f32[4,32,10,128]{3,1,2,0:T(8,128)} %copy.8), channel_id=1, source_target_pairs={{4,0},{8,4},{12,8},{0,12},{5,1},{9,5},{13,9},{1,13},{6,2},{10,6},{... | collective-permute-start | bytes 1966088 | tf_op jit(solution)/shard_map/ppermute | solution.py:178
  13.2 19.3 %collective-permute-start = (f32[4,32,10,128]{3,1,2,0:T(8,128)S(1)}, f32[4,32,10,128]{3,1,2,0:T(8,128)S(1)}, u32[]{:S(2)}, u32[]{:S(2)}) collective-permute-start(f32[4,32,10,128]{3,1,2,0:T(8,128)S(1)} %copy.7), channel_id=1, source_target_pairs={{0,4},{4,8},{8,12},{12,0},{1,5},{5,9},{9,13},{13,1},{2,6},{6,10},{... | collective-permute-start | bytes 1966088 | tf_op jit(solution)/shard_map/ppermute | solution.py:177
  32.5 0.9 copy-start.2
  33.3 14.7 %copy-start = (f32[4,32,52,128]{3,2,1,0:T(8,128)}, f32[4,32,52,128]{3,2,1,0:T(8,128)S(1)}, u32[]{:S(2)}) copy-start(f32[4,32,52,128]{3,2,1,0:T(8,128)S(1)} %pad_maximum_fusion) | copy-start | bytes 10223620
  33.4 25.4 %collective-permute-start.3 = (f32[3,46,128]{2,1,0:T(8,128)S(1)}, f32[3,46,128]{2,1,0:T(8,128)S(1)}, u32[]{:S(2)}, u32[]{:S(2)}) collective-permute-start(f32[3,46,128]{2,1,0:T(8,128)S(1)} %get-tuple-element.44), channel_id=1, source_target_pairs={{16,0},{32,16},{48,32},{64,48},{80,64},{96,80},{112,96},{128,112},... | collective-permute-start | bytes 211976 | tf_op jit(solution)/shard_map/ppermute | solution.py:155
  45.8 13.1 %collective-permute-start.2 = (f32[3,46,128]{2,1,0:T(8,128)S(1)}, f32[3,46,128]{2,1,0:T(8,128)S(1)}, u32[]{:S(2)}, u32[]{:S(2)}) collective-permute-start(f32[3,46,128]{2,1,0:T(8,128)S(1)} %get-tuple-element.45), channel_id=1, source_target_pairs={{0,16},{16,32},{32,48},{48,64},{64,80},{80,96},{96,112},{112,128},... | collective-permute-start | bytes 211976 | tf_op jit(solution)/shard_map/ppermute | solution.py:154
  48.3 7.1 %collective-permute-start.4 = (f32[32,46,3]{1,0,2:T(8,128)S(1)}, f32[32,46,3]{1,0,2:T(8,128)S(1)}, u32[]{:S(2)}, u32[]{:S(2)}) collective-permute-start(f32[32,46,3]{1,0,2:T(8,128)S(1)} %copy.11), channel_id=1, source_target_pairs={{0,1},{1,2},{2,3},{3,0},{4,5},{5,6},{6,7},{7,4},{8,9},{9,10},{10,1... | collective-permute-start | bytes 53000 | tf_op jit(solution)/shard_map/ppermute | solution.py:63
  51.6 6.0 %collective-permute-start.5 = (f32[32,46,3]{1,0,2:T(8,128)S(1)}, f32[32,46,3]{1,0,2:T(8,128)S(1)}, u32[]{:S(2)}, u32[]{:S(2)}) collective-permute-start(f32[32,46,3]{1,0,2:T(8,128)S(1)} %copy.13), channel_id=1, source_target_pairs={{1,0},{2,1},{3,2},{0,3},{5,4},{6,5},{7,6},{4,7},{9,8},{10,9},{11,1... | collective-permute-start | bytes 53000 | tf_op jit(solution)/shard_map/ppermute | solution.py:64
  77.9 22.7 %collective-permute-start.7 = (f32[3,40,128]{2,1,0:T(8,128)S(1)}, f32[3,40,128]{2,1,0:T(8,128)S(1)}, u32[]{:S(2)}, u32[]{:S(2)}) collective-permute-start(f32[3,40,128]{2,1,0:T(8,128)S(1)} %get-tuple-element.48), channel_id=1, source_target_pairs={{16,0},{32,16},{48,32},{64,48},{80,64},{96,80},{112,96},{128,112},... | collective-permute-start | bytes 184328 | tf_op jit(solution)/shard_map/ppermute | solution.py:155
  86.2 14.4 %collective-permute-start.6 = (f32[3,40,128]{2,1,0:T(8,128)S(1)}, f32[3,40,128]{2,1,0:T(8,128)S(1)}, u32[]{:S(2)}, u32[]{:S(2)}) collective-permute-start(f32[3,40,128]{2,1,0:T(8,128)S(1)} %get-tuple-element.49), channel_id=1, source_target_pairs={{0,16},{16,32},{32,48},{48,64},{64,80},{80,96},{96,112},{112,128},... | collective-permute-start | bytes 184328 | tf_op jit(solution)/shard_map/ppermute | solution.py:154
  88.6 9.4 %collective-permute-start.8 = (f32[32,40,3]{1,0,2:T(8,128)S(1)}, f32[32,40,3]{1,0,2:T(8,128)S(1)}, u32[]{:S(2)}, u32[]{:S(2)}) collective-permute-start(f32[32,40,3]{1,0,2:T(8,128)S(1)} %copy.15), channel_id=1, source_target_pairs={{0,1},{1,2},{2,3},{3,0},{4,5},{5,6},{6,7},{7,4},{8,9},{9,10},{10,1... | collective-permute-start | bytes 46088 | tf_op jit(solution)/shard_map/ppermute | solution.py:63
  92.0 7.5 %collective-permute-start.9 = (f32[32,40,3]{1,0,2:T(8,128)S(1)}, f32[32,40,3]{1,0,2:T(8,128)S(1)}, u32[]{:S(2)}, u32[]{:S(2)}) collective-permute-start(f32[32,40,3]{1,0,2:T(8,128)S(1)} %copy.17), channel_id=1, source_target_pairs={{1,0},{2,1},{3,2},{0,3},{5,4},{6,5},{7,6},{4,7},{9,8},{10,9},{11,1... | collective-permute-start | bytes 46088 | tf_op jit(solution)/shard_map/ppermute | solution.py:64
  114.3 25.3 %collective-permute-start.11 = (f32[3,34,128]{2,1,0:T(8,128)}, f32[3,34,128]{2,1,0:T(8,128)}, u32[]{:S(2)}, u32[]{:S(2)}) collective-permute-start(f32[3,34,128]{2,1,0:T(8,128)} %get-tuple-element.63), channel_id=1, source_target_pairs={{16,0},{32,16},{48,32},{64,48},{80,64},{96,80},{112,96},{128,112},... | collective-permute-start | bytes 156680 | tf_op jit(solution)/shard_map/ppermute | solution.py:155
  123.5 16.2 %collective-permute-start.10 = (f32[3,34,128]{2,1,0:T(8,128)}, f32[3,34,128]{2,1,0:T(8,128)}, u32[]{:S(2)}, u32[]{:S(2)}) collective-permute-start(f32[3,34,128]{2,1,0:T(8,128)} %get-tuple-element.64), channel_id=1, source_target_pairs={{0,16},{16,32},{32,48},{48,64},{64,80},{80,96},{96,112},{112,128},... | collective-permute-start | bytes 156680 | tf_op jit(solution)/shard_map/ppermute | solution.py:154
  126.7 11.8 %collective-permute-start.13 = (f32[32,34,3]{1,0,2:T(8,128)}, f32[32,34,3]{1,0,2:T(8,128)S(1)}, u32[]{:S(2)}, u32[]{:S(2)}) collective-permute-start(f32[32,34,3]{1,0,2:T(8,128)} %copy.21), channel_id=1, source_target_pairs={{1,0},{2,1},{3,2},{0,3},{5,4},{6,5},{7,6},{4,7},{9,8},{10,9},{11,1... | collective-permute-start | bytes 39176 | tf_op jit(solution)/shard_map/ppermute | solution.py:64
  132.1 6.0 %collective-permute-start.12 = (f32[32,34,3]{1,0,2:T(8,128)S(1)}, f32[32,34,3]{1,0,2:T(8,128)S(1)}, u32[]{:S(2)}, u32[]{:S(2)}) collective-permute-start(f32[32,34,3]{1,0,2:T(8,128)S(1)} %copy.19), channel_id=1, source_target_pairs={{0,1},{1,2},{2,3},{3,0},{4,5},{5,6},{6,7},{7,4},{8,9},{9,10},{10,1... | collective-permute-start | bytes 39176 | tf_op jit(solution)/shard_map/ppermute | solution.py:63
  139.6 24.8 %copy-start.3 = (s32[4]{0:T(128)S(1)}, s32[4]{0:T(128)}, u32[]{:S(2)}) copy-start(s32[4]{0:T(128)} %param.11) | copy-start | bytes 52
  152.7 13.7 %collective-permute-start.14 = (f32[1,34,128]{2,1,0:T(8,128)S(1)}, f32[1,34,128]{2,1,0:T(8,128)S(1)}, u32[]{:S(2)}, u32[]{:S(2)}) collective-permute-start(f32[1,34,128]{2,1,0:T(8,128)S(1)} %get-tuple-element.59), channel_id=1, source_target_pairs={{0,16},{16,32},{32,48},{48,64},{64,80},{80,96},{96,112},{112,128},... | collective-permute-start | bytes 52232 | tf_op jit(solution)/shard_map/ppermute | solution.py:154
  154.6 11.8 %collective-permute-start.15 = (f32[1,34,128]{2,1,0:T(8,128)S(1)}, f32[1,34,128]{2,1,0:T(8,128)S(1)}, u32[]{:S(2)}, u32[]{:S(2)}) collective-permute-start(f32[1,34,128]{2,1,0:T(8,128)S(1)} %get-tuple-element.60), channel_id=1, source_target_pairs={{16,0},{32,16},{48,32},{64,48},{80,64},{96,80},{112,96},{128,112},... | collective-permute-start | bytes 52232 | tf_op jit(solution)/shard_map/ppermute | solution.py:155
  173.9 11.0 %all-to-all-start = ((f32[4,1,4096]{2,1,0:T(1,128)}), f32[4,1,4096]{2,1,0:T(1,128)S(1)}, u32[]{:S(2)}, u32[]{:S(2)}) async-start(f32[4,1,4096]{2,1,0:T(1,128)} %reshape.192), calls=%async_computation | async-start | bytes 131072 | tf_op jit(solution)/shard_map/all_to_all | solution.py:218

commit v10 on v6

--- a/solution.py
+++ b/solution.py
@@ -197,17 +197,29 @@
     edge_after = jnp.concatenate([after[:1], after[SPAN:]], 0)[:, ring]
     wide = x_faces(section_two, SPAN + 1)
     inner = wide[SPAN:-SPAN, SPAN:-SPAN]
-    padded = [wide[:, SPAN:-SPAN], wide[SPAN:-SPAN], z_faces(inner)]
-    speed_three = jnp.concatenate(
-        [edge_before[1:4][:, None], speed_two[:, :, SPAN:-SPAN], edge_after[1:4][:, None]], 1
-    )
-    rate = local_rate(padded, speed_three)
-    level_ring = jnp.concatenate(
-        [edge_before[:1], level_ext[:, 3 * SPAN : -3 * SPAN], edge_after[:1]], 0
-    )
-    flag_three = jnp.concatenate([edge_before[4:5], flag_ring, edge_after[4:5]], 0)
-    advanced = level_ring / 3.0 + 2.0 / 3.0 * (inner + time_step * rate)
-    rim = jnp.where(flag_three > 0, advanced, level_ring)
+    across, along, depth = wide[:, SPAN:-SPAN], wide[SPAN:-SPAN], z_faces(inner)
+    rows = inner.shape[0]
+
+    def part(lo, hi, speeds, level, flag):
+        padded = [across[lo : hi + 2 * SPAN], along[lo:hi], depth[lo:hi]]
+        rate = local_rate(padded, speeds)
+        advanced = level / 3.0 + 2.0 / 3.0 * (inner[lo:hi] + time_step * rate)
+        return jnp.where(flag > 0, advanced, level)
+
+    rim = jnp.concatenate(
+        [
+            part(0, 1, edge_before[1:4][:, None], edge_before[:1], edge_before[4:5]),
+            part(
+                1,
+                rows - 1,
+                speed_two[:, :, SPAN:-SPAN],
+                level_ext[:, 3 * SPAN : -3 * SPAN],
+                flag_ring,
+            ),
+            part(rows - 1, rows, edge_after[1:4][:, None], edge_after[:1], edge_after[4:5]),
+        ],
+        0,
+    )
     level_out = rim[1:-1, 1:-1]
 
     group = lax.axis_size("gz")

time: 194 us -> 188 us (0.969)
  the two profiles are of different devices: /device:TPU:8 before, /device:TPU:135 now
where the time goes in v10:
time: 188 us; the launch traced here: 187 us
  starting transfers between devices  68.8 us (37%)
  other arithmetic  49.7 us (26%)
  waiting for transfers between devices  36.6 us (19%)
  local copies, waits for them, and re-layouts  22.6 us (12%)
  matrix products  5.9 us (3%)
  between operations  3.12 us (2%)
    ppermute x2, starting transfers between devices, x_faces(): before = lax.ppermute(x[length - width:], 'gx', up)  20.9 us
    ppermute x3, starting transfers between devices, z_faces(): after = lax.ppermute(x[:, :, :SPAN], 'gz', down)  15.4 us
    select_n x3, other arithmetic, part(): return jnp.where(flag > 0, advanced, level)  15.1 us
    add x1, other arithmetic, shards(): section_one = inner + time_step * local_rate(padded, speed_one)  15 us
    ppermute x1, waiting for transfers between devices, exchange(): after = lax.ppermute(first, axis, down)  14.7 us
    add x1, other arithmetic, shards(): 0.75 * level_ext[:, 2 * SPAN:-2 * SPAN] + 0.25 * (inner + time_step * rate)  13 us
    ppermute x1, starting transfers between devices, shards(): before = lax.ppermute(last, 'gx', up)  10.4 us
    ppermute x2, waiting for transfers between devices, x_faces(): after = lax.ppermute(x[:width], 'gx', down)  9.96 us
  transfers between devices with their start and end apart: 15, of which 7 were waited for; matrix products, arithmetic and copies ran while one was open for 6% of the time, Pallas kernels for 0%

profile of v10, /device:TPU:135, one launch (start us, length us, event | category | flops | bytes accessed | tf_op | source)
XLA Modules:
  0.0 186.7 jit_solution(18389746766915587586)
XLA Ops:
  1.4 1.1 bitcast_dynamic-update-slice_fusion
  2.4 1.0 convert_dynamic-update-slice_fusion.2
  4.1 4.6 %collective-permute-start.1 = (f32[5,32,10,128]{3,1,2,0:T(8,128)S(1)}, f32[5,32,10,128]{3,1,2,0:T(8,128)S(1)}, u32[]{:S(2)}, u32[]{:S(2)}) collective-permute-start(f32[5,32,10,128]{3,1,2,0:T(8,128)S(1)} %copy.8), channel_id=1, source_target_pairs={{4,0},{8,4},{12,8},{0,12},{5,1},{9,5},{13,9},{1,13},{6,2},{10,6},{... | collective-permute-start | bytes 2457608 | tf_op jit(solution)/shard_map/ppermute | solution.py:24
  9.0 1.9 %collective-permute-start = (f32[5,32,10,128]{3,1,2,0:T(8,128)S(1)}, f32[5,32,10,128]{3,1,2,0:T(8,128)S(1)}, u32[]{:S(2)}, u32[]{:S(2)}) collective-permute-start(f32[5,32,10,128]{3,1,2,0:T(8,128)S(1)} %copy.7), channel_id=1, source_target_pairs={{0,4},{4,8},{8,12},{12,0},{1,5},{5,9},{9,13},{13,1},{2,6},{6,10},{... | collective-permute-start | bytes 2457608 | tf_op jit(solution)/shard_map/ppermute | solution.py:23
  11.0 14.7 %collective-permute-done.1 = f32[5,32,10,128]{3,1,2,0:T(8,128)S(1)} collective-permute-done((f32[5,32,10,128]{3,1,2,0:T(8,128)S(1)}, f32[5,32,10,128]{3,1,2,0:T(8,128)S(1)}, u32[]{:S(2)}, u32[]{:S(2)}) %collective-permute-start.1) | collective-permute-done | bytes 819232 | tf_op jit(solution)/shard_map/ppermute | solution.py:24
  26.2 4.8 %collective-permute-done = f32[5,32,10,128]{3,1,2,0:T(8,128)S(1)} collective-permute-done((f32[5,32,10,128]{3,1,2,0:T(8,128)S(1)}, f32[5,32,10,128]{3,1,2,0:T(8,128)S(1)}, u32[]{:S(2)}, u32[]{:S(2)}) %collective-permute-start) | collective-permute-done | bytes 819232 | tf_op jit(solution)/shard_map/ppermute | solution.py:23
  32.1 0.8 slice_dynamic-update-slice_fusion
  32.9 1.1 constant_dynamic-update-slice_fusion.7
  34.2 0.6 constant_dynamic-update-slice_fusion.6
  36.0 10.4 %collective-permute-start.2 = (f32[7,46,128]{2,1,0:T(8,128)}, f32[7,46,128]{2,1,0:T(8,128)S(1)}, u32[]{:S(2)}, u32[]{:S(2)}) collective-permute-start(f32[7,46,128]{2,1,0:T(8,128)} %get-tuple-element.19), channel_id=1, source_target_pairs={{0,16},{16,32},{32,48},{48,64},{64,80},{80,96},{96,112},{112,128},... | collective-permute-start | bytes 494600 | tf_op jit(solution)/shard_map/ppermute | solution.py:184
  46.4 1.9 %collective-permute-start.3 = (f32[7,46,128]{2,1,0:T(8,128)}, f32[7,46,128]{2,1,0:T(8,128)}, u32[]{:S(2)}, u32[]{:S(2)}) collective-permute-start(f32[7,46,128]{2,1,0:T(8,128)} %get-tuple-element.18), channel_id=1, source_target_pairs={{16,0},{32,16},{48,32},{64,48},{80,64},{96,80},{112,96},{128,112},... | collective-permute-start | bytes 494600 | tf_op jit(solution)/shard_map/ppermute | solution.py:185
  49.0 2.6 %collective-permute-start.4 = (f32[32,46,3]{1,0,2:T(8,128)S(1)}, f32[32,46,3]{1,0,2:T(8,128)S(1)}, u32[]{:S(2)}, u32[]{:S(2)}) collective-permute-start(f32[32,46,3]{1,0,2:T(8,128)S(1)} %copy.11), channel_id=1, source_target_pairs={{0,1},{1,2},{2,3},{3,0},{4,5},{5,6},{6,7},{7,4},{8,9},{9,10},{10,1... | collective-permute-start | bytes 53000 | tf_op jit(solution)/shard_map/ppermute | solution.py:63
  52.0 4.4 %collective-permute-start.5 = (f32[32,46,3]{1,0,2:T(8,128)S(1)}, f32[32,46,3]{1,0,2:T(8,128)S(1)}, u32[]{:S(2)}, u32[]{:S(2)}) collective-permute-start(f32[32,46,3]{1,0,2:T(8,128)S(1)} %copy.13), channel_id=1, source_target_pairs={{1,0},{2,1},{3,2},{0,3},{5,4},{6,5},{7,6},{4,7},{9,8},{10,9},{11,1... | collective-permute-start | bytes 53000 | tf_op jit(solution)/shard_map/ppermute | solution.py:64
  56.5 1.3 copy.12
  57.8 1.3 copy.14
  59.1 3.0 %collective-permute-done.3 = f32[7,46,128]{2,1,0:T(8,128)} collective-permute-done((f32[7,46,128]{2,1,0:T(8,128)}, f32[7,46,128]{2,1,0:T(8,128)}, u32[]{:S(2)}, u32[]{:S(2)}) %collective-permute-start.3) | collective-permute-done | bytes 164896 | tf_op jit(solution)/shard_map/ppermute | solution.py:185
  62.1 0.9 slice.985
  63.0 15.0 %fusion.21 = f32[32,46,128]{2,1,0:T(8,128)S(1)} fusion(f32[32,46,128]{2,1,0:T(8,128)S(1)} %slice.976, f32[32,46,3]{2,1,0:T(8,128)} %copy.14, f32[32,46,3]{2,1,0:T(8,128)} %copy.12, f32[5,32,52,128]{3,2,1,0:T(8,128)} %copy-done, f32[32,52,128]{2,1,0:T(8,128)S(1)} %slice_bitcast_fusion, f32[3,46,128]{2,1,0:T(8,128)S(1)} %slice.979, f32[3,46,128]{2,1,0:T(8,128)S(1)} %slice.985), kind=kLoop, calls=%fused_computation.99 | loop fusion | flops 79511552 | bytes 8466944 | tf_op jit(solution)/shard_map/add | solution.py:191
  78.0 10.1 %collective-permute-start.6 = (f32[3,40,128]{2,1,0:T(8,128)S(1)}, f32[3,40,128]{2,1,0:T(8,128)S(1)}, u32[]{:S(2)}, u32[]{:S(2)}) collective-permute-start(f32[3,40,128]{2,1,0:T(8,128)S(1)} %get-tuple-element.35), channel_id=1, source_target_pairs={{0,16},{16,32},{32,48},{48,64},{64,80},{80,96},{96,112},{112,128},... | collective-permute-start | bytes 184328 | tf_op jit(solution)/shard_map/ppermute | solution.py:154
  88.2 1.9 %collective-permute-start.7 = (f32[3,40,128]{2,1,0:T(8,128)S(1)}, f32[3,40,128]{2,1,0:T(8,128)S(1)}, u32[]{:S(2)}, u32[]{:S(2)}) collective-permute-start(f32[3,40,128]{2,1,0:T(8,128)S(1)} %get-tuple-element.34), channel_id=1, source_target_pairs={{16,0},{32,16},{48,32},{64,48},{80,64},{96,80},{112,96},{128,112},... | collective-permute-start | bytes 184328 | tf_op jit(solution)/shard_map/ppermute | solution.py:155
  90.6 1.9 %collective-permute-start.8 = (f32[32,40,3]{1,0,2:T(8,128)S(1)}, f32[32,40,3]{1,0,2:T(8,128)S(1)}, u32[]{:S(2)}, u32[]{:S(2)}) collective-permute-start(f32[32,40,3]{1,0,2:T(8,128)S(1)} %copy.15), channel_id=1, source_target_pairs={{0,1},{1,2},{2,3},{3,0},{4,5},{5,6},{6,7},{7,4},{8,9},{9,10},{10,1... | collective-permute-start | bytes 46088 | tf_op jit(solution)/shard_map/ppermute | solution.py:63
  92.6 0.9 copy.17
  93.5 5.1 %collective-permute-start.9 = (f32[32,40,3]{1,0,2:T(8,128)}, f32[32,40,3]{1,0,2:T(8,128)S(1)}, u32[]{:S(2)}, u32[]{:S(2)}) collective-permute-start(f32[32,40,3]{1,0,2:T(8,128)} %copy.17), channel_id=1, source_target_pairs={{1,0},{2,1},{3,2},{0,3},{5,4},{6,5},{7,6},{4,7},{9,8},{10,9},{11,1... | collective-permute-start | bytes 46088 | tf_op jit(solution)/shard_map/ppermute | solution.py:64
  98.7 1.2 copy.16
  100.1 1.2 copy.18
  101.3 13.0 %fusion.174 = f32[32,40,128]{2,1,0:T(8,128)S(1)} fusion(f32[32,52,128]{2,1,0:T(8,128)S(1)} %slice_bitcast_fusion, f32[32,40,128]{2,1,0:T(8,128)S(1)} %slice.1008, f32[32,40,3]{2,1,0:T(8,128)} %copy.18, f32[32,40,3]{2,1,0:T(8,128)} %copy.16, f32[5,32,52,128]{3,2,1,0:T(8,128)} %copy-done, f32[32,46,128]{2,1,0:T(8,128)S(1)} %fusion.21, ...), kind=kLoop, calls=%fused_computation.299 | loop fusion | flops 69632000 | bytes 8017920 | tf_op jit(solution)/shard_map/add | solution.py:193
  114.3 10.8 %collective-permute-start.10 = (f32[4,40,128]{2,1,0:T(8,128)S(1)}, f32[4,40,128]{2,1,0:T(8,128)S(1)}, u32[]{:S(2)}, u32[]{:S(2)}) collective-permute-start(f32[4,40,128]{2,1,0:T(8,128)S(1)} %get-tuple-element.44), channel_id=1, source_target_pairs={{0,16},{16,32},{32,48},{48,64},{64,80},{80,96},{96,112},{112,128},... | collective-permute-start | bytes 245768 | tf_op jit(solution)/shard_map/ppermute | solution.py:154
  125.1 1.9 %collective-permute-start.11 = (f32[4,40,128]{2,1,0:T(8,128)S(1)}, f32[4,40,128]{2,1,0:T(8,128)S(1)}, u32[]{:S(2)}, u32[]{:S(2)}) collective-permute-start(f32[4,40,128]{2,1,0:T(8,128)S(1)} %get-tuple-element.45), channel_id=1, source_target_pairs={{16,0},{32,16},{48,32},{64,48},{80,64},{96,80},{112,96},{128,112},... | collective-permute-start | bytes 245768 | tf_op jit(solution)/shard_map/ppermute | solution.py:155
  127.2 10.0 %collective-permute-done.11 = f32[4,40,128]{2,1,0:T(8,128)S(1)} collective-permute-done((f32[4,40,128]{2,1,0:T(8,128)S(1)}, f32[4,40,128]{2,1,0:T(8,128)S(1)}, u32[]{:S(2)}, u32[]{:S(2)}) %collective-permute-start.11) | collective-permute-done | bytes 81952 | tf_op jit(solution)/shard_map/ppermute | solution.py:155
  137.2 1.1 fusion.456
  138.3 1.5 copy.19
  139.8 1.9 %collective-permute-start.12 = (f32[34,34,3]{1,0,2:T(8,128)S(1)}, f32[34,34,3]{1,0,2:T(8,128)S(1)}, u32[]{:S(2)}, u32[]{:S(2)}) collective-permute-start(f32[34,34,3]{1,0,2:T(8,128)S(1)} %copy.19), channel_id=1, source_target_pairs={{0,1},{1,2},{2,3},{3,0},{4,5},{5,6},{6,7},{7,4},{8,9},{9,10},{10,1... | collective-permute-start | bytes 41624 | tf_op jit(solution)/shard_map/ppermute | solution.py:63
  141.7 1.0 copy.21
  142.7 5.8 %collective-permute-start.13 = (f32[34,34,3]{1,0,2:T(8,128)}, f32[34,34,3]{1,0,2:T(8,128)S(1)}, u32[]{:S(2)}, u32[]{:S(2)}) collective-permute-start(f32[34,34,3]{1,0,2:T(8,128)} %copy.21), channel_id=1, source_target_pairs={{1,0},{2,1},{3,2},{0,3},{5,4},{6,5},{7,6},{4,7},{9,8},{10,9},{11,1... | collective-permute-start | bytes 41624 | tf_op jit(solution)/shard_map/ppermute | solution.py:64
  150.3 0.9 slice.1059
  152.0 1.5 add_select_fusion
  153.8 13.2 %fusion.181 = f32[32,34,128]{2,1,0:T(8,128)S(1)} fusion(f32[34,34,3]{2,1,0:T(8,128)S(1)} %copy.22, f32[34,34,128]{2,1,0:T(8,128)S(1)} %copy-done.1, f32[34,34,3]{2,1,0:T(8,128)S(1)} %copy.20, f32[5,32,52,128]{3,2,1,0:T(8,128)} %copy-done, f32[32,40,128]{2,1,0:T(8,128)S(1)} %fusion.174, f32[4,40,128]{2,1,0:T(8,128)S(1)} %collective-permute-done.11, ...), kind=kLoop, calls=%fused_computation.308 | loop fusion | flops 59465728 | bytes 10936320 | tf_op jit(solution)/shard_map/jit(_where)/select_n | solution.py:207
  167.9 1.2 multiply_reduce_fusion.7
  169.1 1.2 multiply_reduce_fusion.5
  170.2 1.2 multiply_reduce_fusion.3
  171.4 1.2 multiply_reduce_fusion.1
  172.7 1.3 copy.23
  174.0 0.7 copy.24
  174.7 0.8 reshape.120
  175.5 3.3 %all-to-all-start = ((f32[4,1,4096]{2,1,0:T(1,128)}), f32[4,1,4096]{2,1,0:T(1,128)S(1)}, u32[]{:S(2)}, u32[]{:S(2)}) async-start(f32[4,1,4096]{2,1,0:T(1,128)} %reshape.120), calls=%async_computation | async-start | bytes 131072 | tf_op jit(solution)/shard_map/all_to_all | solution.py:240
  178.8 0.9 slice.1073
  179.6 3.7 %all-to-all-done = f32[4,1,4096]{2,1,0:T(1,128)S(1)} async-done(((f32[4,1,4096]{2,1,0:T(1,128)}), f32[4,1,4096]{2,1,0:T(1,128)S(1)}, u32[]{:S(2)}, u32[]{:S(2)}) %all-to-all-start) | async-done | bytes 65568 | tf_op jit(solution)/shard_map/all_to_all | solution.py:240
  183.8 0.8 reduce
  (71 shorter events, 11.1 us)
Async XLA Ops:
  0.6 2.8 %copy-start.4 = (bf16[3,32,32,128]{3,2,1,0:T(8,128)(2,1)S(1)}, bf16[3,32,32,128]{3,2,1,0:T(8,128)(2,1)}, u32[]{:S(2)}) copy-start(bf16[3,32,32,128]{3,2,1,0:T(8,128)(2,1)} %param.5) | copy-start | bytes 2359300
  4.1 21.6 %collective-permute-start.1 = (f32[5,32,10,128]{3,1,2,0:T(8,128)S(1)}, f32[5,32,10,128]{3,1,2,0:T(8,128)S(1)}, u32[]{:S(2)}, u32[]{:S(2)}) collective-permute-start(f32[5,32,10,128]{3,1,2,0:T(8,128)S(1)} %copy.8), channel_id=1, source_target_pairs={{4,0},{8,4},{12,8},{0,12},{5,1},{9,5},{13,9},{1,13},{6,2},{10,6},{... | collective-permute-start | bytes 2457608 | tf_op jit(solution)/shard_map/ppermute | solution.py:24
  9.0 22.0 %collective-permute-start = (f32[5,32,10,128]{3,1,2,0:T(8,128)S(1)}, f32[5,32,10,128]{3,1,2,0:T(8,128)S(1)}, u32[]{:S(2)}, u32[]{:S(2)}) collective-permute-start(f32[5,32,10,128]{3,1,2,0:T(8,128)S(1)} %copy.7), channel_id=1, source_target_pairs={{0,4},{4,8},{8,12},{12,0},{1,5},{5,9},{9,13},{13,1},{2,6},{6,10},{... | collective-permute-start | bytes 2457608 | tf_op jit(solution)/shard_map/ppermute | solution.py:23
  32.0 2.1 %copy-start = (f32[5,32,52,128]{3,2,1,0:T(8,128)}, f32[5,32,52,128]{3,2,1,0:T(8,128)S(1)}, u32[]{:S(2)}) copy-start(f32[5,32,52,128]{3,2,1,0:T(8,128)S(1)} %pad_maximum_fusion) | copy-start | bytes 12779524
  36.0 23.0 %collective-permute-start.2 = (f32[7,46,128]{2,1,0:T(8,128)}, f32[7,46,128]{2,1,0:T(8,128)S(1)}, u32[]{:S(2)}, u32[]{:S(2)}) collective-permute-start(f32[7,46,128]{2,1,0:T(8,128)} %get-tuple-element.19), channel_id=1, source_target_pairs={{0,16},{16,32},{32,48},{48,64},{64,80},{80,96},{96,112},{112,128},... | collective-permute-start | bytes 494600 | tf_op jit(solution)/shard_map/ppermute | solution.py:184
  46.4 15.7 %collective-permute-start.3 = (f32[7,46,128]{2,1,0:T(8,128)}, f32[7,46,128]{2,1,0:T(8,128)}, u32[]{:S(2)}, u32[]{:S(2)}) collective-permute-start(f32[7,46,128]{2,1,0:T(8,128)} %get-tuple-element.18), channel_id=1, source_target_pairs={{16,0},{32,16},{48,32},{64,48},{80,64},{96,80},{112,96},{128,112},... | collective-permute-start | bytes 494600 | tf_op jit(solution)/shard_map/ppermute | solution.py:185
  49.0 7.5 %collective-permute-start.4 = (f32[32,46,3]{1,0,2:T(8,128)S(1)}, f32[32,46,3]{1,0,2:T(8,128)S(1)}, u32[]{:S(2)}, u32[]{:S(2)}) collective-permute-start(f32[32,46,3]{1,0,2:T(8,128)S(1)} %copy.11), channel_id=1, source_target_pairs={{0,1},{1,2},{2,3},{3,0},{4,5},{5,6},{6,7},{7,4},{8,9},{9,10},{10,1... | collective-permute-start | bytes 53000 | tf_op jit(solution)/shard_map/ppermute | solution.py:63
  52.0 5.8 %collective-permute-start.5 = (f32[32,46,3]{1,0,2:T(8,128)S(1)}, f32[32,46,3]{1,0,2:T(8,128)S(1)}, u32[]{:S(2)}, u32[]{:S(2)}) collective-permute-start(f32[32,46,3]{1,0,2:T(8,128)S(1)} %copy.13), channel_id=1, source_target_pairs={{1,0},{2,1},{3,2},{0,3},{5,4},{6,5},{7,6},{4,7},{9,8},{10,9},{11,1... | collective-permute-start | bytes 53000 | tf_op jit(solution)/shard_map/ppermute | solution.py:64
  78.0 23.2 %collective-permute-start.6 = (f32[3,40,128]{2,1,0:T(8,128)S(1)}, f32[3,40,128]{2,1,0:T(8,128)S(1)}, u32[]{:S(2)}, u32[]{:S(2)}) collective-permute-start(f32[3,40,128]{2,1,0:T(8,128)S(1)} %get-tuple-element.35), channel_id=1, source_target_pairs={{0,16},{16,32},{32,48},{48,64},{64,80},{80,96},{96,112},{112,128},... | collective-permute-start | bytes 184328 | tf_op jit(solution)/shard_map/ppermute | solution.py:154
  88.2 13.1 %collective-permute-start.7 = (f32[3,40,128]{2,1,0:T(8,128)S(1)}, f32[3,40,128]{2,1,0:T(8,128)S(1)}, u32[]{:S(2)}, u32[]{:S(2)}) collective-permute-start(f32[3,40,128]{2,1,0:T(8,128)S(1)} %get-tuple-element.34), channel_id=1, source_target_pairs={{16,0},{32,16},{48,32},{64,48},{80,64},{96,80},{112,96},{128,112},... | collective-permute-start | bytes 184328 | tf_op jit(solution)/shard_map/ppermute | solution.py:155
  90.6 8.1 %collective-permute-start.8 = (f32[32,40,3]{1,0,2:T(8,128)S(1)}, f32[32,40,3]{1,0,2:T(8,128)S(1)}, u32[]{:S(2)}, u32[]{:S(2)}) collective-permute-start(f32[32,40,3]{1,0,2:T(8,128)S(1)} %copy.15), channel_id=1, source_target_pairs={{0,1},{1,2},{2,3},{3,0},{4,5},{5,6},{6,7},{7,4},{8,9},{9,10},{10,1... | collective-permute-start | bytes 46088 | tf_op jit(solution)/shard_map/ppermute | solution.py:63
  93.5 6.6 %collective-permute-start.9 = (f32[32,40,3]{1,0,2:T(8,128)}, f32[32,40,3]{1,0,2:T(8,128)S(1)}, u32[]{:S(2)}, u32[]{:S(2)}) collective-permute-start(f32[32,40,3]{1,0,2:T(8,128)} %copy.17), channel_id=1, source_target_pairs={{1,0},{2,1},{3,2},{0,3},{5,4},{6,5},{7,6},{4,7},{9,8},{10,9},{11,1... | collective-permute-start | bytes 46088 | tf_op jit(solution)/shard_map/ppermute | solution.py:64
  114.3 12.8 %collective-permute-start.10 = (f32[4,40,128]{2,1,0:T(8,128)S(1)}, f32[4,40,128]{2,1,0:T(8,128)S(1)}, u32[]{:S(2)}, u32[]{:S(2)}) collective-permute-start(f32[4,40,128]{2,1,0:T(8,128)S(1)} %get-tuple-element.44), channel_id=1, source_target_pairs={{0,16},{16,32},{32,48},{48,64},{64,80},{80,96},{96,112},{112,128},... | collective-permute-start | bytes 245768 | tf_op jit(solution)/shard_map/ppermute | solution.py:154
  125.1 12.0 %collective-permute-start.11 = (f32[4,40,128]{2,1,0:T(8,128)S(1)}, f32[4,40,128]{2,1,0:T(8,128)S(1)}, u32[]{:S(2)}, u32[]{:S(2)}) collective-permute-start(f32[4,40,128]{2,1,0:T(8,128)S(1)} %get-tuple-element.45), channel_id=1, source_target_pairs={{16,0},{32,16},{48,32},{64,48},{80,64},{96,80},{112,96},{128,112},... | collective-permute-start | bytes 245768 | tf_op jit(solution)/shard_map/ppermute | solution.py:155
  137.2 11.3 %copy-start.5 = (s32[4]{0:T(128)S(1)}, s32[4]{0:T(128)}, u32[]{:S(2)}) copy-start(s32[4]{0:T(128)} %param.7) | copy-start | bytes 52
  139.8 11.5 %collective-permute-start.12 = (f32[34,34,3]{1,0,2:T(8,128)S(1)}, f32[34,34,3]{1,0,2:T(8,128)S(1)}, u32[]{:S(2)}, u32[]{:S(2)}) collective-permute-start(f32[34,34,3]{1,0,2:T(8,128)S(1)} %copy.19), channel_id=1, source_target_pairs={{0,1},{1,2},{2,3},{3,0},{4,5},{5,6},{6,7},{7,4},{8,9},{9,10},{10,1... | collective-permute-start | bytes 41624 | tf_op jit(solution)/shard_map/ppermute | solution.py:63
  142.7 8.9 %collective-permute-start.13 = (f32[34,34,3]{1,0,2:T(8,128)}, f32[34,34,3]{1,0,2:T(8,128)S(1)}, u32[]{:S(2)}, u32[]{:S(2)}) collective-permute-start(f32[34,34,3]{1,0,2:T(8,128)} %copy.21), channel_id=1, source_target_pairs={{1,0},{2,1},{3,2},{0,3},{5,4},{6,5},{7,6},{4,7},{9,8},{10,9},{11,1... | collective-permute-start | bytes 41624 | tf_op jit(solution)/shard_map/ppermute | solution.py:64
  152.0 1.5 copy-start.1
  167.1 0.8 copy-start.2
  174.0 4.7 %copy-start.3 = (f32[32,34,128]{2,1,0:T(8,128)S(1)}, f32[32,34,128]{2,1,0:T(8,128)}, u32[]{:S(2)}) copy-start(f32[32,34,128]{2,1,0:T(8,128)} %copy-done.2) | copy-start | bytes 1671172
  175.5 7.9 %all-to-all-start = ((f32[4,1,4096]{2,1,0:T(1,128)}), f32[4,1,4096]{2,1,0:T(1,128)S(1)}, u32[]{:S(2)}, u32[]{:S(2)}) async-start(f32[4,1,4096]{2,1,0:T(1,128)} %reshape.120), calls=%async_computation | async-start | bytes 131072 | tf_op jit(solution)/shard_map/all_to_all | solution.py:240

commit v11 on v10

--- a/solution.py
+++ b/solution.py
@@ -165,22 +165,35 @@
 def shards(level_set, velocity, active_brick, depth_order):
     alive = active_brick[0, 0, 0] > 0
     alive_float = alive.astype(jnp.float32)
-    flags = jnp.broadcast_to(alive_float, level_set.shape)
-    stacked = jnp.stack([level_set] + [velocity[d].astype(jnp.float32) for d in range(3)] + [flags])
+    stacked = jnp.stack([level_set] + [velocity[d].astype(jnp.float32) for d in range(3)])
     halo = 3 * SPAN + 1
-    stacked = exchange([stacked], "gy", [halo], 1)[0]
+    size, length = (lax.axis_size("gy"), stacked.shape[2])
+    up = [(i, (i + 1) % size) for i in range(size)]
+    down = [(j, i) for i, j in up]
+    last = stacked[:, :, length - halo :].at[1, :, 0].set(alive_float)
+    first = stacked[:, :, :halo].at[1, :, halo - 1].set(alive_float)
+    y_before = lax.ppermute(last, "gy", up)
+    y_after = lax.ppermute(first, "gy", down)
+    stacked = jnp.concatenate([y_before, stacked, y_after], axis=2)
+    flag_low, flag_high = y_before[1, 0, 0, 0], y_after[1, 0, halo - 1, 0]
+
+    def flag_column(width):
+        place = lax.broadcasted_iota(jnp.int32, (1, length + 2 * width, 1), 1)
+        low = jnp.where(place < width, flag_low, alive_float)
+        return jnp.where(place >= length + width, flag_high, low)
+
     level_ext = stacked[0]
-    carried = stacked[1:5, :, SPAN:-SPAN]
-    speed_one = carried[:3]
+    speed_one = stacked[1:4, :, SPAN:-SPAN]
     speed_two = speed_one[:, :, SPAN:-SPAN]
-    flag_ring = stacked[4, :, 3 * SPAN : -3 * SPAN]
+    flag_ring = flag_column(1)
 
     size = lax.axis_size("gx")
     up = [(i, (i + 1) % size) for i in range(size)]
     down = [(j, i) for i, j in up]
     inner = level_ext[:, SPAN:-SPAN]
-    last = jnp.concatenate([inner[-SPAN:]] + [carried[c, -1:] for c in range(4)], 0)
-    first = jnp.concatenate([inner[:SPAN]] + [carried[c, :1] for c in range(4)], 0)
+    flag_row = jnp.broadcast_to(flag_column(halo - SPAN), (1,) + inner.shape[1:])
+    last = jnp.concatenate([inner[-SPAN:]] + [speed_one[c, -1:] for c in range(3)] + [flag_row], 0)
+    first = jnp.concatenate([inner[:SPAN]] + [speed_one[c, :1] for c in range(3)] + [flag_row], 0)
     before = lax.ppermute(last, "gx", up)
     after = lax.ppermute(first, "gx", down)
     padded = [

time: 188 us -> 189 us (level)
  the two profiles are of different devices: /device:TPU:135 before, /device:TPU:32 now
where the time goes in v11:
time: 189 us; the launch traced here: 188 us
  starting transfers between devices  67.2 us (36%)
  other arithmetic  50.7 us (27%)
  local copies, waits for them, and re-layouts  30.7 us (16%)
  waiting for transfers between devices  30.2 us (16%)
  matrix products  5.92 us (3%)
  between operations  3.17 us (2%)
    ppermute x2, starting transfers between devices, x_faces(): after = lax.ppermute(x[:width], 'gx', down)  17.5 us
    add x1, other arithmetic, shards(): section_one = inner + time_step * local_rate(padded, speed_one)  15 us
    select_n x3, other arithmetic, part(): return jnp.where(flag > 0, advanced, level)  14.5 us
    add x1, other arithmetic, shards(): 0.75 * level_ext[:, 2 * SPAN:-2 * SPAN] + 0.25 * (inner + time_step * rate)  12.8 us
    ppermute x1, starting transfers between devices, shards(): after = lax.ppermute(first, 'gx', down)  12.3 us
    ppermute x3, starting transfers between devices, z_faces(): before = lax.ppermute(x[:, :, length - SPAN:], 'gz', up)  9.89 us
    ppermute x1, waiting for transfers between devices, shards(): y_after = lax.ppermute(first, 'gy', down)  9.28 us
    ppermute x3, starting transfers between devices, z_faces(): after = lax.ppermute(x[:, :, :SPAN], 'gz', down)  7.8 us
  transfers between devices with their start and end apart: 15, of which 8 were waited for; matrix products, arithmetic and copies ran while one was open for 8% of the time, Pallas kernels for 0%

profile of v11, /device:TPU:32, one launch (start us, length us, event | category | flops | bytes accessed | tf_op | source)
XLA Modules:
  0.0 187.9 jit_solution(517205348676524119)
XLA Ops:
  1.3 1.3 slice_convert_fusion.2
  2.9 1.5 fusion.460
  4.4 1.6 scatter.6
  6.0 2.3 %copy.7 = f32[4,32,10,128]{3,1,2,0:T(8,128)} copy(f32[4,32,10,128]{3,2,1,0:T(8,128)} %scatter.6) | data formatting | bytes 1310720 | tf_op jit(solution)/shard_map/scatter | solution.py:174
  8.3 4.9 %collective-permute-start = (f32[4,32,10,128]{3,1,2,0:T(8,128)}, f32[4,32,10,128]{3,1,2,0:T(8,128)S(1)}, u32[]{:S(2)}, u32[]{:S(2)}) collective-permute-start(f32[4,32,10,128]{3,1,2,0:T(8,128)} %copy.7), channel_id=1, source_target_pairs={{4,0},{8,4},{12,8},{0,12},{5,1},{9,5},{13,9},{1,13},{6,2},{10,6},{... | collective-permute-start | bytes 1966088 | tf_op jit(solution)/shard_map/ppermute | solution.py:176
  13.2 1.6 scatter.9
  14.9 1.4 copy.8
  16.3 1.9 %collective-permute-start.1 = (f32[4,32,10,128]{3,1,2,0:T(8,128)S(1)}, f32[4,32,10,128]{3,1,2,0:T(8,128)S(1)}, u32[]{:S(2)}, u32[]{:S(2)}) collective-permute-start(f32[4,32,10,128]{3,1,2,0:T(8,128)S(1)} %copy.8), channel_id=1, source_target_pairs={{0,4},{4,8},{8,12},{12,0},{1,5},{5,9},{9,13},{13,1},{2,6},{6,10},{... | collective-permute-start | bytes 1966088 | tf_op jit(solution)/shard_map/ppermute | solution.py:175
  18.2 9.3 %collective-permute-done = f32[4,32,10,128]{3,1,2,0:T(8,128)S(1)} collective-permute-done((f32[4,32,10,128]{3,1,2,0:T(8,128)}, f32[4,32,10,128]{3,1,2,0:T(8,128)S(1)}, u32[]{:S(2)}, u32[]{:S(2)}) %collective-permute-start) | collective-permute-done | bytes 655392 | tf_op jit(solution)/shard_map/ppermute | solution.py:176
  27.9 7.7 %collective-permute-done.1 = f32[4,32,10,128]{3,1,2,0:T(8,128)S(1)} collective-permute-done((f32[4,32,10,128]{3,1,2,0:T(8,128)S(1)}, f32[4,32,10,128]{3,1,2,0:T(8,128)S(1)}, u32[]{:S(2)}, u32[]{:S(2)}) %collective-permute-start.1) | collective-permute-done | bytes 655392 | tf_op jit(solution)/shard_map/ppermute | solution.py:175
  37.3 1.3 slice.1019
  39.1 1.2 compare_select_fusion.1
  42.9 12.3 %collective-permute-start.3 = (f32[7,46,128]{2,1,0:T(8,128)}, f32[7,46,128]{2,1,0:T(8,128)S(1)}, u32[]{:S(2)}, u32[]{:S(2)}) collective-permute-start(f32[7,46,128]{2,1,0:T(8,128)} %get-tuple-element.77), channel_id=1, source_target_pairs={{16,0},{32,16},{48,32},{64,48},{80,64},{96,80},{112,96},{128,112},... | collective-permute-start | bytes 494600 | tf_op jit(solution)/shard_map/ppermute | solution.py:198
  55.2 1.9 %collective-permute-start.2 = (f32[7,46,128]{2,1,0:T(8,128)}, f32[7,46,128]{2,1,0:T(8,128)}, u32[]{:S(2)}, u32[]{:S(2)}) collective-permute-start(f32[7,46,128]{2,1,0:T(8,128)} %get-tuple-element.78), channel_id=1, source_target_pairs={{0,16},{16,32},{32,48},{48,64},{64,80},{80,96},{96,112},{112,128},... | collective-permute-start | bytes 494600 | tf_op jit(solution)/shard_map/ppermute | solution.py:197
  57.8 2.9 %collective-permute-start.4 = (f32[32,46,3]{1,0,2:T(8,128)S(1)}, f32[32,46,3]{1,0,2:T(8,128)S(1)}, u32[]{:S(2)}, u32[]{:S(2)}) collective-permute-start(f32[32,46,3]{1,0,2:T(8,128)S(1)} %copy.11), channel_id=1, source_target_pairs={{0,1},{1,2},{2,3},{3,0},{4,5},{5,6},{6,7},{7,4},{8,9},{9,10},{10,1... | collective-permute-start | bytes 53000 | tf_op jit(solution)/shard_map/ppermute | solution.py:63
  61.1 2.9 %collective-permute-start.5 = (f32[32,46,3]{1,0,2:T(8,128)S(1)}, f32[32,46,3]{1,0,2:T(8,128)S(1)}, u32[]{:S(2)}, u32[]{:S(2)}) collective-permute-start(f32[32,46,3]{1,0,2:T(8,128)S(1)} %copy.13), channel_id=1, source_target_pairs={{1,0},{2,1},{3,2},{0,3},{5,4},{6,5},{7,6},{4,7},{9,8},{10,9},{11,1... | collective-permute-start | bytes 53000 | tf_op jit(solution)/shard_map/ppermute | solution.py:64
  64.1 1.3 copy.12
  65.3 1.7 collective-permute-done.5
  67.0 1.3 copy.14
  68.3 3.3 %collective-permute-done.2 = f32[7,46,128]{2,1,0:T(8,128)} collective-permute-done((f32[7,46,128]{2,1,0:T(8,128)}, f32[7,46,128]{2,1,0:T(8,128)}, u32[]{:S(2)}, u32[]{:S(2)}) %collective-permute-start.2) | collective-permute-done | bytes 164896 | tf_op jit(solution)/shard_map/ppermute | solution.py:197
  72.5 15.0 %fusion.21 = f32[32,46,128]{2,1,0:T(8,128)S(1)} fusion(f32[32,46,128]{2,1,0:T(8,128)S(1)} %slice.1025, f32[32,46,3]{2,1,0:T(8,128)} %copy.14, f32[32,46,3]{2,1,0:T(8,128)} %copy.12, f32[4,32,52,128]{3,2,1,0:T(8,128)} %copy-done, f32[32,52,128]{2,1,0:T(8,128)S(1)} %slice_bitcast_fusion, f32[3,46,128]{2,1,0:T(8,128)S(1)} %slice.1028, ...), kind=kLoop, calls=%fused_computation.100 | loop fusion | flops 79511552 | bytes 8466944 | tf_op jit(solution)/shard_map/add | solution.py:204
  87.5 7.9 %collective-permute-start.7 = (f32[3,40,128]{2,1,0:T(8,128)S(1)}, f32[3,40,128]{2,1,0:T(8,128)S(1)}, u32[]{:S(2)}, u32[]{:S(2)}) collective-permute-start(f32[3,40,128]{2,1,0:T(8,128)S(1)} %get-tuple-element.56), channel_id=1, source_target_pairs={{16,0},{32,16},{48,32},{64,48},{80,64},{96,80},{112,96},{128,112},... | collective-permute-start | bytes 184328 | tf_op jit(solution)/shard_map/ppermute | solution.py:155
  95.4 1.9 %collective-permute-start.6 = (f32[3,40,128]{2,1,0:T(8,128)S(1)}, f32[3,40,128]{2,1,0:T(8,128)S(1)}, u32[]{:S(2)}, u32[]{:S(2)}) collective-permute-start(f32[3,40,128]{2,1,0:T(8,128)S(1)} %get-tuple-element.57), channel_id=1, source_target_pairs={{0,16},{16,32},{32,48},{48,64},{64,80},{80,96},{96,112},{112,128},... | collective-permute-start | bytes 184328 | tf_op jit(solution)/shard_map/ppermute | solution.py:154
  97.9 3.2 %collective-permute-start.8 = (f32[32,40,3]{1,0,2:T(8,128)S(1)}, f32[32,40,3]{1,0,2:T(8,128)S(1)}, u32[]{:S(2)}, u32[]{:S(2)}) collective-permute-start(f32[32,40,3]{1,0,2:T(8,128)S(1)} %copy.15), channel_id=1, source_target_pairs={{0,1},{1,2},{2,3},{3,0},{4,5},{5,6},{6,7},{7,4},{8,9},{9,10},{10,1... | collective-permute-start | bytes 46088 | tf_op jit(solution)/shard_map/ppermute | solution.py:63
  101.1 0.9 copy.17
  102.0 2.6 %collective-permute-start.9 = (f32[32,40,3]{1,0,2:T(8,128)}, f32[32,40,3]{1,0,2:T(8,128)S(1)}, u32[]{:S(2)}, u32[]{:S(2)}) collective-permute-start(f32[32,40,3]{1,0,2:T(8,128)} %copy.17), channel_id=1, source_target_pairs={{1,0},{2,1},{3,2},{0,3},{5,4},{6,5},{7,6},{4,7},{9,8},{10,9},{11,1... | collective-permute-start | bytes 46088 | tf_op jit(solution)/shard_map/ppermute | solution.py:64
  104.7 1.1 copy.16
  105.8 2.4 %collective-permute-done.9 = f32[32,40,3]{1,0,2:T(8,128)S(1)} collective-permute-done((f32[32,40,3]{1,0,2:T(8,128)}, f32[32,40,3]{1,0,2:T(8,128)S(1)}, u32[]{:S(2)}, u32[]{:S(2)}) %collective-permute-start.9) | collective-permute-done | bytes 15392 | tf_op jit(solution)/shard_map/ppermute | solution.py:64
  108.2 1.1 copy.18
  109.4 12.8 %fusion.174 = f32[32,40,128]{2,1,0:T(8,128)S(1)} fusion(f32[32,52,128]{2,1,0:T(8,128)S(1)} %slice_bitcast_fusion, f32[32,40,128]{2,1,0:T(8,128)S(1)} %slice.1057, f32[32,40,3]{2,1,0:T(8,128)} %copy.18, f32[32,40,3]{2,1,0:T(8,128)} %copy.16, f32[4,32,52,128]{3,2,1,0:T(8,128)} %copy-done, f32[32,46,128]{2,1,0:T(8,128)S(1)} %fusion.21, ...), kind=kLoop, calls=%fused_computation.300 | loop fusion | flops 69632000 | bytes 8017920 | tf_op jit(solution)/shard_map/add | solution.py:206
  122.2 1.9 %collective-permute-start.10 = (f32[4,40,128]{2,1,0:T(8,128)S(1)}, f32[4,40,128]{2,1,0:T(8,128)S(1)}, u32[]{:S(2)}, u32[]{:S(2)}) collective-permute-start(f32[4,40,128]{2,1,0:T(8,128)S(1)} %get-tuple-element.69), channel_id=1, source_target_pairs={{0,16},{16,32},{32,48},{48,64},{64,80},{80,96},{96,112},{112,128},... | collective-permute-start | bytes 245768 | tf_op jit(solution)/shard_map/ppermute | solution.py:154
  124.2 9.7 %collective-permute-start.11 = (f32[4,40,128]{2,1,0:T(8,128)S(1)}, f32[4,40,128]{2,1,0:T(8,128)S(1)}, u32[]{:S(2)}, u32[]{:S(2)}) collective-permute-start(f32[4,40,128]{2,1,0:T(8,128)S(1)} %get-tuple-element.70), channel_id=1, source_target_pairs={{16,0},{32,16},{48,32},{64,48},{80,64},{96,80},{112,96},{128,112},... | collective-permute-start | bytes 245768 | tf_op jit(solution)/shard_map/ppermute | solution.py:155
  136.2 1.1 fusion.462
  137.3 1.5 copy.19
  139.2 2.3 %collective-permute-start.13 = (f32[34,34,3]{1,0,2:T(8,128)S(1)}, f32[34,34,3]{1,0,2:T(8,128)S(1)}, u32[]{:S(2)}, u32[]{:S(2)}) collective-permute-start(f32[34,34,3]{1,0,2:T(8,128)S(1)} %copy.21), channel_id=1, source_target_pairs={{1,0},{2,1},{3,2},{0,3},{5,4},{6,5},{7,6},{4,7},{9,8},{10,9},{11,1... | collective-permute-start | bytes 41624 | tf_op jit(solution)/shard_map/ppermute | solution.py:64
  141.5 3.7 %collective-permute-start.12 = (f32[34,34,3]{1,0,2:T(8,128)S(1)}, f32[34,34,3]{1,0,2:T(8,128)S(1)}, u32[]{:S(2)}, u32[]{:S(2)}) collective-permute-start(f32[34,34,3]{1,0,2:T(8,128)S(1)} %copy.19), channel_id=1, source_target_pairs={{0,1},{1,2},{2,3},{3,0},{4,5},{5,6},{6,7},{7,4},{8,9},{9,10},{10,1... | collective-permute-start | bytes 41624 | tf_op jit(solution)/shard_map/ppermute | solution.py:63
  145.2 1.2 fusion.442
  147.4 1.6 collective-permute-done.12
  149.8 1.4 add_select_fusion
  151.2 1.3 add_select_fusion.1
  152.5 11.8 %fusion.181 = f32[32,34,128]{2,1,0:T(8,128)S(1)} fusion(f32[34,34,3]{2,1,0:T(8,128)S(1)} %copy.22, f32[34,34,128]{2,1,0:T(8,128)S(1)} %copy-done.3, f32[34,34,3]{2,1,0:T(8,128)S(1)} %copy.20, f32[4,32,52,128]{3,2,1,0:T(8,128)S(1)} %copy-done.1, f32[32,40,128]{2,1,0:T(8,128)S(1)} %fusion.174, f32[4,40,128]{2,1,0:T(8,128)S(1)} %collective-permute-done.11, ...), kind=kLoop, calls=%fused_computation.308 | loop fusion | flops 59326464 | bytes 10674688 | tf_op jit(solution)/shard_map/jit(_where)/select_n | solution.py:220
  165.2 1.2 multiply_reduce_fusion.3
  166.4 1.2 multiply_reduce_fusion.1
  167.5 1.2 multiply_reduce_fusion.5
  168.7 1.2 multiply_reduce_fusion.7
  170.0 1.3 copy.23
  172.8 7.1 %all-to-all-start = ((f32[4,1,4096]{2,1,0:T(1,128)}), f32[4,1,4096]{2,1,0:T(1,128)S(1)}, u32[]{:S(2)}, u32[]{:S(2)}) async-start(f32[4,1,4096]{2,1,0:T(1,128)} %reshape.219), calls=%async_computation | async-start | bytes 131072 | tf_op jit(solution)/shard_map/all_to_all | solution.py:253
  180.7 3.8 %all-to-all-done = f32[4,1,4096]{2,1,0:T(1,128)S(1)} async-done(((f32[4,1,4096]{2,1,0:T(1,128)}), f32[4,1,4096]{2,1,0:T(1,128)S(1)}, u32[]{:S(2)}, u32[]{:S(2)}) %all-to-all-start) | async-done | bytes 65568 | tf_op jit(solution)/shard_map/all_to_all | solution.py:253
  (79 shorter events, 17.6 us)
Async XLA Ops:
  0.6 2.0 %copy-start.2 = (f32[32,32,128]{2,1,0:T(8,128)S(1)}, f32[32,32,128]{2,1,0:T(8,128)}, u32[]{:S(2)}) copy-start(f32[32,32,128]{2,1,0:T(8,128)} %param.8) | copy-start | bytes 1572868
  8.3 19.2 %collective-permute-start = (f32[4,32,10,128]{3,1,2,0:T(8,128)}, f32[4,32,10,128]{3,1,2,0:T(8,128)S(1)}, u32[]{:S(2)}, u32[]{:S(2)}) collective-permute-start(f32[4,32,10,128]{3,1,2,0:T(8,128)} %copy.7), channel_id=1, source_target_pairs={{4,0},{8,4},{12,8},{0,12},{5,1},{9,5},{13,9},{1,13},{6,2},{10,6},{... | collective-permute-start | bytes 1966088 | tf_op jit(solution)/shard_map/ppermute | solution.py:176
  16.3 19.3 %collective-permute-start.1 = (f32[4,32,10,128]{3,1,2,0:T(8,128)S(1)}, f32[4,32,10,128]{3,1,2,0:T(8,128)S(1)}, u32[]{:S(2)}, u32[]{:S(2)}) collective-permute-start(f32[4,32,10,128]{3,1,2,0:T(8,128)S(1)} %copy.8), channel_id=1, source_target_pairs={{0,4},{4,8},{8,12},{12,0},{1,5},{5,9},{9,13},{13,1},{2,6},{6,10},{... | collective-permute-start | bytes 1966088 | tf_op jit(solution)/shard_map/ppermute | solution.py:175
  27.5 8.5 %copy-start.6 = (f32[4,32,10,128]{3,1,2,0:T(8,128)}, f32[4,32,10,128]{3,1,2,0:T(8,128)S(1)}, u32[]{:S(2)}) copy-start(f32[4,32,10,128]{3,1,2,0:T(8,128)S(1)} %collective-permute-done) | copy-start | bytes 1966084
  36.4 4.5 %copy-start = (f32[4,32,52,128]{3,2,1,0:T(8,128)}, f32[4,32,52,128]{3,2,1,0:T(8,128)S(1)}, u32[]{:S(2)}) copy-start(f32[4,32,52,128]{3,2,1,0:T(8,128)S(1)} %pad_maximum_fusion) | copy-start | bytes 10223620
  42.9 25.4 %collective-permute-start.3 = (f32[7,46,128]{2,1,0:T(8,128)}, f32[7,46,128]{2,1,0:T(8,128)S(1)}, u32[]{:S(2)}, u32[]{:S(2)}) collective-permute-start(f32[7,46,128]{2,1,0:T(8,128)} %get-tuple-element.77), channel_id=1, source_target_pairs={{16,0},{32,16},{48,32},{64,48},{80,64},{96,80},{112,96},{128,112},... | collective-permute-start | bytes 494600 | tf_op jit(solution)/shard_map/ppermute | solution.py:198
  55.2 16.4 %collective-permute-start.2 = (f32[7,46,128]{2,1,0:T(8,128)}, f32[7,46,128]{2,1,0:T(8,128)}, u32[]{:S(2)}, u32[]{:S(2)}) collective-permute-start(f32[7,46,128]{2,1,0:T(8,128)} %get-tuple-element.78), channel_id=1, source_target_pairs={{0,16},{16,32},{32,48},{48,64},{64,80},{80,96},{96,112},{112,128},... | collective-permute-start | bytes 494600 | tf_op jit(solution)/shard_map/ppermute | solution.py:197
  57.8 6.3 %collective-permute-start.4 = (f32[32,46,3]{1,0,2:T(8,128)S(1)}, f32[32,46,3]{1,0,2:T(8,128)S(1)}, u32[]{:S(2)}, u32[]{:S(2)}) collective-permute-start(f32[32,46,3]{1,0,2:T(8,128)S(1)} %copy.11), channel_id=1, source_target_pairs={{0,1},{1,2},{2,3},{3,0},{4,5},{5,6},{6,7},{7,4},{8,9},{9,10},{10,1... | collective-permute-start | bytes 53000 | tf_op jit(solution)/shard_map/ppermute | solution.py:63
  61.1 6.0 %collective-permute-start.5 = (f32[32,46,3]{1,0,2:T(8,128)S(1)}, f32[32,46,3]{1,0,2:T(8,128)S(1)}, u32[]{:S(2)}, u32[]{:S(2)}) collective-permute-start(f32[32,46,3]{1,0,2:T(8,128)S(1)} %copy.13), channel_id=1, source_target_pairs={{1,0},{2,1},{3,2},{0,3},{5,4},{6,5},{7,6},{4,7},{9,8},{10,9},{11,1... | collective-permute-start | bytes 53000 | tf_op jit(solution)/shard_map/ppermute | solution.py:64
  87.5 21.8 %collective-permute-start.7 = (f32[3,40,128]{2,1,0:T(8,128)S(1)}, f32[3,40,128]{2,1,0:T(8,128)S(1)}, u32[]{:S(2)}, u32[]{:S(2)}) collective-permute-start(f32[3,40,128]{2,1,0:T(8,128)S(1)} %get-tuple-element.56), channel_id=1, source_target_pairs={{16,0},{32,16},{48,32},{64,48},{80,64},{96,80},{112,96},{128,112},... | collective-permute-start | bytes 184328 | tf_op jit(solution)/shard_map/ppermute | solution.py:155
  95.4 13.9 %collective-permute-start.6 = (f32[3,40,128]{2,1,0:T(8,128)S(1)}, f32[3,40,128]{2,1,0:T(8,128)S(1)}, u32[]{:S(2)}, u32[]{:S(2)}) collective-permute-start(f32[3,40,128]{2,1,0:T(8,128)S(1)} %get-tuple-element.57), channel_id=1, source_target_pairs={{0,16},{16,32},{32,48},{48,64},{64,80},{80,96},{96,112},{112,128},... | collective-permute-start | bytes 184328 | tf_op jit(solution)/shard_map/ppermute | solution.py:154
  97.9 6.8 %collective-permute-start.8 = (f32[32,40,3]{1,0,2:T(8,128)S(1)}, f32[32,40,3]{1,0,2:T(8,128)S(1)}, u32[]{:S(2)}, u32[]{:S(2)}) collective-permute-start(f32[32,40,3]{1,0,2:T(8,128)S(1)} %copy.15), channel_id=1, source_target_pairs={{0,1},{1,2},{2,3},{3,0},{4,5},{5,6},{6,7},{7,4},{8,9},{9,10},{10,1... | collective-permute-start | bytes 46088 | tf_op jit(solution)/shard_map/ppermute | solution.py:63
  102.0 6.2 %collective-permute-start.9 = (f32[32,40,3]{1,0,2:T(8,128)}, f32[32,40,3]{1,0,2:T(8,128)S(1)}, u32[]{:S(2)}, u32[]{:S(2)}) collective-permute-start(f32[32,40,3]{1,0,2:T(8,128)} %copy.17), channel_id=1, source_target_pairs={{1,0},{2,1},{3,2},{0,3},{5,4},{6,5},{7,6},{4,7},{9,8},{10,9},{11,1... | collective-permute-start | bytes 46088 | tf_op jit(solution)/shard_map/ppermute | solution.py:64
  109.3 24.5 %copy-start.7 = (s32[4]{0:T(128)S(1)}, s32[4]{0:T(128)}, u32[]{:S(2)}) copy-start(s32[4]{0:T(128)} %param.11) | copy-start | bytes 52
  122.2 13.5 %collective-permute-start.10 = (f32[4,40,128]{2,1,0:T(8,128)S(1)}, f32[4,40,128]{2,1,0:T(8,128)S(1)}, u32[]{:S(2)}, u32[]{:S(2)}) collective-permute-start(f32[4,40,128]{2,1,0:T(8,128)S(1)} %get-tuple-element.69), channel_id=1, source_target_pairs={{0,16},{16,32},{32,48},{48,64},{64,80},{80,96},{96,112},{112,128},... | collective-permute-start | bytes 245768 | tf_op jit(solution)/shard_map/ppermute | solution.py:154
  124.2 12.0 %collective-permute-start.11 = (f32[4,40,128]{2,1,0:T(8,128)S(1)}, f32[4,40,128]{2,1,0:T(8,128)S(1)}, u32[]{:S(2)}, u32[]{:S(2)}) collective-permute-start(f32[4,40,128]{2,1,0:T(8,128)S(1)} %get-tuple-element.70), channel_id=1, source_target_pairs={{16,0},{32,16},{48,32},{64,48},{80,64},{96,80},{112,96},{128,112},... | collective-permute-start | bytes 245768 | tf_op jit(solution)/shard_map/ppermute | solution.py:155
  139.2 10.2 %collective-permute-start.13 = (f32[34,34,3]{1,0,2:T(8,128)S(1)}, f32[34,34,3]{1,0,2:T(8,128)S(1)}, u32[]{:S(2)}, u32[]{:S(2)}) collective-permute-start(f32[34,34,3]{1,0,2:T(8,128)S(1)} %copy.21), channel_id=1, source_target_pairs={{1,0},{2,1},{3,2},{0,3},{5,4},{6,5},{7,6},{4,7},{9,8},{10,9},{11,1... | collective-permute-start | bytes 41624 | tf_op jit(solution)/shard_map/ppermute | solution.py:64
  141.5 7.5 %collective-permute-start.12 = (f32[34,34,3]{1,0,2:T(8,128)S(1)}, f32[34,34,3]{1,0,2:T(8,128)S(1)}, u32[]{:S(2)}, u32[]{:S(2)}) collective-permute-start(f32[34,34,3]{1,0,2:T(8,128)S(1)} %copy.19), channel_id=1, source_target_pairs={{0,1},{1,2},{2,3},{3,0},{4,5},{5,6},{6,7},{7,4},{8,9},{9,10},{10,1... | collective-permute-start | bytes 41624 | tf_op jit(solution)/shard_map/ppermute | solution.py:63
  149.8 2.8 %copy-start.1 = (f32[4,32,52,128]{3,2,1,0:T(8,128)S(1)}, f32[4,32,52,128]{3,2,1,0:T(8,128)}, u32[]{:S(2)}) copy-start(f32[4,32,52,128]{3,2,1,0:T(8,128)} %copy-done) | copy-start | bytes 10223620
  149.8 2.8 %copy-start.3 = (f32[34,34,128]{2,1,0:T(8,128)S(1)}, f32[34,34,128]{2,1,0:T(8,128)}, u32[]{:S(2)}) copy-start(f32[34,34,128]{2,1,0:T(8,128)} %slice.1108) | copy-start | bytes 1775620
  164.3 0.8 copy-start.4
  170.0 9.8 %copy-start.5 = (f32[32,34,128]{2,1,0:T(8,128)S(1)}, f32[32,34,128]{2,1,0:T(8,128)}, u32[]{:S(2)}) copy-start(f32[32,34,128]{2,1,0:T(8,128)} %copy-done.4) | copy-start | bytes 1671172
  172.8 11.7 %all-to-all-start = ((f32[4,1,4096]{2,1,0:T(1,128)}), f32[4,1,4096]{2,1,0:T(1,128)S(1)}, u32[]{:S(2)}, u32[]{:S(2)}) async-start(f32[4,1,4096]{2,1,0:T(1,128)} %reshape.219), calls=%async_computation | async-start | bytes 131072 | tf_op jit(solution)/shard_map/all_to_all | solution.py:253

commit v12 on v10

--- a/solution.py
+++ b/solution.py
@@ -246,8 +246,8 @@
         0,
     )
     for rank_value in range(group):
-        chooser = (depth_order == rank_value).astype(jnp.float32)
-        piece_now = jnp.einsum("s,csij->cij", chooser, received, precision=lax.Precision.HIGHEST)
+        slab_index = jnp.sum(jnp.where(depth_order == rank_value, jnp.arange(group), 0))
+        piece_now = lax.dynamic_index_in_dim(received, slab_index, axis=1, keepdims=False)
         blended = over(blended, piece_now)
     image = jnp.concatenate([blended[:3], 1.0 - blended[3:]], 0)
     return (level_out, image)

time: 188 us -> 188 us (level)
  the two profiles are of different devices: /device:TPU:135 before, /device:TPU:143 now
where the time goes in v12:
time: 188 us; the launch traced here: 187 us
  starting transfers between devices  67.6 us (36%)
  other arithmetic  50.5 us (27%)
  waiting for transfers between devices  31.5 us (17%)
  local copies, waits for them, and re-layouts  22.6 us (12%)
  between operations  10.7 us (6%)
  matrix products  4.65 us (2%)
    ppermute x2, starting transfers between devices, x_faces(): before = lax.ppermute(x[length - width:], 'gx', up)  20.9 us
    ppermute x1, waiting for transfers between devices, exchange(): before = lax.ppermute(last, axis, up)  15.5 us
    ppermute x3, starting transfers between devices, z_faces(): after = lax.ppermute(x[:, :, :SPAN], 'gz', down)  15.4 us
    select_n x3, other arithmetic, part(): return jnp.where(flag > 0, advanced, level)  15.1 us
    add x1, other arithmetic, shards(): section_one = inner + time_step * local_rate(padded, speed_one)  15 us
    add x1, other arithmetic, shards(): 0.75 * level_ext[:, 2 * SPAN:-2 * SPAN] + 0.25 * (inner + time_step * rate)  13 us
    ppermute x1, starting transfers between devices, shards(): before = lax.ppermute(last, 'gx', up)  10.4 us
    ppermute x2, waiting for transfers between devices, x_faces(): after = lax.ppermute(x[:width], 'gx', down)  9.96 us
  transfers between devices with their start and end apart: 15, of which 6 were waited for; matrix products, arithmetic and copies ran while one was open for 7% of the time, Pallas kernels for 0%

profile of v12, /device:TPU:143, one launch (start us, length us, event | category | flops | bytes accessed | tf_op | source)
XLA Modules:
  0.0 187.5 jit_solution(6379482429368090631)
XLA Ops:
  1.4 1.1 bitcast_dynamic-update-slice_fusion
  2.4 1.0 convert_dynamic-update-slice_fusion.2
  4.1 3.2 %collective-permute-start = (f32[5,32,10,128]{3,1,2,0:T(8,128)S(1)}, f32[5,32,10,128]{3,1,2,0:T(8,128)S(1)}, u32[]{:S(2)}, u32[]{:S(2)}) collective-permute-start(f32[5,32,10,128]{3,1,2,0:T(8,128)S(1)} %copy.23), channel_id=1, source_target_pairs={{0,4},{4,8},{8,12},{12,0},{1,5},{5,9},{9,13},{13,1},{2,6},{6,10},{... | collective-permute-start | bytes 2457608 | tf_op jit(solution)/shard_map/ppermute | solution.py:23
  7.6 2.1 %collective-permute-start.1 = (f32[5,32,10,128]{3,1,2,0:T(8,128)S(1)}, f32[5,32,10,128]{3,1,2,0:T(8,128)S(1)}, u32[]{:S(2)}, u32[]{:S(2)}) collective-permute-start(f32[5,32,10,128]{3,1,2,0:T(8,128)S(1)} %copy.24), channel_id=1, source_target_pairs={{4,0},{8,4},{12,8},{0,12},{5,1},{9,5},{13,9},{1,13},{6,2},{10,6},{... | collective-permute-start | bytes 2457608 | tf_op jit(solution)/shard_map/ppermute | solution.py:24
  9.7 15.5 %collective-permute-done = f32[5,32,10,128]{3,1,2,0:T(8,128)S(1)} collective-permute-done((f32[5,32,10,128]{3,1,2,0:T(8,128)S(1)}, f32[5,32,10,128]{3,1,2,0:T(8,128)S(1)}, u32[]{:S(2)}, u32[]{:S(2)}) %collective-permute-start) | collective-permute-done | bytes 819232 | tf_op jit(solution)/shard_map/ppermute | solution.py:23
  25.6 2.7 %collective-permute-done.1 = f32[5,32,10,128]{3,1,2,0:T(8,128)S(1)} collective-permute-done((f32[5,32,10,128]{3,1,2,0:T(8,128)S(1)}, f32[5,32,10,128]{3,1,2,0:T(8,128)S(1)}, u32[]{:S(2)}, u32[]{:S(2)}) %collective-permute-start.1) | collective-permute-done | bytes 819232 | tf_op jit(solution)/shard_map/ppermute | solution.py:24
  29.5 0.8 slice_dynamic-update-slice_fusion
  30.2 1.1 constant_dynamic-update-slice_fusion.7
  31.5 0.6 constant_dynamic-update-slice_fusion.6
  33.4 10.4 %collective-permute-start.2 = (f32[7,46,128]{2,1,0:T(8,128)}, f32[7,46,128]{2,1,0:T(8,128)S(1)}, u32[]{:S(2)}, u32[]{:S(2)}) collective-permute-start(f32[7,46,128]{2,1,0:T(8,128)} %get-tuple-element.29), channel_id=1, source_target_pairs={{0,16},{16,32},{32,48},{48,64},{64,80},{80,96},{96,112},{112,128},... | collective-permute-start | bytes 494600 | tf_op jit(solution)/shard_map/ppermute | solution.py:184
  43.8 1.9 %collective-permute-start.3 = (f32[7,46,128]{2,1,0:T(8,128)}, f32[7,46,128]{2,1,0:T(8,128)}, u32[]{:S(2)}, u32[]{:S(2)}) collective-permute-start(f32[7,46,128]{2,1,0:T(8,128)} %get-tuple-element.28), channel_id=1, source_target_pairs={{16,0},{32,16},{48,32},{64,48},{80,64},{96,80},{112,96},{128,112},... | collective-permute-start | bytes 494600 | tf_op jit(solution)/shard_map/ppermute | solution.py:185
  46.4 2.6 %collective-permute-start.4 = (f32[32,46,3]{1,0,2:T(8,128)S(1)}, f32[32,46,3]{1,0,2:T(8,128)S(1)}, u32[]{:S(2)}, u32[]{:S(2)}) collective-permute-start(f32[32,46,3]{1,0,2:T(8,128)S(1)} %copy.27), channel_id=1, source_target_pairs={{0,1},{1,2},{2,3},{3,0},{4,5},{5,6},{6,7},{7,4},{8,9},{9,10},{10,1... | collective-permute-start | bytes 53000 | tf_op jit(solution)/shard_map/ppermute | solution.py:63
  49.4 4.4 %collective-permute-start.5 = (f32[32,46,3]{1,0,2:T(8,128)S(1)}, f32[32,46,3]{1,0,2:T(8,128)S(1)}, u32[]{:S(2)}, u32[]{:S(2)}) collective-permute-start(f32[32,46,3]{1,0,2:T(8,128)S(1)} %copy.29), channel_id=1, source_target_pairs={{1,0},{2,1},{3,2},{0,3},{5,4},{6,5},{7,6},{4,7},{9,8},{10,9},{11,1... | collective-permute-start | bytes 53000 | tf_op jit(solution)/shard_map/ppermute | solution.py:64
  53.9 1.3 copy.28
  55.2 1.3 copy.30
  56.4 3.0 %collective-permute-done.3 = f32[7,46,128]{2,1,0:T(8,128)} collective-permute-done((f32[7,46,128]{2,1,0:T(8,128)}, f32[7,46,128]{2,1,0:T(8,128)}, u32[]{:S(2)}, u32[]{:S(2)}) %collective-permute-start.3) | collective-permute-done | bytes 164896 | tf_op jit(solution)/shard_map/ppermute | solution.py:185
  59.5 0.9 slice.1011
  60.4 15.0 %fusion.21 = f32[32,46,128]{2,1,0:T(8,128)S(1)} fusion(f32[32,46,128]{2,1,0:T(8,128)S(1)} %slice.1002, f32[32,46,3]{2,1,0:T(8,128)} %copy.30, f32[32,46,3]{2,1,0:T(8,128)} %copy.28, f32[5,32,52,128]{3,2,1,0:T(8,128)} %copy-done, f32[32,52,128]{2,1,0:T(8,128)S(1)} %slice_bitcast_fusion, f32[3,46,128]{2,1,0:T(8,128)S(1)} %slice.1005, f32[3,46,128]{2,1,0:T(8,128)S(1)} %slice.1011), kind=kLoop, calls=%fused_computation.99 | loop fusion | flops 79511552 | bytes 8466944 | tf_op jit(solution)/shard_map/add | solution.py:191
  75.4 10.1 %collective-permute-start.6 = (f32[3,40,128]{2,1,0:T(8,128)S(1)}, f32[3,40,128]{2,1,0:T(8,128)S(1)}, u32[]{:S(2)}, u32[]{:S(2)}) collective-permute-start(f32[3,40,128]{2,1,0:T(8,128)S(1)} %get-tuple-element.45), channel_id=1, source_target_pairs={{0,16},{16,32},{32,48},{48,64},{64,80},{80,96},{96,112},{112,128},... | collective-permute-start | bytes 184328 | tf_op jit(solution)/shard_map/ppermute | solution.py:154
  85.5 1.9 %collective-permute-start.7 = (f32[3,40,128]{2,1,0:T(8,128)S(1)}, f32[3,40,128]{2,1,0:T(8,128)S(1)}, u32[]{:S(2)}, u32[]{:S(2)}) collective-permute-start(f32[3,40,128]{2,1,0:T(8,128)S(1)} %get-tuple-element.44), channel_id=1, source_target_pairs={{16,0},{32,16},{48,32},{64,48},{80,64},{96,80},{112,96},{128,112},... | collective-permute-start | bytes 184328 | tf_op jit(solution)/shard_map/ppermute | solution.py:155
  88.0 1.9 %collective-permute-start.8 = (f32[32,40,3]{1,0,2:T(8,128)S(1)}, f32[32,40,3]{1,0,2:T(8,128)S(1)}, u32[]{:S(2)}, u32[]{:S(2)}) collective-permute-start(f32[32,40,3]{1,0,2:T(8,128)S(1)} %copy.31), channel_id=1, source_target_pairs={{0,1},{1,2},{2,3},{3,0},{4,5},{5,6},{6,7},{7,4},{8,9},{9,10},{10,1... | collective-permute-start | bytes 46088 | tf_op jit(solution)/shard_map/ppermute | solution.py:63
  89.9 0.9 copy.33
  90.8 5.1 %collective-permute-start.9 = (f32[32,40,3]{1,0,2:T(8,128)}, f32[32,40,3]{1,0,2:T(8,128)S(1)}, u32[]{:S(2)}, u32[]{:S(2)}) collective-permute-start(f32[32,40,3]{1,0,2:T(8,128)} %copy.33), channel_id=1, source_target_pairs={{1,0},{2,1},{3,2},{0,3},{5,4},{6,5},{7,6},{4,7},{9,8},{10,9},{11,1... | collective-permute-start | bytes 46088 | tf_op jit(solution)/shard_map/ppermute | solution.py:64
  96.1 1.2 copy.32
  97.5 1.2 copy.34
  98.6 13.0 %fusion.174 = f32[32,40,128]{2,1,0:T(8,128)S(1)} fusion(f32[32,52,128]{2,1,0:T(8,128)S(1)} %slice_bitcast_fusion, f32[32,40,128]{2,1,0:T(8,128)S(1)} %slice.1034, f32[32,40,3]{2,1,0:T(8,128)} %copy.34, f32[32,40,3]{2,1,0:T(8,128)} %copy.32, f32[5,32,52,128]{3,2,1,0:T(8,128)} %copy-done, f32[32,46,128]{2,1,0:T(8,128)S(1)} %fusion.21, ...), kind=kLoop, calls=%fused_computation.299 | loop fusion | flops 69632000 | bytes 8017920 | tf_op jit(solution)/shard_map/add | solution.py:193
  111.7 10.8 %collective-permute-start.10 = (f32[4,40,128]{2,1,0:T(8,128)S(1)}, f32[4,40,128]{2,1,0:T(8,128)S(1)}, u32[]{:S(2)}, u32[]{:S(2)}) collective-permute-start(f32[4,40,128]{2,1,0:T(8,128)S(1)} %get-tuple-element.54), channel_id=1, source_target_pairs={{0,16},{16,32},{32,48},{48,64},{64,80},{80,96},{96,112},{112,128},... | collective-permute-start | bytes 245768 | tf_op jit(solution)/shard_map/ppermute | solution.py:154
  122.5 1.9 %collective-permute-start.11 = (f32[4,40,128]{2,1,0:T(8,128)S(1)}, f32[4,40,128]{2,1,0:T(8,128)S(1)}, u32[]{:S(2)}, u32[]{:S(2)}) collective-permute-start(f32[4,40,128]{2,1,0:T(8,128)S(1)} %get-tuple-element.55), channel_id=1, source_target_pairs={{16,0},{32,16},{48,32},{64,48},{80,64},{96,80},{112,96},{128,112},... | collective-permute-start | bytes 245768 | tf_op jit(solution)/shard_map/ppermute | solution.py:155
  124.5 10.0 %collective-permute-done.11 = f32[4,40,128]{2,1,0:T(8,128)S(1)} collective-permute-done((f32[4,40,128]{2,1,0:T(8,128)S(1)}, f32[4,40,128]{2,1,0:T(8,128)S(1)}, u32[]{:S(2)}, u32[]{:S(2)}) %collective-permute-start.11) | collective-permute-done | bytes 81952 | tf_op jit(solution)/shard_map/ppermute | solution.py:155
  134.5 1.1 fusion.439
  135.6 1.5 copy.35
  137.1 1.9 %collective-permute-start.12 = (f32[34,34,3]{1,0,2:T(8,128)S(1)}, f32[34,34,3]{1,0,2:T(8,128)S(1)}, u32[]{:S(2)}, u32[]{:S(2)}) collective-permute-start(f32[34,34,3]{1,0,2:T(8,128)S(1)} %copy.35), channel_id=1, source_target_pairs={{0,1},{1,2},{2,3},{3,0},{4,5},{5,6},{6,7},{7,4},{8,9},{9,10},{10,1... | collective-permute-start | bytes 41624 | tf_op jit(solution)/shard_map/ppermute | solution.py:63
  139.0 1.0 copy.37
  140.0 5.8 %collective-permute-start.13 = (f32[34,34,3]{1,0,2:T(8,128)}, f32[34,34,3]{1,0,2:T(8,128)S(1)}, u32[]{:S(2)}, u32[]{:S(2)}) collective-permute-start(f32[34,34,3]{1,0,2:T(8,128)} %copy.37), channel_id=1, source_target_pairs={{1,0},{2,1},{3,2},{0,3},{5,4},{6,5},{7,6},{4,7},{9,8},{10,9},{11,1... | collective-permute-start | bytes 41624 | tf_op jit(solution)/shard_map/ppermute | solution.py:64
  147.7 0.9 slice.1085
  149.3 1.5 add_select_fusion
  151.2 13.2 %fusion.181 = f32[32,34,128]{2,1,0:T(8,128)S(1)} fusion(f32[34,34,3]{2,1,0:T(8,128)S(1)} %copy.38, f32[34,34,128]{2,1,0:T(8,128)S(1)} %copy-done.1, f32[34,34,3]{2,1,0:T(8,128)S(1)} %copy.36, f32[5,32,52,128]{3,2,1,0:T(8,128)} %copy-done, f32[32,40,128]{2,1,0:T(8,128)S(1)} %fusion.174, f32[4,40,128]{2,1,0:T(8,128)S(1)} %collective-permute-done.11, ...), kind=kLoop, calls=%fused_computation.308 | loop fusion | flops 59465728 | bytes 10936320 | tf_op jit(solution)/shard_map/jit(_where)/select_n | solution.py:207
  165.2 1.2 multiply_reduce_fusion.7
  166.4 1.2 multiply_reduce_fusion.5
  167.6 1.2 multiply_reduce_fusion.3
  168.8 1.2 multiply_reduce_fusion.1
  170.1 1.3 copy.39
  171.4 0.7 copy.40
  172.1 0.8 reshape.189
  172.8 3.3 %all-to-all-start = ((f32[4,1,4096]{2,1,0:T(1,128)}), f32[4,1,4096]{2,1,0:T(1,128)S(1)}, u32[]{:S(2)}, u32[]{:S(2)}) async-start(f32[4,1,4096]{2,1,0:T(1,128)} %reshape.189), calls=%async_computation | async-start | bytes 131072 | tf_op jit(solution)/shard_map/all_to_all | solution.py:240
  176.1 0.7 fusion.426
  184.5 0.9 slice.1099
  185.9 0.8 reduce
  (70 shorter events, 9.9 us)
Async XLA Ops:
  0.6 2.8 %copy-start.4 = (bf16[3,32,32,128]{3,2,1,0:T(8,128)(2,1)S(1)}, bf16[3,32,32,128]{3,2,1,0:T(8,128)(2,1)}, u32[]{:S(2)}) copy-start(bf16[3,32,32,128]{3,2,1,0:T(8,128)(2,1)} %param.5) | copy-start | bytes 2359300
  4.1 21.0 %collective-permute-start = (f32[5,32,10,128]{3,1,2,0:T(8,128)S(1)}, f32[5,32,10,128]{3,1,2,0:T(8,128)S(1)}, u32[]{:S(2)}, u32[]{:S(2)}) collective-permute-start(f32[5,32,10,128]{3,1,2,0:T(8,128)S(1)} %copy.23), channel_id=1, source_target_pairs={{0,4},{4,8},{8,12},{12,0},{1,5},{5,9},{9,13},{13,1},{2,6},{6,10},{... | collective-permute-start | bytes 2457608 | tf_op jit(solution)/shard_map/ppermute | solution.py:23
  7.6 20.7 %collective-permute-start.1 = (f32[5,32,10,128]{3,1,2,0:T(8,128)S(1)}, f32[5,32,10,128]{3,1,2,0:T(8,128)S(1)}, u32[]{:S(2)}, u32[]{:S(2)}) collective-permute-start(f32[5,32,10,128]{3,1,2,0:T(8,128)S(1)} %copy.24), channel_id=1, source_target_pairs={{4,0},{8,4},{12,8},{0,12},{5,1},{9,5},{13,9},{1,13},{6,2},{10,6},{... | collective-permute-start | bytes 2457608 | tf_op jit(solution)/shard_map/ppermute | solution.py:24
  29.4 2.1 %copy-start = (f32[5,32,52,128]{3,2,1,0:T(8,128)}, f32[5,32,52,128]{3,2,1,0:T(8,128)S(1)}, u32[]{:S(2)}) copy-start(f32[5,32,52,128]{3,2,1,0:T(8,128)S(1)} %pad_maximum_fusion) | copy-start | bytes 12779524
  33.4 23.0 %collective-permute-start.2 = (f32[7,46,128]{2,1,0:T(8,128)}, f32[7,46,128]{2,1,0:T(8,128)S(1)}, u32[]{:S(2)}, u32[]{:S(2)}) collective-permute-start(f32[7,46,128]{2,1,0:T(8,128)} %get-tuple-element.29), channel_id=1, source_target_pairs={{0,16},{16,32},{32,48},{48,64},{64,80},{80,96},{96,112},{112,128},... | collective-permute-start | bytes 494600 | tf_op jit(solution)/shard_map/ppermute | solution.py:184
  43.8 15.7 %collective-permute-start.3 = (f32[7,46,128]{2,1,0:T(8,128)}, f32[7,46,128]{2,1,0:T(8,128)}, u32[]{:S(2)}, u32[]{:S(2)}) collective-permute-start(f32[7,46,128]{2,1,0:T(8,128)} %get-tuple-element.28), channel_id=1, source_target_pairs={{16,0},{32,16},{48,32},{64,48},{80,64},{96,80},{112,96},{128,112},... | collective-permute-start | bytes 494600 | tf_op jit(solution)/shard_map/ppermute | solution.py:185
  46.4 7.5 %collective-permute-start.4 = (f32[32,46,3]{1,0,2:T(8,128)S(1)}, f32[32,46,3]{1,0,2:T(8,128)S(1)}, u32[]{:S(2)}, u32[]{:S(2)}) collective-permute-start(f32[32,46,3]{1,0,2:T(8,128)S(1)} %copy.27), channel_id=1, source_target_pairs={{0,1},{1,2},{2,3},{3,0},{4,5},{5,6},{6,7},{7,4},{8,9},{9,10},{10,1... | collective-permute-start | bytes 53000 | tf_op jit(solution)/shard_map/ppermute | solution.py:63
  49.4 5.8 %collective-permute-start.5 = (f32[32,46,3]{1,0,2:T(8,128)S(1)}, f32[32,46,3]{1,0,2:T(8,128)S(1)}, u32[]{:S(2)}, u32[]{:S(2)}) collective-permute-start(f32[32,46,3]{1,0,2:T(8,128)S(1)} %copy.29), channel_id=1, source_target_pairs={{1,0},{2,1},{3,2},{0,3},{5,4},{6,5},{7,6},{4,7},{9,8},{10,9},{11,1... | collective-permute-start | bytes 53000 | tf_op jit(solution)/shard_map/ppermute | solution.py:64
  75.4 23.2 %collective-permute-start.6 = (f32[3,40,128]{2,1,0:T(8,128)S(1)}, f32[3,40,128]{2,1,0:T(8,128)S(1)}, u32[]{:S(2)}, u32[]{:S(2)}) collective-permute-start(f32[3,40,128]{2,1,0:T(8,128)S(1)} %get-tuple-element.45), channel_id=1, source_target_pairs={{0,16},{16,32},{32,48},{48,64},{64,80},{80,96},{96,112},{112,128},... | collective-permute-start | bytes 184328 | tf_op jit(solution)/shard_map/ppermute | solution.py:154
  85.5 13.1 %collective-permute-start.7 = (f32[3,40,128]{2,1,0:T(8,128)S(1)}, f32[3,40,128]{2,1,0:T(8,128)S(1)}, u32[]{:S(2)}, u32[]{:S(2)}) collective-permute-start(f32[3,40,128]{2,1,0:T(8,128)S(1)} %get-tuple-element.44), channel_id=1, source_target_pairs={{16,0},{32,16},{48,32},{64,48},{80,64},{96,80},{112,96},{128,112},... | collective-permute-start | bytes 184328 | tf_op jit(solution)/shard_map/ppermute | solution.py:155
  88.0 8.1 %collective-permute-start.8 = (f32[32,40,3]{1,0,2:T(8,128)S(1)}, f32[32,40,3]{1,0,2:T(8,128)S(1)}, u32[]{:S(2)}, u32[]{:S(2)}) collective-permute-start(f32[32,40,3]{1,0,2:T(8,128)S(1)} %copy.31), channel_id=1, source_target_pairs={{0,1},{1,2},{2,3},{3,0},{4,5},{5,6},{6,7},{7,4},{8,9},{9,10},{10,1... | collective-permute-start | bytes 46088 | tf_op jit(solution)/shard_map/ppermute | solution.py:63
  90.8 6.6 %collective-permute-start.9 = (f32[32,40,3]{1,0,2:T(8,128)}, f32[32,40,3]{1,0,2:T(8,128)S(1)}, u32[]{:S(2)}, u32[]{:S(2)}) collective-permute-start(f32[32,40,3]{1,0,2:T(8,128)} %copy.33), channel_id=1, source_target_pairs={{1,0},{2,1},{3,2},{0,3},{5,4},{6,5},{7,6},{4,7},{9,8},{10,9},{11,1... | collective-permute-start | bytes 46088 | tf_op jit(solution)/shard_map/ppermute | solution.py:64
  111.7 12.8 %collective-permute-start.10 = (f32[4,40,128]{2,1,0:T(8,128)S(1)}, f32[4,40,128]{2,1,0:T(8,128)S(1)}, u32[]{:S(2)}, u32[]{:S(2)}) collective-permute-start(f32[4,40,128]{2,1,0:T(8,128)S(1)} %get-tuple-element.54), channel_id=1, source_target_pairs={{0,16},{16,32},{32,48},{48,64},{64,80},{80,96},{96,112},{112,128},... | collective-permute-start | bytes 245768 | tf_op jit(solution)/shard_map/ppermute | solution.py:154
  122.5 12.0 %collective-permute-start.11 = (f32[4,40,128]{2,1,0:T(8,128)S(1)}, f32[4,40,128]{2,1,0:T(8,128)S(1)}, u32[]{:S(2)}, u32[]{:S(2)}) collective-permute-start(f32[4,40,128]{2,1,0:T(8,128)S(1)} %get-tuple-element.55), channel_id=1, source_target_pairs={{16,0},{32,16},{48,32},{64,48},{80,64},{96,80},{112,96},{128,112},... | collective-permute-start | bytes 245768 | tf_op jit(solution)/shard_map/ppermute | solution.py:155
  134.5 11.3 %copy-start.5 = (s32[4]{0:T(128)S(1)}, s32[4]{0:T(128)}, u32[]{:S(2)}) copy-start(s32[4]{0:T(128)} %param.7) | copy-start | bytes 52
  137.1 11.5 %collective-permute-start.12 = (f32[34,34,3]{1,0,2:T(8,128)S(1)}, f32[34,34,3]{1,0,2:T(8,128)S(1)}, u32[]{:S(2)}, u32[]{:S(2)}) collective-permute-start(f32[34,34,3]{1,0,2:T(8,128)S(1)} %copy.35), channel_id=1, source_target_pairs={{0,1},{1,2},{2,3},{3,0},{4,5},{5,6},{6,7},{7,4},{8,9},{9,10},{10,1... | collective-permute-start | bytes 41624 | tf_op jit(solution)/shard_map/ppermute | solution.py:63
  140.0 8.9 %collective-permute-start.13 = (f32[34,34,3]{1,0,2:T(8,128)}, f32[34,34,3]{1,0,2:T(8,128)S(1)}, u32[]{:S(2)}, u32[]{:S(2)}) collective-permute-start(f32[34,34,3]{1,0,2:T(8,128)} %copy.37), channel_id=1, source_target_pairs={{1,0},{2,1},{3,2},{0,3},{5,4},{6,5},{7,6},{4,7},{9,8},{10,9},{11,1... | collective-permute-start | bytes 41624 | tf_op jit(solution)/shard_map/ppermute | solution.py:64
  149.3 1.5 copy-start.1
  164.4 0.8 copy-start.2
  171.4 13.1 %copy-start.3 = (f32[32,34,128]{2,1,0:T(8,128)S(1)}, f32[32,34,128]{2,1,0:T(8,128)}, u32[]{:S(2)}) copy-start(f32[32,34,128]{2,1,0:T(8,128)} %copy-done.2) | copy-start | bytes 1671172
  172.8 12.5 %all-to-all-start = ((f32[4,1,4096]{2,1,0:T(1,128)}), f32[4,1,4096]{2,1,0:T(1,128)S(1)}, u32[]{:S(2)}, u32[]{:S(2)}) async-start(f32[4,1,4096]{2,1,0:T(1,128)} %reshape.189), calls=%async_computation | async-start | bytes 131072 | tf_op jit(solution)/shard_map/all_to_all | solution.py:240

commit v13 on v10

--- a/solution.py
+++ b/solution.py
@@ -124,7 +124,7 @@
         ascending, depth[:, None] < depth[None, :], depth[:, None] > depth[None, :]
     ).astype(jnp.float32)
     flat_logs = log_clear.reshape(-1, CZ)
-    before = jnp.dot(flat_logs, ahead, precision=lax.Precision.HIGHEST).reshape(log_clear.shape)
+    before = jnp.dot(flat_logs, ahead, precision=lax.Precision.HIGH).reshape(log_clear.shape)
     weight = jnp.exp(before) * opacity
     bright = jnp.tanh(samples)
     red = jnp.sum(weight * (0.5 + 0.5 * bright), -1)

time: 188 us -> 187 us (level)
  no operation moved by 1% of the time
where the time goes in v13:
time: 187 us; the launch traced here: 186 us
  starting transfers between devices  68.8 us (37%)
  other arithmetic  49.7 us (27%)
  waiting for transfers between devices  36.6 us (20%)
  local copies, waits for them, and re-layouts  22.6 us (12%)
  matrix products  5.36 us (3%)
  between operations  3.14 us (2%)
    ppermute x2, starting transfers between devices, x_faces(): before = lax.ppermute(x[length - width:], 'gx', up)  20.9 us
    ppermute x3, starting transfers between devices, z_faces(): after = lax.ppermute(x[:, :, :SPAN], 'gz', down)  15.4 us
    select_n x3, other arithmetic, part(): return jnp.where(flag > 0, advanced, level)  15.1 us
    add x1, other arithmetic, shards(): section_one = inner + time_step * local_rate(padded, speed_one)  15 us
    ppermute x1, waiting for transfers between devices, exchange(): after = lax.ppermute(first, axis, down)  14.7 us
    add x1, other arithmetic, shards(): 0.75 * level_ext[:, 2 * SPAN:-2 * SPAN] + 0.25 * (inner + time_step * rate)  13 us
    ppermute x1, starting transfers between devices, shards(): before = lax.ppermute(last, 'gx', up)  10.4 us
    ppermute x2, waiting for transfers between devices, x_faces(): after = lax.ppermute(x[:width], 'gx', down)  9.96 us
  transfers between devices with their start and end apart: 15, of which 7 were waited for; matrix products, arithmetic and copies ran while one was open for 6% of the time, Pallas kernels for 0%

profile of v13, /device:TPU:135, one launch (start us, length us, event | category | flops | bytes accessed | tf_op | source)
XLA Modules:
  0.0 186.2 jit_solution(2061402217357418076)
XLA Ops:
  1.4 1.1 bitcast_dynamic-update-slice_fusion
  2.4 1.0 convert_dynamic-update-slice_fusion.2
  4.1 4.6 %collective-permute-start.1 = (f32[5,32,10,128]{3,1,2,0:T(8,128)S(1)}, f32[5,32,10,128]{3,1,2,0:T(8,128)S(1)}, u32[]{:S(2)}, u32[]{:S(2)}) collective-permute-start(f32[5,32,10,128]{3,1,2,0:T(8,128)S(1)} %copy.8), channel_id=1, source_target_pairs={{4,0},{8,4},{12,8},{0,12},{5,1},{9,5},{13,9},{1,13},{6,2},{10,6},{... | collective-permute-start | bytes 2457608 | tf_op jit(solution)/shard_map/ppermute | solution.py:24
  9.0 1.9 %collective-permute-start = (f32[5,32,10,128]{3,1,2,0:T(8,128)S(1)}, f32[5,32,10,128]{3,1,2,0:T(8,128)S(1)}, u32[]{:S(2)}, u32[]{:S(2)}) collective-permute-start(f32[5,32,10,128]{3,1,2,0:T(8,128)S(1)} %copy.7), channel_id=1, source_target_pairs={{0,4},{4,8},{8,12},{12,0},{1,5},{5,9},{9,13},{13,1},{2,6},{6,10},{... | collective-permute-start | bytes 2457608 | tf_op jit(solution)/shard_map/ppermute | solution.py:23
  11.0 14.7 %collective-permute-done.1 = f32[5,32,10,128]{3,1,2,0:T(8,128)S(1)} collective-permute-done((f32[5,32,10,128]{3,1,2,0:T(8,128)S(1)}, f32[5,32,10,128]{3,1,2,0:T(8,128)S(1)}, u32[]{:S(2)}, u32[]{:S(2)}) %collective-permute-start.1) | collective-permute-done | bytes 819232 | tf_op jit(solution)/shard_map/ppermute | solution.py:24
  26.2 4.8 %collective-permute-done = f32[5,32,10,128]{3,1,2,0:T(8,128)S(1)} collective-permute-done((f32[5,32,10,128]{3,1,2,0:T(8,128)S(1)}, f32[5,32,10,128]{3,1,2,0:T(8,128)S(1)}, u32[]{:S(2)}, u32[]{:S(2)}) %collective-permute-start) | collective-permute-done | bytes 819232 | tf_op jit(solution)/shard_map/ppermute | solution.py:23
  32.1 0.8 slice_dynamic-update-slice_fusion
  32.9 1.1 constant_dynamic-update-slice_fusion.7
  34.2 0.6 constant_dynamic-update-slice_fusion.6
  36.0 10.4 %collective-permute-start.2 = (f32[7,46,128]{2,1,0:T(8,128)}, f32[7,46,128]{2,1,0:T(8,128)S(1)}, u32[]{:S(2)}, u32[]{:S(2)}) collective-permute-start(f32[7,46,128]{2,1,0:T(8,128)} %get-tuple-element.19), channel_id=1, source_target_pairs={{0,16},{16,32},{32,48},{48,64},{64,80},{80,96},{96,112},{112,128},... | collective-permute-start | bytes 494600 | tf_op jit(solution)/shard_map/ppermute | solution.py:184
  46.4 1.9 %collective-permute-start.3 = (f32[7,46,128]{2,1,0:T(8,128)}, f32[7,46,128]{2,1,0:T(8,128)}, u32[]{:S(2)}, u32[]{:S(2)}) collective-permute-start(f32[7,46,128]{2,1,0:T(8,128)} %get-tuple-element.18), channel_id=1, source_target_pairs={{16,0},{32,16},{48,32},{64,48},{80,64},{96,80},{112,96},{128,112},... | collective-permute-start | bytes 494600 | tf_op jit(solution)/shard_map/ppermute | solution.py:185
  49.0 2.6 %collective-permute-start.4 = (f32[32,46,3]{1,0,2:T(8,128)S(1)}, f32[32,46,3]{1,0,2:T(8,128)S(1)}, u32[]{:S(2)}, u32[]{:S(2)}) collective-permute-start(f32[32,46,3]{1,0,2:T(8,128)S(1)} %copy.11), channel_id=1, source_target_pairs={{0,1},{1,2},{2,3},{3,0},{4,5},{5,6},{6,7},{7,4},{8,9},{9,10},{10,1... | collective-permute-start | bytes 53000 | tf_op jit(solution)/shard_map/ppermute | solution.py:63
  52.0 4.4 %collective-permute-start.5 = (f32[32,46,3]{1,0,2:T(8,128)S(1)}, f32[32,46,3]{1,0,2:T(8,128)S(1)}, u32[]{:S(2)}, u32[]{:S(2)}) collective-permute-start(f32[32,46,3]{1,0,2:T(8,128)S(1)} %copy.13), channel_id=1, source_target_pairs={{1,0},{2,1},{3,2},{0,3},{5,4},{6,5},{7,6},{4,7},{9,8},{10,9},{11,1... | collective-permute-start | bytes 53000 | tf_op jit(solution)/shard_map/ppermute | solution.py:64
  56.5 1.3 copy.12
  57.8 1.3 copy.14
  59.1 3.0 %collective-permute-done.3 = f32[7,46,128]{2,1,0:T(8,128)} collective-permute-done((f32[7,46,128]{2,1,0:T(8,128)}, f32[7,46,128]{2,1,0:T(8,128)}, u32[]{:S(2)}, u32[]{:S(2)}) %collective-permute-start.3) | collective-permute-done | bytes 164896 | tf_op jit(solution)/shard_map/ppermute | solution.py:185
  62.1 0.9 slice.985
  63.0 15.0 %fusion.21 = f32[32,46,128]{2,1,0:T(8,128)S(1)} fusion(f32[32,46,128]{2,1,0:T(8,128)S(1)} %slice.976, f32[32,46,3]{2,1,0:T(8,128)} %copy.14, f32[32,46,3]{2,1,0:T(8,128)} %copy.12, f32[5,32,52,128]{3,2,1,0:T(8,128)} %copy-done, f32[32,52,128]{2,1,0:T(8,128)S(1)} %slice_bitcast_fusion, f32[3,46,128]{2,1,0:T(8,128)S(1)} %slice.979, f32[3,46,128]{2,1,0:T(8,128)S(1)} %slice.985), kind=kLoop, calls=%fused_computation.99 | loop fusion | flops 79511552 | bytes 8466944 | tf_op jit(solution)/shard_map/add | solution.py:191
  78.0 10.1 %collective-permute-start.6 = (f32[3,40,128]{2,1,0:T(8,128)S(1)}, f32[3,40,128]{2,1,0:T(8,128)S(1)}, u32[]{:S(2)}, u32[]{:S(2)}) collective-permute-start(f32[3,40,128]{2,1,0:T(8,128)S(1)} %get-tuple-element.35), channel_id=1, source_target_pairs={{0,16},{16,32},{32,48},{48,64},{64,80},{80,96},{96,112},{112,128},... | collective-permute-start | bytes 184328 | tf_op jit(solution)/shard_map/ppermute | solution.py:154
  88.2 1.9 %collective-permute-start.7 = (f32[3,40,128]{2,1,0:T(8,128)S(1)}, f32[3,40,128]{2,1,0:T(8,128)S(1)}, u32[]{:S(2)}, u32[]{:S(2)}) collective-permute-start(f32[3,40,128]{2,1,0:T(8,128)S(1)} %get-tuple-element.34), channel_id=1, source_target_pairs={{16,0},{32,16},{48,32},{64,48},{80,64},{96,80},{112,96},{128,112},... | collective-permute-start | bytes 184328 | tf_op jit(solution)/shard_map/ppermute | solution.py:155
  90.6 1.9 %collective-permute-start.8 = (f32[32,40,3]{1,0,2:T(8,128)S(1)}, f32[32,40,3]{1,0,2:T(8,128)S(1)}, u32[]{:S(2)}, u32[]{:S(2)}) collective-permute-start(f32[32,40,3]{1,0,2:T(8,128)S(1)} %copy.15), channel_id=1, source_target_pairs={{0,1},{1,2},{2,3},{3,0},{4,5},{5,6},{6,7},{7,4},{8,9},{9,10},{10,1... | collective-permute-start | bytes 46088 | tf_op jit(solution)/shard_map/ppermute | solution.py:63
  92.6 0.9 copy.17
  93.5 5.1 %collective-permute-start.9 = (f32[32,40,3]{1,0,2:T(8,128)}, f32[32,40,3]{1,0,2:T(8,128)S(1)}, u32[]{:S(2)}, u32[]{:S(2)}) collective-permute-start(f32[32,40,3]{1,0,2:T(8,128)} %copy.17), channel_id=1, source_target_pairs={{1,0},{2,1},{3,2},{0,3},{5,4},{6,5},{7,6},{4,7},{9,8},{10,9},{11,1... | collective-permute-start | bytes 46088 | tf_op jit(solution)/shard_map/ppermute | solution.py:64
  98.7 1.2 copy.16
  100.1 1.2 copy.18
  101.3 13.0 %fusion.174 = f32[32,40,128]{2,1,0:T(8,128)S(1)} fusion(f32[32,52,128]{2,1,0:T(8,128)S(1)} %slice_bitcast_fusion, f32[32,40,128]{2,1,0:T(8,128)S(1)} %slice.1008, f32[32,40,3]{2,1,0:T(8,128)} %copy.18, f32[32,40,3]{2,1,0:T(8,128)} %copy.16, f32[5,32,52,128]{3,2,1,0:T(8,128)} %copy-done, f32[32,46,128]{2,1,0:T(8,128)S(1)} %fusion.21, ...), kind=kLoop, calls=%fused_computation.299 | loop fusion | flops 69632000 | bytes 8017920 | tf_op jit(solution)/shard_map/add | solution.py:193
  114.3 10.8 %collective-permute-start.10 = (f32[4,40,128]{2,1,0:T(8,128)S(1)}, f32[4,40,128]{2,1,0:T(8,128)S(1)}, u32[]{:S(2)}, u32[]{:S(2)}) collective-permute-start(f32[4,40,128]{2,1,0:T(8,128)S(1)} %get-tuple-element.44), channel_id=1, source_target_pairs={{0,16},{16,32},{32,48},{48,64},{64,80},{80,96},{96,112},{112,128},... | collective-permute-start | bytes 245768 | tf_op jit(solution)/shard_map/ppermute | solution.py:154
  125.1 1.9 %collective-permute-start.11 = (f32[4,40,128]{2,1,0:T(8,128)S(1)}, f32[4,40,128]{2,1,0:T(8,128)S(1)}, u32[]{:S(2)}, u32[]{:S(2)}) collective-permute-start(f32[4,40,128]{2,1,0:T(8,128)S(1)} %get-tuple-element.45), channel_id=1, source_target_pairs={{16,0},{32,16},{48,32},{64,48},{80,64},{96,80},{112,96},{128,112},... | collective-permute-start | bytes 245768 | tf_op jit(solution)/shard_map/ppermute | solution.py:155
  127.2 10.0 %collective-permute-done.11 = f32[4,40,128]{2,1,0:T(8,128)S(1)} collective-permute-done((f32[4,40,128]{2,1,0:T(8,128)S(1)}, f32[4,40,128]{2,1,0:T(8,128)S(1)}, u32[]{:S(2)}, u32[]{:S(2)}) %collective-permute-start.11) | collective-permute-done | bytes 81952 | tf_op jit(solution)/shard_map/ppermute | solution.py:155
  137.2 1.1 fusion.456
  138.3 1.5 copy.19
  139.8 1.9 %collective-permute-start.12 = (f32[34,34,3]{1,0,2:T(8,128)S(1)}, f32[34,34,3]{1,0,2:T(8,128)S(1)}, u32[]{:S(2)}, u32[]{:S(2)}) collective-permute-start(f32[34,34,3]{1,0,2:T(8,128)S(1)} %copy.19), channel_id=1, source_target_pairs={{0,1},{1,2},{2,3},{3,0},{4,5},{5,6},{6,7},{7,4},{8,9},{9,10},{10,1... | collective-permute-start | bytes 41624 | tf_op jit(solution)/shard_map/ppermute | solution.py:63
  141.7 1.0 copy.21
  142.7 5.8 %collective-permute-start.13 = (f32[34,34,3]{1,0,2:T(8,128)}, f32[34,34,3]{1,0,2:T(8,128)S(1)}, u32[]{:S(2)}, u32[]{:S(2)}) collective-permute-start(f32[34,34,3]{1,0,2:T(8,128)} %copy.21), channel_id=1, source_target_pairs={{1,0},{2,1},{3,2},{0,3},{5,4},{6,5},{7,6},{4,7},{9,8},{10,9},{11,1... | collective-permute-start | bytes 41624 | tf_op jit(solution)/shard_map/ppermute | solution.py:64
  150.3 0.9 slice.1059
  152.0 1.5 add_select_fusion
  153.8 13.2 %fusion.181 = f32[32,34,128]{2,1,0:T(8,128)S(1)} fusion(f32[34,34,3]{2,1,0:T(8,128)S(1)} %copy.22, f32[34,34,128]{2,1,0:T(8,128)S(1)} %copy-done.1, f32[34,34,3]{2,1,0:T(8,128)S(1)} %copy.20, f32[5,32,52,128]{3,2,1,0:T(8,128)} %copy-done, f32[32,40,128]{2,1,0:T(8,128)S(1)} %fusion.174, f32[4,40,128]{2,1,0:T(8,128)S(1)} %collective-permute-done.11, ...), kind=kLoop, calls=%fused_computation.308 | loop fusion | flops 59465728 | bytes 10936320 | tf_op jit(solution)/shard_map/jit(_where)/select_n | solution.py:207
  167.9 1.0 multiply_reduce_fusion.7
  168.9 1.0 multiply_reduce_fusion.5
  170.0 1.0 multiply_reduce_fusion.3
  171.0 1.0 multiply_reduce_fusion.1
  172.2 1.3 copy.23
  173.5 0.7 copy.24
  174.2 0.8 reshape.120
  175.0 3.3 %all-to-all-start = ((f32[4,1,4096]{2,1,0:T(1,128)}), f32[4,1,4096]{2,1,0:T(1,128)S(1)}, u32[]{:S(2)}, u32[]{:S(2)}) async-start(f32[4,1,4096]{2,1,0:T(1,128)} %reshape.120), calls=%async_computation | async-start | bytes 131072 | tf_op jit(solution)/shard_map/all_to_all | solution.py:240
  178.3 0.9 slice.1073
  179.1 3.7 %all-to-all-done = f32[4,1,4096]{2,1,0:T(1,128)S(1)} async-done(((f32[4,1,4096]{2,1,0:T(1,128)}), f32[4,1,4096]{2,1,0:T(1,128)S(1)}, u32[]{:S(2)}, u32[]{:S(2)}) %all-to-all-start) | async-done | bytes 65568 | tf_op jit(solution)/shard_map/all_to_all | solution.py:240
  183.3 0.8 reduce
  (71 shorter events, 11.1 us)
Async XLA Ops:
  0.6 2.8 %copy-start.4 = (bf16[3,32,32,128]{3,2,1,0:T(8,128)(2,1)S(1)}, bf16[3,32,32,128]{3,2,1,0:T(8,128)(2,1)}, u32[]{:S(2)}) copy-start(bf16[3,32,32,128]{3,2,1,0:T(8,128)(2,1)} %param.5) | copy-start | bytes 2359300
  4.1 21.6 %collective-permute-start.1 = (f32[5,32,10,128]{3,1,2,0:T(8,128)S(1)}, f32[5,32,10,128]{3,1,2,0:T(8,128)S(1)}, u32[]{:S(2)}, u32[]{:S(2)}) collective-permute-start(f32[5,32,10,128]{3,1,2,0:T(8,128)S(1)} %copy.8), channel_id=1, source_target_pairs={{4,0},{8,4},{12,8},{0,12},{5,1},{9,5},{13,9},{1,13},{6,2},{10,6},{... | collective-permute-start | bytes 2457608 | tf_op jit(solution)/shard_map/ppermute | solution.py:24
  9.0 22.0 %collective-permute-start = (f32[5,32,10,128]{3,1,2,0:T(8,128)S(1)}, f32[5,32,10,128]{3,1,2,0:T(8,128)S(1)}, u32[]{:S(2)}, u32[]{:S(2)}) collective-permute-start(f32[5,32,10,128]{3,1,2,0:T(8,128)S(1)} %copy.7), channel_id=1, source_target_pairs={{0,4},{4,8},{8,12},{12,0},{1,5},{5,9},{9,13},{13,1},{2,6},{6,10},{... | collective-permute-start | bytes 2457608 | tf_op jit(solution)/shard_map/ppermute | solution.py:23
  32.0 2.1 %copy-start = (f32[5,32,52,128]{3,2,1,0:T(8,128)}, f32[5,32,52,128]{3,2,1,0:T(8,128)S(1)}, u32[]{:S(2)}) copy-start(f32[5,32,52,128]{3,2,1,0:T(8,128)S(1)} %pad_maximum_fusion) | copy-start | bytes 12779524
  36.0 23.0 %collective-permute-start.2 = (f32[7,46,128]{2,1,0:T(8,128)}, f32[7,46,128]{2,1,0:T(8,128)S(1)}, u32[]{:S(2)}, u32[]{:S(2)}) collective-permute-start(f32[7,46,128]{2,1,0:T(8,128)} %get-tuple-element.19), channel_id=1, source_target_pairs={{0,16},{16,32},{32,48},{48,64},{64,80},{80,96},{96,112},{112,128},... | collective-permute-start | bytes 494600 | tf_op jit(solution)/shard_map/ppermute | solution.py:184
  46.4 15.7 %collective-permute-start.3 = (f32[7,46,128]{2,1,0:T(8,128)}, f32[7,46,128]{2,1,0:T(8,128)}, u32[]{:S(2)}, u32[]{:S(2)}) collective-permute-start(f32[7,46,128]{2,1,0:T(8,128)} %get-tuple-element.18), channel_id=1, source_target_pairs={{16,0},{32,16},{48,32},{64,48},{80,64},{96,80},{112,96},{128,112},... | collective-permute-start | bytes 494600 | tf_op jit(solution)/shard_map/ppermute | solution.py:185
  49.0 7.5 %collective-permute-start.4 = (f32[32,46,3]{1,0,2:T(8,128)S(1)}, f32[32,46,3]{1,0,2:T(8,128)S(1)}, u32[]{:S(2)}, u32[]{:S(2)}) collective-permute-start(f32[32,46,3]{1,0,2:T(8,128)S(1)} %copy.11), channel_id=1, source_target_pairs={{0,1},{1,2},{2,3},{3,0},{4,5},{5,6},{6,7},{7,4},{8,9},{9,10},{10,1... | collective-permute-start | bytes 53000 | tf_op jit(solution)/shard_map/ppermute | solution.py:63
  52.0 5.8 %collective-permute-start.5 = (f32[32,46,3]{1,0,2:T(8,128)S(1)}, f32[32,46,3]{1,0,2:T(8,128)S(1)}, u32[]{:S(2)}, u32[]{:S(2)}) collective-permute-start(f32[32,46,3]{1,0,2:T(8,128)S(1)} %copy.13), channel_id=1, source_target_pairs={{1,0},{2,1},{3,2},{0,3},{5,4},{6,5},{7,6},{4,7},{9,8},{10,9},{11,1... | collective-permute-start | bytes 53000 | tf_op jit(solution)/shard_map/ppermute | solution.py:64
  78.0 23.2 %collective-permute-start.6 = (f32[3,40,128]{2,1,0:T(8,128)S(1)}, f32[3,40,128]{2,1,0:T(8,128)S(1)}, u32[]{:S(2)}, u32[]{:S(2)}) collective-permute-start(f32[3,40,128]{2,1,0:T(8,128)S(1)} %get-tuple-element.35), channel_id=1, source_target_pairs={{0,16},{16,32},{32,48},{48,64},{64,80},{80,96},{96,112},{112,128},... | collective-permute-start | bytes 184328 | tf_op jit(solution)/shard_map/ppermute | solution.py:154
  88.2 13.1 %collective-permute-start.7 = (f32[3,40,128]{2,1,0:T(8,128)S(1)}, f32[3,40,128]{2,1,0:T(8,128)S(1)}, u32[]{:S(2)}, u32[]{:S(2)}) collective-permute-start(f32[3,40,128]{2,1,0:T(8,128)S(1)} %get-tuple-element.34), channel_id=1, source_target_pairs={{16,0},{32,16},{48,32},{64,48},{80,64},{96,80},{112,96},{128,112},... | collective-permute-start | bytes 184328 | tf_op jit(solution)/shard_map/ppermute | solution.py:155
  90.6 8.1 %collective-permute-start.8 = (f32[32,40,3]{1,0,2:T(8,128)S(1)}, f32[32,40,3]{1,0,2:T(8,128)S(1)}, u32[]{:S(2)}, u32[]{:S(2)}) collective-permute-start(f32[32,40,3]{1,0,2:T(8,128)S(1)} %copy.15), channel_id=1, source_target_pairs={{0,1},{1,2},{2,3},{3,0},{4,5},{5,6},{6,7},{7,4},{8,9},{9,10},{10,1... | collective-permute-start | bytes 46088 | tf_op jit(solution)/shard_map/ppermute | solution.py:63
  93.5 6.6 %collective-permute-start.9 = (f32[32,40,3]{1,0,2:T(8,128)}, f32[32,40,3]{1,0,2:T(8,128)S(1)}, u32[]{:S(2)}, u32[]{:S(2)}) collective-permute-start(f32[32,40,3]{1,0,2:T(8,128)} %copy.17), channel_id=1, source_target_pairs={{1,0},{2,1},{3,2},{0,3},{5,4},{6,5},{7,6},{4,7},{9,8},{10,9},{11,1... | collective-permute-start | bytes 46088 | tf_op jit(solution)/shard_map/ppermute | solution.py:64
  114.3 12.8 %collective-permute-start.10 = (f32[4,40,128]{2,1,0:T(8,128)S(1)}, f32[4,40,128]{2,1,0:T(8,128)S(1)}, u32[]{:S(2)}, u32[]{:S(2)}) collective-permute-start(f32[4,40,128]{2,1,0:T(8,128)S(1)} %get-tuple-element.44), channel_id=1, source_target_pairs={{0,16},{16,32},{32,48},{48,64},{64,80},{80,96},{96,112},{112,128},... | collective-permute-start | bytes 245768 | tf_op jit(solution)/shard_map/ppermute | solution.py:154
  125.1 12.0 %collective-permute-start.11 = (f32[4,40,128]{2,1,0:T(8,128)S(1)}, f32[4,40,128]{2,1,0:T(8,128)S(1)}, u32[]{:S(2)}, u32[]{:S(2)}) collective-permute-start(f32[4,40,128]{2,1,0:T(8,128)S(1)} %get-tuple-element.45), channel_id=1, source_target_pairs={{16,0},{32,16},{48,32},{64,48},{80,64},{96,80},{112,96},{128,112},... | collective-permute-start | bytes 245768 | tf_op jit(solution)/shard_map/ppermute | solution.py:155
  137.2 11.3 %copy-start.5 = (s32[4]{0:T(128)S(1)}, s32[4]{0:T(128)}, u32[]{:S(2)}) copy-start(s32[4]{0:T(128)} %param.7) | copy-start | bytes 52
  139.8 11.5 %collective-permute-start.12 = (f32[34,34,3]{1,0,2:T(8,128)S(1)}, f32[34,34,3]{1,0,2:T(8,128)S(1)}, u32[]{:S(2)}, u32[]{:S(2)}) collective-permute-start(f32[34,34,3]{1,0,2:T(8,128)S(1)} %copy.19), channel_id=1, source_target_pairs={{0,1},{1,2},{2,3},{3,0},{4,5},{5,6},{6,7},{7,4},{8,9},{9,10},{10,1... | collective-permute-start | bytes 41624 | tf_op jit(solution)/shard_map/ppermute | solution.py:63
  142.7 8.9 %collective-permute-start.13 = (f32[34,34,3]{1,0,2:T(8,128)}, f32[34,34,3]{1,0,2:T(8,128)S(1)}, u32[]{:S(2)}, u32[]{:S(2)}) collective-permute-start(f32[34,34,3]{1,0,2:T(8,128)} %copy.21), channel_id=1, source_target_pairs={{1,0},{2,1},{3,2},{0,3},{5,4},{6,5},{7,6},{4,7},{9,8},{10,9},{11,1... | collective-permute-start | bytes 41624 | tf_op jit(solution)/shard_map/ppermute | solution.py:64
  152.0 1.5 copy-start.1
  167.1 0.8 copy-start.2
  173.5 4.7 %copy-start.3 = (f32[32,34,128]{2,1,0:T(8,128)S(1)}, f32[32,34,128]{2,1,0:T(8,128)}, u32[]{:S(2)}) copy-start(f32[32,34,128]{2,1,0:T(8,128)} %copy-done.2) | copy-start | bytes 1671172
  175.0 7.9 %all-to-all-start = ((f32[4,1,4096]{2,1,0:T(1,128)}), f32[4,1,4096]{2,1,0:T(1,128)S(1)}, u32[]{:S(2)}, u32[]{:S(2)}) async-start(f32[4,1,4096]{2,1,0:T(1,128)} %reshape.120), calls=%async_computation | async-start | bytes 131072 | tf_op jit(solution)/shard_map/all_to_all | solution.py:240
